TPU v7x, 256 devices: a whole 4x4x8 slice. The times are simulated.
256 devices in a mesh: sky: 64 (over y, z, core), visit: 4 (over x).
Axes of the slice: x: 4, y: 4, z: 8, core: 2. Of those that a mesh axis runs over, the one named last changes fastest.
Arguments:
- science: float32 [32, 4096, 256], P('visit', 'sky'), may hold values from -6 to 6
- inv_variance: float32 [32, 4096, 256], P('visit', 'sky'), may hold values from 0.3 to 3
- psf_kernel: float32 [11, 11], replicated, may hold values from 0.01 to 0.12
- offsets: int32 [32, 16], replicated, may hold values from -2 to 2, as said below
Outputs:
- likelihood: float32 [16, 4096, 256], P(None, ('sky', 'visit'))
Inputs may be any that keep to these rules, and one draw needn't show every extreme that they name: offsets[0, k] is 0 for every velocity; offsets[31, 0] is 2 and offsets[31, 1] is -2.
All inputs are finite; a program needn't handle non-finite values.
Results may differ from a plain program's by a relative error of at most 0.0001.
Values sent between devices are 32-bit elements; how exact they have to be, the bound alone decides.
No kernel may reach another device: no remote copies, remote signals or barrier semaphores. Data moves between devices by JAX's collectives and lax.ppermute only.
A program may use at most 64 MiB of HBM per device.

v0:
```python
import jax
import jax.numpy as jnp
from jax import lax
from jax.sharding import PartitionSpec as P

BR = 8
MAXOFF = 2


def padded_2(block, sides, width):
    for axis, dim in sides:
        count = lax.axis_size(axis)
        forward = [(i, i + 1) for i in range(count - 1)]
        backward = [(target, source) for source, target in forward]
        low = lax.ppermute(
            lax.slice_in_dim(block, block.shape[dim] - width, None, axis=dim), axis, forward
        )
        high = lax.ppermute(lax.slice_in_dim(block, 0, width, axis=dim), axis, backward)
        block = jnp.concatenate([low, block, high], axis=dim)
    return block


def correlate(bordered, psf_kernel, radius):
    kernel_size = 2 * radius + 1
    row_count = bordered.shape[2] - 2 * radius
    col_count = bordered.shape[3]
    weights = jnp.stack([psf_kernel, psf_kernel * psf_kernel])
    padded = jnp.pad(bordered, ((0, 0), (0, 0), (0, 0), (radius, radius)))
    running = jnp.zeros((bordered.shape[0], bordered.shape[1], row_count, col_count), jnp.float32)
    for row_tap in range(kernel_size):
        for col_tap in range(kernel_size):
            running = (
                running
                + weights[:, row_tap, col_tap][:, None, None, None]
                * padded[:, :, row_tap : row_tap + row_count, col_tap : col_tap + col_count]
            )
    return running


def stack_shifted(padded, visit_offsets, reach_rows, row_count):
    stacked = jnp.zeros((2, visit_offsets.shape[1], row_count, padded.shape[3]), jnp.float32)
    for offset_value in range(-MAXOFF, MAXOFF + 1):
        onehot = (visit_offsets == offset_value).astype(jnp.float32)
        start_row = reach_rows + offset_value * BR
        window = padded[:, :, start_row : start_row + row_count, :]
        stacked = stacked + jnp.einsum(
            "tk,ctrw->ckrw", onehot, window, precision=lax.Precision.HIGHEST
        )
    return stacked


def shards(science, inv_variance, psf_kernel, offsets):
    radius = (psf_kernel.shape[0] - 1) // 2
    paired = jnp.stack([science * inv_variance, inv_variance])
    bordered = padded_2(paired, (("sky", 2),), radius)
    images = correlate(bordered, psf_kernel, radius)
    reach_rows = MAXOFF * BR
    regrouped = lax.all_to_all(images, "visit", split_axis=2, concat_axis=1, tiled=True)
    padded = padded_2(regrouped, ((("sky", "visit"), 2),), reach_rows)
    stacked = stack_shifted(padded, offsets, reach_rows, regrouped.shape[2])
    return stacked[0] / jnp.sqrt(stacked[1])


def solution(mesh):
    return jax.shard_map(
        shards,
        mesh=mesh,
        in_specs=(P("visit", "sky", None), P("visit", "sky", None), P(), P()),
        out_specs=P(None, ("sky", "visit"), None),
        check_vma=False,
    )
```

profile of v0, /device:TPU:17, one launch (start us, length us, event | category | flops | bytes accessed | tf_op | source)
XLA Modules:
  0.0 95.5 jit_solution(13174553676128363934)
XLA Ops:
  0.0 1.8 %copy_bitcast_fusion.1 = (f32[1,8,64,256]{3,1,0,2:T(8,128)S(1)}, f32[1,8,64,256]{3,1,0,2:T(8,128)S(1)}) fusion(f32[8,64,256]{2,1,0:T(8,128)} %param.5, f32[8,64,256]{2,1,0:T(8,128)} %param.4), kind=kLoop, calls=%fused_computation.270 | loop fusion | flops 131072 | bytes 2097152 | tf_op jit(solution)/shard_map/stack | solution.py:54
  1.8 4.1 %collective-permute-start = (f32[2,8,5,256]{3,1,0,2:T(8,128)S(1)}, f32[2,8,5,256]{3,1,0,2:T(8,128)S(1)}, u32[]{:S(2)}, u32[]{:S(2)}) collective-permute-start(f32[2,8,5,256]{3,1,0,2:T(8,128)S(1)} %get-tuple-element.128), channel_id=1, source_target_pairs={{0,4},{4,8},{8,12},{12,16},{16,20},{20,24},{24,28},{28,32},{32,36}... | collective-permute-start | bytes 245768 | tf_op jit(solution)/shard_map/ppermute | solution.py:15
  5.9 1.9 %collective-permute-start.1 = (f32[2,8,5,256]{3,1,0,2:T(8,128)S(1)}, f32[2,8,5,256]{3,1,0,2:T(8,128)S(1)}, u32[]{:S(2)}, u32[]{:S(2)}) collective-permute-start(f32[2,8,5,256]{3,1,0,2:T(8,128)S(1)} %get-tuple-element.129), channel_id=1, source_target_pairs={{4,0},{8,4},{12,8},{16,12},{20,16},{24,20},{28,24},{32,28},{36,32}... | collective-permute-start | bytes 245768 | tf_op jit(solution)/shard_map/ppermute | solution.py:18
  7.9 0.2 fusion.284
  8.1 0.2 fusion.392
  8.3 0.2 fusion.293
  8.5 0.2 fusion.356
  8.7 0.2 fusion.374
  8.8 0.2 fusion.365
  9.0 0.2 fusion.302
  9.2 0.2 fusion.347
  9.4 0.2 fusion.383
  9.6 0.2 fusion.311
  9.8 0.2 fusion.338
  10.0 0.2 fusion.320
  10.2 0.2 fusion.329
  10.4 0.2 fusion.401
  10.6 1.1 %collective-permute-done.1 = f32[2,8,5,256]{3,1,0,2:T(8,128)S(1)} collective-permute-done((f32[2,8,5,256]{3,1,0,2:T(8,128)S(1)}, f32[2,8,5,256]{3,1,0,2:T(8,128)S(1)}, u32[]{:S(2)}, u32[]{:S(2)}) %collective-permute-start.1) | collective-permute-done | bytes 81952 | tf_op jit(solution)/shard_map/ppermute | solution.py:18
  11.7 0.5 select_maximum_fusion
  12.2 0.2 maximum_maximum_fusion
  12.4 29.4 %fusion.42 = f32[2,8,64,256]{3,1,0,2:T(8,128)S(1)} fusion(f32[2,8,74,266]{3,1,0,2:T(8,128)S(1)} %select_maximum_fusion, f32[2,8,69,256]{3,1,0,2:T(8,128)S(1)} %get-tuple-element.127, f32[1,8,64,256]{3,1,0,2:T(8,128)S(1)} %get-tuple-element.130, f32[1,8,64,256]{3,1,0,2:T(8,128)S(1)} %get-tuple-element.131, f32[2,8,69,256]{3,1,0,2:T(8,128)S(1)} %get-tuple-element.126, ...), kind=kLoop, calls=%fused_computation.50 | loop fusion | flops 63438848 | bytes 127927240 | tf_op jit(solution)/shard_map/add | solution.py:33
  41.8 15.8 %all_to_all.18 = f32[2,8,64,256]{3,1,0,2:T(8,128)S(1)} all-to-all(f32[2,8,64,256]{3,1,0,2:T(8,128)S(1)} %fusion.42), channel_id=1, replica_groups=mesh['sky'=64,'visit'=4] {'visit'}, dimensions={2} | all-to-all | bytes 2097152 | tf_op jit(solution)/shard_map/all_to_all | solution.py:58
  57.8 6.7 %collective-permute-start.3 = (f32[2,32,16,256]{3,1,2,0:T(8,128)S(1)}, f32[2,32,16,256]{3,1,2,0:T(8,128)S(1)}, u32[]{:S(2)}, u32[]{:S(2)}) collective-permute-start(f32[2,32,16,256]{3,1,2,0:T(8,128)S(1)} %bitcast.45), channel_id=1, source_target_pairs={{1,0},{2,1},{3,2},{4,3},{5,4},{6,5},{7,6},{8,7},{9,8},{10,9},{11,1... | collective-permute-start | bytes 3145736 | tf_op jit(solution)/shard_map/ppermute | solution.py:18
  64.5 1.9 %collective-permute-start.2 = (f32[2,32,16,256]{3,1,2,0:T(8,128)S(1)}, f32[2,32,16,256]{3,1,2,0:T(8,128)S(1)}, u32[]{:S(2)}, u32[]{:S(2)}) collective-permute-start(f32[2,32,16,256]{3,1,2,0:T(8,128)S(1)} %bitcast.46), channel_id=1, source_target_pairs={{0,1},{1,2},{2,3},{3,4},{4,5},{5,6},{6,7},{7,8},{8,9},{9,10},{10,1... | collective-permute-start | bytes 3145736 | tf_op jit(solution)/shard_map/ppermute | solution.py:15
  66.5 0.5 fusion.148
  66.9 20.5 %collective-permute-done.3 = f32[2,32,16,256]{3,1,2,0:T(8,128)S(1)} collective-permute-done((f32[2,32,16,256]{3,1,2,0:T(8,128)S(1)}, f32[2,32,16,256]{3,1,2,0:T(8,128)S(1)}, u32[]{:S(2)}, u32[]{:S(2)}) %collective-permute-start.3) | collective-permute-done | bytes 1048608 | tf_op jit(solution)/shard_map/ppermute | solution.py:18
  87.5 0.5 fusion.145
  88.0 5.1 %collective-permute-done.2 = f32[2,32,16,256]{3,1,2,0:T(8,128)S(1)} collective-permute-done((f32[2,32,16,256]{3,1,2,0:T(8,128)S(1)}, f32[2,32,16,256]{3,1,2,0:T(8,128)S(1)}, u32[]{:S(2)}, u32[]{:S(2)}) %collective-permute-start.2) | collective-permute-done | bytes 1048608 | tf_op jit(solution)/shard_map/ppermute | solution.py:15
  93.1 0.5 fusion
  93.6 0.5 fusion.18
  94.1 0.5 fusion.15
  94.6 0.9 copy.13
  (9 shorter events, 0.2 us)
Async XLA Ops:
  0.0 7.9 %copy-start = (f32[11,11]{1,0:T(8,128)S(1)}, f32[11,11]{1,0:T(8,128)}, u32[]{:S(2)}) copy-start(f32[11,11]{1,0:T(8,128)} %param.6) | copy-start | bytes 1456
  1.8 8.7 %collective-permute-start = (f32[2,8,5,256]{3,1,0,2:T(8,128)S(1)}, f32[2,8,5,256]{3,1,0,2:T(8,128)S(1)}, u32[]{:S(2)}, u32[]{:S(2)}) collective-permute-start(f32[2,8,5,256]{3,1,0,2:T(8,128)S(1)} %get-tuple-element.128), channel_id=1, source_target_pairs={{0,4},{4,8},{8,12},{12,16},{16,20},{20,24},{24,28},{28,32},{32,36}... | collective-permute-start | bytes 245768 | tf_op jit(solution)/shard_map/ppermute | solution.py:15
  5.9 5.8 %collective-permute-start.1 = (f32[2,8,5,256]{3,1,0,2:T(8,128)S(1)}, f32[2,8,5,256]{3,1,0,2:T(8,128)S(1)}, u32[]{:S(2)}, u32[]{:S(2)}) collective-permute-start(f32[2,8,5,256]{3,1,0,2:T(8,128)S(1)} %get-tuple-element.129), channel_id=1, source_target_pairs={{4,0},{8,4},{12,8},{16,12},{20,16},{24,20},{28,24},{32,28},{36,32}... | collective-permute-start | bytes 245768 | tf_op jit(solution)/shard_map/ppermute | solution.py:18
  41.8 24.6 %copy-start.1 = (s32[32,16]{0,1:T(8,128)S(1)}, s32[32,16]{0,1:T(8,128)}, u32[]{:S(2)}) copy-start(s32[32,16]{0,1:T(8,128)} %param.7) | copy-start | bytes 6148
  57.8 29.7 %collective-permute-start.3 = (f32[2,32,16,256]{3,1,2,0:T(8,128)S(1)}, f32[2,32,16,256]{3,1,2,0:T(8,128)S(1)}, u32[]{:S(2)}, u32[]{:S(2)}) collective-permute-start(f32[2,32,16,256]{3,1,2,0:T(8,128)S(1)} %bitcast.45), channel_id=1, source_target_pairs={{1,0},{2,1},{3,2},{4,3},{5,4},{6,5},{7,6},{8,7},{9,8},{10,9},{11,1... | collective-permute-start | bytes 3145736 | tf_op jit(solution)/shard_map/ppermute | solution.py:18
  64.5 28.6 %collective-permute-start.2 = (f32[2,32,16,256]{3,1,2,0:T(8,128)S(1)}, f32[2,32,16,256]{3,1,2,0:T(8,128)S(1)}, u32[]{:S(2)}, u32[]{:S(2)}) collective-permute-start(f32[2,32,16,256]{3,1,2,0:T(8,128)S(1)} %bitcast.46), channel_id=1, source_target_pairs={{0,1},{1,2},{2,3},{3,4},{4,5},{5,6},{6,7},{7,8},{8,9},{9,10},{10,1... | collective-permute-start | bytes 3145736 | tf_op jit(solution)/shard_map/ppermute | solution.py:15
where the time goes:
time: 95.7 us; the launch traced here: 95.5 us
  other arithmetic  34.5 us (36%)
  waiting for transfers between devices  26.8 us (28%)
  blocking collectives  15.8 us (17%)
  starting transfers between devices  14.7 us (15%)
  matrix products  2.37 us (2%)
  local copies, waits for them, and re-layouts  1 us (1%)
    add x1, other arithmetic, correlate(): running + weights[:, row_tap, col_tap][:, None, None, None] * padded[:, :...  29.4 us
    ppermute x2, waiting for transfers between devices, padded_2(): lax.ppermute(lax.slice_in_dim(block, 0, width, axis=dim), axis, backward)  21.7 us
    all_to_all x1, blocking collectives, shards(): lax.all_to_all(images, 'visit', split_axis=2, concat_axis=1, tiled=True)  15.8 us
    ppermute x2, starting transfers between devices, padded_2(): lax.ppermute(lax.slice_in_dim(block, 0, width, axis=dim), axis, backward)  8.62 us
    ppermute x2, starting transfers between devices, padded_2(): lax.ppermute(lax.slice_in_dim(block, block.shape[dim] - width, None, axis...  6.03 us
    ppermute x2, waiting for transfers between devices, padded_2(): lax.ppermute(lax.slice_in_dim(block, block.shape[dim] - width, None, axis...  5.13 us
    slice x14, other arithmetic, correlate(): weights[:, row_tap, col_tap][:, None, None, None]  2.58 us
    dot_general x5, matrix products, stack_shifted(): jnp.einsum('tk,ctrw->ckrw', onehot, window, precision=lax.Precision.HIGHEST)  2.37 us
  transfers between devices with their start and end apart: 4, of which 3 were waited for; matrix products, arithmetic and copies ran while one was open for 4% of the time, Pallas kernels for 0%

commit v1 on v0

v1 whole, which is shorter than its diff:
```python
import jax
import jax.numpy as jnp
from jax import lax
from jax.sharding import PartitionSpec as P

BR = 8
MAXOFF = 2


def bordered_rows(block, axis, width):
    count = lax.axis_size(axis)
    forward = [(i, i + 1) for i in range(count - 1)]
    backward = [(target, source) for source, target in forward]
    dim = block.ndim - 2
    low = lax.ppermute(
        lax.slice_in_dim(block, block.shape[dim] - width, None, axis=dim), axis, forward
    )
    high = lax.ppermute(lax.slice_in_dim(block, 0, width, axis=dim), axis, backward)
    return jnp.concatenate([low, block, high], axis=dim)


def toeplitz(taps, cols):
    size = taps.shape[1]
    radius = (size - 1) // 2
    w = lax.broadcasted_iota(jnp.int32, (size, cols, cols), 1)
    v = lax.broadcasted_iota(jnp.int32, (size, cols, cols), 2)
    b = lax.broadcasted_iota(jnp.int32, (size, cols, cols), 0)
    onehot = (w - v + radius == b).astype(jnp.float32)
    return jnp.einsum("ab,bwv->awv", taps, onehot, precision=lax.Precision.HIGHEST)


def correlate_rows(bordered, kernel):
    return lax.conv_general_dilated(
        bordered,
        kernel,
        window_strides=(1,),
        padding="VALID",
        dimension_numbers=("NHC", "HIO", "NHC"),
        precision=lax.Precision.HIGH,
        preferred_element_type=jnp.float32,
    )


def shards(science, inv_variance, psf_kernel, offsets):
    radius = (psf_kernel.shape[0] - 1) // 2
    reach = MAXOFF * BR
    visits, rows, cols = science.shape
    total_rows = rows * lax.axis_size("sky")

    weighted = science * inv_variance
    both = jnp.stack([weighted, inv_variance])
    bordered = bordered_rows(both, "sky", radius + reach)

    psi = correlate_rows(bordered[0], toeplitz(psf_kernel, cols))
    phi = correlate_rows(bordered[1], toeplitz(psf_kernel * psf_kernel, cols))
    images = jnp.stack([psi, phi])

    first = lax.axis_index("sky") * rows - reach
    row_ids = first + lax.broadcasted_iota(jnp.int32, (1, 1, rows + 2 * reach, 1), 2)
    inside = (row_ids >= 0) & (row_ids < total_rows)
    images = jnp.where(inside, images, 0.0)

    mine = lax.dynamic_slice_in_dim(offsets, lax.axis_index("visit") * visits, visits, 0)
    partial = jnp.zeros((2, offsets.shape[1], rows, cols), jnp.float32)
    for offset_value in range(-MAXOFF, MAXOFF + 1):
        onehot = (mine == offset_value).astype(jnp.float32)
        start = reach + offset_value * BR
        window = images[:, :, start : start + rows, :]
        partial = partial + jnp.einsum(
            "tk,ctrw->ckrw", onehot, window, precision=lax.Precision.HIGHEST
        )

    stacked = lax.psum_scatter(partial, "visit", scatter_dimension=2, tiled=True)
    return stacked[0] / jnp.sqrt(stacked[1])


def solution(mesh):
    return jax.shard_map(
        shards,
        mesh=mesh,
        in_specs=(P("visit", "sky", None), P("visit", "sky", None), P(), P()),
        out_specs=P(None, ("sky", "visit"), None),
        check_vma=False,
    )
```

time: 95.7 us -> 85.1 us (0.89)
  the two profiles are of different devices: /device:TPU:17 before, /device:TPU:1 now
where the time goes in v1:
time: 85.1 us; the launch traced here: 84.9 us
  waiting for transfers between devices  36.2 us (43%)
  matrix products  21.3 us (25%)
  between operations  13.5 us (16%)
  starting transfers between devices  6.86 us (8%)
  local copies, waits for them, and re-layouts  4.95 us (6%)
  other arithmetic  2.09 us (2%)
    unnamed x2, waiting for transfers between devices  35.3 us
    conv_general_dilated x2, matrix products, correlate_rows(): lax.conv_general_dilated(bordered, kernel, window_strides=(1,), padding='...  9.81 us
    dot_general x5, matrix products, shards(): jnp.einsum('tk,ctrw->ckrw', onehot, window, precision=lax.Precision.HIGHEST)  5.87 us
    dot_general x2, matrix products, toeplitz(): jnp.einsum('ab,bwv->awv', taps, onehot, precision=lax.Precision.HIGHEST)  5.61 us
    ppermute x1, starting transfers between devices, bordered_rows(): lax.ppermute(lax.slice_in_dim(block, block.shape[dim] - width, None, axis...  4.94 us
    unnamed x10, local copies, waits for them, and re-layouts  4.02 us
    ppermute x1, starting transfers between devices, bordered_rows(): lax.ppermute(lax.slice_in_dim(block, 0, width, axis=dim), axis, backward)  1.92 us
    another operation x1, other arithmetic, shards(): both = jnp.stack([weighted, inv_variance])  1.83 us
  transfers between devices with their start and end apart: 3, of which 2 were waited for; matrix products, arithmetic and copies ran while one was open for 7% of the time, Pallas kernels for 0%

profile of v1, /device:TPU:1, one launch (start us, length us, event | category | flops | bytes accessed | tf_op | source)
XLA Modules:
  0.0 84.9 jit_solution(14344252661655849950)
XLA Ops:
  6.5 0.0 copy-start
  6.5 0.0 copy-start.2
  6.5 0.0 reduce-scatter.5.cloned.1.call-start
  6.5 1.8 %fusion.14 = (f32[1,8,64,256]{3,1,2,0:T(8,128)S(1)}, f32[1,8,64,256]{3,1,2,0:T(8,128)S(1)}) fusion(f32[8,64,256]{2,1,0:T(8,128)} %param.4, f32[8,64,256]{2,1,0:T(8,128)} %param.5), kind=kLoop, calls=%fused_computation.17 | loop fusion | flops 131072 | bytes 2097152 | tf_op jit(solution)/shard_map/stack | solution.py:51
  8.4 0.1 pad_maximum_fusion.2
  8.4 4.9 %collective-permute-start = (f32[2,8,21,256]{3,1,2,0:T(8,128)S(1)}, f32[2,8,21,256]{3,1,2,0:T(8,128)S(1)}, u32[]{:S(2)}, u32[]{:S(2)}) collective-permute-start(f32[2,8,21,256]{3,1,2,0:T(8,128)S(1)} %get-tuple-element.5), channel_id=1, source_target_pairs={{0,4},{4,8},{8,12},{12,16},{16,20},{20,24},{24,28},{28,32},{32,36}... | collective-permute-start | bytes 1032200 | tf_op jit(solution)/shard_map/ppermute | solution.py:15
  13.4 1.9 %collective-permute-start.1 = (f32[2,8,21,256]{3,1,2,0:T(8,128)S(1)}, f32[2,8,21,256]{3,1,2,0:T(8,128)S(1)}, u32[]{:S(2)}, u32[]{:S(2)}) collective-permute-start(f32[2,8,21,256]{3,1,2,0:T(8,128)S(1)} %get-tuple-element.6), channel_id=1, source_target_pairs={{4,0},{8,4},{12,8},{16,12},{20,16},{24,20},{28,24},{32,28},{36,32}... | collective-permute-start | bytes 1032200 | tf_op jit(solution)/shard_map/ppermute | solution.py:18
  15.3 0.0 copy-done.2
  15.3 3.4 %fusion = f32[11,256,256]{2,0,1:T(8,128)} fusion(f32[11,11]{1,0:T(8,128)S(1)} %copy-done.2), kind=kOutput, calls=%fused_computation.1 | convolution fusion | flops 97321080 | bytes 2884068 | tf_op jit(solution)/shard_map/ab,bwv->awv/dot_general | solution.py:29
  18.7 0.0 copy-done
  18.7 0.1 constant_dynamic-slice_fusion
  18.8 0.1 copy.26
  18.9 0.0 copy-start.1
  18.9 2.2 %fusion.1 = f32[256,256,11]{1,2,0:T(8,128)S(1)} fusion(f32[11,11]{1,0:T(8,128)S(1)} %copy-done.2), kind=kOutput, calls=%fused_computation.2 | convolution fusion | flops 97320960 | bytes 2884068 | tf_op jit(solution)/shard_map/ab,bwv->awv/dot_general | solution.py:29
  21.1 0.0 collective-permute-done
  21.1 0.8 collective-permute-done.1
  22.0 0.1 pad_maximum_fusion
  22.1 0.0 copy-done.1
  22.1 4.8 %fusion.11 = f32[1,8,96,256]{3,1,2,0:T(8,128)S(1)} fusion(f32[11,256,256]{2,0,1:T(8,128)S(1)} %copy-done.1, f32[2,8,106,256]{3,1,2,0:T(8,128)S(1)} %pad_maximum_fusion), kind=kOutput, calls=%fused_computation.13 | convolution fusion | flops 3321888768 | bytes 5849088 | tf_op jit(solution)/shard_map/conv_general_dilated | solution.py:33
  26.9 5.0 %fusion.8 = f32[1,8,96,256]{3,1,2,0:T(8,128)S(1)} fusion(f32[256,256,11]{1,2,0:T(8,128)S(1)} %fusion.1, f32[2,8,106,256]{3,1,2,0:T(8,128)S(1)} %pad_maximum_fusion), kind=kOutput, calls=%fused_computation.12 | convolution fusion | flops 3321888768 | bytes 5849088 | tf_op jit(solution)/shard_map/conv_general_dilated | solution.py:33
  31.9 1.1 %fusion.26 = f32[2,64,256,16]{2,3,1,0:T(8,128)S(1)} fusion(s32[8,16]{1,0:T(8,128)S(1)} %copy.26, f32[1,8,96,256]{3,1,2,0:T(8,128)S(1)} %fusion.11, f32[1,8,96,256]{3,1,2,0:T(8,128)S(1)} %fusion.8, pred[96]{0:T(512)(128)(4,1)S(1)} %compare_and_fusion), kind=kOutput, calls=%fused_computation.34 | convolution fusion | flops 51118208 | bytes 3670624 | tf_op jit(solution)/shard_map/tk,ctrw->ckrw/dot_general | solution.py:69
  33.0 1.1 %fusion.24 = f32[2,64,256,16]{2,3,1,0:T(8,128)S(1)} fusion(s32[8,16]{1,0:T(8,128)S(1)} %copy.26, f32[1,8,96,256]{3,1,2,0:T(8,128)S(1)} %fusion.11, f32[1,8,96,256]{3,1,2,0:T(8,128)S(1)} %fusion.8, pred[96]{0:T(512)(128)(4,1)S(1)} %compare_and_fusion), kind=kOutput, calls=%fused_computation.32 | convolution fusion | flops 51118208 | bytes 3670624 | tf_op jit(solution)/shard_map/tk,ctrw->ckrw/dot_general | solution.py:69
  34.1 1.1 %fusion.22 = f32[2,64,256,16]{2,3,1,0:T(8,128)S(1)} fusion(s32[8,16]{1,0:T(8,128)S(1)} %copy.26, f32[1,8,96,256]{3,1,2,0:T(8,128)S(1)} %fusion.11, f32[1,8,96,256]{3,1,2,0:T(8,128)S(1)} %fusion.8, pred[96]{0:T(512)(128)(4,1)S(1)} %compare_and_fusion), kind=kOutput, calls=%fused_computation.30 | convolution fusion | flops 51118208 | bytes 3670624 | tf_op jit(solution)/shard_map/tk,ctrw->ckrw/dot_general | solution.py:69
  35.2 1.1 %fusion.28 = f32[2,64,256,16]{2,3,1,0:T(8,128)S(1)} fusion(s32[8,16]{1,0:T(8,128)S(1)} %copy.26, f32[1,8,96,256]{3,1,2,0:T(8,128)S(1)} %fusion.11, f32[1,8,96,256]{3,1,2,0:T(8,128)S(1)} %fusion.8, pred[96]{0:T(512)(128)(4,1)S(1)} %compare_and_fusion), kind=kOutput, calls=%fused_computation.36 | convolution fusion | flops 51118208 | bytes 3670624 | tf_op jit(solution)/shard_map/tk,ctrw->ckrw/dot_general | solution.py:69
  36.2 1.6 %add_bitcast_fusion = f32[2,16,64,256]{3,1,2,0:T(8,128)S(1)} fusion(f32[2,64,256,16]{2,3,1,0:T(8,128)S(1)} %fusion.22, f32[2,64,256,16]{2,3,1,0:T(8,128)S(1)} %fusion.24, f32[2,64,256,16]{2,3,1,0:T(8,128)S(1)} %fusion.28, f32[2,64,256,16]{2,3,1,0:T(8,128)S(1)} %fusion.26, s32[8,16]{1,0:T(8,128)S(1)} %copy.26, f32[1,8,96,256]{3,1,2,0:T(8,128)S(1)} %fusion.11, ...), kind=kOutput, calls=%fused_computation.7 | convolution fusion | flops 53215360 | bytes 12059232 | tf_op jit(solution)/shard_map/tk,ctrw->ckrw/dot_general | solution.py:69
  37.9 0.2 copy.24
  38.1 2.5 %copy.29 = f32[8,8,32,256]{3,1,2,0:T(8,128)} copy(f32[8,8,32,256]{3,2,1,0:T(8,128)S(1)} %bitcast.74) | data formatting | bytes 4194304
  40.6 0.0 reduce-scatter.5.cloned.1.call-update
  40.6 35.3 %reduce-scatter.5.cloned.1.call-done = f32[16,8192]{1,0:T(8,128)} async-done(((f32[64,8192]{1,0:T(8,128)}), f32[16,8192]{1,0:T(8,128)}) %reduce-scatter.5.cloned.1.call-update) | async-done | bytes 524304
  75.9 1.2 %copy.30 = f32[2,8,32,256]{3,2,1,0:T(8,128)S(1)} copy(f32[2,8,32,256]{3,1,2,0:T(8,128)} %bitcast.76) | data formatting | bytes 1048576
  77.2 0.9 %copy.18 = f32[16,16,256]{2,1,0:T(8,128)} copy(f32[16,16,256]{2,0,1:T(8,128)S(1)} %fusion.17) | data formatting | bytes 524288 | tf_op jit(solution)/shard_map/div | solution.py:74
  (2 shorter events, 0.1 us)
Async XLA Ops:
  6.5 12.2 %copy-start = (s32[32,16]{0,1:T(8,128)S(1)}, s32[32,16]{0,1:T(8,128)}, u32[]{:S(2)}) copy-start(s32[32,16]{0,1:T(8,128)} %param.7) | copy-start | bytes 6148
  6.5 8.8 %copy-start.2 = (f32[11,11]{1,0:T(8,128)S(1)}, f32[11,11]{1,0:T(8,128)}, u32[]{:S(2)}) copy-start(f32[11,11]{1,0:T(8,128)} %param.6) | copy-start | bytes 1456
  6.5 69.4 %reduce-scatter.5.cloned.1.call-start = ((), (), s32[]{:S(2)}) async-start(), calls=%async_computation.1 | async-start | bytes 2621440
  8.4 12.7 %collective-permute-start = (f32[2,8,21,256]{3,1,2,0:T(8,128)S(1)}, f32[2,8,21,256]{3,1,2,0:T(8,128)S(1)}, u32[]{:S(2)}, u32[]{:S(2)}) collective-permute-start(f32[2,8,21,256]{3,1,2,0:T(8,128)S(1)} %get-tuple-element.5), channel_id=1, source_target_pairs={{0,4},{4,8},{8,12},{12,16},{16,20},{20,24},{24,28},{28,32},{32,36}... | collective-permute-start | bytes 1032200 | tf_op jit(solution)/shard_map/ppermute | solution.py:15
  13.4 8.6 %collective-permute-start.1 = (f32[2,8,21,256]{3,1,2,0:T(8,128)S(1)}, f32[2,8,21,256]{3,1,2,0:T(8,128)S(1)}, u32[]{:S(2)}, u32[]{:S(2)}) collective-permute-start(f32[2,8,21,256]{3,1,2,0:T(8,128)S(1)} %get-tuple-element.6), channel_id=1, source_target_pairs={{4,0},{8,4},{12,8},{16,12},{20,16},{24,20},{28,24},{32,28},{36,32}... | collective-permute-start | bytes 1032200 | tf_op jit(solution)/shard_map/ppermute | solution.py:18
  18.9 3.2 %copy-start.1 = (f32[11,256,256]{2,0,1:T(8,128)S(1)}, f32[11,256,256]{2,0,1:T(8,128)}, u32[]{:S(2)}) copy-start(f32[11,256,256]{2,0,1:T(8,128)} %fusion) | copy-start | bytes 8650756
Sparse Core Ops, SparseCore 0:
  40.8 35.1 reduce-scatter.4

commit v2 on v1

--- a/solution.py
+++ b/solution.py
@@ -41,6 +41,31 @@
     )
 
 
+def ring_reduce_scatter(partial, axis):
+    count = lax.axis_size(axis)
+    if count != 4:
+        return lax.psum_scatter(partial, axis, scatter_dimension=2, tiled=True)
+    me = lax.axis_index(axis)
+    rows = partial.shape[2] // count
+    half = partial.shape[3] // 2
+    right = [(i, (i + 1) % count) for i in range(count)]
+    left = [(i, (i - 1) % count) for i in range(count)]
+
+    def block(step):
+        return lax.dynamic_slice_in_dim(partial, ((me + step) % count) * rows, rows, axis=2)
+
+    far = block(2)
+    from_left = lax.ppermute(far[..., :half], axis, right)
+    from_right = lax.ppermute(far[..., half:], axis, left)
+    ahead = block(1)
+    ahead = jnp.concatenate([ahead[..., :half] + from_left, ahead[..., half:]], axis=-1)
+    behind = block(count - 1)
+    behind = jnp.concatenate([behind[..., :half], behind[..., half:] + from_right], axis=-1)
+    got_left = lax.ppermute(ahead, axis, right)
+    got_right = lax.ppermute(behind, axis, left)
+    return block(0) + got_left + got_right
+
+
 def shards(science, inv_variance, psf_kernel, offsets):
     radius = (psf_kernel.shape[0] - 1) // 2
     reach = MAXOFF * BR
@@ -70,7 +95,7 @@
             "tk,ctrw->ckrw", onehot, window, precision=lax.Precision.HIGHEST
         )
 
-    stacked = lax.psum_scatter(partial, "visit", scatter_dimension=2, tiled=True)
+    stacked = ring_reduce_scatter(partial, "visit")
     return stacked[0] / jnp.sqrt(stacked[1])
 
 

time: 85.1 us -> 58.4 us (0.69)
  the two profiles are of different devices: /device:TPU:1 before, /device:TPU:54 now
where the time goes in v2:
time: 58.4 us; the launch traced here: 58.2 us
  waiting for transfers between devices  21.3 us (36%)
  matrix products  21.2 us (36%)
  starting transfers between devices  9.72 us (17%)
  other arithmetic  4.04 us (7%)
  local copies, waits for them, and re-layouts  1.72 us (3%)
    ppermute x1, waiting for transfers between devices, ring_reduce_scatter(): got_left = lax.ppermute(ahead, axis, right)  10.9 us
    conv_general_dilated x2, matrix products, correlate_rows(): lax.conv_general_dilated(bordered, kernel, window_strides=(1,), padding='...  9.81 us
    ppermute x1, waiting for transfers between devices, ring_reduce_scatter(): from_left = lax.ppermute(far[..., :half], axis, right)  6.83 us
    dot_general x5, matrix products, shards(): jnp.einsum('tk,ctrw->ckrw', onehot, window, precision=lax.Precision.HIGHEST)  5.89 us
    dot_general x2, matrix products, toeplitz(): jnp.einsum('ab,bwv->awv', taps, onehot, precision=lax.Precision.HIGHEST)  5.55 us
    ppermute x1, starting transfers between devices, bordered_rows(): lax.ppermute(lax.slice_in_dim(block, 0, width, axis=dim), axis, backward)  3.64 us
    ppermute x1, waiting for transfers between devices, ring_reduce_scatter(): got_right = lax.ppermute(behind, axis, left)  3.53 us
    ppermute x1, starting transfers between devices, bordered_rows(): lax.ppermute(lax.slice_in_dim(block, block.shape[dim] - width, None, axis...  1.92 us
  transfers between devices with their start and end apart: 6, of which 3 were waited for; matrix products, arithmetic and copies ran while one was open for 13% of the time, Pallas kernels for 0%

profile of v2, /device:TPU:54, one launch (start us, length us, event | category | flops | bytes accessed | tf_op | source)
XLA Modules:
  0.0 58.2 jit_solution(12556886629040924010)
XLA Ops:
  0.0 1.8 %fusion.15 = (f32[1,8,64,256]{3,1,2,0:T(8,128)S(1)}, f32[1,8,64,256]{3,1,2,0:T(8,128)S(1)}) fusion(f32[8,64,256]{2,1,0:T(8,128)} %param.4, f32[8,64,256]{2,1,0:T(8,128)} %param.5), kind=kLoop, calls=%fused_computation.21 | loop fusion | flops 131072 | bytes 2097152 | tf_op jit(solution)/shard_map/stack | solution.py:76
  1.8 0.1 pad_maximum_fusion.4
  1.9 1.9 %collective-permute-start = (f32[2,8,21,256]{3,1,2,0:T(8,128)S(1)}, f32[2,8,21,256]{3,1,2,0:T(8,128)S(1)}, u32[]{:S(2)}, u32[]{:S(2)}) collective-permute-start(f32[2,8,21,256]{3,1,2,0:T(8,128)S(1)} %get-tuple-element.8), channel_id=1, source_target_pairs={{0,4},{4,8},{8,12},{12,16},{16,20},{20,24},{24,28},{28,32},{32,36}... | collective-permute-start | bytes 1032200 | tf_op jit(solution)/shard_map/ppermute | solution.py:15
  3.8 3.6 %collective-permute-start.1 = (f32[2,8,21,256]{3,1,2,0:T(8,128)S(1)}, f32[2,8,21,256]{3,1,2,0:T(8,128)S(1)}, u32[]{:S(2)}, u32[]{:S(2)}) collective-permute-start(f32[2,8,21,256]{3,1,2,0:T(8,128)S(1)} %get-tuple-element.9), channel_id=1, source_target_pairs={{4,0},{8,4},{12,8},{16,12},{20,16},{24,20},{28,24},{32,28},{36,32}... | collective-permute-start | bytes 1032200 | tf_op jit(solution)/shard_map/ppermute | solution.py:18
  7.5 4.1 %fusion.1 = f32[256,256,11]{1,2,0:T(8,128)} fusion(f32[11,11]{1,0:T(8,128)S(1)} %copy-done.2), kind=kOutput, calls=%fused_computation.2 | convolution fusion | flops 97320960 | bytes 2884068 | tf_op jit(solution)/shard_map/ab,bwv->awv/dot_general | solution.py:29
  11.6 0.1 constant_dynamic-slice_fusion
  11.7 0.1 copy.17
  11.7 1.5 %fusion = f32[11,256,256]{2,0,1:T(8,128)S(1)} fusion(f32[11,11]{1,0:T(8,128)S(1)} %copy-done.2), kind=kOutput, calls=%fused_computation.1 | convolution fusion | flops 97321080 | bytes 2884068 | tf_op jit(solution)/shard_map/ab,bwv->awv/dot_general | solution.py:29
  13.2 0.0 collective-permute-done
  13.2 0.1 pad_maximum_fusion
  13.4 0.5 copy-done.1
  13.9 4.8 %fusion.8 = f32[1,8,96,256]{3,1,2,0:T(8,128)S(1)} fusion(f32[256,256,11]{1,2,0:T(8,128)S(1)} %copy-done.1, f32[2,8,106,256]{3,1,2,0:T(8,128)S(1)} %pad_maximum_fusion), kind=kOutput, calls=%fused_computation.12 | convolution fusion | flops 3321888768 | bytes 5849088 | tf_op jit(solution)/shard_map/conv_general_dilated | solution.py:33
  18.7 5.0 %fusion.11 = f32[1,8,96,256]{3,1,2,0:T(8,128)S(1)} fusion(f32[11,256,256]{2,0,1:T(8,128)S(1)} %fusion, f32[2,8,106,256]{3,1,2,0:T(8,128)S(1)} %pad_maximum_fusion), kind=kOutput, calls=%fused_computation.13 | convolution fusion | flops 3321888768 | bytes 5849088 | tf_op jit(solution)/shard_map/conv_general_dilated | solution.py:33
  23.7 1.1 %fusion.26 = f32[2,64,256,16]{2,3,1,0:T(8,128)S(1)} fusion(s32[8,16]{1,0:T(8,128)S(1)} %copy.17, f32[1,8,96,256]{3,1,2,0:T(8,128)S(1)} %fusion.11, f32[1,8,96,256]{3,1,2,0:T(8,128)S(1)} %fusion.8, pred[96]{0:T(512)(128)(4,1)S(1)} %compare_and_fusion), kind=kOutput, calls=%fused_computation.41 | convolution fusion | flops 51118208 | bytes 3670624 | tf_op jit(solution)/shard_map/tk,ctrw->ckrw/dot_general | solution.py:94
  24.8 1.1 %fusion.28 = f32[2,64,256,16]{2,3,1,0:T(8,128)S(1)} fusion(s32[8,16]{1,0:T(8,128)S(1)} %copy.17, f32[1,8,96,256]{3,1,2,0:T(8,128)S(1)} %fusion.11, f32[1,8,96,256]{3,1,2,0:T(8,128)S(1)} %fusion.8, pred[96]{0:T(512)(128)(4,1)S(1)} %compare_and_fusion), kind=kOutput, calls=%fused_computation.43 | convolution fusion | flops 51118208 | bytes 3670624 | tf_op jit(solution)/shard_map/tk,ctrw->ckrw/dot_general | solution.py:94
  25.9 1.1 %fusion.24 = f32[2,64,256,16]{2,3,1,0:T(8,128)S(1)} fusion(s32[8,16]{1,0:T(8,128)S(1)} %copy.17, f32[1,8,96,256]{3,1,2,0:T(8,128)S(1)} %fusion.11, f32[1,8,96,256]{3,1,2,0:T(8,128)S(1)} %fusion.8, pred[96]{0:T(512)(128)(4,1)S(1)} %compare_and_fusion), kind=kOutput, calls=%fused_computation.39 | convolution fusion | flops 51118208 | bytes 3670624 | tf_op jit(solution)/shard_map/tk,ctrw->ckrw/dot_general | solution.py:94
  27.0 1.1 %fusion.22 = f32[2,64,256,16]{2,3,1,0:T(8,128)S(1)} fusion(s32[8,16]{1,0:T(8,128)S(1)} %copy.17, f32[1,8,96,256]{3,1,2,0:T(8,128)S(1)} %fusion.11, f32[1,8,96,256]{3,1,2,0:T(8,128)S(1)} %fusion.8, pred[96]{0:T(512)(128)(4,1)S(1)} %compare_and_fusion), kind=kOutput, calls=%fused_computation.37 | convolution fusion | flops 51118208 | bytes 3670624 | tf_op jit(solution)/shard_map/tk,ctrw->ckrw/dot_general | solution.py:94
  28.0 1.6 %add_add_fusion = f32[2,64,256,16]{2,3,1,0:T(8,128)S(1)} fusion(f32[2,64,256,16]{2,3,1,0:T(8,128)S(1)} %fusion.22, f32[2,64,256,16]{2,3,1,0:T(8,128)S(1)} %fusion.24, f32[2,64,256,16]{2,3,1,0:T(8,128)S(1)} %fusion.28, f32[2,64,256,16]{2,3,1,0:T(8,128)S(1)} %fusion.26, s32[8,16]{1,0:T(8,128)S(1)} %copy.17, f32[1,8,96,256]{3,1,2,0:T(8,128)S(1)} %fusion.11, ...), kind=kOutput, calls=%fused_computation.7 | convolution fusion | flops 53215360 | bytes 12059232 | tf_op jit(solution)/shard_map/tk,ctrw->ckrw/dot_general | solution.py:94
  29.7 0.1 dynamic-slice_bitcast_fusion.2
  29.9 0.5 collective-permute-start.2
  30.4 1.6 %collective-permute-start.4 = (f32[2,16,16,128]{3,1,2,0:T(8,128)S(1)}, f32[2,16,16,128]{3,1,2,0:T(8,128)S(1)}, u32[]{:S(2)}, u32[]{:S(2)}) collective-permute-start(f32[2,16,16,128]{3,1,2,0:T(8,128)S(1)} %get-tuple-element.13), channel_id=1, source_target_pairs={{0,3},{1,0},{2,1},{3,2},{4,7},{5,4},{6,5},{7,6},{8,11},{9,8},{10,9... | collective-permute-start | bytes 786440 | tf_op jit(solution)/shard_map/ppermute | solution.py:59
  32.0 6.8 %collective-permute-done.2 = f32[2,16,16,128]{3,1,2,0:T(8,128)S(1)} collective-permute-done((f32[2,16,16,128]{3,1,2,0:T(8,128)S(1)}, f32[2,16,16,128]{3,1,2,0:T(8,128)S(1)}, u32[]{:S(2)}, u32[]{:S(2)}) %collective-permute-start.2) | collective-permute-done | bytes 262176 | tf_op jit(solution)/shard_map/ppermute | solution.py:58
  38.8 0.1 slice_add_fusion.1
  38.9 0.8 %pad_maximum_fusion.1 = f32[2,16,16,256]{3,1,2,0:T(8,128)} fusion(f32[2,16,16,128]{3,1,2,0:T(8,128)S(1)} %get-tuple-element.11, f32[2,16,16,128]{3,1,2,0:T(8,128)S(1)} %get-tuple-element.10), kind=kLoop, calls=%fused_computation.16 | loop fusion | flops 131072 | bytes 1048576 | tf_op jit(solution)/shard_map/concatenate | solution.py:61
  39.7 1.7 %collective-permute-start.3 = (f32[2,16,16,256]{3,1,2,0:T(8,128)}, f32[2,16,16,256]{3,1,2,0:T(8,128)S(1)}, u32[]{:S(2)}, u32[]{:S(2)}) collective-permute-start(f32[2,16,16,256]{3,1,2,0:T(8,128)} %pad_maximum_fusion.1), channel_id=1, source_target_pairs={{0,1},{1,2},{2,3},{3,0},{4,5},{5,6},{6,7},{7,4},{8,9},{9,10},{10,1... | collective-permute-start | bytes 1572872 | tf_op jit(solution)/shard_map/ppermute | solution.py:64
  41.4 0.1 fusion.48
  41.5 0.8 %pad_maximum_fusion.2 = f32[2,16,16,256]{3,1,2,0:T(8,128)} fusion(f32[2,16,16,128]{3,1,2,0:T(8,128)S(1)} %get-tuple-element.15, f32[2,16,16,128]{3,1,2,0:T(8,128)S(1)} %get-tuple-element.14), kind=kLoop, calls=%fused_computation.17 | loop fusion | flops 131072 | bytes 1048576 | tf_op jit(solution)/shard_map/concatenate | solution.py:63
  42.3 0.3 collective-permute-start.5
  42.7 10.9 %collective-permute-done.3 = f32[2,16,16,256]{3,1,2,0:T(8,128)S(1)} collective-permute-done((f32[2,16,16,256]{3,1,2,0:T(8,128)}, f32[2,16,16,256]{3,1,2,0:T(8,128)S(1)}, u32[]{:S(2)}, u32[]{:S(2)}) %collective-permute-start.3) | collective-permute-done | bytes 524320 | tf_op jit(solution)/shard_map/ppermute | solution.py:64
  53.6 3.5 %collective-permute-done.5 = f32[2,16,16,256]{3,1,2,0:T(8,128)S(1)} collective-permute-done((f32[2,16,16,256]{3,1,2,0:T(8,128)}, f32[2,16,16,256]{3,1,2,0:T(8,128)S(1)}, u32[]{:S(2)}, u32[]{:S(2)}) %collective-permute-start.5) | collective-permute-done | bytes 524320 | tf_op jit(solution)/shard_map/ppermute | solution.py:65
  57.1 0.1 fusion.14
  57.3 0.9 %copy.11 = f32[16,16,256]{2,1,0:T(8,128)} copy(f32[16,16,256]{2,0,1:T(8,128)S(1)} %fusion.17) | data formatting | bytes 524288 | tf_op jit(solution)/shard_map/div | solution.py:99
  (10 shorter events, 0.1 us)
Async XLA Ops:
  0.0 11.6 %copy-start = (s32[32,16]{0,1:T(8,128)S(1)}, s32[32,16]{0,1:T(8,128)}, u32[]{:S(2)}) copy-start(s32[32,16]{0,1:T(8,128)} %param.7) | copy-start | bytes 6148
  0.0 7.5 %copy-start.2 = (f32[11,11]{1,0:T(8,128)S(1)}, f32[11,11]{1,0:T(8,128)}, u32[]{:S(2)}) copy-start(f32[11,11]{1,0:T(8,128)} %param.6) | copy-start | bytes 1456
  1.9 11.3 %collective-permute-start = (f32[2,8,21,256]{3,1,2,0:T(8,128)S(1)}, f32[2,8,21,256]{3,1,2,0:T(8,128)S(1)}, u32[]{:S(2)}, u32[]{:S(2)}) collective-permute-start(f32[2,8,21,256]{3,1,2,0:T(8,128)S(1)} %get-tuple-element.8), channel_id=1, source_target_pairs={{0,4},{4,8},{8,12},{12,16},{16,20},{20,24},{24,28},{28,32},{32,36}... | collective-permute-start | bytes 1032200 | tf_op jit(solution)/shard_map/ppermute | solution.py:15
  3.8 9.4 %collective-permute-start.1 = (f32[2,8,21,256]{3,1,2,0:T(8,128)S(1)}, f32[2,8,21,256]{3,1,2,0:T(8,128)S(1)}, u32[]{:S(2)}, u32[]{:S(2)}) collective-permute-start(f32[2,8,21,256]{3,1,2,0:T(8,128)S(1)} %get-tuple-element.9), channel_id=1, source_target_pairs={{4,0},{8,4},{12,8},{16,12},{20,16},{24,20},{28,24},{32,28},{36,32}... | collective-permute-start | bytes 1032200 | tf_op jit(solution)/shard_map/ppermute | solution.py:18
  11.7 2.2 %copy-start.1 = (f32[256,256,11]{1,2,0:T(8,128)S(1)}, f32[256,256,11]{1,2,0:T(8,128)}, u32[]{:S(2)}) copy-start(f32[256,256,11]{1,2,0:T(8,128)} %fusion.1) | copy-start | bytes 8650756
  29.9 9.0 %collective-permute-start.2 = (f32[2,16,16,128]{3,1,2,0:T(8,128)S(1)}, f32[2,16,16,128]{3,1,2,0:T(8,128)S(1)}, u32[]{:S(2)}, u32[]{:S(2)}) collective-permute-start(f32[2,16,16,128]{3,1,2,0:T(8,128)S(1)} %get-tuple-element.12), channel_id=1, source_target_pairs={{0,1},{1,2},{2,3},{3,0},{4,5},{5,6},{6,7},{7,4},{8,9},{9,10},{10,1... | collective-permute-start | bytes 786440 | tf_op jit(solution)/shard_map/ppermute | solution.py:58
  30.4 11.0 %collective-permute-start.4 = (f32[2,16,16,128]{3,1,2,0:T(8,128)S(1)}, f32[2,16,16,128]{3,1,2,0:T(8,128)S(1)}, u32[]{:S(2)}, u32[]{:S(2)}) collective-permute-start(f32[2,16,16,128]{3,1,2,0:T(8,128)S(1)} %get-tuple-element.13), channel_id=1, source_target_pairs={{0,3},{1,0},{2,1},{3,2},{4,7},{5,4},{6,5},{7,6},{8,11},{9,8},{10,9... | collective-permute-start | bytes 786440 | tf_op jit(solution)/shard_map/ppermute | solution.py:59
  39.7 13.9 %collective-permute-start.3 = (f32[2,16,16,256]{3,1,2,0:T(8,128)}, f32[2,16,16,256]{3,1,2,0:T(8,128)S(1)}, u32[]{:S(2)}, u32[]{:S(2)}) collective-permute-start(f32[2,16,16,256]{3,1,2,0:T(8,128)} %pad_maximum_fusion.1), channel_id=1, source_target_pairs={{0,1},{1,2},{2,3},{3,0},{4,5},{5,6},{6,7},{7,4},{8,9},{9,10},{10,1... | collective-permute-start | bytes 1572872 | tf_op jit(solution)/shard_map/ppermute | solution.py:64
  42.3 14.8 %collective-permute-start.5 = (f32[2,16,16,256]{3,1,2,0:T(8,128)}, f32[2,16,16,256]{3,1,2,0:T(8,128)S(1)}, u32[]{:S(2)}, u32[]{:S(2)}) collective-permute-start(f32[2,16,16,256]{3,1,2,0:T(8,128)} %pad_maximum_fusion.2), channel_id=1, source_target_pairs={{0,3},{1,0},{2,1},{3,2},{4,7},{5,4},{6,5},{7,6},{8,11},{9,8},{10,9... | collective-permute-start | bytes 1572872 | tf_op jit(solution)/shard_map/ppermute | solution.py:65

commit v3 on v2

v3 whole, which is shorter than its diff:
```python
import jax
import jax.numpy as jnp
from jax import lax
from jax.sharding import PartitionSpec as P

BR = 8
MAXOFF = 2


def bordered_rows(block, axis, width):
    count = lax.axis_size(axis)
    forward = [(i, i + 1) for i in range(count - 1)]
    backward = [(target, source) for source, target in forward]
    dim = block.ndim - 2
    low = lax.ppermute(
        lax.slice_in_dim(block, block.shape[dim] - width, None, axis=dim), axis, forward
    )
    high = lax.ppermute(lax.slice_in_dim(block, 0, width, axis=dim), axis, backward)
    return jnp.concatenate([low, block, high], axis=dim)


def toeplitz(taps, cols):
    size = taps.shape[1]
    shape = (size, cols + size - 1, cols)
    i = lax.broadcasted_iota(jnp.int32, shape, 1)
    o = lax.broadcasted_iota(jnp.int32, shape, 2)
    b = lax.broadcasted_iota(jnp.int32, shape, 0)
    onehot = (i - o == b).astype(jnp.float32)
    return jnp.einsum("ab,bio->aio", taps, onehot, precision=lax.Precision.HIGHEST)


def correlate_rows(bordered, kernel):
    return lax.conv_general_dilated(
        bordered,
        kernel,
        window_strides=(1,),
        padding="VALID",
        dimension_numbers=("NHC", "HIO", "NHC"),
        precision=lax.Precision.HIGH,
        preferred_element_type=jnp.float32,
    )


def ring_reduce_scatter(partial, axis):
    count = lax.axis_size(axis)
    if count != 4:
        return lax.psum_scatter(partial, axis, scatter_dimension=2, tiled=True)
    me = lax.axis_index(axis)
    rows = partial.shape[2] // count
    half = partial.shape[1] // 2
    right = [(i, (i + 1) % count) for i in range(count)]
    left = [(i, (i - 1) % count) for i in range(count)]

    def block(step):
        return lax.dynamic_slice_in_dim(partial, ((me + step) % count) * rows, rows, axis=2)

    far = block(2)
    from_left = lax.ppermute(far[:, :half], axis, right)
    from_right = lax.ppermute(far[:, half:], axis, left)
    ahead = block(1)
    ahead = jnp.concatenate([ahead[:, :half] + from_left, ahead[:, half:]], axis=1)
    behind = block(count - 1)
    behind = jnp.concatenate([behind[:, :half], behind[:, half:] + from_right], axis=1)
    got_left = lax.ppermute(ahead, axis, right)
    got_right = lax.ppermute(behind, axis, left)
    return block(0) + got_left + got_right


def shards(science, inv_variance, psf_kernel, offsets):
    radius = (psf_kernel.shape[0] - 1) // 2
    reach = MAXOFF * BR
    visits, rows, cols = science.shape
    total_rows = rows * lax.axis_size("sky")

    weighted = science * inv_variance
    both = jnp.stack([weighted, inv_variance])
    bordered = bordered_rows(both, "sky", radius + reach)

    chunk = 128 if cols % 128 == 0 else cols
    padded = jnp.pad(bordered, ((0, 0), (0, 0), (0, 0), (radius, radius)))
    kernels = [toeplitz(psf_kernel, chunk), toeplitz(psf_kernel * psf_kernel, chunk)]

    first = lax.axis_index("sky") * rows - reach
    row_ids = first + lax.broadcasted_iota(jnp.int32, (1, 1, rows + 2 * reach, 1), 2)
    inside = (row_ids >= 0) & (row_ids < total_rows)
    mine = lax.dynamic_slice_in_dim(offsets, lax.axis_index("visit") * visits, visits, 0)

    pieces = []
    for start_col in range(0, cols, chunk):
        window = padded[..., start_col : start_col + chunk + 2 * radius]
        images = jnp.stack([correlate_rows(window[c], kernels[c]) for c in range(2)])
        images = jnp.where(inside, images, 0.0)
        partial = jnp.zeros((2, offsets.shape[1], rows, chunk), jnp.float32)
        for offset_value in range(-MAXOFF, MAXOFF + 1):
            onehot = (mine == offset_value).astype(jnp.float32)
            start = reach + offset_value * BR
            shifted = images[:, :, start : start + rows, :]
            partial = partial + jnp.einsum(
                "tk,ctrw->ckrw", onehot, shifted, precision=lax.Precision.HIGHEST
            )
        stacked = ring_reduce_scatter(partial, "visit")
        pieces.append(stacked[0] / jnp.sqrt(stacked[1]))
    return jnp.concatenate(pieces, axis=-1)


def solution(mesh):
    return jax.shard_map(
        shards,
        mesh=mesh,
        in_specs=(P("visit", "sky", None), P("visit", "sky", None), P(), P()),
        out_specs=P(None, ("sky", "visit"), None),
        check_vma=False,
    )
```

time: 58.4 us -> 64 us (1.096)
  the two profiles are of different devices: /device:TPU:54 before, /device:TPU:97 now
where the time goes in v3:
time: 64 us; the launch traced here: 63.8 us
  matrix products  20.3 us (32%)
  waiting for transfers between devices  19.3 us (30%)
  starting transfers between devices  18.6 us (29%)
  other arithmetic  4.01 us (6%)
  local copies, waits for them, and re-layouts  1.19 us (2%)
    conv_general_dilated x4, matrix products, correlate_rows(): lax.conv_general_dilated(bordered, kernel, window_strides=(1,), padding='...  12.6 us
    ppermute x2, waiting for transfers between devices, ring_reduce_scatter(): got_left = lax.ppermute(ahead, axis, right)  11.2 us
    dot_general x10, matrix products, shards(): jnp.einsum('tk,ctrw->ckrw', onehot, shifted, precision=lax.Precision.HIGH...  6.42 us
    ppermute x2, starting transfers between devices, ring_reduce_scatter(): got_right = lax.ppermute(behind, axis, left)  5.92 us
    ppermute x1, waiting for transfers between devices, bordered_rows(): lax.ppermute(lax.slice_in_dim(block, 0, width, axis=dim), axis, backward)  5.71 us
    ppermute x1, starting transfers between devices, bordered_rows(): lax.ppermute(lax.slice_in_dim(block, block.shape[dim] - width, None, axis...  5.32 us
    ppermute x2, starting transfers between devices, ring_reduce_scatter(): from_right = lax.ppermute(far[:, half:], axis, left)  5.22 us
    ppermute x1, starting transfers between devices, bordered_rows(): lax.ppermute(lax.slice_in_dim(block, 0, width, axis=dim), axis, backward)  1.92 us
  transfers between devices with their start and end apart: 10, of which 6 were waited for; matrix products, arithmetic and copies ran while one was open for 3% of the time, Pallas kernels for 0%

profile of v3, /device:TPU:97, one launch (start us, length us, event | category | flops | bytes accessed | tf_op | source)
XLA Modules:
  0.0 63.8 jit_solution(1191719227792896329)
XLA Ops:
  0.0 1.8 %fusion.7 = (f32[1,8,64,256]{3,1,2,0:T(8,128)S(1)}, f32[1,8,64,256]{3,1,2,0:T(8,128)S(1)}) fusion(f32[8,64,256]{2,1,0:T(8,128)} %param.4, f32[8,64,256]{2,1,0:T(8,128)} %param.5), kind=kLoop, calls=%fused_computation.32 | loop fusion | flops 131072 | bytes 2097152 | tf_op jit(solution)/shard_map/stack | solution.py:76
  1.9 5.3 %collective-permute-start = (f32[2,8,21,256]{3,1,2,0:T(8,128)S(1)}, f32[2,8,21,256]{3,1,2,0:T(8,128)S(1)}, u32[]{:S(2)}, u32[]{:S(2)}) collective-permute-start(f32[2,8,21,256]{3,1,2,0:T(8,128)S(1)} %get-tuple-element.11), channel_id=1, source_target_pairs={{0,4},{4,8},{8,12},{12,16},{16,20},{20,24},{24,28},{28,32},{32,36}... | collective-permute-start | bytes 1032200 | tf_op jit(solution)/shard_map/ppermute | solution.py:15
  7.2 1.9 %collective-permute-start.1 = (f32[2,8,21,256]{3,1,2,0:T(8,128)S(1)}, f32[2,8,21,256]{3,1,2,0:T(8,128)}, u32[]{:S(2)}, u32[]{:S(2)}) collective-permute-start(f32[2,8,21,256]{3,1,2,0:T(8,128)S(1)} %get-tuple-element.12), channel_id=1, source_target_pairs={{4,0},{8,4},{12,8},{16,12},{20,16},{24,20},{28,24},{32,28},{36,32}... | collective-permute-start | bytes 1032200 | tf_op jit(solution)/shard_map/ppermute | solution.py:18
  9.4 0.6 fusion.1
  10.1 0.7 %fusion.2 = f32[138,128,11]{1,2,0:T(8,128)S(1)} fusion(f32[11,11]{1,0:T(8,128)S(1)} %copy-done.1), kind=kOutput, calls=%fused_computation.20 | convolution fusion | flops 26036736 | bytes 777700 | tf_op jit(solution)/shard_map/ab,bio->aio/dot_general | solution.py:29
  10.7 0.7 %collective-permute-done = f32[2,8,21,256]{3,1,2,0:T(8,128)S(1)} collective-permute-done((f32[2,8,21,256]{3,1,2,0:T(8,128)S(1)}, f32[2,8,21,256]{3,1,2,0:T(8,128)S(1)}, u32[]{:S(2)}, u32[]{:S(2)}) %collective-permute-start) | collective-permute-done | bytes 344096 | tf_op jit(solution)/shard_map/ppermute | solution.py:15
  11.4 5.7 %collective-permute-done.1 = f32[2,8,21,256]{3,1,2,0:T(8,128)} collective-permute-done((f32[2,8,21,256]{3,1,2,0:T(8,128)S(1)}, f32[2,8,21,256]{3,1,2,0:T(8,128)}, u32[]{:S(2)}, u32[]{:S(2)}) %collective-permute-start.1) | collective-permute-done | bytes 344096 | tf_op jit(solution)/shard_map/ppermute | solution.py:18
  17.1 1.7 %select_maximum_fusion = f32[2,8,106,266]{3,1,2,0:T(8,128)S(1)} fusion(f32[2,8,21,256]{3,1,2,0:T(8,128)} %collective-permute-done.1, f32[2,8,21,256]{3,1,2,0:T(8,128)S(1)} %collective-permute-done, f32[1,8,64,256]{3,1,2,0:T(8,128)S(1)} %get-tuple-element.14, f32[1,8,64,256]{3,1,2,0:T(8,128)S(1)} %get-tuple-element.13), kind=kLoop, calls=%fused_computation.2 | loop fusion | flops 4511360 | bytes 3541248 | tf_op jit(solution)/shard_map/concatenate | solution.py:19
  18.8 3.1 %convolution_bitcast_fusion = f32[1,8,96,128]{3,1,2,0:T(8,128)S(1)} fusion(f32[2,8,106,266]{3,1,2,0:T(8,128)S(1)} %select_maximum_fusion, f32[11,138,128]{2,0,1:T(8,128)S(1)} %fusion.1), kind=kOutput, calls=%fused_computation.14 | convolution fusion | flops 895352832 | bytes 2392064 | tf_op jit(solution)/shard_map/conv_general_dilated | solution.py:33
  21.9 3.1 %convolution_bitcast_fusion.2 = f32[1,8,96,128]{3,1,2,0:T(8,128)S(1)} fusion(f32[2,8,106,266]{3,1,2,0:T(8,128)S(1)} %select_maximum_fusion, f32[11,138,128]{2,0,1:T(8,128)S(1)} %fusion.1), kind=kOutput, calls=%fused_computation.16 | convolution fusion | flops 895352832 | bytes 2392064 | tf_op jit(solution)/shard_map/conv_general_dilated | solution.py:33
  25.0 3.1 %convolution_bitcast_fusion.1 = f32[1,8,96,128]{3,1,2,0:T(8,128)S(1)} fusion(f32[2,8,106,266]{3,1,2,0:T(8,128)S(1)} %select_maximum_fusion, f32[138,128,11]{1,2,0:T(8,128)S(1)} %fusion.2), kind=kOutput, calls=%fused_computation.15 | convolution fusion | flops 895352832 | bytes 2392064 | tf_op jit(solution)/shard_map/conv_general_dilated | solution.py:33
  28.1 3.3 %convolution_bitcast_fusion.3 = f32[1,8,96,128]{3,1,2,0:T(8,128)S(1)} fusion(f32[2,8,106,266]{3,1,2,0:T(8,128)S(1)} %select_maximum_fusion, f32[138,128,11]{1,2,0:T(8,128)S(1)} %fusion.2), kind=kOutput, calls=%fused_computation.17 | convolution fusion | flops 895352832 | bytes 2392064 | tf_op jit(solution)/shard_map/conv_general_dilated | solution.py:33
  31.4 0.6 %fusion.27 = f32[2,64,128,16]{2,3,1,0:T(8,128)S(1)} fusion(pred[8,16]{1,0:T(8,128)(4,1)S(1)} %get-tuple-element.31, f32[1,8,96,128]{3,1,2,0:T(8,128)S(1)} %convolution_bitcast_fusion.2, f32[1,8,96,128]{3,1,2,0:T(8,128)S(1)} %convolution_bitcast_fusion.3, pred[96]{0:T(512)(128)(4,1)S(1)} %compare_and_fusion), kind=kOutput, calls=%fused_computation.74 | convolution fusion | flops 25559040 | bytes 1835232 | tf_op jit(solution)/shard_map/tk,ctrw->ckrw/dot_general | solution.py:98
  32.1 0.6 %convolution_add_fusion.7 = f32[2,64,128,16]{2,3,1,0:T(8,128)S(1)} fusion(f32[2,64,128,16]{2,3,1,0:T(8,128)S(1)} %fusion.27, pred[8,16]{1,0:T(8,128)(4,1)S(1)} %get-tuple-element.30, f32[1,8,96,128]{3,1,2,0:T(8,128)S(1)} %convolution_bitcast_fusion.2, f32[1,8,96,128]{3,1,2,0:T(8,128)S(1)} %convolution_bitcast_fusion.3, pred[96]{0:T(512)(128)(4,1)S(1)} %compare_and_fusion), kind=kOutput, calls=%fused_computation.13 | convolution fusion | flops 25821184 | bytes 2883808 | tf_op jit(solution)/shard_map/tk,ctrw->ckrw/dot_general | solution.py:98
  32.7 0.6 %fusion.25 = f32[2,64,128,16]{2,3,1,0:T(8,128)S(1)} fusion(pred[8,16]{1,0:T(8,128)(4,1)S(1)} %get-tuple-element.31, f32[1,8,96,128]{3,1,2,0:T(8,128)S(1)} %convolution_bitcast_fusion, f32[1,8,96,128]{3,1,2,0:T(8,128)S(1)} %convolution_bitcast_fusion.1, pred[96]{0:T(512)(128)(4,1)S(1)} %compare_and_fusion), kind=kOutput, calls=%fused_computation.72 | convolution fusion | flops 25559040 | bytes 1835232 | tf_op jit(solution)/shard_map/tk,ctrw->ckrw/dot_general | solution.py:98
  33.4 0.6 %convolution_add_fusion.3 = f32[2,64,128,16]{2,3,1,0:T(8,128)S(1)} fusion(f32[2,64,128,16]{2,3,1,0:T(8,128)S(1)} %fusion.25, pred[8,16]{1,0:T(8,128)(4,1)S(1)} %get-tuple-element.30, f32[1,8,96,128]{3,1,2,0:T(8,128)S(1)} %convolution_bitcast_fusion, f32[1,8,96,128]{3,1,2,0:T(8,128)S(1)} %convolution_bitcast_fusion.1, pred[96]{0:T(512)(128)(4,1)S(1)} %compare_and_fusion), kind=kOutput, calls=%fused_computation.9 | convolution fusion | flops 25821184 | bytes 2883808 | tf_op jit(solution)/shard_map/tk,ctrw->ckrw/dot_general | solution.py:98
  34.0 0.6 %convolution_add_fusion.6 = f32[2,64,128,16]{2,3,1,0:T(8,128)S(1)} fusion(f32[2,64,128,16]{2,3,1,0:T(8,128)S(1)} %convolution_add_fusion.7, pred[8,16]{1,0:T(8,128)(4,1)S(1)} %get-tuple-element.29, f32[1,8,96,128]{3,1,2,0:T(8,128)S(1)} %convolution_bitcast_fusion.2, f32[1,8,96,128]{3,1,2,0:T(8,128)S(1)} %convolution_bitcast_fusion.3, ...), kind=kOutput, calls=%fused_computation.12 | convolution fusion | flops 25821184 | bytes 2883808 | tf_op jit(solution)/shard_map/tk,ctrw->ckrw/dot_general | solution.py:98
  34.7 0.6 %convolution_add_fusion.2 = f32[2,64,128,16]{2,3,1,0:T(8,128)S(1)} fusion(f32[2,64,128,16]{2,3,1,0:T(8,128)S(1)} %convolution_add_fusion.3, pred[8,16]{1,0:T(8,128)(4,1)S(1)} %get-tuple-element.29, f32[1,8,96,128]{3,1,2,0:T(8,128)S(1)} %convolution_bitcast_fusion, f32[1,8,96,128]{3,1,2,0:T(8,128)S(1)} %convolution_bitcast_fusion.1, ...), kind=kOutput, calls=%fused_computation.8 | convolution fusion | flops 25821184 | bytes 2883808 | tf_op jit(solution)/shard_map/tk,ctrw->ckrw/dot_general | solution.py:98
  35.3 0.6 %convolution_add_fusion.5 = f32[2,64,128,16]{2,3,1,0:T(8,128)S(1)} fusion(f32[2,64,128,16]{2,3,1,0:T(8,128)S(1)} %convolution_add_fusion.6, pred[8,16]{1,0:T(8,128)(4,1)S(1)} %get-tuple-element.28, f32[1,8,96,128]{3,1,2,0:T(8,128)S(1)} %convolution_bitcast_fusion.2, f32[1,8,96,128]{3,1,2,0:T(8,128)S(1)} %convolution_bitcast_fusion.3, ...), kind=kOutput, calls=%fused_computation.11 | convolution fusion | flops 25821184 | bytes 2883808 | tf_op jit(solution)/shard_map/tk,ctrw->ckrw/dot_general | solution.py:98
  36.0 0.6 %convolution_add_fusion.1 = f32[2,64,128,16]{2,3,1,0:T(8,128)S(1)} fusion(f32[2,64,128,16]{2,3,1,0:T(8,128)S(1)} %convolution_add_fusion.2, pred[8,16]{1,0:T(8,128)(4,1)S(1)} %get-tuple-element.28, f32[1,8,96,128]{3,1,2,0:T(8,128)S(1)} %convolution_bitcast_fusion, f32[1,8,96,128]{3,1,2,0:T(8,128)S(1)} %convolution_bitcast_fusion.1, ...), kind=kOutput, calls=%fused_computation.7 | convolution fusion | flops 25821184 | bytes 2883808 | tf_op jit(solution)/shard_map/tk,ctrw->ckrw/dot_general | solution.py:98
  36.6 0.6 %convolution_add_fusion.4 = f32[2,64,128,16]{2,3,1,0:T(8,128)S(1)} fusion(f32[2,64,128,16]{2,3,1,0:T(8,128)S(1)} %convolution_add_fusion.5, pred[8,16]{1,0:T(8,128)(4,1)S(1)} %get-tuple-element.27, f32[1,8,96,128]{3,1,2,0:T(8,128)S(1)} %convolution_bitcast_fusion.2, f32[1,8,96,128]{3,1,2,0:T(8,128)S(1)} %convolution_bitcast_fusion.3, ...), kind=kOutput, calls=%fused_computation.10 | convolution fusion | flops 25821184 | bytes 2883808 | tf_op jit(solution)/shard_map/tk,ctrw->ckrw/dot_general | solution.py:98
  37.3 0.6 %convolution_add_fusion = f32[2,64,128,16]{2,3,1,0:T(8,128)S(1)} fusion(f32[2,64,128,16]{2,3,1,0:T(8,128)S(1)} %convolution_add_fusion.1, pred[8,16]{1,0:T(8,128)(4,1)S(1)} %get-tuple-element.27, f32[1,8,96,128]{3,1,2,0:T(8,128)S(1)} %convolution_bitcast_fusion, f32[1,8,96,128]{3,1,2,0:T(8,128)S(1)} %convolution_bitcast_fusion.1, ...), kind=kOutput, calls=%fused_computation.6 | convolution fusion | flops 25821184 | bytes 2883808 | tf_op jit(solution)/shard_map/tk,ctrw->ckrw/dot_general | solution.py:98
  37.9 0.1 dynamic-slice_bitcast_fusion.2
  38.1 2.6 %collective-permute-start.4 = (f32[2,8,16,128]{3,1,2,0:T(8,128)S(1)}, f32[2,8,16,128]{3,1,2,0:T(8,128)S(1)}, u32[]{:S(2)}, u32[]{:S(2)}) collective-permute-start(f32[2,8,16,128]{3,1,2,0:T(8,128)S(1)} %get-tuple-element.18), channel_id=1, source_target_pairs={{0,3},{1,0},{2,1},{3,2},{4,7},{5,4},{6,5},{7,6},{8,11},{9,8},{10,9... | collective-permute-start | bytes 393224 | tf_op jit(solution)/shard_map/ppermute | solution.py:59
  40.8 2.7 %collective-permute-start.8 = (f32[2,8,16,128]{3,1,2,0:T(8,128)S(1)}, f32[2,8,16,128]{3,1,2,0:T(8,128)S(1)}, u32[]{:S(2)}, u32[]{:S(2)}) collective-permute-start(f32[2,8,16,128]{3,1,2,0:T(8,128)S(1)} %get-tuple-element.24), channel_id=1, source_target_pairs={{0,3},{1,0},{2,1},{3,2},{4,7},{5,4},{6,5},{7,6},{8,11},{9,8},{10,9... | collective-permute-start | bytes 393224 | tf_op jit(solution)/shard_map/ppermute | solution.py:59
  43.4 0.1 collective-permute-done.4
  43.6 3.2 %collective-permute-start.5 = (f32[2,16,16,128]{3,1,2,0:T(8,128)S(1)}, f32[2,16,16,128]{3,1,2,0:T(8,128)S(1)}, u32[]{:S(2)}, u32[]{:S(2)}) collective-permute-start(f32[2,16,16,128]{3,1,2,0:T(8,128)S(1)} %pad_maximum_fusion.3), channel_id=1, source_target_pairs={{0,3},{1,0},{2,1},{3,2},{4,7},{5,4},{6,5},{7,6},{8,11},{9,8},{10,9... | collective-permute-start | bytes 786440 | tf_op jit(solution)/shard_map/ppermute | solution.py:65
  46.8 1.7 %collective-permute-done.2 = f32[2,8,16,128]{3,1,2,0:T(8,128)S(1)} collective-permute-done((f32[2,8,16,128]{3,1,2,0:T(8,128)S(1)}, f32[2,8,16,128]{3,1,2,0:T(8,128)S(1)}, u32[]{:S(2)}, u32[]{:S(2)}) %collective-permute-start.2) | collective-permute-done | bytes 131104 | tf_op jit(solution)/shard_map/ppermute | solution.py:58
  48.7 2.7 %collective-permute-start.9 = (f32[2,16,16,128]{3,1,2,0:T(8,128)S(1)}, f32[2,16,16,128]{3,1,2,0:T(8,128)S(1)}, u32[]{:S(2)}, u32[]{:S(2)}) collective-permute-start(f32[2,16,16,128]{3,1,2,0:T(8,128)S(1)} %pad_maximum_fusion.5), channel_id=1, source_target_pairs={{0,3},{1,0},{2,1},{3,2},{4,7},{5,4},{6,5},{7,6},{8,11},{9,8},{10,9... | collective-permute-start | bytes 786440 | tf_op jit(solution)/shard_map/ppermute | solution.py:65
  51.6 6.5 %collective-permute-done.3 = f32[2,16,16,128]{3,1,2,0:T(8,128)S(1)} collective-permute-done((f32[2,16,16,128]{3,1,2,0:T(8,128)S(1)}, f32[2,16,16,128]{3,1,2,0:T(8,128)S(1)}, u32[]{:S(2)}, u32[]{:S(2)}) %collective-permute-start.3) | collective-permute-done | bytes 262176 | tf_op jit(solution)/shard_map/ppermute | solution.py:64
  58.2 4.7 %collective-permute-done.7 = f32[2,16,16,128]{3,1,2,0:T(8,128)S(1)} collective-permute-done((f32[2,16,16,128]{3,1,2,0:T(8,128)S(1)}, f32[2,16,16,128]{3,1,2,0:T(8,128)S(1)}, u32[]{:S(2)}, u32[]{:S(2)}) %collective-permute-start.7) | collective-permute-done | bytes 262176 | tf_op jit(solution)/shard_map/ppermute | solution.py:64
  63.0 0.9 %copy.13 = f32[16,16,256]{2,1,0:T(8,128)} copy(f32[16,16,256]{2,0,1:T(8,128)S(1)} %pad_maximum_fusion.6) | data formatting | bytes 524288 | tf_op jit(solution)/shard_map/concatenate | solution.py:103
  (32 shorter events, 0.9 us)
Async XLA Ops:
  0.0 9.2 %copy-start = (s32[32,16]{0,1:T(8,128)S(1)}, s32[32,16]{0,1:T(8,128)}, u32[]{:S(2)}) copy-start(s32[32,16]{0,1:T(8,128)} %param.7) | copy-start | bytes 6148
  0.0 9.4 %copy-start.1 = (f32[11,11]{1,0:T(8,128)S(1)}, f32[11,11]{1,0:T(8,128)}, u32[]{:S(2)}) copy-start(f32[11,11]{1,0:T(8,128)} %param.6) | copy-start | bytes 1456
  1.9 9.5 %collective-permute-start = (f32[2,8,21,256]{3,1,2,0:T(8,128)S(1)}, f32[2,8,21,256]{3,1,2,0:T(8,128)S(1)}, u32[]{:S(2)}, u32[]{:S(2)}) collective-permute-start(f32[2,8,21,256]{3,1,2,0:T(8,128)S(1)} %get-tuple-element.11), channel_id=1, source_target_pairs={{0,4},{4,8},{8,12},{12,16},{16,20},{20,24},{24,28},{28,32},{32,36}... | collective-permute-start | bytes 1032200 | tf_op jit(solution)/shard_map/ppermute | solution.py:15
  7.2 9.9 %collective-permute-start.1 = (f32[2,8,21,256]{3,1,2,0:T(8,128)S(1)}, f32[2,8,21,256]{3,1,2,0:T(8,128)}, u32[]{:S(2)}, u32[]{:S(2)}) collective-permute-start(f32[2,8,21,256]{3,1,2,0:T(8,128)S(1)} %get-tuple-element.12), channel_id=1, source_target_pairs={{4,0},{8,4},{12,8},{16,12},{20,16},{24,20},{28,24},{32,28},{36,32}... | collective-permute-start | bytes 1032200 | tf_op jit(solution)/shard_map/ppermute | solution.py:18
  38.1 5.5 %collective-permute-start.4 = (f32[2,8,16,128]{3,1,2,0:T(8,128)S(1)}, f32[2,8,16,128]{3,1,2,0:T(8,128)S(1)}, u32[]{:S(2)}, u32[]{:S(2)}) collective-permute-start(f32[2,8,16,128]{3,1,2,0:T(8,128)S(1)} %get-tuple-element.18), channel_id=1, source_target_pairs={{0,3},{1,0},{2,1},{3,2},{4,7},{5,4},{6,5},{7,6},{8,11},{9,8},{10,9... | collective-permute-start | bytes 393224 | tf_op jit(solution)/shard_map/ppermute | solution.py:59
  40.7 10.7 %collective-permute-start.6 = (f32[2,8,16,128]{3,1,2,0:T(8,128)S(1)}, f32[2,8,16,128]{3,1,2,0:T(8,128)S(1)}, u32[]{:S(2)}, u32[]{:S(2)}) collective-permute-start(f32[2,8,16,128]{3,1,2,0:T(8,128)S(1)} %get-tuple-element.23), channel_id=1, source_target_pairs={{0,1},{1,2},{2,3},{3,0},{4,5},{5,6},{6,7},{7,4},{8,9},{9,10},{10,1... | collective-permute-start | bytes 393224 | tf_op jit(solution)/shard_map/ppermute | solution.py:58
  40.8 7.8 %collective-permute-start.8 = (f32[2,8,16,128]{3,1,2,0:T(8,128)S(1)}, f32[2,8,16,128]{3,1,2,0:T(8,128)S(1)}, u32[]{:S(2)}, u32[]{:S(2)}) collective-permute-start(f32[2,8,16,128]{3,1,2,0:T(8,128)S(1)} %get-tuple-element.24), channel_id=1, source_target_pairs={{0,3},{1,0},{2,1},{3,2},{4,7},{5,4},{6,5},{7,6},{8,11},{9,8},{10,9... | collective-permute-start | bytes 393224 | tf_op jit(solution)/shard_map/ppermute | solution.py:59
  43.4 5.0 %collective-permute-start.2 = (f32[2,8,16,128]{3,1,2,0:T(8,128)S(1)}, f32[2,8,16,128]{3,1,2,0:T(8,128)S(1)}, u32[]{:S(2)}, u32[]{:S(2)}) collective-permute-start(f32[2,8,16,128]{3,1,2,0:T(8,128)S(1)} %get-tuple-element.17), channel_id=1, source_target_pairs={{0,1},{1,2},{2,3},{3,0},{4,5},{5,6},{6,7},{7,4},{8,9},{9,10},{10,1... | collective-permute-start | bytes 393224 | tf_op jit(solution)/shard_map/ppermute | solution.py:58
  43.6 7.9 %collective-permute-start.5 = (f32[2,16,16,128]{3,1,2,0:T(8,128)S(1)}, f32[2,16,16,128]{3,1,2,0:T(8,128)S(1)}, u32[]{:S(2)}, u32[]{:S(2)}) collective-permute-start(f32[2,16,16,128]{3,1,2,0:T(8,128)S(1)} %pad_maximum_fusion.3), channel_id=1, source_target_pairs={{0,3},{1,0},{2,1},{3,2},{4,7},{5,4},{6,5},{7,6},{8,11},{9,8},{10,9... | collective-permute-start | bytes 786440 | tf_op jit(solution)/shard_map/ppermute | solution.py:65
  48.5 9.5 %collective-permute-start.3 = (f32[2,16,16,128]{3,1,2,0:T(8,128)S(1)}, f32[2,16,16,128]{3,1,2,0:T(8,128)S(1)}, u32[]{:S(2)}, u32[]{:S(2)}) collective-permute-start(f32[2,16,16,128]{3,1,2,0:T(8,128)S(1)} %pad_maximum_fusion.2), channel_id=1, source_target_pairs={{0,1},{1,2},{2,3},{3,0},{4,5},{5,6},{6,7},{7,4},{8,9},{9,10},{10,1... | collective-permute-start | bytes 786440 | tf_op jit(solution)/shard_map/ppermute | solution.py:64
  48.7 9.5 %collective-permute-start.9 = (f32[2,16,16,128]{3,1,2,0:T(8,128)S(1)}, f32[2,16,16,128]{3,1,2,0:T(8,128)S(1)}, u32[]{:S(2)}, u32[]{:S(2)}) collective-permute-start(f32[2,16,16,128]{3,1,2,0:T(8,128)S(1)} %pad_maximum_fusion.5), channel_id=1, source_target_pairs={{0,3},{1,0},{2,1},{3,2},{4,7},{5,4},{6,5},{7,6},{8,11},{9,8},{10,9... | collective-permute-start | bytes 786440 | tf_op jit(solution)/shard_map/ppermute | solution.py:65
  51.5 11.4 %collective-permute-start.7 = (f32[2,16,16,128]{3,1,2,0:T(8,128)S(1)}, f32[2,16,16,128]{3,1,2,0:T(8,128)S(1)}, u32[]{:S(2)}, u32[]{:S(2)}) collective-permute-start(f32[2,16,16,128]{3,1,2,0:T(8,128)S(1)} %pad_maximum_fusion.4), channel_id=1, source_target_pairs={{0,1},{1,2},{2,3},{3,0},{4,5},{5,6},{6,7},{7,4},{8,9},{9,10},{10,1... | collective-permute-start | bytes 786440 | tf_op jit(solution)/shard_map/ppermute | solution.py:64

commit v4 on v3

v4 whole, which is shorter than its diff:
```python
import jax
import jax.numpy as jnp
from jax import lax
from jax.sharding import PartitionSpec as P

BR = 8
MAXOFF = 2


def bordered_rows(block, axis, width):
    count = lax.axis_size(axis)
    forward = [(i, i + 1) for i in range(count - 1)]
    backward = [(target, source) for source, target in forward]
    dim = block.ndim - 2
    low = lax.ppermute(
        lax.slice_in_dim(block, block.shape[dim] - width, None, axis=dim), axis, forward
    )
    high = lax.ppermute(lax.slice_in_dim(block, 0, width, axis=dim), axis, backward)
    return jnp.concatenate([low, block, high], axis=dim)


def toeplitz(taps, cols):
    size = taps.shape[1]
    shape = (size, cols + size - 1, cols)
    i = lax.broadcasted_iota(jnp.int32, shape, 1)
    o = lax.broadcasted_iota(jnp.int32, shape, 2)
    b = lax.broadcasted_iota(jnp.int32, shape, 0)
    onehot = (i - o == b).astype(jnp.float32)
    return jnp.einsum("ab,bio->aio", taps, onehot, precision=lax.Precision.HIGHEST)


def correlate_rows(bordered, kernel):
    return lax.conv_general_dilated(
        bordered,
        kernel,
        window_strides=(1,),
        padding="VALID",
        dimension_numbers=("NHC", "HIO", "NHC"),
        precision=lax.Precision.HIGH,
        preferred_element_type=jnp.float32,
    )


def ring_step_one(partial, axis):
    me = lax.axis_index(axis)
    count = lax.axis_size(axis)
    rows = partial.shape[1] // count
    half = partial.shape[0] // 2
    blocks = [
        lax.dynamic_slice_in_dim(partial, ((me + step) % count) * rows, rows, axis=1)
        for step in range(count)
    ]
    right = [(i, (i + 1) % count) for i in range(count)]
    left = [(i, (i - 1) % count) for i in range(count)]
    from_left = lax.ppermute(blocks[2][:half], axis, right)
    from_right = lax.ppermute(blocks[2][half:], axis, left)
    return blocks, from_left, from_right


def ring_step_two(blocks, from_left, from_right, axis):
    count = lax.axis_size(axis)
    half = blocks[0].shape[0] // 2
    right = [(i, (i + 1) % count) for i in range(count)]
    left = [(i, (i - 1) % count) for i in range(count)]
    ahead = jnp.concatenate([blocks[1][:half] + from_left, blocks[1][half:]], axis=0)
    behind = jnp.concatenate([blocks[3][:half], blocks[3][half:] + from_right], axis=0)
    got_left = lax.ppermute(ahead, axis, right)
    got_right = lax.ppermute(behind, axis, left)
    return blocks[0] + got_left + got_right


def full_toeplitz(taps, cols, chunk):
    size = taps.shape[1]
    radius = (size - 1) // 2
    block = toeplitz(taps, chunk)
    parts = []
    for start_col in range(0, cols, chunk):
        low = start_col - radius
        first, last = max(0, -low), min(block.shape[1], cols - low)
        part = block[:, first:last, :]
        parts.append(jnp.pad(part, ((0, 0), (low + first, cols - (low + last)), (0, 0))))
    return jnp.concatenate(parts, axis=2)


def partial_sums(images, mine, rows):
    reach = MAXOFF * BR
    partial = jnp.zeros((mine.shape[1], rows, images.shape[2]), jnp.float32)
    for offset_value in range(-MAXOFF, MAXOFF + 1):
        onehot = (mine == offset_value).astype(jnp.float32)
        start = reach + offset_value * BR
        shifted = images[:, start : start + rows, :]
        partial = partial + jnp.einsum(
            "tk,trw->krw", onehot, shifted, precision=lax.Precision.HIGHEST
        )
    return partial


def shards(science, inv_variance, psf_kernel, offsets):
    radius = (psf_kernel.shape[0] - 1) // 2
    reach = MAXOFF * BR
    visits, rows, cols = science.shape
    total_rows = rows * lax.axis_size("sky")
    chunk = 128 if cols % 128 == 0 else cols

    first = lax.axis_index("sky") * rows - reach
    row_ids = first + lax.broadcasted_iota(jnp.int32, (1, rows + 2 * reach, 1), 1)
    inside = (row_ids >= 0) & (row_ids < total_rows)
    mine = lax.dynamic_slice_in_dim(offsets, lax.axis_index("visit") * visits, visits, 0)

    weighted = bordered_rows(science * inv_variance, "sky", radius + reach)
    inverse = bordered_rows(inv_variance, "sky", radius + reach)

    if lax.axis_size("visit") != 4:
        psi = correlate_rows(weighted, full_toeplitz(psf_kernel, cols, chunk))
        phi = correlate_rows(inverse, full_toeplitz(psf_kernel * psf_kernel, cols, chunk))
        both = jnp.stack([partial_sums(jnp.where(inside, x, 0.0), mine, rows) for x in (psi, phi)])
        both = lax.psum_scatter(both, "visit", scatter_dimension=2, tiled=True)
        return both[0] / jnp.sqrt(both[1])

    psi = correlate_rows(weighted, full_toeplitz(psf_kernel, cols, chunk))
    psi = partial_sums(jnp.where(inside, psi, 0.0), mine, rows)
    psi, inverse = lax.optimization_barrier((psi, inverse))
    blocks, from_left, from_right = ring_step_one(psi, "visit")

    phi = correlate_rows(inverse, full_toeplitz(psf_kernel * psf_kernel, cols, chunk))
    phi = jnp.where(inside, phi, 0.0)
    from_left, from_right, phi = lax.optimization_barrier((from_left, from_right, phi))
    psi = ring_step_two(blocks, from_left, from_right, "visit")

    phi = partial_sums(phi, mine, rows)
    phi = ring_step_two(*ring_step_one(phi, "visit"), "visit")
    return psi / jnp.sqrt(phi)


def solution(mesh):
    return jax.shard_map(
        shards,
        mesh=mesh,
        in_specs=(P("visit", "sky", None), P("visit", "sky", None), P(), P()),
        out_specs=P(None, ("sky", "visit"), None),
        check_vma=False,
    )
```

time: 64 us -> 78.2 us (1.22)
  the two profiles are of different devices: /device:TPU:97 before, /device:TPU:30 now
where the time goes in v4:
time: 78.2 us; the launch traced here: 77.9 us
  starting transfers between devices  29.5 us (38%)
  matrix products  19.6 us (25%)
  waiting for transfers between devices  11.5 us (15%)
  other arithmetic  9.8 us (13%)
  local copies, waits for them, and re-layouts  7.1 us (9%)
    ppermute x2, starting transfers between devices, bordered_rows(): lax.ppermute(lax.slice_in_dim(block, 0, width, axis=dim), axis, backward)  13.1 us
    conv_general_dilated x2, matrix products, correlate_rows(): lax.conv_general_dilated(bordered, kernel, window_strides=(1,), padding='...  12 us
    ppermute x2, waiting for transfers between devices, ring_step_two(): got_right = lax.ppermute(behind, axis, left)  7.33 us
    ppermute x2, starting transfers between devices, ring_step_two(): got_left = lax.ppermute(ahead, axis, right)  6.95 us
    dot_general x10, matrix products, partial_sums(): jnp.einsum('tk,trw->krw', onehot, shifted, precision=lax.Precision.HIGHEST)  6.32 us
    concatenate x2, other arithmetic, full_toeplitz(): return jnp.concatenate(parts, axis=2)  5.08 us
    ppermute x2, starting transfers between devices, bordered_rows(): lax.ppermute(lax.slice_in_dim(block, block.shape[dim] - width, None, axis...  3.82 us
    ppermute x2, starting transfers between devices, ring_step_one(): from_left = lax.ppermute(blocks[2][:half], axis, right)  2.98 us
  transfers between devices with their start and end apart: 12, of which 5 were waited for; matrix products, arithmetic and copies ran while one was open for 34% of the time, Pallas kernels for 0%

profile of v4, /device:TPU:30, one launch (start us, length us, event | category | flops | bytes accessed | tf_op | source)
XLA Modules:
  0.0 77.9 jit_solution(10736041683993592998)
XLA Ops:
  0.0 1.8 %copy_multiply_fusion = f32[8,64,256]{2,0,1:T(8,128)S(1)} fusion(f32[8,64,256]{2,1,0:T(8,128)} %param.5, f32[8,64,256]{2,1,0:T(8,128)} %param.4), kind=kLoop, calls=%fused_computation.34 | loop fusion | flops 131072 | bytes 1572864 | tf_op jit(solution)/shard_map/mul | solution.py:110
  1.8 0.8 %fusion.46 = (f32[8,21,256]{2,0,1:T(8,128)}, f32[8,21,256]{2,0,1:T(8,128)}) fusion(f32[8,64,256]{2,0,1:T(8,128)S(1)} %copy_multiply_fusion), kind=kLoop, calls=%fused_computation.82 | loop fusion | bytes 688128 | tf_op jit(solution)/shard_map/slice | solution.py:16
  2.6 1.9 %collective-permute-start = (f32[8,21,256]{2,0,1:T(8,128)}, f32[8,21,256]{2,0,1:T(8,128)}, u32[]{:S(2)}, u32[]{:S(2)}) collective-permute-start(f32[8,21,256]{2,0,1:T(8,128)} %get-tuple-element.33), channel_id=1, source_target_pairs={{0,4},{4,8},{8,12},{12,16},{16,20},{20,24},{24,28},{28,32},{32,36}... | collective-permute-start | bytes 516104 | tf_op jit(solution)/shard_map/ppermute | solution.py:15
  4.6 7.4 %collective-permute-start.1 = (f32[8,21,256]{2,0,1:T(8,128)}, f32[8,21,256]{2,0,1:T(8,128)}, u32[]{:S(2)}, u32[]{:S(2)}) collective-permute-start(f32[8,21,256]{2,0,1:T(8,128)} %get-tuple-element.34), channel_id=1, source_target_pairs={{4,0},{8,4},{12,8},{16,12},{20,16},{24,20},{28,24},{32,28},{36,32}... | collective-permute-start | bytes 516104 | tf_op jit(solution)/shard_map/ppermute | solution.py:18
  11.9 1.8 %fusion.45 = (f32[8,21,256]{2,1,0:T(8,128)}, f32[8,21,256]{2,1,0:T(8,128)}) fusion(f32[8,64,256]{2,1,0:T(8,128)} %param.5), kind=kLoop, calls=%fused_computation.81 | loop fusion | bytes 688128 | tf_op jit(solution)/shard_map/slice | solution.py:16
  13.8 1.9 %collective-permute-start.2 = (f32[8,21,256]{2,1,0:T(8,128)}, f32[8,21,256]{2,1,0:T(8,128)S(1)}, u32[]{:S(2)}, u32[]{:S(2)}) collective-permute-start(f32[8,21,256]{2,1,0:T(8,128)} %get-tuple-element.31), channel_id=1, source_target_pairs={{0,4},{4,8},{8,12},{12,16},{16,20},{20,24},{24,28},{28,32},{32,36}... | collective-permute-start | bytes 516104 | tf_op jit(solution)/shard_map/ppermute | solution.py:15
  15.7 5.8 %collective-permute-start.3 = (f32[8,21,256]{2,1,0:T(8,128)}, f32[8,21,256]{2,1,0:T(8,128)}, u32[]{:S(2)}, u32[]{:S(2)}) collective-permute-start(f32[8,21,256]{2,1,0:T(8,128)} %get-tuple-element.32), channel_id=1, source_target_pairs={{4,0},{8,4},{12,8},{16,12},{20,16},{24,20},{28,24},{32,28},{36,32}... | collective-permute-start | bytes 516104 | tf_op jit(solution)/shard_map/ppermute | solution.py:18
  21.5 0.7 convolution_bitcast_fusion
  22.1 0.6 fusion.10
  22.9 0.7 copy.12
  23.5 1.2 %fusion.44 = (f32[11,133,128]{2,0,1:T(8,128)S(1)}, f32[11,133,128]{2,0,1:T(8,128)}) fusion(f32[11,138,128]{2,0,1:T(8,128)S(1)} %convolution_bitcast_fusion), kind=kLoop, calls=%fused_computation.80 | loop fusion | bytes 2996224 | tf_op jit(solution)/shard_map/slice | solution.py:80
  24.7 1.5 %fusion.43 = (f32[11,133,128]{2,0,1:T(8,128)}, f32[11,133,128]{2,0,1:T(8,128)}) fusion(f32[11,138,128]{2,0,1:T(8,128)S(1)} %fusion.10), kind=kLoop, calls=%fused_computation.79 | loop fusion | bytes 2996224 | tf_op jit(solution)/shard_map/slice | solution.py:80
  26.3 2.6 %select_maximum_fusion.1 = f32[11,256,256]{2,0,1:T(8,128)} fusion(f32[11,133,128]{2,0,1:T(8,128)S(1)} %copy-done.1, f32[11,133,128]{2,0,1:T(8,128)S(1)} %get-tuple-element.17), kind=kLoop, calls=%fused_computation.1 | loop fusion | flops 3604480 | bytes 4381696 | tf_op jit(solution)/shard_map/concatenate | solution.py:82
  28.9 2.5 %select_maximum_fusion = f32[11,256,256]{2,0,1:T(8,128)} fusion(f32[11,133,128]{2,0,1:T(8,128)S(1)} %copy-done.3, f32[11,133,128]{2,0,1:T(8,128)S(1)} %copy-done.2), kind=kLoop, calls=%fused_computation | loop fusion | flops 3604480 | bytes 4381696 | tf_op jit(solution)/shard_map/concatenate | solution.py:82
  31.5 6.9 %fusion.4 = f32[8,96,256]{2,0,1:T(8,128)S(1)} fusion(f32[11,256,256]{2,0,1:T(8,128)} %select_maximum_fusion.1, f32[8,21,256]{2,0,1:T(8,128)} %collective-permute-done.1, f32[8,64,256]{2,0,1:T(8,128)S(1)} %copy-done.7, f32[8,21,256]{2,0,1:T(8,128)} %collective-permute-done, pred[96]{0:T(512)(128)(4,1)S(1)} %compare_and_fusion), kind=kOutput, calls=%fused_computation.17 | convolution fusion | flops 3322519552 | bytes 4538464 | tf_op jit(solution)/shard_map/conv_general_dilated | solution.py:33
  39.0 0.6 convolution_add_fusion.7
  41.0 0.7 convolution_add_fusion.4
  41.7 1.4 %pad_maximum_fusion = f32[8,106,256]{2,1,0:T(8,128)S(1)} fusion(f32[8,21,256]{2,1,0:T(8,128)} %collective-permute-done.3, f32[8,64,256]{2,1,0:T(8,128)S(1)} %copy-done.5, f32[8,21,256]{2,1,0:T(8,128)S(1)} %collective-permute-done.2), kind=kLoop, calls=%fused_computation.21 | loop fusion | flops 434176 | bytes 1736704 | tf_op jit(solution)/shard_map/concatenate | solution.py:19
  43.6 1.5 %collective-permute-start.5 = (f32[8,16,256]{2,0,1:T(8,128)S(1)}, f32[8,16,256]{2,0,1:T(8,128)S(1)}, u32[]{:S(2)}, u32[]{:S(2)}) collective-permute-start(f32[8,16,256]{2,0,1:T(8,128)S(1)} %get-tuple-element.29), channel_id=1, source_target_pairs={{0,3},{1,0},{2,1},{3,2},{4,7},{5,4},{6,5},{7,6},{8,11},{9,8},{10,9... | collective-permute-start | bytes 393224 | tf_op jit(solution)/shard_map/ppermute | solution.py:56
  45.2 5.0 %fusion.7 = f32[8,96,256]{2,0,1:T(8,128)S(1)} fusion(f32[11,256,256]{2,0,1:T(8,128)S(1)} %copy-done.4, f32[8,106,256]{2,1,0:T(8,128)S(1)} %pad_maximum_fusion, pred[96]{0:T(512)(128)(4,1)S(1)} %compare_and_fusion), kind=kOutput, calls=%fused_computation.18 | convolution fusion | flops 3322085376 | bytes 4538464 | tf_op jit(solution)/shard_map/conv_general_dilated | solution.py:33
  52.2 0.6 convolution_add_fusion.1
  52.8 0.7 convolution_add_fusion
  53.5 0.9 %collective-permute-start.10 = (f32[8,16,256]{2,0,1:T(8,128)S(1)}, f32[8,16,256]{2,0,1:T(8,128)S(1)}, u32[]{:S(2)}, u32[]{:S(2)}) collective-permute-start(f32[8,16,256]{2,0,1:T(8,128)S(1)} %get-tuple-element.28), channel_id=1, source_target_pairs={{0,3},{1,0},{2,1},{3,2},{4,7},{5,4},{6,5},{7,6},{8,11},{9,8},{10,9... | collective-permute-start | bytes 393224 | tf_op jit(solution)/shard_map/ppermute | solution.py:56
  54.4 2.4 %collective-permute-start.8 = (f32[8,16,256]{2,0,1:T(8,128)S(1)}, f32[8,16,256]{2,0,1:T(8,128)S(1)}, u32[]{:S(2)}, u32[]{:S(2)}) collective-permute-start(f32[8,16,256]{2,0,1:T(8,128)S(1)} %get-tuple-element.27), channel_id=1, source_target_pairs={{0,1},{1,2},{2,3},{3,0},{4,5},{5,6},{6,7},{7,4},{8,9},{9,10},{10,1... | collective-permute-start | bytes 393224 | tf_op jit(solution)/shard_map/ppermute | solution.py:55
  56.8 2.9 %collective-permute-done.10 = f32[8,16,256]{2,0,1:T(8,128)S(1)} collective-permute-done((f32[8,16,256]{2,0,1:T(8,128)S(1)}, f32[8,16,256]{2,0,1:T(8,128)S(1)}, u32[]{:S(2)}, u32[]{:S(2)}) %collective-permute-start.10) | collective-permute-done | bytes 131104 | tf_op jit(solution)/shard_map/ppermute | solution.py:56
  59.8 0.9 %collective-permute-done.8 = f32[8,16,256]{2,0,1:T(8,128)S(1)} collective-permute-done((f32[8,16,256]{2,0,1:T(8,128)S(1)}, f32[8,16,256]{2,0,1:T(8,128)S(1)}, u32[]{:S(2)}, u32[]{:S(2)}) %collective-permute-start.8) | collective-permute-done | bytes 131104 | tf_op jit(solution)/shard_map/ppermute | solution.py:55
  60.9 3.7 %collective-permute-start.6 = (f32[16,16,256]{2,0,1:T(8,128)S(1)}, f32[16,16,256]{2,0,1:T(8,128)S(1)}, u32[]{:S(2)}, u32[]{:S(2)}) collective-permute-start(f32[16,16,256]{2,0,1:T(8,128)S(1)} %pad_maximum_fusion.1), channel_id=1, source_target_pairs={{0,1},{1,2},{2,3},{3,0},{4,5},{5,6},{6,7},{7,4},{8,9},{9,10},{10,1... | collective-permute-start | bytes 786440 | tf_op jit(solution)/shard_map/ppermute | solution.py:67
  64.7 3.3 %collective-permute-start.9 = (f32[16,16,256]{2,0,1:T(8,128)S(1)}, f32[16,16,256]{2,0,1:T(8,128)}, u32[]{:S(2)}, u32[]{:S(2)}) collective-permute-start(f32[16,16,256]{2,0,1:T(8,128)S(1)} %pad_maximum_fusion.3), channel_id=1, source_target_pairs={{0,1},{1,2},{2,3},{3,0},{4,5},{5,6},{6,7},{7,4},{8,9},{9,10},{10,1... | collective-permute-start | bytes 786440 | tf_op jit(solution)/shard_map/ppermute | solution.py:67
  68.4 3.9 %collective-permute-done.7 = f32[16,16,256]{2,0,1:T(8,128)} collective-permute-done((f32[16,16,256]{2,0,1:T(8,128)S(1)}, f32[16,16,256]{2,0,1:T(8,128)}, u32[]{:S(2)}, u32[]{:S(2)}) %collective-permute-start.7) | collective-permute-done | bytes 262176 | tf_op jit(solution)/shard_map/ppermute | solution.py:68
  72.3 3.4 %collective-permute-done.11 = f32[16,16,256]{2,0,1:T(8,128)} collective-permute-done((f32[16,16,256]{2,0,1:T(8,128)S(1)}, f32[16,16,256]{2,0,1:T(8,128)}, u32[]{:S(2)}, u32[]{:S(2)}) %collective-permute-start.11) | collective-permute-done | bytes 262176 | tf_op jit(solution)/shard_map/ppermute | solution.py:68
  75.7 1.3 %rsqrt_multiply_fusion = f32[16,16,256]{2,0,1:T(8,128)S(1)} fusion(f32[16,16,256]{2,0,1:T(8,128)} %collective-permute-done.11, f32[16,16,256]{2,0,1:T(8,128)} %collective-permute-done.9, f32[16,64,256]{2,0,1:T(8,128)S(1)} %convolution_add_fusion, s32[]{:T(128)S(6)} %select_n.56, f32[16,16,256]{2,0,1:T(8,128)} %collective-permute-done.7, ...), kind=kLoop, calls=%fused_computation.45 | loop fusion | flops 327680 | bytes 1835012 | tf_op jit(solution)/shard_map/div | solution.py:132
  77.0 0.9 %copy.11 = f32[16,16,256]{2,1,0:T(8,128)} copy(f32[16,16,256]{2,0,1:T(8,128)S(1)} %rsqrt_multiply_fusion) | data formatting | bytes 524288 | tf_op jit(solution)/shard_map/div | solution.py:132
  (47 shorter events, 5.3 us)
Async XLA Ops:
  0.0 22.8 %copy-start = (s32[32,16]{0,1:T(8,128)S(1)}, s32[32,16]{0,1:T(8,128)}, u32[]{:S(2)}) copy-start(s32[32,16]{0,1:T(8,128)} %param.7) | copy-start | bytes 6148
  0.0 21.4 %copy-start.8 = (f32[11,11]{1,0:T(8,128)S(1)}, f32[11,11]{1,0:T(8,128)}, u32[]{:S(2)}) copy-start(f32[11,11]{1,0:T(8,128)} %param.6) | copy-start | bytes 1456
  1.8 19.6 %copy-start.6 = (f32[8,64,256]{2,0,1:T(8,128)}, f32[8,64,256]{2,0,1:T(8,128)S(1)}, u32[]{:S(2)}) copy-start(f32[8,64,256]{2,0,1:T(8,128)S(1)} %copy_multiply_fusion) | copy-start | bytes 1572868
  2.6 28.8 %collective-permute-start = (f32[8,21,256]{2,0,1:T(8,128)}, f32[8,21,256]{2,0,1:T(8,128)}, u32[]{:S(2)}, u32[]{:S(2)}) collective-permute-start(f32[8,21,256]{2,0,1:T(8,128)} %get-tuple-element.33), channel_id=1, source_target_pairs={{0,4},{4,8},{8,12},{12,16},{16,20},{20,24},{24,28},{28,32},{32,36}... | collective-permute-start | bytes 516104 | tf_op jit(solution)/shard_map/ppermute | solution.py:15
  4.6 26.9 %collective-permute-start.1 = (f32[8,21,256]{2,0,1:T(8,128)}, f32[8,21,256]{2,0,1:T(8,128)}, u32[]{:S(2)}, u32[]{:S(2)}) collective-permute-start(f32[8,21,256]{2,0,1:T(8,128)} %get-tuple-element.34), channel_id=1, source_target_pairs={{4,0},{8,4},{12,8},{16,12},{20,16},{24,20},{28,24},{32,28},{36,32}... | collective-permute-start | bytes 516104 | tf_op jit(solution)/shard_map/ppermute | solution.py:18
  13.8 27.9 %collective-permute-start.2 = (f32[8,21,256]{2,1,0:T(8,128)}, f32[8,21,256]{2,1,0:T(8,128)S(1)}, u32[]{:S(2)}, u32[]{:S(2)}) collective-permute-start(f32[8,21,256]{2,1,0:T(8,128)} %get-tuple-element.31), channel_id=1, source_target_pairs={{0,4},{4,8},{8,12},{12,16},{16,20},{20,24},{24,28},{28,32},{32,36}... | collective-permute-start | bytes 516104 | tf_op jit(solution)/shard_map/ppermute | solution.py:15
  15.7 26.0 %collective-permute-start.3 = (f32[8,21,256]{2,1,0:T(8,128)}, f32[8,21,256]{2,1,0:T(8,128)}, u32[]{:S(2)}, u32[]{:S(2)}) collective-permute-start(f32[8,21,256]{2,1,0:T(8,128)} %get-tuple-element.32), channel_id=1, source_target_pairs={{4,0},{8,4},{12,8},{16,12},{20,16},{24,20},{28,24},{32,28},{36,32}... | collective-permute-start | bytes 516104 | tf_op jit(solution)/shard_map/ppermute | solution.py:18
  24.7 1.6 %copy-start.1 = (f32[11,133,128]{2,0,1:T(8,128)S(1)}, f32[11,133,128]{2,0,1:T(8,128)}, u32[]{:S(2)}) copy-start(f32[11,133,128]{2,0,1:T(8,128)} %get-tuple-element.18) | copy-start | bytes 2247172
  26.3 2.6 %copy-start.2 = (f32[11,133,128]{2,0,1:T(8,128)S(1)}, f32[11,133,128]{2,0,1:T(8,128)}, u32[]{:S(2)}) copy-start(f32[11,133,128]{2,0,1:T(8,128)} %get-tuple-element.15) | copy-start | bytes 2247172
  26.3 2.6 %copy-start.3 = (f32[11,133,128]{2,0,1:T(8,128)S(1)}, f32[11,133,128]{2,0,1:T(8,128)}, u32[]{:S(2)}) copy-start(f32[11,133,128]{2,0,1:T(8,128)} %get-tuple-element.16) | copy-start | bytes 2247172
  28.9 2.5 %copy-start.9 = (s32[8,16]{1,0:T(8,128)S(1)}, s32[8,16]{1,0:T(8,128)}, u32[]{:S(2)}) copy-start(s32[8,16]{1,0:T(8,128)} %copy.12) | copy-start | bytes 1540
  28.9 2.5 %copy-start.7 = (f32[8,64,256]{2,0,1:T(8,128)S(1)}, f32[8,64,256]{2,0,1:T(8,128)}, u32[]{:S(2)}) copy-start(f32[8,64,256]{2,0,1:T(8,128)} %copy-done.6) | copy-start | bytes 1572868
  40.3 1.3 %copy-start.5 = (f32[8,64,256]{2,1,0:T(8,128)S(1)}, f32[8,64,256]{2,1,0:T(8,128)}, u32[]{:S(2)}) copy-start(f32[8,64,256]{2,1,0:T(8,128)} %param.5) | copy-start | bytes 1572868
  41.0 4.2 %copy-start.4 = (f32[11,256,256]{2,0,1:T(8,128)S(1)}, f32[11,256,256]{2,0,1:T(8,128)}, u32[]{:S(2)}) copy-start(f32[11,256,256]{2,0,1:T(8,128)} %select_maximum_fusion) | copy-start | bytes 8650756
  43.1 7.2 %collective-permute-start.4 = (f32[8,16,256]{2,0,1:T(8,128)S(1)}, f32[8,16,256]{2,0,1:T(8,128)S(1)}, u32[]{:S(2)}, u32[]{:S(2)}) collective-permute-start(f32[8,16,256]{2,0,1:T(8,128)S(1)} %get-tuple-element.30), channel_id=1, source_target_pairs={{0,1},{1,2},{2,3},{3,0},{4,5},{5,6},{6,7},{7,4},{8,9},{9,10},{10,1... | collective-permute-start | bytes 393224 | tf_op jit(solution)/shard_map/ppermute | solution.py:55
  43.6 6.6 %collective-permute-start.5 = (f32[8,16,256]{2,0,1:T(8,128)S(1)}, f32[8,16,256]{2,0,1:T(8,128)S(1)}, u32[]{:S(2)}, u32[]{:S(2)}) collective-permute-start(f32[8,16,256]{2,0,1:T(8,128)S(1)} %get-tuple-element.29), channel_id=1, source_target_pairs={{0,3},{1,0},{2,1},{3,2},{4,7},{5,4},{6,5},{7,6},{8,11},{9,8},{10,9... | collective-permute-start | bytes 393224 | tf_op jit(solution)/shard_map/ppermute | solution.py:56
  53.5 6.3 %collective-permute-start.10 = (f32[8,16,256]{2,0,1:T(8,128)S(1)}, f32[8,16,256]{2,0,1:T(8,128)S(1)}, u32[]{:S(2)}, u32[]{:S(2)}) collective-permute-start(f32[8,16,256]{2,0,1:T(8,128)S(1)} %get-tuple-element.28), channel_id=1, source_target_pairs={{0,3},{1,0},{2,1},{3,2},{4,7},{5,4},{6,5},{7,6},{8,11},{9,8},{10,9... | collective-permute-start | bytes 393224 | tf_op jit(solution)/shard_map/ppermute | solution.py:56
  54.4 6.3 %collective-permute-start.8 = (f32[8,16,256]{2,0,1:T(8,128)S(1)}, f32[8,16,256]{2,0,1:T(8,128)S(1)}, u32[]{:S(2)}, u32[]{:S(2)}) collective-permute-start(f32[8,16,256]{2,0,1:T(8,128)S(1)} %get-tuple-element.27), channel_id=1, source_target_pairs={{0,1},{1,2},{2,3},{3,0},{4,5},{5,6},{6,7},{7,4},{8,9},{9,10},{10,1... | collective-permute-start | bytes 393224 | tf_op jit(solution)/shard_map/ppermute | solution.py:55
  60.9 7.5 %collective-permute-start.6 = (f32[16,16,256]{2,0,1:T(8,128)S(1)}, f32[16,16,256]{2,0,1:T(8,128)S(1)}, u32[]{:S(2)}, u32[]{:S(2)}) collective-permute-start(f32[16,16,256]{2,0,1:T(8,128)S(1)} %pad_maximum_fusion.1), channel_id=1, source_target_pairs={{0,1},{1,2},{2,3},{3,0},{4,5},{5,6},{6,7},{7,4},{8,9},{9,10},{10,1... | collective-permute-start | bytes 786440 | tf_op jit(solution)/shard_map/ppermute | solution.py:67
  64.5 7.8 %collective-permute-start.7 = (f32[16,16,256]{2,0,1:T(8,128)S(1)}, f32[16,16,256]{2,0,1:T(8,128)}, u32[]{:S(2)}, u32[]{:S(2)}) collective-permute-start(f32[16,16,256]{2,0,1:T(8,128)S(1)} %pad_maximum_fusion.2), channel_id=1, source_target_pairs={{0,3},{1,0},{2,1},{3,2},{4,7},{5,4},{6,5},{7,6},{8,11},{9,8},{10,9... | collective-permute-start | bytes 786440 | tf_op jit(solution)/shard_map/ppermute | solution.py:68
  64.7 7.6 %collective-permute-start.9 = (f32[16,16,256]{2,0,1:T(8,128)S(1)}, f32[16,16,256]{2,0,1:T(8,128)}, u32[]{:S(2)}, u32[]{:S(2)}) collective-permute-start(f32[16,16,256]{2,0,1:T(8,128)S(1)} %pad_maximum_fusion.3), channel_id=1, source_target_pairs={{0,1},{1,2},{2,3},{3,0},{4,5},{5,6},{6,7},{7,4},{8,9},{9,10},{10,1... | collective-permute-start | bytes 786440 | tf_op jit(solution)/shard_map/ppermute | solution.py:67
  68.0 7.8 %collective-permute-start.11 = (f32[16,16,256]{2,0,1:T(8,128)S(1)}, f32[16,16,256]{2,0,1:T(8,128)}, u32[]{:S(2)}, u32[]{:S(2)}) collective-permute-start(f32[16,16,256]{2,0,1:T(8,128)S(1)} %pad_maximum_fusion.4), channel_id=1, source_target_pairs={{0,3},{1,0},{2,1},{3,2},{4,7},{5,4},{6,5},{7,6},{8,11},{9,8},{10,9... | collective-permute-start | bytes 786440 | tf_op jit(solution)/shard_map/ppermute | solution.py:68

commit v5 on v2

--- a/solution.py
+++ b/solution.py
@@ -2,6 +2,8 @@
 import jax.numpy as jnp
 from jax import lax
 from jax.sharding import PartitionSpec as P
+from jax.experimental import pallas as pl
+from jax.experimental.pallas import tpu as pltpu
 
 BR = 8
 MAXOFF = 2
@@ -66,6 +68,40 @@
     return block(0) + got_left + got_right
 
 
+def stack_kernel(offsets_ref, images_ref, out_ref):
+    visits = images_ref.shape[1]
+    rows = out_ref.shape[2]
+    reach = MAXOFF * BR
+    for k in range(out_ref.shape[1]):
+        total = None
+        for t in range(visits):
+            start = pl.multiple_of(reach + BR * offsets_ref[t, k], BR)
+            term = images_ref[0, t, pl.ds(start, rows), :]
+            total = term if total is None else total + term
+        out_ref[0, k] = total
+
+
+def partial_sums(images, mine):
+    channels, visits, extended, cols = images.shape
+    rows = extended - 2 * MAXOFF * BR
+    velocities = mine.shape[1]
+    return pl.pallas_call(
+        stack_kernel,
+        out_shape=jax.ShapeDtypeStruct((channels, velocities, rows, cols), jnp.float32),
+        grid_spec=pltpu.PrefetchScalarGridSpec(
+            num_scalar_prefetch=1,
+            grid=(channels,),
+            in_specs=[pl.BlockSpec((1, visits, extended, cols), lambda c, off: (c, 0, 0, 0))],
+            out_specs=pl.BlockSpec((1, velocities, rows, cols), lambda c, off: (c, 0, 0, 0)),
+        ),
+        cost_estimate=pl.CostEstimate(
+            flops=channels * velocities * visits * rows * cols,
+            transcendentals=0,
+            bytes_accessed=4 * channels * (visits * extended + velocities * rows) * cols,
+        ),
+    )(mine, images)
+
+
 def shards(science, inv_variance, psf_kernel, offsets):
     radius = (psf_kernel.shape[0] - 1) // 2
     reach = MAXOFF * BR
@@ -86,14 +122,7 @@
     images = jnp.where(inside, images, 0.0)
 
     mine = lax.dynamic_slice_in_dim(offsets, lax.axis_index("visit") * visits, visits, 0)
-    partial = jnp.zeros((2, offsets.shape[1], rows, cols), jnp.float32)
-    for offset_value in range(-MAXOFF, MAXOFF + 1):
-        onehot = (mine == offset_value).astype(jnp.float32)
-        start = reach + offset_value * BR
-        window = images[:, :, start : start + rows, :]
-        partial = partial + jnp.einsum(
-            "tk,ctrw->ckrw", onehot, window, precision=lax.Precision.HIGHEST
-        )
+    partial = partial_sums(images, mine)
 
     stacked = ring_reduce_scatter(partial, "visit")
     return stacked[0] / jnp.sqrt(stacked[1])

time: 58.4 us -> 60.7 us (1.039)
  the two profiles are of different devices: /device:TPU:54 before, /device:TPU:119 now
where the time goes in v5:
time: 60.7 us; the launch traced here: 60.3 us
  waiting for transfers between devices  21.8 us (36%)
  matrix products  14.8 us (24%)
  starting transfers between devices  10.4 us (17%)
  other arithmetic  6.91 us (11%)
  Pallas kernels  3.96 us (7%)
  local copies, waits for them, and re-layouts  2.29 us (4%)
    ppermute x1, waiting for transfers between devices, ring_reduce_scatter(): got_left = lax.ppermute(ahead, axis, right)  12.2 us
    conv_general_dilated x2, matrix products, correlate_rows(): lax.conv_general_dilated(bordered, kernel, window_strides=(1,), padding='...  9.32 us
    dot_general x2, matrix products, toeplitz(): jnp.einsum('ab,bwv->awv', taps, onehot, precision=lax.Precision.HIGHEST)  5.51 us
    ppermute x1, starting transfers between devices, bordered_rows(): lax.ppermute(lax.slice_in_dim(block, block.shape[dim] - width, None, axis...  5.32 us
    ppermute x1, waiting for transfers between devices, ring_reduce_scatter(): from_left = lax.ppermute(far[..., :half], axis, right)  5.32 us
    pallas_call x1, Pallas kernels, partial_sums(): pl.pallas_call(stack_kernel, out_shape=jax.ShapeDtypeStruct((channels, ve...  3.96 us
    ppermute x1, starting transfers between devices, bordered_rows(): lax.ppermute(lax.slice_in_dim(block, 0, width, axis=dim), axis, backward)  1.92 us
    another operation x1, other arithmetic, shards(): both = jnp.stack([weighted, inv_variance])  1.84 us
  transfers between devices with their start and end apart: 6, of which 5 were waited for; matrix products, arithmetic and copies ran while one was open for 10% of the time, Pallas kernels for 0%

profile of v5, /device:TPU:119, one launch (start us, length us, event | category | flops | bytes accessed | tf_op | source)
XLA Modules:
  0.0 60.3 jit_solution(770762447766042131)
XLA Ops:
  0.0 0.0 copy-start
  0.0 1.8 %fusion.8 = (f32[1,8,64,256]{3,1,2,0:T(8,128)S(1)}, f32[1,8,64,256]{3,1,2,0:T(8,128)S(1)}) fusion(f32[8,64,256]{2,1,0:T(8,128)} %param.4, f32[8,64,256]{2,1,0:T(8,128)} %param.5), kind=kLoop, calls=%fused_computation.18 | loop fusion | flops 131072 | bytes 2097152 | tf_op jit(solution)/shard_map/stack | solution.py:112
  1.8 0.1 pad_maximum_fusion.4
  1.9 5.3 %collective-permute-start = (f32[2,8,21,256]{3,1,2,0:T(8,128)S(1)}, f32[2,8,21,256]{3,1,2,0:T(8,128)S(1)}, u32[]{:S(2)}, u32[]{:S(2)}) collective-permute-start(f32[2,8,21,256]{3,1,2,0:T(8,128)S(1)} %get-tuple-element.11), channel_id=1, source_target_pairs={{0,4},{4,8},{8,12},{12,16},{16,20},{20,24},{24,28},{28,32},{32,36}... | collective-permute-start | bytes 1032200 | tf_op jit(solution)/shard_map/ppermute | solution.py:17
  7.2 1.9 %collective-permute-start.1 = (f32[2,8,21,256]{3,1,2,0:T(8,128)S(1)}, f32[2,8,21,256]{3,1,2,0:T(8,128)S(1)}, u32[]{:S(2)}, u32[]{:S(2)}) collective-permute-start(f32[2,8,21,256]{3,1,2,0:T(8,128)S(1)} %get-tuple-element.12), channel_id=1, source_target_pairs={{4,0},{8,4},{12,8},{16,12},{20,16},{24,20},{28,24},{32,28},{36,32}... | collective-permute-start | bytes 1032200 | tf_op jit(solution)/shard_map/ppermute | solution.py:20
  9.2 0.0 copy-done.2
  9.2 4.1 %fusion.1 = f32[256,256,11]{1,2,0:T(8,128)} fusion(f32[11,11]{1,0:T(8,128)S(1)} %copy-done.2), kind=kOutput, calls=%fused_computation.2 | convolution fusion | flops 97320960 | bytes 2884068 | tf_op jit(solution)/shard_map/ab,bwv->awv/dot_general | solution.py:31
  13.2 0.0 copy-done
  13.2 0.1 constant_dynamic-slice_fusion.4
  13.3 0.7 %copy.13.offsets_ref = s32[8,16]{1,0:T(8,128)} copy(s32[8,16]{0,1:T(8,128)S(1)} %constant_dynamic-slice_fusion.4) | data formatting | bytes 1024
  14.0 1.4 %fusion = f32[11,256,256]{2,0,1:T(8,128)S(1)} fusion(f32[11,11]{1,0:T(8,128)S(1)} %copy-done.2), kind=kOutput, calls=%fused_computation.1 | convolution fusion | flops 97321080 | bytes 2884068 | tf_op jit(solution)/shard_map/ab,bwv->awv/dot_general | solution.py:31
  15.4 0.0 collective-permute-done
  15.4 1.6 %collective-permute-done.1 = f32[2,8,21,256]{3,1,2,0:T(8,128)S(1)} collective-permute-done((f32[2,8,21,256]{3,1,2,0:T(8,128)S(1)}, f32[2,8,21,256]{3,1,2,0:T(8,128)S(1)}, u32[]{:S(2)}, u32[]{:S(2)}) %collective-permute-start.1) | collective-permute-done | bytes 344096 | tf_op jit(solution)/shard_map/ppermute | solution.py:20
  17.0 0.1 pad_maximum_fusion
  17.2 0.0 copy-done.1
  17.2 4.6 %fusion.4 = f32[8,96,256]{2,0,1:T(8,128)S(1)} fusion(f32[256,256,11]{1,2,0:T(8,128)S(1)} %copy-done.1, f32[2,8,106,256]{3,1,2,0:T(8,128)S(1)} %pad_maximum_fusion), kind=kOutput, calls=%fused_computation.5 | convolution fusion | flops 3321888768 | bytes 5849088 | tf_op jit(solution)/shard_map/conv_general_dilated | solution.py:35
  21.7 4.8 %fusion.2 = f32[8,96,256]{2,0,1:T(8,128)S(1)} fusion(f32[11,256,256]{2,0,1:T(8,128)S(1)} %fusion, f32[2,8,106,256]{3,1,2,0:T(8,128)S(1)} %pad_maximum_fusion), kind=kOutput, calls=%fused_computation.3 | convolution fusion | flops 3321888768 | bytes 5849088 | tf_op jit(solution)/shard_map/conv_general_dilated | solution.py:35
  26.5 0.5 copy_bitcast_fusion
  27.0 1.5 %maximum_select_fusion.images_ref = f32[2,8,96,256]{3,2,1,0:T(8,128)} fusion(f32[1,8,96,256]{3,2,1,0:T(8,128)S(1)} %get-tuple-element.15, f32[1,8,96,256]{3,2,1,0:T(8,128)S(1)} %get-tuple-element.16, pred[96]{0:T(512)(128)(4,1)S(1)} %compare_and_fusion), kind=kLoop, calls=%fused_computation.10 | loop fusion | flops 786432 | bytes 3145824 | tf_op jit(solution)/shard_map/jit(_where)/select_n | solution.py:122
  28.4 4.0 %shard_map.46 = f32[2,16,64,256]{3,2,1,0:T(8,128)} custom-call(s32[8,16]{1,0:T(8,128)} %copy.13.offsets_ref, f32[2,8,96,256]{3,2,1,0:T(8,128)} %maximum_select_fusion.images_ref), custom_call_target="tpu_custom_call" | custom-call | flops 4194304 | bytes 3670016 | tf_op jit(solution)/shard_map/pallas_call | solution.py:88
  32.4 1.1 %constant_dynamic-slice_fusion.1 = (f32[2,16,16,128]{3,2,1,0:T(8,128)S(1)}, f32[2,16,16,128]{3,2,1,0:T(8,128)S(1)}) fusion(f32[2,16,64,256]{3,2,1,0:T(8,128)} %shard_map.46, s32[]{:T(128)S(6)} %select_n.45, s32[]{:T(128)S(6)} %add.86), kind=kLoop, calls=%fused_computation.32 | loop fusion | bytes 1048584 | tf_op jit(solution)/shard_map/slice | solution.py:60
  33.5 0.2 collective-permute-start.2
  33.7 1.3 %collective-permute-start.4 = (f32[2,16,16,128]{3,2,1,0:T(8,128)S(1)}, f32[2,16,16,128]{3,2,1,0:T(8,128)S(1)}, u32[]{:S(2)}, u32[]{:S(2)}) collective-permute-start(f32[2,16,16,128]{3,2,1,0:T(8,128)S(1)} %get-tuple-element.10), channel_id=1, source_target_pairs={{0,3},{1,0},{2,1},{3,2},{4,7},{5,4},{6,5},{7,6},{8,11},{9,8},{10,9... | collective-permute-start | bytes 786440 | tf_op jit(solution)/shard_map/ppermute | solution.py:61
  35.0 5.3 %collective-permute-done.2 = f32[2,16,16,128]{3,2,1,0:T(8,128)S(1)} collective-permute-done((f32[2,16,16,128]{3,2,1,0:T(8,128)S(1)}, f32[2,16,16,128]{3,2,1,0:T(8,128)S(1)}, u32[]{:S(2)}, u32[]{:S(2)}) %collective-permute-start.2) | collective-permute-done | bytes 262176 | tf_op jit(solution)/shard_map/ppermute | solution.py:60
  40.3 1.4 %collective-permute-done.4 = f32[2,16,16,128]{3,2,1,0:T(8,128)S(1)} collective-permute-done((f32[2,16,16,128]{3,2,1,0:T(8,128)S(1)}, f32[2,16,16,128]{3,2,1,0:T(8,128)S(1)}, u32[]{:S(2)}, u32[]{:S(2)}) %collective-permute-start.4) | collective-permute-done | bytes 262176 | tf_op jit(solution)/shard_map/ppermute | solution.py:61
  41.7 1.4 %dynamic-slice_add_fusion.1 = (f32[2,16,16,128]{3,2,1,0:T(8,128)S(1)}, f32[2,16,16,128]{3,2,1,0:T(8,128)S(1)}, f32[2,16,16,128]{3,2,1,0:T(8,128)S(1)}, f32[2,16,16,128]{3,2,1,0:T(8,128)S(1)}) fusion(f32[2,16,16,128]{3,2,1,0:T(8,128)S(1)} %collective-permute-done.2, f32[2,16,64,256]{3,2,1,0:T(8,128)} %shard_map.46, s32[]{:T(128)S(6)} %select_n.43, ...), kind=kLoop, calls=%fused_computation.27 | loop fusion | flops 131072 | bytes 2621452 | tf_op jit(solution)/shard_map/add | solution.py:63
  43.1 0.1 collective-permute-start.3
  43.3 1.5 %collective-permute-start.5 = (f32[2,16,16,256]{3,2,1,0:T(8,128)S(1)}, f32[2,16,16,256]{3,2,1,0:T(8,128)S(1)}, u32[]{:S(2)}, u32[]{:S(2)}) collective-permute-start(f32[2,16,16,256]{3,2,1,0:T(8,128)S(1)} %pad_maximum_fusion.2), channel_id=1, source_target_pairs={{0,3},{1,0},{2,1},{3,2},{4,7},{5,4},{6,5},{7,6},{8,11},{9,8},{10,9... | collective-permute-start | bytes 1572872 | tf_op jit(solution)/shard_map/ppermute | solution.py:67
  44.8 12.2 %collective-permute-done.3 = f32[2,16,16,256]{3,2,1,0:T(8,128)S(1)} collective-permute-done((f32[2,16,16,256]{3,2,1,0:T(8,128)S(1)}, f32[2,16,16,256]{3,2,1,0:T(8,128)S(1)}, u32[]{:S(2)}, u32[]{:S(2)}) %collective-permute-start.3) | collective-permute-done | bytes 524320 | tf_op jit(solution)/shard_map/ppermute | solution.py:66
  57.0 1.4 %collective-permute-done.5 = f32[2,16,16,256]{3,2,1,0:T(8,128)S(1)} collective-permute-done((f32[2,16,16,256]{3,2,1,0:T(8,128)S(1)}, f32[2,16,16,256]{3,2,1,0:T(8,128)S(1)}, u32[]{:S(2)}, u32[]{:S(2)}) %collective-permute-start.5) | collective-permute-done | bytes 524320 | tf_op jit(solution)/shard_map/ppermute | solution.py:67
  58.4 1.2 %add_add_fusion = f32[2,16,16,256]{3,2,1,0:T(8,128)S(1)} fusion(f32[2,16,16,256]{3,2,1,0:T(8,128)S(1)} %collective-permute-done.5, f32[2,16,16,256]{3,2,1,0:T(8,128)S(1)} %collective-permute-done.3, f32[2,16,64,256]{3,2,1,0:T(8,128)} %shard_map.46, s32[]{:T(128)S(6)} %select_n.41), kind=kLoop, calls=%fused_computation.19 | loop fusion | flops 262144 | bytes 2097156 | tf_op jit(solution)/shard_map/add | solution.py:68
  59.6 0.7 %fusion.10 = f32[16,16,256]{2,1,0:T(8,128)} fusion(f32[2,16,16,256]{3,2,1,0:T(8,128)S(1)} %add_add_fusion), kind=kLoop, calls=%fused_computation.25 | loop fusion | flops 65536 | bytes 786432 | tf_op jit(solution)/shard_map/div | solution.py:128
  (5 shorter events, 0.1 us)
Async XLA Ops:
  0.0 13.2 %copy-start = (s32[32,16]{0,1:T(8,128)S(1)}, s32[32,16]{0,1:T(8,128)}, u32[]{:S(2)}) copy-start(s32[32,16]{0,1:T(8,128)} %param.7) | copy-start | bytes 6148
  0.0 9.2 %copy-start.2 = (f32[11,11]{1,0:T(8,128)S(1)}, f32[11,11]{1,0:T(8,128)}, u32[]{:S(2)}) copy-start(f32[11,11]{1,0:T(8,128)} %param.6) | copy-start | bytes 1456
  1.9 13.5 %collective-permute-start = (f32[2,8,21,256]{3,1,2,0:T(8,128)S(1)}, f32[2,8,21,256]{3,1,2,0:T(8,128)S(1)}, u32[]{:S(2)}, u32[]{:S(2)}) collective-permute-start(f32[2,8,21,256]{3,1,2,0:T(8,128)S(1)} %get-tuple-element.11), channel_id=1, source_target_pairs={{0,4},{4,8},{8,12},{12,16},{16,20},{20,24},{24,28},{28,32},{32,36}... | collective-permute-start | bytes 1032200 | tf_op jit(solution)/shard_map/ppermute | solution.py:17
  7.2 9.8 %collective-permute-start.1 = (f32[2,8,21,256]{3,1,2,0:T(8,128)S(1)}, f32[2,8,21,256]{3,1,2,0:T(8,128)S(1)}, u32[]{:S(2)}, u32[]{:S(2)}) collective-permute-start(f32[2,8,21,256]{3,1,2,0:T(8,128)S(1)} %get-tuple-element.12), channel_id=1, source_target_pairs={{4,0},{8,4},{12,8},{16,12},{20,16},{24,20},{28,24},{32,28},{36,32}... | collective-permute-start | bytes 1032200 | tf_op jit(solution)/shard_map/ppermute | solution.py:20
  14.0 3.2 %copy-start.1 = (f32[256,256,11]{1,2,0:T(8,128)S(1)}, f32[256,256,11]{1,2,0:T(8,128)}, u32[]{:S(2)}) copy-start(f32[256,256,11]{1,2,0:T(8,128)} %fusion.1) | copy-start | bytes 8650756
  33.5 6.9 %collective-permute-start.2 = (f32[2,16,16,128]{3,2,1,0:T(8,128)S(1)}, f32[2,16,16,128]{3,2,1,0:T(8,128)S(1)}, u32[]{:S(2)}, u32[]{:S(2)}) collective-permute-start(f32[2,16,16,128]{3,2,1,0:T(8,128)S(1)} %get-tuple-element.9), channel_id=1, source_target_pairs={{0,1},{1,2},{2,3},{3,0},{4,5},{5,6},{6,7},{7,4},{8,9},{9,10},{10,1... | collective-permute-start | bytes 786440 | tf_op jit(solution)/shard_map/ppermute | solution.py:60
  33.7 8.0 %collective-permute-start.4 = (f32[2,16,16,128]{3,2,1,0:T(8,128)S(1)}, f32[2,16,16,128]{3,2,1,0:T(8,128)S(1)}, u32[]{:S(2)}, u32[]{:S(2)}) collective-permute-start(f32[2,16,16,128]{3,2,1,0:T(8,128)S(1)} %get-tuple-element.10), channel_id=1, source_target_pairs={{0,3},{1,0},{2,1},{3,2},{4,7},{5,4},{6,5},{7,6},{8,11},{9,8},{10,9... | collective-permute-start | bytes 786440 | tf_op jit(solution)/shard_map/ppermute | solution.py:61
  43.1 13.9 %collective-permute-start.3 = (f32[2,16,16,256]{3,2,1,0:T(8,128)S(1)}, f32[2,16,16,256]{3,2,1,0:T(8,128)S(1)}, u32[]{:S(2)}, u32[]{:S(2)}) collective-permute-start(f32[2,16,16,256]{3,2,1,0:T(8,128)S(1)} %pad_maximum_fusion.1), channel_id=1, source_target_pairs={{0,1},{1,2},{2,3},{3,0},{4,5},{5,6},{6,7},{7,4},{8,9},{9,10},{10,1... | collective-permute-start | bytes 1572872 | tf_op jit(solution)/shard_map/ppermute | solution.py:66
  43.3 15.1 %collective-permute-start.5 = (f32[2,16,16,256]{3,2,1,0:T(8,128)S(1)}, f32[2,16,16,256]{3,2,1,0:T(8,128)S(1)}, u32[]{:S(2)}, u32[]{:S(2)}) collective-permute-start(f32[2,16,16,256]{3,2,1,0:T(8,128)S(1)} %pad_maximum_fusion.2), channel_id=1, source_target_pairs={{0,3},{1,0},{2,1},{3,2},{4,7},{5,4},{6,5},{7,6},{8,11},{9,8},{10,9... | collective-permute-start | bytes 1572872 | tf_op jit(solution)/shard_map/ppermute | solution.py:67

commit v6 on v5

--- a/solution.py
+++ b/solution.py
@@ -68,45 +68,50 @@
     return block(0) + got_left + got_right
 
 
-def stack_kernel(offsets_ref, images_ref, out_ref):
-    visits = images_ref.shape[1]
-    rows = out_ref.shape[2]
+def stack_kernel(offsets_ref, keep_ref, images_ref, out_ref, held_ref):
+    visits, extended, _ = held_ref.shape
+    rows = out_ref.shape[1]
     reach = MAXOFF * BR
-    for k in range(out_ref.shape[1]):
+    low = images_ref[:, 0:reach, :]
+    high = images_ref[:, extended - reach :, :]
+    held_ref[:, 0:reach, :] = jnp.where(keep_ref[0] > 0, low, 0.0)
+    held_ref[:, reach : extended - reach, :] = images_ref[:, reach : extended - reach, :]
+    held_ref[:, extended - reach :, :] = jnp.where(keep_ref[1] > 0, high, 0.0)
+    for k in range(out_ref.shape[0]):
         total = None
         for t in range(visits):
             start = pl.multiple_of(reach + BR * offsets_ref[t, k], BR)
-            term = images_ref[0, t, pl.ds(start, rows), :]
+            term = held_ref[t, pl.ds(start, rows), :]
             total = term if total is None else total + term
-        out_ref[0, k] = total
+        out_ref[k] = total
 
 
-def partial_sums(images, mine):
-    channels, visits, extended, cols = images.shape
+def partial_sums(images, mine, keep):
+    visits, extended, cols = images.shape
     rows = extended - 2 * MAXOFF * BR
     velocities = mine.shape[1]
     return pl.pallas_call(
         stack_kernel,
-        out_shape=jax.ShapeDtypeStruct((channels, velocities, rows, cols), jnp.float32),
+        out_shape=jax.ShapeDtypeStruct((velocities, rows, cols), jnp.float32),
         grid_spec=pltpu.PrefetchScalarGridSpec(
-            num_scalar_prefetch=1,
-            grid=(channels,),
-            in_specs=[pl.BlockSpec((1, visits, extended, cols), lambda c, off: (c, 0, 0, 0))],
-            out_specs=pl.BlockSpec((1, velocities, rows, cols), lambda c, off: (c, 0, 0, 0)),
+            num_scalar_prefetch=2,
+            grid=(1,),
+            in_specs=[pl.BlockSpec((visits, extended, cols), lambda i, off, keep: (0, 0, 0))],
+            out_specs=pl.BlockSpec((velocities, rows, cols), lambda i, off, keep: (0, 0, 0)),
+            scratch_shapes=[pltpu.VMEM((visits, extended, cols), jnp.float32)],
         ),
         cost_estimate=pl.CostEstimate(
-            flops=channels * velocities * visits * rows * cols,
+            flops=velocities * visits * rows * cols,
             transcendentals=0,
-            bytes_accessed=4 * channels * (visits * extended + velocities * rows) * cols,
+            bytes_accessed=4 * (visits * extended + velocities * rows) * cols,
         ),
-    )(mine, images)
+    )(mine, keep, images)
 
 
 def shards(science, inv_variance, psf_kernel, offsets):
     radius = (psf_kernel.shape[0] - 1) // 2
     reach = MAXOFF * BR
     visits, rows, cols = science.shape
-    total_rows = rows * lax.axis_size("sky")
 
     weighted = science * inv_variance
     both = jnp.stack([weighted, inv_variance])
@@ -114,15 +119,11 @@
 
     psi = correlate_rows(bordered[0], toeplitz(psf_kernel, cols))
     phi = correlate_rows(bordered[1], toeplitz(psf_kernel * psf_kernel, cols))
-    images = jnp.stack([psi, phi])
 
-    first = lax.axis_index("sky") * rows - reach
-    row_ids = first + lax.broadcasted_iota(jnp.int32, (1, 1, rows + 2 * reach, 1), 2)
-    inside = (row_ids >= 0) & (row_ids < total_rows)
-    images = jnp.where(inside, images, 0.0)
-
+    sky = lax.axis_index("sky")
+    keep = jnp.stack([sky > 0, sky < lax.axis_size("sky") - 1]).astype(jnp.int32)
     mine = lax.dynamic_slice_in_dim(offsets, lax.axis_index("visit") * visits, visits, 0)
-    partial = partial_sums(images, mine)
+    partial = jnp.stack([partial_sums(psi, mine, keep), partial_sums(phi, mine, keep)])
 
     stacked = ring_reduce_scatter(partial, "visit")
     return stacked[0] / jnp.sqrt(stacked[1])

time: 60.7 us -> 65.8 us (1.084)
  the two profiles are of different devices: /device:TPU:119 before, /device:TPU:24 now
where the time goes in v6:
time: 65.8 us; the launch traced here: 65.4 us
  waiting for transfers between devices  18.4 us (28%)
  starting transfers between devices  15.5 us (24%)
  matrix products  15.2 us (23%)
  Pallas kernels  6.64 us (10%)
  other arithmetic  6.44 us (10%)
  local copies, waits for them, and re-layouts  3.1 us (5%)
    conv_general_dilated x2, matrix products, correlate_rows(): lax.conv_general_dilated(bordered, kernel, window_strides=(1,), padding='...  9.6 us
    ppermute x1, starting transfers between devices, bordered_rows(): lax.ppermute(lax.slice_in_dim(block, 0, width, axis=dim), axis, backward)  7.38 us
    pallas_call x2, Pallas kernels, partial_sums(): pl.pallas_call(stack_kernel, out_shape=jax.ShapeDtypeStruct((velocities,...  6.64 us
    ppermute x1, waiting for transfers between devices, ring_reduce_scatter(): got_right = lax.ppermute(behind, axis, left)  6.48 us
    ppermute x1, waiting for transfers between devices, ring_reduce_scatter(): from_right = lax.ppermute(far[..., half:], axis, left)  6.15 us
    dot_general x2, matrix products, toeplitz(): jnp.einsum('ab,bwv->awv', taps, onehot, precision=lax.Precision.HIGHEST)  5.55 us
    ppermute x1, waiting for transfers between devices, ring_reduce_scatter(): got_left = lax.ppermute(ahead, axis, right)  3.99 us
    ppermute x1, starting transfers between devices, ring_reduce_scatter(): got_right = lax.ppermute(behind, axis, left)  3.29 us
  transfers between devices with their start and end apart: 6, of which 4 were waited for; matrix products, arithmetic and copies ran while one was open for 11% of the time, Pallas kernels for 0%

profile of v6, /device:TPU:24, one launch (start us, length us, event | category | flops | bytes accessed | tf_op | source)
XLA Modules:
  0.0 65.4 jit_solution(17536703627776023055)
XLA Ops:
  0.0 0.0 copy-start
  0.0 1.8 %fusion.14 = (f32[1,8,64,256]{3,1,2,0:T(8,128)S(1)}, f32[1,8,64,256]{3,1,2,0:T(8,128)S(1)}) fusion(f32[8,64,256]{2,1,0:T(8,128)} %param.4, f32[8,64,256]{2,1,0:T(8,128)} %param.5), kind=kLoop, calls=%fused_computation.29 | loop fusion | flops 131072 | bytes 2097152 | tf_op jit(solution)/shard_map/stack | solution.py:117
  1.8 0.1 pad_maximum_fusion.4
  1.9 7.4 %collective-permute-start.1 = (f32[2,8,21,256]{3,1,2,0:T(8,128)S(1)}, f32[2,8,21,256]{3,1,2,0:T(8,128)S(1)}, u32[]{:S(2)}, u32[]{:S(2)}) collective-permute-start(f32[2,8,21,256]{3,1,2,0:T(8,128)S(1)} %get-tuple-element.9), channel_id=1, source_target_pairs={{4,0},{8,4},{12,8},{16,12},{20,16},{24,20},{28,24},{32,28},{36,32}... | collective-permute-start | bytes 1032200 | tf_op jit(solution)/shard_map/ppermute | solution.py:20
  9.3 1.9 %collective-permute-start = (f32[2,8,21,256]{3,1,2,0:T(8,128)S(1)}, f32[2,8,21,256]{3,1,2,0:T(8,128)S(1)}, u32[]{:S(2)}, u32[]{:S(2)}) collective-permute-start(f32[2,8,21,256]{3,1,2,0:T(8,128)S(1)} %get-tuple-element.8), channel_id=1, source_target_pairs={{0,4},{4,8},{8,12},{12,16},{16,20},{20,24},{24,28},{28,32},{32,36}... | collective-permute-start | bytes 1032200 | tf_op jit(solution)/shard_map/ppermute | solution.py:17
  11.2 4.1 %fusion.1 = f32[256,256,11]{1,2,0:T(8,128)} fusion(f32[11,11]{1,0:T(8,128)S(1)} %copy-done.4), kind=kOutput, calls=%fused_computation.2 | convolution fusion | flops 97320960 | bytes 2884068 | tf_op jit(solution)/shard_map/ab,bwv->awv/dot_general | solution.py:31
  15.3 0.1 constant_dynamic-slice_fusion
  15.4 0.7 %add_convert_fusion.keep_ref = s32[2]{0:T(128)} fusion(pred[1]{0:T(512)(128)(4,1)} %bitcast.1, pred[1]{0:T(512)(128)(4,1)} %bitcast), kind=kLoop, calls=%fused_computation.42 | loop fusion | flops 4 | bytes 10 | tf_op jit(solution)/shard_map/convert_element_type | solution.py:124
  16.1 0.7 %copy.13.offsets_ref = s32[8,16]{1,0:T(8,128)} copy(s32[8,16]{0,1:T(8,128)S(1)} %constant_dynamic-slice_fusion) | data formatting | bytes 1024
  16.7 1.5 %fusion = f32[11,256,256]{2,0,1:T(8,128)S(1)} fusion(f32[11,11]{1,0:T(8,128)S(1)} %copy-done.4), kind=kOutput, calls=%fused_computation.1 | convolution fusion | flops 97321080 | bytes 2884068 | tf_op jit(solution)/shard_map/ab,bwv->awv/dot_general | solution.py:31
  18.2 0.0 collective-permute-done.1
  18.2 1.8 %collective-permute-done = f32[2,8,21,256]{3,1,2,0:T(8,128)S(1)} collective-permute-done((f32[2,8,21,256]{3,1,2,0:T(8,128)S(1)}, f32[2,8,21,256]{3,1,2,0:T(8,128)S(1)}, u32[]{:S(2)}, u32[]{:S(2)}) %collective-permute-start) | collective-permute-done | bytes 344096 | tf_op jit(solution)/shard_map/ppermute | solution.py:17
  20.0 0.1 pad_maximum_fusion
  20.1 4.7 %fusion.4 = f32[8,96,256]{2,0,1:T(8,128)S(1)} fusion(f32[256,256,11]{1,2,0:T(8,128)S(1)} %copy-done.3, f32[2,8,106,256]{3,1,2,0:T(8,128)S(1)} %pad_maximum_fusion), kind=kOutput, calls=%fused_computation.13 | convolution fusion | flops 3321888768 | bytes 5849088 | tf_op jit(solution)/shard_map/conv_general_dilated | solution.py:35
  24.8 1.2 %copy.10.images_ref = f32[8,96,256]{2,1,0:T(8,128)} copy(f32[8,96,256]{2,0,1:T(8,128)S(1)} %fusion.4) | data formatting | bytes 1572864 | tf_op jit(solution)/shard_map/conv_general_dilated | solution.py:35
  26.0 4.9 %fusion.2 = f32[8,96,256]{2,0,1:T(8,128)S(1)} fusion(f32[11,256,256]{2,0,1:T(8,128)S(1)} %fusion, f32[2,8,106,256]{3,1,2,0:T(8,128)S(1)} %pad_maximum_fusion), kind=kOutput, calls=%fused_computation.11 | convolution fusion | flops 3321888768 | bytes 5849088 | tf_op jit(solution)/shard_map/conv_general_dilated | solution.py:35
  30.9 1.1 %copy.12.images_ref = f32[8,96,256]{2,1,0:T(8,128)} copy(f32[8,96,256]{2,0,1:T(8,128)S(1)} %fusion.2) | data formatting | bytes 1572864 | tf_op jit(solution)/shard_map/conv_general_dilated | solution.py:35
  32.0 3.3 %shard_map.46 = f32[16,64,256]{2,1,0:T(8,128)} custom-call(s32[8,16]{1,0:T(8,128)} %copy.13.offsets_ref, s32[2]{0:T(128)} %add_convert_fusion.keep_ref, f32[8,96,256]{2,1,0:T(8,128)} %copy.10.images_ref), custom_call_target="tpu_custom_call" | custom-call | flops 2097152 | bytes 1835008 | tf_op jit(solution)/shard_map/pallas_call | solution.py:93
  35.3 3.3 %shard_map.47 = f32[16,64,256]{2,1,0:T(8,128)} custom-call(s32[8,16]{1,0:T(8,128)} %copy.13.offsets_ref, s32[2]{0:T(128)} %add_convert_fusion.keep_ref, f32[8,96,256]{2,1,0:T(8,128)} %copy.12.images_ref), custom_call_target="tpu_custom_call" | custom-call | flops 2097152 | bytes 1835008 | tf_op jit(solution)/shard_map/pallas_call | solution.py:93
  38.7 1.5 %fusion.12 = (f32[2,16,16,256]{3,2,1,0:T(8,128)S(1)}, f32[2,16,16,256]{3,2,1,0:T(8,128)S(1)}, f32[2,16,16,256]{3,2,1,0:T(8,128)S(1)}) fusion(s32[]{:T(128)S(6)} %select_n.38, f32[1,16,64,256]{3,2,1,0:T(8,128)} %bitcast.22, f32[1,16,64,256]{3,2,1,0:T(8,128)} %bitcast.24, s32[]{:T(128)S(6)} %select_n.40, s32[]{:T(128)S(6)} %select_n.42), kind=kLoop, calls=%fused_computation.24 | loop fusion | flops 393216 | bytes 3670028 | tf_op jit(solution)/shard_map/stack | solution.py:126
  40.2 2.8 %collective-permute-start.4 = (f32[2,16,16,128]{3,2,1,0:T(8,128)S(1)}, f32[2,16,16,128]{3,2,1,0:T(8,128)S(1)}, u32[]{:S(2)}, u32[]{:S(2)}) collective-permute-start(f32[2,16,16,128]{3,2,1,0:T(8,128)S(1)} %get-tuple-element.13), channel_id=1, source_target_pairs={{0,3},{1,0},{2,1},{3,2},{4,7},{5,4},{6,5},{7,6},{8,11},{9,8},{10,9... | collective-permute-start | bytes 786440 | tf_op jit(solution)/shard_map/ppermute | solution.py:61
  43.0 0.0 collective-permute-start.2
  43.0 6.1 %collective-permute-done.4 = f32[2,16,16,128]{3,2,1,0:T(8,128)S(1)} collective-permute-done((f32[2,16,16,128]{3,2,1,0:T(8,128)S(1)}, f32[2,16,16,128]{3,2,1,0:T(8,128)S(1)}, u32[]{:S(2)}, u32[]{:S(2)}) %collective-permute-start.4) | collective-permute-done | bytes 262176 | tf_op jit(solution)/shard_map/ppermute | solution.py:61
  49.2 0.1 fusion.23
  49.3 3.3 %collective-permute-start.5 = (f32[2,16,16,256]{3,2,1,0:T(8,128)S(1)}, f32[2,16,16,256]{3,2,1,0:T(8,128)}, u32[]{:S(2)}, u32[]{:S(2)}) collective-permute-start(f32[2,16,16,256]{3,2,1,0:T(8,128)S(1)} %pad_maximum_fusion.2), channel_id=1, source_target_pairs={{0,3},{1,0},{2,1},{3,2},{4,7},{5,4},{6,5},{7,6},{8,11},{9,8},{10,9... | collective-permute-start | bytes 1572872 | tf_op jit(solution)/shard_map/ppermute | solution.py:67
  52.6 0.0 collective-permute-done.2
  52.6 0.1 slice_add_fusion.1
  52.7 0.1 collective-permute-start.3
  52.8 6.5 %collective-permute-done.5 = f32[2,16,16,256]{3,2,1,0:T(8,128)} collective-permute-done((f32[2,16,16,256]{3,2,1,0:T(8,128)S(1)}, f32[2,16,16,256]{3,2,1,0:T(8,128)}, u32[]{:S(2)}, u32[]{:S(2)}) %collective-permute-start.5) | collective-permute-done | bytes 524320 | tf_op jit(solution)/shard_map/ppermute | solution.py:67
  59.3 4.0 %collective-permute-done.3 = f32[2,16,16,256]{3,2,1,0:T(8,128)} collective-permute-done((f32[2,16,16,256]{3,2,1,0:T(8,128)S(1)}, f32[2,16,16,256]{3,2,1,0:T(8,128)}, u32[]{:S(2)}, u32[]{:S(2)}) %collective-permute-start.3) | collective-permute-done | bytes 524320 | tf_op jit(solution)/shard_map/ppermute | solution.py:66
  63.3 1.4 %fusion.11 = f32[2,16,16,256]{3,2,1,0:T(8,128)S(1)} fusion(f32[2,16,16,256]{3,2,1,0:T(8,128)} %collective-permute-done.5, f32[2,16,16,256]{3,2,1,0:T(8,128)} %collective-permute-done.3, s32[]{:T(128)S(6)} %select_n.36, f32[1,16,64,256]{3,2,1,0:T(8,128)S(1)} %bitcast.23, f32[1,16,64,256]{3,2,1,0:T(8,128)S(1)} %bitcast.25), kind=kLoop, calls=%fused_computation.23 | loop fusion | flops 393216 | bytes 3670020 | tf_op jit(solution)/shard_map/add | solution.py:68
  64.6 0.7 %fusion.16 = f32[16,16,256]{2,1,0:T(8,128)} fusion(f32[2,16,16,256]{3,2,1,0:T(8,128)S(1)} %fusion.11), kind=kLoop, calls=%fused_computation.35 | loop fusion | flops 65536 | bytes 786432 | tf_op jit(solution)/shard_map/div | solution.py:129
  (12 shorter events, 0.1 us)
Async XLA Ops:
  0.0 15.3 %copy-start = (s32[32,16]{0,1:T(8,128)S(1)}, s32[32,16]{0,1:T(8,128)}, u32[]{:S(2)}) copy-start(s32[32,16]{0,1:T(8,128)} %param.7) | copy-start | bytes 6148
  0.0 11.2 %copy-start.4 = (f32[11,11]{1,0:T(8,128)S(1)}, f32[11,11]{1,0:T(8,128)}, u32[]{:S(2)}) copy-start(f32[11,11]{1,0:T(8,128)} %param.6) | copy-start | bytes 1456
  1.9 16.3 %collective-permute-start.1 = (f32[2,8,21,256]{3,1,2,0:T(8,128)S(1)}, f32[2,8,21,256]{3,1,2,0:T(8,128)S(1)}, u32[]{:S(2)}, u32[]{:S(2)}) collective-permute-start(f32[2,8,21,256]{3,1,2,0:T(8,128)S(1)} %get-tuple-element.9), channel_id=1, source_target_pairs={{4,0},{8,4},{12,8},{16,12},{20,16},{24,20},{28,24},{32,28},{36,32}... | collective-permute-start | bytes 1032200 | tf_op jit(solution)/shard_map/ppermute | solution.py:20
  9.3 10.7 %collective-permute-start = (f32[2,8,21,256]{3,1,2,0:T(8,128)S(1)}, f32[2,8,21,256]{3,1,2,0:T(8,128)S(1)}, u32[]{:S(2)}, u32[]{:S(2)}) collective-permute-start(f32[2,8,21,256]{3,1,2,0:T(8,128)S(1)} %get-tuple-element.8), channel_id=1, source_target_pairs={{0,4},{4,8},{8,12},{12,16},{16,20},{20,24},{24,28},{28,32},{32,36}... | collective-permute-start | bytes 1032200 | tf_op jit(solution)/shard_map/ppermute | solution.py:17
  16.7 3.4 %copy-start.3 = (f32[256,256,11]{1,2,0:T(8,128)S(1)}, f32[256,256,11]{1,2,0:T(8,128)}, u32[]{:S(2)}) copy-start(f32[256,256,11]{1,2,0:T(8,128)} %fusion.1) | copy-start | bytes 8650756
  40.1 23.1 %copy-start.1 = (f32[16,64,256]{2,1,0:T(8,128)S(1)}, f32[16,64,256]{2,1,0:T(8,128)}, u32[]{:S(2)}) copy-start(f32[16,64,256]{2,1,0:T(8,128)} %shard_map.46) | copy-start | bytes 3145732
  40.2 23.1 %copy-start.2 = (f32[16,64,256]{2,1,0:T(8,128)S(1)}, f32[16,64,256]{2,1,0:T(8,128)}, u32[]{:S(2)}) copy-start(f32[16,64,256]{2,1,0:T(8,128)} %shard_map.47) | copy-start | bytes 3145732
  40.2 9.0 %collective-permute-start.4 = (f32[2,16,16,128]{3,2,1,0:T(8,128)S(1)}, f32[2,16,16,128]{3,2,1,0:T(8,128)S(1)}, u32[]{:S(2)}, u32[]{:S(2)}) collective-permute-start(f32[2,16,16,128]{3,2,1,0:T(8,128)S(1)} %get-tuple-element.13), channel_id=1, source_target_pairs={{0,3},{1,0},{2,1},{3,2},{4,7},{5,4},{6,5},{7,6},{8,11},{9,8},{10,9... | collective-permute-start | bytes 786440 | tf_op jit(solution)/shard_map/ppermute | solution.py:61
  43.0 9.6 %collective-permute-start.2 = (f32[2,16,16,128]{3,2,1,0:T(8,128)S(1)}, f32[2,16,16,128]{3,2,1,0:T(8,128)S(1)}, u32[]{:S(2)}, u32[]{:S(2)}) collective-permute-start(f32[2,16,16,128]{3,2,1,0:T(8,128)S(1)} %get-tuple-element.12), channel_id=1, source_target_pairs={{0,1},{1,2},{2,3},{3,0},{4,5},{5,6},{6,7},{7,4},{8,9},{9,10},{10,1... | collective-permute-start | bytes 786440 | tf_op jit(solution)/shard_map/ppermute | solution.py:60
  49.3 10.0 %collective-permute-start.5 = (f32[2,16,16,256]{3,2,1,0:T(8,128)S(1)}, f32[2,16,16,256]{3,2,1,0:T(8,128)}, u32[]{:S(2)}, u32[]{:S(2)}) collective-permute-start(f32[2,16,16,256]{3,2,1,0:T(8,128)S(1)} %pad_maximum_fusion.2), channel_id=1, source_target_pairs={{0,3},{1,0},{2,1},{3,2},{4,7},{5,4},{6,5},{7,6},{8,11},{9,8},{10,9... | collective-permute-start | bytes 1572872 | tf_op jit(solution)/shard_map/ppermute | solution.py:67
  52.7 10.6 %collective-permute-start.3 = (f32[2,16,16,256]{3,2,1,0:T(8,128)S(1)}, f32[2,16,16,256]{3,2,1,0:T(8,128)}, u32[]{:S(2)}, u32[]{:S(2)}) collective-permute-start(f32[2,16,16,256]{3,2,1,0:T(8,128)S(1)} %pad_maximum_fusion.1), channel_id=1, source_target_pairs={{0,1},{1,2},{2,3},{3,0},{4,5},{5,6},{6,7},{7,4},{8,9},{9,10},{10,1... | collective-permute-start | bytes 1572872 | tf_op jit(solution)/shard_map/ppermute | solution.py:66

commit v7 on v4

--- a/solution.py
+++ b/solution.py
@@ -69,17 +69,14 @@
     return blocks[0] + got_left + got_right
 
 
-def full_toeplitz(taps, cols, chunk):
+def toeplitz_full(taps, cols):
     size = taps.shape[1]
     radius = (size - 1) // 2
-    block = toeplitz(taps, chunk)
-    parts = []
-    for start_col in range(0, cols, chunk):
-        low = start_col - radius
-        first, last = max(0, -low), min(block.shape[1], cols - low)
-        part = block[:, first:last, :]
-        parts.append(jnp.pad(part, ((0, 0), (low + first, cols - (low + last)), (0, 0))))
-    return jnp.concatenate(parts, axis=2)
+    w = lax.broadcasted_iota(jnp.int32, (size, cols, cols), 1)
+    v = lax.broadcasted_iota(jnp.int32, (size, cols, cols), 2)
+    b = lax.broadcasted_iota(jnp.int32, (size, cols, cols), 0)
+    onehot = (w - v + radius == b).astype(jnp.float32)
+    return jnp.einsum("ab,bwv->awv", taps, onehot, precision=lax.Precision.HIGHEST)
 
 
 def partial_sums(images, mine, rows):
@@ -100,29 +97,28 @@
     reach = MAXOFF * BR
     visits, rows, cols = science.shape
     total_rows = rows * lax.axis_size("sky")
-    chunk = 128 if cols % 128 == 0 else cols
 
     first = lax.axis_index("sky") * rows - reach
     row_ids = first + lax.broadcasted_iota(jnp.int32, (1, rows + 2 * reach, 1), 1)
     inside = (row_ids >= 0) & (row_ids < total_rows)
     mine = lax.dynamic_slice_in_dim(offsets, lax.axis_index("visit") * visits, visits, 0)
 
-    weighted = bordered_rows(science * inv_variance, "sky", radius + reach)
-    inverse = bordered_rows(inv_variance, "sky", radius + reach)
+    bordered = bordered_rows(jnp.stack([science * inv_variance, inv_variance]), "sky", radius + reach)
+    weighted, inverse = bordered[0], bordered[1]
 
     if lax.axis_size("visit") != 4:
-        psi = correlate_rows(weighted, full_toeplitz(psf_kernel, cols, chunk))
-        phi = correlate_rows(inverse, full_toeplitz(psf_kernel * psf_kernel, cols, chunk))
+        psi = correlate_rows(weighted, toeplitz_full(psf_kernel, cols))
+        phi = correlate_rows(inverse, toeplitz_full(psf_kernel * psf_kernel, cols))
         both = jnp.stack([partial_sums(jnp.where(inside, x, 0.0), mine, rows) for x in (psi, phi)])
         both = lax.psum_scatter(both, "visit", scatter_dimension=2, tiled=True)
         return both[0] / jnp.sqrt(both[1])
 
-    psi = correlate_rows(weighted, full_toeplitz(psf_kernel, cols, chunk))
+    psi = correlate_rows(weighted, toeplitz_full(psf_kernel, cols))
     psi = partial_sums(jnp.where(inside, psi, 0.0), mine, rows)
     psi, inverse = lax.optimization_barrier((psi, inverse))
     blocks, from_left, from_right = ring_step_one(psi, "visit")
 
-    phi = correlate_rows(inverse, full_toeplitz(psf_kernel * psf_kernel, cols, chunk))
+    phi = correlate_rows(inverse, toeplitz_full(psf_kernel * psf_kernel, cols))
     phi = jnp.where(inside, phi, 0.0)
     from_left, from_right, phi = lax.optimization_barrier((from_left, from_right, phi))
     psi = ring_step_two(blocks, from_left, from_right, "visit")

time: 78.2 us -> 59.9 us (0.77)
  the two profiles are of different devices: /device:TPU:30 before, /device:TPU:110 now
where the time goes in v7:
time: 59.9 us; the launch traced here: 59.7 us
  matrix products  22 us (37%)
  waiting for transfers between devices  18 us (30%)
  starting transfers between devices  14.3 us (24%)
  other arithmetic  3.56 us (6%)
  local copies, waits for them, and re-layouts  1.58 us (3%)
    conv_general_dilated x2, matrix products, correlate_rows(): lax.conv_general_dilated(bordered, kernel, window_strides=(1,), padding='...  9.41 us
    ppermute x2, waiting for transfers between devices, ring_step_two(): got_left = lax.ppermute(ahead, axis, right)  8.58 us
    dot_general x10, matrix products, partial_sums(): jnp.einsum('tk,trw->krw', onehot, shifted, precision=lax.Precision.HIGHEST)  6.32 us
    dot_general x2, matrix products, toeplitz_full(): jnp.einsum('ab,bwv->awv', taps, onehot, precision=lax.Precision.HIGHEST)  6.25 us
    ppermute x1, starting transfers between devices, bordered_rows(): lax.ppermute(lax.slice_in_dim(block, 0, width, axis=dim), axis, backward)  3.64 us
    ppermute x2, waiting for transfers between devices, ring_step_one(): from_left = lax.ppermute(blocks[2][:half], axis, right)  3.52 us
    ppermute x2, waiting for transfers between devices, ring_step_one(): from_right = lax.ppermute(blocks[2][half:], axis, left)  3.16 us
    ppermute x2, starting transfers between devices, ring_step_two(): got_right = lax.ppermute(behind, axis, left)  2.96 us
  transfers between devices with their start and end apart: 10, of which 7 were waited for; matrix products, arithmetic and copies ran while one was open for 19% of the time, Pallas kernels for 0%

profile of v7, /device:TPU:110, one launch (start us, length us, event | category | flops | bytes accessed | tf_op | source)
XLA Modules:
  0.0 59.7 jit_solution(18400332336288566972)
XLA Ops:
  0.0 1.8 %fusion.20 = (f32[1,8,64,256]{3,1,2,0:T(8,128)S(1)}, f32[1,8,64,256]{3,1,2,0:T(8,128)S(1)}) fusion(f32[8,64,256]{2,1,0:T(8,128)} %param.4, f32[8,64,256]{2,1,0:T(8,128)} %param.5), kind=kLoop, calls=%fused_computation.29 | loop fusion | flops 131072 | bytes 2097152 | tf_op jit(solution)/shard_map/stack | solution.py:106
  1.9 1.9 %collective-permute-start = (f32[2,8,21,256]{3,1,2,0:T(8,128)S(1)}, f32[2,8,21,256]{3,1,2,0:T(8,128)S(1)}, u32[]{:S(2)}, u32[]{:S(2)}) collective-permute-start(f32[2,8,21,256]{3,1,2,0:T(8,128)S(1)} %get-tuple-element.27), channel_id=1, source_target_pairs={{0,4},{4,8},{8,12},{12,16},{16,20},{20,24},{24,28},{28,32},{32,36}... | collective-permute-start | bytes 1032200 | tf_op jit(solution)/shard_map/ppermute | solution.py:15
  3.8 3.6 %collective-permute-start.1 = (f32[2,8,21,256]{3,1,2,0:T(8,128)S(1)}, f32[2,8,21,256]{3,1,2,0:T(8,128)S(1)}, u32[]{:S(2)}, u32[]{:S(2)}) collective-permute-start(f32[2,8,21,256]{3,1,2,0:T(8,128)S(1)} %get-tuple-element.28), channel_id=1, source_target_pairs={{4,0},{8,4},{12,8},{16,12},{20,16},{24,20},{28,24},{32,28},{36,32}... | collective-permute-start | bytes 1032200 | tf_op jit(solution)/shard_map/ppermute | solution.py:18
  7.7 4.8 %fusion.1 = f32[256,256,11]{1,2,0:T(8,128)} fusion(f32[11,11]{1,0:T(8,128)} %param.6), kind=kOutput, calls=%fused_computation.2 | convolution fusion | flops 97320960 | bytes 2884068 | tf_op jit(solution)/shard_map/ab,bwv->awv/dot_general | solution.py:79
  12.5 1.5 %fusion = f32[11,256,256]{2,0,1:T(8,128)S(1)} fusion(f32[11,11]{1,0:T(8,128)S(1)} %copy-done.2), kind=kOutput, calls=%fused_computation.1 | convolution fusion | flops 97321080 | bytes 2884068 | tf_op jit(solution)/shard_map/ab,bwv->awv/dot_general | solution.py:79
  14.2 0.5 copy-done.1
  14.6 4.7 %fusion.8 = f32[8,96,256]{2,0,1:T(8,128)S(1)} fusion(f32[256,256,11]{1,2,0:T(8,128)S(1)} %copy-done.1, f32[2,8,106,256]{3,1,2,0:T(8,128)S(1)} %pad_maximum_fusion, pred[96]{0:T(512)(128)(4,1)S(1)} %compare_and_fusion), kind=kOutput, calls=%fused_computation.18 | convolution fusion | flops 3322085376 | bytes 5849600 | tf_op jit(solution)/shard_map/conv_general_dilated | solution.py:33
  19.3 0.6 %fusion.18 = f32[16,64,256]{2,0,1:T(8,128)S(1)} fusion(f32[8,96,256]{2,0,1:T(8,128)S(1)} %fusion.8, pred[8,16]{1,0:T(8,128)(4,1)S(1)} %get-tuple-element.35), kind=kOutput, calls=%fused_computation.26 | convolution fusion | flops 25165824 | bytes 1573888 | tf_op jit(solution)/shard_map/tk,trw->krw/dot_general | solution.py:89
  20.0 0.6 %convolution_add_fusion.7 = f32[16,64,256]{2,0,1:T(8,128)S(1)} fusion(f32[16,64,256]{2,0,1:T(8,128)S(1)} %fusion.18, f32[8,96,256]{2,0,1:T(8,128)S(1)} %fusion.8, pred[8,16]{1,0:T(8,128)(4,1)S(1)} %get-tuple-element.34), kind=kOutput, calls=%fused_computation.17 | convolution fusion | flops 25427968 | bytes 2622464 | tf_op jit(solution)/shard_map/tk,trw->krw/dot_general | solution.py:89
  20.6 0.6 %convolution_add_fusion.6 = f32[16,64,256]{2,0,1:T(8,128)S(1)} fusion(f32[16,64,256]{2,0,1:T(8,128)S(1)} %convolution_add_fusion.7, f32[8,96,256]{2,0,1:T(8,128)S(1)} %fusion.8, pred[8,16]{1,0:T(8,128)(4,1)S(1)} %get-tuple-element.33), kind=kOutput, calls=%fused_computation.16 | convolution fusion | flops 25427968 | bytes 2622464 | tf_op jit(solution)/shard_map/tk,trw->krw/dot_general | solution.py:89
  21.2 0.6 %convolution_add_fusion.5 = f32[16,64,256]{2,0,1:T(8,128)S(1)} fusion(f32[16,64,256]{2,0,1:T(8,128)S(1)} %convolution_add_fusion.6, f32[8,96,256]{2,0,1:T(8,128)S(1)} %fusion.8, pred[8,16]{1,0:T(8,128)(4,1)S(1)} %get-tuple-element.32), kind=kOutput, calls=%fused_computation.15 | convolution fusion | flops 25427968 | bytes 2622464 | tf_op jit(solution)/shard_map/tk,trw->krw/dot_general | solution.py:89
  21.9 0.7 %convolution_add_fusion.4 = f32[16,64,256]{2,0,1:T(8,128)S(1)} fusion(f32[16,64,256]{2,0,1:T(8,128)S(1)} %convolution_add_fusion.5, f32[8,96,256]{2,0,1:T(8,128)S(1)} %fusion.8, pred[8,16]{1,0:T(8,128)(4,1)S(1)} %get-tuple-element.31), kind=kOutput, calls=%fused_computation.14 | convolution fusion | flops 25427968 | bytes 2622464 | tf_op jit(solution)/shard_map/tk,trw->krw/dot_general | solution.py:89
  22.6 0.7 %collective-permute-start.2 = (f32[8,16,256]{2,0,1:T(8,128)S(1)}, f32[8,16,256]{2,0,1:T(8,128)S(1)}, u32[]{:S(2)}, u32[]{:S(2)}) collective-permute-start(f32[8,16,256]{2,0,1:T(8,128)S(1)} %get-tuple-element.26), channel_id=1, source_target_pairs={{0,1},{1,2},{2,3},{3,0},{4,5},{5,6},{6,7},{7,4},{8,9},{9,10},{10,1... | collective-permute-start | bytes 393224 | tf_op jit(solution)/shard_map/ppermute | solution.py:55
  23.3 1.5 %collective-permute-start.3 = (f32[8,16,256]{2,0,1:T(8,128)S(1)}, f32[8,16,256]{2,0,1:T(8,128)S(1)}, u32[]{:S(2)}, u32[]{:S(2)}) collective-permute-start(f32[8,16,256]{2,0,1:T(8,128)S(1)} %get-tuple-element.25), channel_id=1, source_target_pairs={{0,3},{1,0},{2,1},{3,2},{4,7},{5,4},{6,5},{7,6},{8,11},{9,8},{10,9... | collective-permute-start | bytes 393224 | tf_op jit(solution)/shard_map/ppermute | solution.py:56
  24.9 4.7 %fusion.11 = f32[8,96,256]{2,0,1:T(8,128)S(1)} fusion(f32[8,106,256]{2,0,1:T(8,128)S(1)} %slice_bitcast_fusion, f32[11,256,256]{2,0,1:T(8,128)S(1)} %fusion, pred[96]{0:T(512)(128)(4,1)S(1)} %compare_and_fusion), kind=kOutput, calls=%fused_computation.19 | convolution fusion | flops 3322085376 | bytes 4538464 | tf_op jit(solution)/shard_map/conv_general_dilated | solution.py:33
  29.7 0.6 %fusion.24 = f32[16,64,256]{2,0,1:T(8,128)S(1)} fusion(f32[8,96,256]{2,0,1:T(8,128)S(1)} %fusion.11, pred[8,16]{1,0:T(8,128)(4,1)S(1)} %get-tuple-element.34), kind=kOutput, calls=%fused_computation.33 | convolution fusion | flops 25165824 | bytes 1573888 | tf_op jit(solution)/shard_map/tk,trw->krw/dot_general | solution.py:89
  30.3 0.6 %convolution_add_fusion.3 = f32[16,64,256]{2,0,1:T(8,128)S(1)} fusion(f32[16,64,256]{2,0,1:T(8,128)S(1)} %fusion.24, f32[8,96,256]{2,0,1:T(8,128)S(1)} %fusion.11, pred[8,16]{1,0:T(8,128)(4,1)S(1)} %get-tuple-element.35), kind=kOutput, calls=%fused_computation.13 | convolution fusion | flops 25427968 | bytes 2622464 | tf_op jit(solution)/shard_map/tk,trw->krw/dot_general | solution.py:89
  30.9 0.6 %convolution_add_fusion.2 = f32[16,64,256]{2,0,1:T(8,128)S(1)} fusion(f32[16,64,256]{2,0,1:T(8,128)S(1)} %convolution_add_fusion.3, f32[8,96,256]{2,0,1:T(8,128)S(1)} %fusion.11, pred[8,16]{1,0:T(8,128)(4,1)S(1)} %get-tuple-element.33), kind=kOutput, calls=%fused_computation.12 | convolution fusion | flops 25427968 | bytes 2622464 | tf_op jit(solution)/shard_map/tk,trw->krw/dot_general | solution.py:89
  31.6 0.6 %convolution_add_fusion.1 = f32[16,64,256]{2,0,1:T(8,128)S(1)} fusion(f32[16,64,256]{2,0,1:T(8,128)S(1)} %convolution_add_fusion.2, f32[8,96,256]{2,0,1:T(8,128)S(1)} %fusion.11, pred[8,16]{1,0:T(8,128)(4,1)S(1)} %get-tuple-element.32), kind=kOutput, calls=%fused_computation.11 | convolution fusion | flops 25427968 | bytes 2622464 | tf_op jit(solution)/shard_map/tk,trw->krw/dot_general | solution.py:89
  32.2 0.7 %convolution_add_fusion = f32[16,64,256]{2,0,1:T(8,128)S(1)} fusion(f32[16,64,256]{2,0,1:T(8,128)S(1)} %convolution_add_fusion.1, f32[8,96,256]{2,0,1:T(8,128)S(1)} %fusion.11, pred[8,16]{1,0:T(8,128)(4,1)S(1)} %get-tuple-element.31), kind=kOutput, calls=%fused_computation.10 | convolution fusion | flops 25427968 | bytes 2622464 | tf_op jit(solution)/shard_map/tk,trw->krw/dot_general | solution.py:89
  32.9 1.7 %collective-permute-start.6 = (f32[8,16,256]{2,0,1:T(8,128)S(1)}, f32[8,16,256]{2,0,1:T(8,128)S(1)}, u32[]{:S(2)}, u32[]{:S(2)}) collective-permute-start(f32[8,16,256]{2,0,1:T(8,128)S(1)} %get-tuple-element.23), channel_id=1, source_target_pairs={{0,1},{1,2},{2,3},{3,0},{4,5},{5,6},{6,7},{7,4},{8,9},{9,10},{10,1... | collective-permute-start | bytes 393224 | tf_op jit(solution)/shard_map/ppermute | solution.py:55
  35.0 3.5 %collective-permute-done.6 = f32[8,16,256]{2,0,1:T(8,128)S(1)} collective-permute-done((f32[8,16,256]{2,0,1:T(8,128)S(1)}, f32[8,16,256]{2,0,1:T(8,128)S(1)}, u32[]{:S(2)}, u32[]{:S(2)}) %collective-permute-start.6) | collective-permute-done | bytes 131104 | tf_op jit(solution)/shard_map/ppermute | solution.py:55
  38.5 3.1 %collective-permute-done.8 = f32[8,16,256]{2,0,1:T(8,128)S(1)} collective-permute-done((f32[8,16,256]{2,0,1:T(8,128)S(1)}, f32[8,16,256]{2,0,1:T(8,128)S(1)}, u32[]{:S(2)}, u32[]{:S(2)}) %collective-permute-start.8) | collective-permute-done | bytes 131104 | tf_op jit(solution)/shard_map/ppermute | solution.py:56
  41.9 2.1 %collective-permute-start.5 = (f32[16,16,256]{2,0,1:T(8,128)S(1)}, f32[16,16,256]{2,0,1:T(8,128)}, u32[]{:S(2)}, u32[]{:S(2)}) collective-permute-start(f32[16,16,256]{2,0,1:T(8,128)S(1)} %pad_maximum_fusion.4), channel_id=1, source_target_pairs={{0,3},{1,0},{2,1},{3,2},{4,7},{5,4},{6,5},{7,6},{8,11},{9,8},{10,9... | collective-permute-start | bytes 786440 | tf_op jit(solution)/shard_map/ppermute | solution.py:68
  44.0 1.3 %collective-permute-start.7 = (f32[16,16,256]{2,0,1:T(8,128)S(1)}, f32[16,16,256]{2,0,1:T(8,128)}, u32[]{:S(2)}, u32[]{:S(2)}) collective-permute-start(f32[16,16,256]{2,0,1:T(8,128)S(1)} %pad_maximum_fusion.5), channel_id=1, source_target_pairs={{0,1},{1,2},{2,3},{3,0},{4,5},{5,6},{6,7},{7,4},{8,9},{9,10},{10,1... | collective-permute-start | bytes 786440 | tf_op jit(solution)/shard_map/ppermute | solution.py:67
  45.3 0.9 %collective-permute-start.9 = (f32[16,16,256]{2,0,1:T(8,128)S(1)}, f32[16,16,256]{2,0,1:T(8,128)}, u32[]{:S(2)}, u32[]{:S(2)}) collective-permute-start(f32[16,16,256]{2,0,1:T(8,128)S(1)} %pad_maximum_fusion.6), channel_id=1, source_target_pairs={{0,3},{1,0},{2,1},{3,2},{4,7},{5,4},{6,5},{7,6},{8,11},{9,8},{10,9... | collective-permute-start | bytes 786440 | tf_op jit(solution)/shard_map/ppermute | solution.py:68
  46.2 4.8 %collective-permute-done.4 = f32[16,16,256]{2,0,1:T(8,128)S(1)} collective-permute-done((f32[16,16,256]{2,0,1:T(8,128)S(1)}, f32[16,16,256]{2,0,1:T(8,128)S(1)}, u32[]{:S(2)}, u32[]{:S(2)}) %collective-permute-start.4) | collective-permute-done | bytes 262176 | tf_op jit(solution)/shard_map/ppermute | solution.py:67
  51.0 1.4 %collective-permute-done.5 = f32[16,16,256]{2,0,1:T(8,128)} collective-permute-done((f32[16,16,256]{2,0,1:T(8,128)S(1)}, f32[16,16,256]{2,0,1:T(8,128)}, u32[]{:S(2)}, u32[]{:S(2)}) %collective-permute-start.5) | collective-permute-done | bytes 262176 | tf_op jit(solution)/shard_map/ppermute | solution.py:68
  52.4 3.8 %collective-permute-done.7 = f32[16,16,256]{2,0,1:T(8,128)} collective-permute-done((f32[16,16,256]{2,0,1:T(8,128)S(1)}, f32[16,16,256]{2,0,1:T(8,128)}, u32[]{:S(2)}, u32[]{:S(2)}) %collective-permute-start.7) | collective-permute-done | bytes 262176 | tf_op jit(solution)/shard_map/ppermute | solution.py:67
  56.2 1.3 %collective-permute-done.9 = f32[16,16,256]{2,0,1:T(8,128)} collective-permute-done((f32[16,16,256]{2,0,1:T(8,128)S(1)}, f32[16,16,256]{2,0,1:T(8,128)}, u32[]{:S(2)}, u32[]{:S(2)}) %collective-permute-start.9) | collective-permute-done | bytes 262176 | tf_op jit(solution)/shard_map/ppermute | solution.py:68
  57.6 1.3 %rsqrt_multiply_fusion = f32[16,16,256]{2,0,1:T(8,128)S(1)} fusion(f32[16,16,256]{2,0,1:T(8,128)} %collective-permute-done.9, f32[16,16,256]{2,0,1:T(8,128)} %collective-permute-done.7, f32[16,64,256]{2,0,1:T(8,128)S(1)} %convolution_add_fusion, s32[]{:T(128)S(6)} %select_n.56, f32[16,16,256]{2,0,1:T(8,128)} %collective-permute-done.5, ...), kind=kLoop, calls=%fused_computation.43 | loop fusion | flops 327680 | bytes 1835012 | tf_op jit(solution)/shard_map/div | solution.py:128
  58.8 0.9 %copy.11 = f32[16,16,256]{2,1,0:T(8,128)} copy(f32[16,16,256]{2,0,1:T(8,128)S(1)} %rsqrt_multiply_fusion) | data formatting | bytes 524288 | tf_op jit(solution)/shard_map/div | solution.py:128
  (25 shorter events, 1.3 us)
Async XLA Ops:
  0.0 7.5 %copy-start = (s32[32,16]{0,1:T(8,128)S(1)}, s32[32,16]{0,1:T(8,128)}, u32[]{:S(2)}) copy-start(s32[32,16]{0,1:T(8,128)} %param.7) | copy-start | bytes 6148
  0.0 12.4 %copy-start.2 = (f32[11,11]{1,0:T(8,128)S(1)}, f32[11,11]{1,0:T(8,128)}, u32[]{:S(2)}) copy-start(f32[11,11]{1,0:T(8,128)} %param.6) | copy-start | bytes 1456
  1.9 12.0 %collective-permute-start = (f32[2,8,21,256]{3,1,2,0:T(8,128)S(1)}, f32[2,8,21,256]{3,1,2,0:T(8,128)S(1)}, u32[]{:S(2)}, u32[]{:S(2)}) collective-permute-start(f32[2,8,21,256]{3,1,2,0:T(8,128)S(1)} %get-tuple-element.27), channel_id=1, source_target_pairs={{0,4},{4,8},{8,12},{12,16},{16,20},{20,24},{24,28},{28,32},{32,36}... | collective-permute-start | bytes 1032200 | tf_op jit(solution)/shard_map/ppermute | solution.py:15
  3.8 10.1 %collective-permute-start.1 = (f32[2,8,21,256]{3,1,2,0:T(8,128)S(1)}, f32[2,8,21,256]{3,1,2,0:T(8,128)S(1)}, u32[]{:S(2)}, u32[]{:S(2)}) collective-permute-start(f32[2,8,21,256]{3,1,2,0:T(8,128)S(1)} %get-tuple-element.28), channel_id=1, source_target_pairs={{4,0},{8,4},{12,8},{16,12},{20,16},{24,20},{28,24},{32,28},{36,32}... | collective-permute-start | bytes 1032200 | tf_op jit(solution)/shard_map/ppermute | solution.py:18
  12.4 2.2 %copy-start.1 = (f32[256,256,11]{1,2,0:T(8,128)S(1)}, f32[256,256,11]{1,2,0:T(8,128)}, u32[]{:S(2)}) copy-start(f32[256,256,11]{1,2,0:T(8,128)} %fusion.1) | copy-start | bytes 8650756
  22.6 7.0 %collective-permute-start.2 = (f32[8,16,256]{2,0,1:T(8,128)S(1)}, f32[8,16,256]{2,0,1:T(8,128)S(1)}, u32[]{:S(2)}, u32[]{:S(2)}) collective-permute-start(f32[8,16,256]{2,0,1:T(8,128)S(1)} %get-tuple-element.26), channel_id=1, source_target_pairs={{0,1},{1,2},{2,3},{3,0},{4,5},{5,6},{6,7},{7,4},{8,9},{9,10},{10,1... | collective-permute-start | bytes 393224 | tf_op jit(solution)/shard_map/ppermute | solution.py:55
  23.3 6.4 %collective-permute-start.3 = (f32[8,16,256]{2,0,1:T(8,128)S(1)}, f32[8,16,256]{2,0,1:T(8,128)S(1)}, u32[]{:S(2)}, u32[]{:S(2)}) collective-permute-start(f32[8,16,256]{2,0,1:T(8,128)S(1)} %get-tuple-element.25), channel_id=1, source_target_pairs={{0,3},{1,0},{2,1},{3,2},{4,7},{5,4},{6,5},{7,6},{8,11},{9,8},{10,9... | collective-permute-start | bytes 393224 | tf_op jit(solution)/shard_map/ppermute | solution.py:56
  32.9 5.6 %collective-permute-start.6 = (f32[8,16,256]{2,0,1:T(8,128)S(1)}, f32[8,16,256]{2,0,1:T(8,128)S(1)}, u32[]{:S(2)}, u32[]{:S(2)}) collective-permute-start(f32[8,16,256]{2,0,1:T(8,128)S(1)} %get-tuple-element.23), channel_id=1, source_target_pairs={{0,1},{1,2},{2,3},{3,0},{4,5},{5,6},{6,7},{7,4},{8,9},{9,10},{10,1... | collective-permute-start | bytes 393224 | tf_op jit(solution)/shard_map/ppermute | solution.py:55
  34.6 7.0 %collective-permute-start.8 = (f32[8,16,256]{2,0,1:T(8,128)S(1)}, f32[8,16,256]{2,0,1:T(8,128)S(1)}, u32[]{:S(2)}, u32[]{:S(2)}) collective-permute-start(f32[8,16,256]{2,0,1:T(8,128)S(1)} %get-tuple-element.24), channel_id=1, source_target_pairs={{0,3},{1,0},{2,1},{3,2},{4,7},{5,4},{6,5},{7,6},{8,11},{9,8},{10,9... | collective-permute-start | bytes 393224 | tf_op jit(solution)/shard_map/ppermute | solution.py:56
  41.8 9.2 %collective-permute-start.4 = (f32[16,16,256]{2,0,1:T(8,128)S(1)}, f32[16,16,256]{2,0,1:T(8,128)S(1)}, u32[]{:S(2)}, u32[]{:S(2)}) collective-permute-start(f32[16,16,256]{2,0,1:T(8,128)S(1)} %pad_maximum_fusion.3), channel_id=1, source_target_pairs={{0,1},{1,2},{2,3},{3,0},{4,5},{5,6},{6,7},{7,4},{8,9},{9,10},{10,1... | collective-permute-start | bytes 786440 | tf_op jit(solution)/shard_map/ppermute | solution.py:67
  41.9 10.5 %collective-permute-start.5 = (f32[16,16,256]{2,0,1:T(8,128)S(1)}, f32[16,16,256]{2,0,1:T(8,128)}, u32[]{:S(2)}, u32[]{:S(2)}) collective-permute-start(f32[16,16,256]{2,0,1:T(8,128)S(1)} %pad_maximum_fusion.4), channel_id=1, source_target_pairs={{0,3},{1,0},{2,1},{3,2},{4,7},{5,4},{6,5},{7,6},{8,11},{9,8},{10,9... | collective-permute-start | bytes 786440 | tf_op jit(solution)/shard_map/ppermute | solution.py:68
  44.0 12.2 %collective-permute-start.7 = (f32[16,16,256]{2,0,1:T(8,128)S(1)}, f32[16,16,256]{2,0,1:T(8,128)}, u32[]{:S(2)}, u32[]{:S(2)}) collective-permute-start(f32[16,16,256]{2,0,1:T(8,128)S(1)} %pad_maximum_fusion.5), channel_id=1, source_target_pairs={{0,1},{1,2},{2,3},{3,0},{4,5},{5,6},{6,7},{7,4},{8,9},{9,10},{10,1... | collective-permute-start | bytes 786440 | tf_op jit(solution)/shard_map/ppermute | solution.py:67
  45.3 12.2 %collective-permute-start.9 = (f32[16,16,256]{2,0,1:T(8,128)S(1)}, f32[16,16,256]{2,0,1:T(8,128)}, u32[]{:S(2)}, u32[]{:S(2)}) collective-permute-start(f32[16,16,256]{2,0,1:T(8,128)S(1)} %pad_maximum_fusion.6), channel_id=1, source_target_pairs={{0,3},{1,0},{2,1},{3,2},{4,7},{5,4},{6,5},{7,6},{8,11},{9,8},{10,9... | collective-permute-start | bytes 786440 | tf_op jit(solution)/shard_map/ppermute | solution.py:68

commit v8 on v2

--- a/solution.py
+++ b/solution.py
@@ -76,8 +76,10 @@
     both = jnp.stack([weighted, inv_variance])
     bordered = bordered_rows(both, "sky", radius + reach)
 
-    psi = correlate_rows(bordered[0], toeplitz(psf_kernel, cols))
-    phi = correlate_rows(bordered[1], toeplitz(psf_kernel * psf_kernel, cols))
+    taps = toeplitz(jnp.concatenate([psf_kernel, psf_kernel * psf_kernel]), cols)
+    size = psf_kernel.shape[0]
+    psi = correlate_rows(bordered[0], taps[:size])
+    phi = correlate_rows(bordered[1], taps[size:])
     images = jnp.stack([psi, phi])
 
     first = lax.axis_index("sky") * rows - reach
@@ -92,7 +94,7 @@
         start = reach + offset_value * BR
         window = images[:, :, start : start + rows, :]
         partial = partial + jnp.einsum(
-            "tk,ctrw->ckrw", onehot, window, precision=lax.Precision.HIGHEST
+            "tk,ctrw->ckrw", onehot, window, precision=lax.Precision.HIGH
         )
 
     stacked = ring_reduce_scatter(partial, "visit")

time: 58.4 us -> 62.1 us (1.063)
  the two profiles are of different devices: /device:TPU:54 before, /device:TPU:136 now
where the time goes in v8:
time: 62.1 us; the launch traced here: 62 us
  waiting for transfers between devices  21.7 us (35%)
  matrix products  19.3 us (31%)
  starting transfers between devices  10.9 us (18%)
  local copies, waits for them, and re-layouts  5.84 us (9%)
  other arithmetic  4.04 us (7%)
    ppermute x1, waiting for transfers between devices, ring_reduce_scatter(): got_right = lax.ppermute(behind, axis, left)  10.9 us
    conv_general_dilated x2, matrix products, correlate_rows(): lax.conv_general_dilated(bordered, kernel, window_strides=(1,), padding='...  9.67 us
    ppermute x1, waiting for transfers between devices, ring_reduce_scatter(): from_right = lax.ppermute(far[..., half:], axis, left)  6.61 us
    dot_general x5, matrix products, shards(): jnp.einsum('tk,ctrw->ckrw', onehot, window, precision=lax.Precision.HIGH)  4.85 us
    dot_general x1, matrix products, toeplitz(): jnp.einsum('ab,bwv->awv', taps, onehot, precision=lax.Precision.HIGHEST)  4.79 us
    slice x1, local copies, waits for them, and re-layouts, shards(): psi = correlate_rows(bordered[0], taps[:size])  4.5 us
    ppermute x1, waiting for transfers between devices, ring_reduce_scatter(): got_left = lax.ppermute(ahead, axis, right)  4.22 us
    ppermute x1, starting transfers between devices, ring_reduce_scatter(): got_right = lax.ppermute(behind, axis, left)  3.69 us
  transfers between devices with their start and end apart: 6, of which 3 were waited for; matrix products, arithmetic and copies ran while one was open for 18% of the time, Pallas kernels for 0%

profile of v8, /device:TPU:136, one launch (start us, length us, event | category | flops | bytes accessed | tf_op | source)
XLA Modules:
  0.0 62.0 jit_solution(14976058178932537564)
XLA Ops:
  0.0 1.8 %fusion.13 = (f32[1,8,64,256]{3,1,2,0:T(8,128)S(1)}, f32[1,8,64,256]{3,1,2,0:T(8,128)S(1)}) fusion(f32[8,64,256]{2,1,0:T(8,128)} %param.4, f32[8,64,256]{2,1,0:T(8,128)} %param.5), kind=kLoop, calls=%fused_computation.19 | loop fusion | flops 131072 | bytes 2097152 | tf_op jit(solution)/shard_map/stack | solution.py:76
  1.8 0.1 pad_maximum_fusion.4
  1.9 1.9 %collective-permute-start.1 = (f32[2,8,21,256]{3,1,2,0:T(8,128)S(1)}, f32[2,8,21,256]{3,1,2,0:T(8,128)S(1)}, u32[]{:S(2)}, u32[]{:S(2)}) collective-permute-start(f32[2,8,21,256]{3,1,2,0:T(8,128)S(1)} %get-tuple-element.11), channel_id=1, source_target_pairs={{4,0},{8,4},{12,8},{16,12},{20,16},{24,20},{28,24},{32,28},{36,32}... | collective-permute-start | bytes 1032200 | tf_op jit(solution)/shard_map/ppermute | solution.py:18
  3.8 2.4 %collective-permute-start = (f32[2,8,21,256]{3,1,2,0:T(8,128)S(1)}, f32[2,8,21,256]{3,1,2,0:T(8,128)S(1)}, u32[]{:S(2)}, u32[]{:S(2)}) collective-permute-start(f32[2,8,21,256]{3,1,2,0:T(8,128)S(1)} %get-tuple-element.10), channel_id=1, source_target_pairs={{0,4},{4,8},{8,12},{12,16},{16,20},{20,24},{24,28},{28,32},{32,36}... | collective-permute-start | bytes 1032200 | tf_op jit(solution)/shard_map/ppermute | solution.py:15
  6.3 0.1 constant_dynamic-slice_fusion
  6.4 0.1 copy.20
  6.4 0.1 copy.10
  6.5 4.8 %fusion = f32[22,256,256]{2,0,1:T(8,128)} fusion(f32[11,11]{0,1:T(8,128)S(1)} %mul.26, f32[11,11]{0,1:T(8,128)S(1)} %copy.10), kind=kOutput, calls=%fused_computation.1 | convolution fusion | flops 192479472 | bytes 5768136 | tf_op jit(solution)/shard_map/ab,bwv->awv/dot_general | solution.py:29
  11.3 4.5 %fusion.44 = (f32[11,256,256]{2,0,1:T(8,128)S(1)}, f32[11,256,256]{2,0,1:T(8,128)S(1)}) fusion(f32[22,256,256]{2,0,1:T(8,128)} %fusion), kind=kLoop, calls=%fused_computation.62 | loop fusion | bytes 11534336 | tf_op jit(solution)/shard_map/slice | solution.py:81
  15.9 0.0 collective-permute-done.1
  15.9 0.1 pad_maximum_fusion
  16.0 4.8 %fusion.9 = f32[1,8,96,256]{3,1,2,0:T(8,128)S(1)} fusion(f32[11,256,256]{2,0,1:T(8,128)S(1)} %get-tuple-element.6, f32[2,8,106,256]{3,1,2,0:T(8,128)S(1)} %pad_maximum_fusion), kind=kOutput, calls=%fused_computation.11 | convolution fusion | flops 3321888768 | bytes 5849088 | tf_op jit(solution)/shard_map/conv_general_dilated | solution.py:33
  20.9 4.8 %fusion.6 = f32[1,8,96,256]{3,1,2,0:T(8,128)S(1)} fusion(f32[11,256,256]{2,0,1:T(8,128)S(1)} %get-tuple-element.5, f32[2,8,106,256]{3,1,2,0:T(8,128)S(1)} %pad_maximum_fusion), kind=kOutput, calls=%fused_computation.10 | convolution fusion | flops 3321888768 | bytes 5849088 | tf_op jit(solution)/shard_map/conv_general_dilated | solution.py:33
  25.7 0.8 %fusion.19 = f32[2,64,256,16]{2,3,1,0:T(8,128)S(1)} fusion(s32[8,16]{1,0:T(8,128)S(1)} %copy.20, f32[1,8,96,256]{3,1,2,0:T(8,128)S(1)} %fusion.9, f32[1,8,96,256]{3,1,2,0:T(8,128)S(1)} %fusion.6, pred[96]{0:T(512)(128)(4,1)S(1)} %compare_and_fusion), kind=kOutput, calls=%fused_computation.35 | convolution fusion | flops 25952384 | bytes 3670624 | tf_op jit(solution)/shard_map/tk,ctrw->ckrw/dot_general | solution.py:96
  26.5 0.8 %fusion.21 = f32[2,64,256,16]{2,3,1,0:T(8,128)S(1)} fusion(s32[8,16]{1,0:T(8,128)S(1)} %copy.20, f32[1,8,96,256]{3,1,2,0:T(8,128)S(1)} %fusion.9, f32[1,8,96,256]{3,1,2,0:T(8,128)S(1)} %fusion.6, pred[96]{0:T(512)(128)(4,1)S(1)} %compare_and_fusion), kind=kOutput, calls=%fused_computation.37 | convolution fusion | flops 25952384 | bytes 3670624 | tf_op jit(solution)/shard_map/tk,ctrw->ckrw/dot_general | solution.py:96
  27.3 1.1 %fusion.25 = f32[2,64,256,16]{2,3,1,0:T(8,128)S(1)} fusion(s32[8,16]{1,0:T(8,128)S(1)} %copy.20, f32[1,8,96,256]{3,1,2,0:T(8,128)S(1)} %fusion.9, f32[1,8,96,256]{3,1,2,0:T(8,128)S(1)} %fusion.6, pred[96]{0:T(512)(128)(4,1)S(1)} %compare_and_fusion), kind=kOutput, calls=%fused_computation.41 | convolution fusion | flops 25952384 | bytes 3670624 | tf_op jit(solution)/shard_map/tk,ctrw->ckrw/dot_general | solution.py:96
  28.4 0.8 %fusion.23 = f32[2,64,256,16]{2,3,1,0:T(8,128)S(1)} fusion(s32[8,16]{1,0:T(8,128)S(1)} %copy.20, f32[1,8,96,256]{3,1,2,0:T(8,128)S(1)} %fusion.9, f32[1,8,96,256]{3,1,2,0:T(8,128)S(1)} %fusion.6, pred[96]{0:T(512)(128)(4,1)S(1)} %compare_and_fusion), kind=kOutput, calls=%fused_computation.39 | convolution fusion | flops 25952384 | bytes 3670624 | tf_op jit(solution)/shard_map/tk,ctrw->ckrw/dot_general | solution.py:96
  29.2 1.4 %add_add_fusion = f32[2,64,256,16]{2,3,1,0:T(8,128)S(1)} fusion(f32[2,64,256,16]{2,3,1,0:T(8,128)S(1)} %fusion.19, f32[2,64,256,16]{2,3,1,0:T(8,128)S(1)} %fusion.21, f32[2,64,256,16]{2,3,1,0:T(8,128)S(1)} %fusion.25, f32[2,64,256,16]{2,3,1,0:T(8,128)S(1)} %fusion.23, s32[8,16]{1,0:T(8,128)S(1)} %copy.20, f32[1,8,96,256]{3,1,2,0:T(8,128)S(1)} %fusion.9, ...), kind=kOutput, calls=%fused_computation.6 | convolution fusion | flops 28049536 | bytes 12059232 | tf_op jit(solution)/shard_map/tk,ctrw->ckrw/dot_general | solution.py:96
  30.6 0.2 dynamic-slice_bitcast_fusion.2
  30.8 2.8 %collective-permute-start.4 = (f32[2,16,16,128]{3,1,2,0:T(8,128)S(1)}, f32[2,16,16,128]{3,1,2,0:T(8,128)S(1)}, u32[]{:S(2)}, u32[]{:S(2)}) collective-permute-start(f32[2,16,16,128]{3,1,2,0:T(8,128)S(1)} %get-tuple-element.15), channel_id=1, source_target_pairs={{0,3},{1,0},{2,1},{3,2},{4,7},{5,4},{6,5},{7,6},{8,11},{9,8},{10,9... | collective-permute-start | bytes 786440 | tf_op jit(solution)/shard_map/ppermute | solution.py:59
  33.7 0.0 collective-permute-start.2
  33.7 6.6 %collective-permute-done.4 = f32[2,16,16,128]{3,1,2,0:T(8,128)S(1)} collective-permute-done((f32[2,16,16,128]{3,1,2,0:T(8,128)S(1)}, f32[2,16,16,128]{3,1,2,0:T(8,128)S(1)}, u32[]{:S(2)}, u32[]{:S(2)}) %collective-permute-start.4) | collective-permute-done | bytes 262176 | tf_op jit(solution)/shard_map/ppermute | solution.py:59
  40.3 0.1 fusion.46
  40.4 0.8 %pad_maximum_fusion.2 = f32[2,16,16,256]{3,1,2,0:T(8,128)} fusion(f32[2,16,16,128]{3,1,2,0:T(8,128)S(1)} %get-tuple-element.17, f32[2,16,16,128]{3,1,2,0:T(8,128)S(1)} %get-tuple-element.16), kind=kLoop, calls=%fused_computation.15 | loop fusion | flops 131072 | bytes 1048576 | tf_op jit(solution)/shard_map/concatenate | solution.py:63
  41.2 3.7 %collective-permute-start.5 = (f32[2,16,16,256]{3,1,2,0:T(8,128)}, f32[2,16,16,256]{3,1,2,0:T(8,128)S(1)}, u32[]{:S(2)}, u32[]{:S(2)}) collective-permute-start(f32[2,16,16,256]{3,1,2,0:T(8,128)} %pad_maximum_fusion.2), channel_id=1, source_target_pairs={{0,3},{1,0},{2,1},{3,2},{4,7},{5,4},{6,5},{7,6},{8,11},{9,8},{10,9... | collective-permute-start | bytes 1572872 | tf_op jit(solution)/shard_map/ppermute | solution.py:65
  44.9 0.0 collective-permute-done.2
  44.9 0.1 slice_add_fusion.1
  45.0 0.8 %pad_maximum_fusion.1 = f32[2,16,16,256]{3,1,2,0:T(8,128)} fusion(f32[2,16,16,128]{3,1,2,0:T(8,128)S(1)} %get-tuple-element.13, f32[2,16,16,128]{3,1,2,0:T(8,128)S(1)} %get-tuple-element.12), kind=kLoop, calls=%fused_computation.14 | loop fusion | flops 131072 | bytes 1048576 | tf_op jit(solution)/shard_map/concatenate | solution.py:61
  45.8 10.9 %collective-permute-done.5 = f32[2,16,16,256]{3,1,2,0:T(8,128)S(1)} collective-permute-done((f32[2,16,16,256]{3,1,2,0:T(8,128)}, f32[2,16,16,256]{3,1,2,0:T(8,128)S(1)}, u32[]{:S(2)}, u32[]{:S(2)}) %collective-permute-start.5) | collective-permute-done | bytes 524320 | tf_op jit(solution)/shard_map/ppermute | solution.py:65
  56.7 4.2 %collective-permute-done.3 = f32[2,16,16,256]{3,1,2,0:T(8,128)S(1)} collective-permute-done((f32[2,16,16,256]{3,1,2,0:T(8,128)}, f32[2,16,16,256]{3,1,2,0:T(8,128)S(1)}, u32[]{:S(2)}, u32[]{:S(2)}) %collective-permute-start.3) | collective-permute-done | bytes 524320 | tf_op jit(solution)/shard_map/ppermute | solution.py:64
  60.9 0.1 fusion.12
  61.1 0.9 %copy.14 = f32[16,16,256]{2,1,0:T(8,128)} copy(f32[16,16,256]{2,0,1:T(8,128)S(1)} %fusion.15) | data formatting | bytes 524288 | tf_op jit(solution)/shard_map/div | solution.py:101
  (10 shorter events, 0.1 us)
Async XLA Ops:
  0.0 6.3 %copy-start = (s32[32,16]{0,1:T(8,128)S(1)}, s32[32,16]{0,1:T(8,128)}, u32[]{:S(2)}) copy-start(s32[32,16]{0,1:T(8,128)} %param.7) | copy-start | bytes 6148
  0.0 6.4 %copy-start.1 = (f32[11,11]{1,0:T(8,128)S(1)}, f32[11,11]{1,0:T(8,128)}, u32[]{:S(2)}) copy-start(f32[11,11]{1,0:T(8,128)} %param.6) | copy-start | bytes 1456
  1.9 14.0 %collective-permute-start.1 = (f32[2,8,21,256]{3,1,2,0:T(8,128)S(1)}, f32[2,8,21,256]{3,1,2,0:T(8,128)S(1)}, u32[]{:S(2)}, u32[]{:S(2)}) collective-permute-start(f32[2,8,21,256]{3,1,2,0:T(8,128)S(1)} %get-tuple-element.11), channel_id=1, source_target_pairs={{4,0},{8,4},{12,8},{16,12},{20,16},{24,20},{28,24},{32,28},{36,32}... | collective-permute-start | bytes 1032200 | tf_op jit(solution)/shard_map/ppermute | solution.py:18
  3.8 12.0 %collective-permute-start = (f32[2,8,21,256]{3,1,2,0:T(8,128)S(1)}, f32[2,8,21,256]{3,1,2,0:T(8,128)S(1)}, u32[]{:S(2)}, u32[]{:S(2)}) collective-permute-start(f32[2,8,21,256]{3,1,2,0:T(8,128)S(1)} %get-tuple-element.10), channel_id=1, source_target_pairs={{0,4},{4,8},{8,12},{12,16},{16,20},{20,24},{24,28},{28,32},{32,36}... | collective-permute-start | bytes 1032200 | tf_op jit(solution)/shard_map/ppermute | solution.py:15
  30.8 9.5 %collective-permute-start.4 = (f32[2,16,16,128]{3,1,2,0:T(8,128)S(1)}, f32[2,16,16,128]{3,1,2,0:T(8,128)S(1)}, u32[]{:S(2)}, u32[]{:S(2)}) collective-permute-start(f32[2,16,16,128]{3,1,2,0:T(8,128)S(1)} %get-tuple-element.15), channel_id=1, source_target_pairs={{0,3},{1,0},{2,1},{3,2},{4,7},{5,4},{6,5},{7,6},{8,11},{9,8},{10,9... | collective-permute-start | bytes 786440 | tf_op jit(solution)/shard_map/ppermute | solution.py:59
  33.7 11.2 %collective-permute-start.2 = (f32[2,16,16,128]{3,1,2,0:T(8,128)S(1)}, f32[2,16,16,128]{3,1,2,0:T(8,128)S(1)}, u32[]{:S(2)}, u32[]{:S(2)}) collective-permute-start(f32[2,16,16,128]{3,1,2,0:T(8,128)S(1)} %get-tuple-element.14), channel_id=1, source_target_pairs={{0,1},{1,2},{2,3},{3,0},{4,5},{5,6},{6,7},{7,4},{8,9},{9,10},{10,1... | collective-permute-start | bytes 786440 | tf_op jit(solution)/shard_map/ppermute | solution.py:58
  41.2 15.5 %collective-permute-start.5 = (f32[2,16,16,256]{3,1,2,0:T(8,128)}, f32[2,16,16,256]{3,1,2,0:T(8,128)S(1)}, u32[]{:S(2)}, u32[]{:S(2)}) collective-permute-start(f32[2,16,16,256]{3,1,2,0:T(8,128)} %pad_maximum_fusion.2), channel_id=1, source_target_pairs={{0,3},{1,0},{2,1},{3,2},{4,7},{5,4},{6,5},{7,6},{8,11},{9,8},{10,9... | collective-permute-start | bytes 1572872 | tf_op jit(solution)/shard_map/ppermute | solution.py:65
  45.8 15.1 %collective-permute-start.3 = (f32[2,16,16,256]{3,1,2,0:T(8,128)}, f32[2,16,16,256]{3,1,2,0:T(8,128)S(1)}, u32[]{:S(2)}, u32[]{:S(2)}) collective-permute-start(f32[2,16,16,256]{3,1,2,0:T(8,128)} %pad_maximum_fusion.1), channel_id=1, source_target_pairs={{0,1},{1,2},{2,3},{3,0},{4,5},{5,6},{6,7},{7,4},{8,9},{9,10},{10,1... | collective-permute-start | bytes 1572872 | tf_op jit(solution)/shard_map/ppermute | solution.py:64

commit v9 on v2

--- a/solution.py
+++ b/solution.py
@@ -41,6 +41,14 @@
     )
 
 
+def split_permute(value, axis, pairs):
+    half = value.shape[1] // 2
+    return jnp.concatenate(
+        [lax.ppermute(value[:, :half], axis, pairs), lax.ppermute(value[:, half:], axis, pairs)],
+        axis=1,
+    )
+
+
 def ring_reduce_scatter(partial, axis):
     count = lax.axis_size(axis)
     if count != 4:
@@ -55,14 +63,14 @@
         return lax.dynamic_slice_in_dim(partial, ((me + step) % count) * rows, rows, axis=2)
 
     far = block(2)
-    from_left = lax.ppermute(far[..., :half], axis, right)
-    from_right = lax.ppermute(far[..., half:], axis, left)
+    from_left = split_permute(far[..., :half], axis, right)
+    from_right = split_permute(far[..., half:], axis, left)
     ahead = block(1)
     ahead = jnp.concatenate([ahead[..., :half] + from_left, ahead[..., half:]], axis=-1)
     behind = block(count - 1)
     behind = jnp.concatenate([behind[..., :half], behind[..., half:] + from_right], axis=-1)
-    got_left = lax.ppermute(ahead, axis, right)
-    got_right = lax.ppermute(behind, axis, left)
+    got_left = split_permute(ahead, axis, right)
+    got_right = split_permute(behind, axis, left)
     return block(0) + got_left + got_right
 
 

time: 58.4 us -> 60.6 us (1.038)
  the two profiles are of different devices: /device:TPU:54 before, /device:TPU:113 now
where the time goes in v9:
time: 60.6 us; the launch traced here: 60.4 us
  matrix products  21.2 us (35%)
  waiting for transfers between devices  18.7 us (31%)
  starting transfers between devices  15.2 us (25%)
  other arithmetic  3.86 us (6%)
  local copies, waits for them, and re-layouts  1.19 us (2%)
    ppermute x4, waiting for transfers between devices, split_permute(): lax.ppermute(value[:, half:], axis, pairs)  11.5 us
    conv_general_dilated x2, matrix products, correlate_rows(): lax.conv_general_dilated(bordered, kernel, window_strides=(1,), padding='...  9.81 us
    ppermute x4, starting transfers between devices, split_permute(): lax.ppermute(value[:, :half], axis, pairs)  7.31 us
    dot_general x5, matrix products, shards(): jnp.einsum('tk,ctrw->ckrw', onehot, window, precision=lax.Precision.HIGHEST)  5.88 us
    dot_general x2, matrix products, toeplitz(): jnp.einsum('ab,bwv->awv', taps, onehot, precision=lax.Precision.HIGHEST)  5.53 us
    ppermute x1, starting transfers between devices, bordered_rows(): lax.ppermute(lax.slice_in_dim(block, block.shape[dim] - width, None, axis...  5.32 us
    ppermute x4, waiting for transfers between devices, split_permute(): lax.ppermute(value[:, :half], axis, pairs)  5.15 us
    ppermute x1, waiting for transfers between devices, bordered_rows(): lax.ppermute(lax.slice_in_dim(block, 0, width, axis=dim), axis, backward)  2.13 us
  transfers between devices with their start and end apart: 10, of which 7 were waited for; matrix products, arithmetic and copies ran while one was open for 12% of the time, Pallas kernels for 0%

profile of v9, /device:TPU:113, one launch (start us, length us, event | category | flops | bytes accessed | tf_op | source)
XLA Modules:
  0.0 60.4 jit_solution(14019301920274805802)
XLA Ops:
  0.0 1.8 %fusion.15 = (f32[1,8,64,256]{3,1,2,0:T(8,128)S(1)}, f32[1,8,64,256]{3,1,2,0:T(8,128)S(1)}) fusion(f32[8,64,256]{2,1,0:T(8,128)} %param.4, f32[8,64,256]{2,1,0:T(8,128)} %param.5), kind=kLoop, calls=%fused_computation.23 | loop fusion | flops 131072 | bytes 2097152 | tf_op jit(solution)/shard_map/stack | solution.py:84
  1.9 5.3 %collective-permute-start = (f32[2,8,21,256]{3,1,2,0:T(8,128)S(1)}, f32[2,8,21,256]{3,1,2,0:T(8,128)S(1)}, u32[]{:S(2)}, u32[]{:S(2)}) collective-permute-start(f32[2,8,21,256]{3,1,2,0:T(8,128)S(1)} %get-tuple-element.8), channel_id=1, source_target_pairs={{0,4},{4,8},{8,12},{12,16},{16,20},{20,24},{24,28},{28,32},{32,36}... | collective-permute-start | bytes 1032200 | tf_op jit(solution)/shard_map/ppermute | solution.py:15
  7.2 1.9 %collective-permute-start.1 = (f32[2,8,21,256]{3,1,2,0:T(8,128)S(1)}, f32[2,8,21,256]{3,1,2,0:T(8,128)S(1)}, u32[]{:S(2)}, u32[]{:S(2)}) collective-permute-start(f32[2,8,21,256]{3,1,2,0:T(8,128)S(1)} %get-tuple-element.9), channel_id=1, source_target_pairs={{4,0},{8,4},{12,8},{16,12},{20,16},{24,20},{28,24},{32,28},{36,32}... | collective-permute-start | bytes 1032200 | tf_op jit(solution)/shard_map/ppermute | solution.py:18
  9.2 4.1 %fusion.1 = f32[256,256,11]{1,2,0:T(8,128)} fusion(f32[11,11]{1,0:T(8,128)S(1)} %copy-done.2), kind=kOutput, calls=%fused_computation.2 | convolution fusion | flops 97320960 | bytes 2884068 | tf_op jit(solution)/shard_map/ab,bwv->awv/dot_general | solution.py:29
  13.2 0.1 constant_dynamic-slice_fusion
  13.3 0.1 copy.17
  13.4 1.5 %fusion = f32[11,256,256]{2,0,1:T(8,128)S(1)} fusion(f32[11,11]{1,0:T(8,128)S(1)} %copy-done.2), kind=kOutput, calls=%fused_computation.1 | convolution fusion | flops 97321080 | bytes 2884068 | tf_op jit(solution)/shard_map/ab,bwv->awv/dot_general | solution.py:29
  14.9 2.1 %collective-permute-done.1 = f32[2,8,21,256]{3,1,2,0:T(8,128)S(1)} collective-permute-done((f32[2,8,21,256]{3,1,2,0:T(8,128)S(1)}, f32[2,8,21,256]{3,1,2,0:T(8,128)S(1)}, u32[]{:S(2)}, u32[]{:S(2)}) %collective-permute-start.1) | collective-permute-done | bytes 344096 | tf_op jit(solution)/shard_map/ppermute | solution.py:18
  17.0 0.1 pad_maximum_fusion
  17.2 4.8 %fusion.8 = f32[1,8,96,256]{3,1,2,0:T(8,128)S(1)} fusion(f32[256,256,11]{1,2,0:T(8,128)S(1)} %copy-done.1, f32[2,8,106,256]{3,1,2,0:T(8,128)S(1)} %pad_maximum_fusion), kind=kOutput, calls=%fused_computation.12 | convolution fusion | flops 3321888768 | bytes 5849088 | tf_op jit(solution)/shard_map/conv_general_dilated | solution.py:33
  22.0 5.0 %fusion.11 = f32[1,8,96,256]{3,1,2,0:T(8,128)S(1)} fusion(f32[11,256,256]{2,0,1:T(8,128)S(1)} %fusion, f32[2,8,106,256]{3,1,2,0:T(8,128)S(1)} %pad_maximum_fusion), kind=kOutput, calls=%fused_computation.13 | convolution fusion | flops 3321888768 | bytes 5849088 | tf_op jit(solution)/shard_map/conv_general_dilated | solution.py:33
  27.0 1.1 %fusion.28 = f32[2,64,256,16]{2,3,1,0:T(8,128)S(1)} fusion(s32[8,16]{1,0:T(8,128)S(1)} %copy.17, f32[1,8,96,256]{3,1,2,0:T(8,128)S(1)} %fusion.11, f32[1,8,96,256]{3,1,2,0:T(8,128)S(1)} %fusion.8, pred[96]{0:T(512)(128)(4,1)S(1)} %compare_and_fusion), kind=kOutput, calls=%fused_computation.47 | convolution fusion | flops 51118208 | bytes 3670624 | tf_op jit(solution)/shard_map/tk,ctrw->ckrw/dot_general | solution.py:102
  28.1 1.1 %fusion.30 = f32[2,64,256,16]{2,3,1,0:T(8,128)S(1)} fusion(s32[8,16]{1,0:T(8,128)S(1)} %copy.17, f32[1,8,96,256]{3,1,2,0:T(8,128)S(1)} %fusion.11, f32[1,8,96,256]{3,1,2,0:T(8,128)S(1)} %fusion.8, pred[96]{0:T(512)(128)(4,1)S(1)} %compare_and_fusion), kind=kOutput, calls=%fused_computation.49 | convolution fusion | flops 51118208 | bytes 3670624 | tf_op jit(solution)/shard_map/tk,ctrw->ckrw/dot_general | solution.py:102
  29.2 1.1 %fusion.26 = f32[2,64,256,16]{2,3,1,0:T(8,128)S(1)} fusion(s32[8,16]{1,0:T(8,128)S(1)} %copy.17, f32[1,8,96,256]{3,1,2,0:T(8,128)S(1)} %fusion.11, f32[1,8,96,256]{3,1,2,0:T(8,128)S(1)} %fusion.8, pred[96]{0:T(512)(128)(4,1)S(1)} %compare_and_fusion), kind=kOutput, calls=%fused_computation.45 | convolution fusion | flops 51118208 | bytes 3670624 | tf_op jit(solution)/shard_map/tk,ctrw->ckrw/dot_general | solution.py:102
  30.2 1.1 %fusion.24 = f32[2,64,256,16]{2,3,1,0:T(8,128)S(1)} fusion(s32[8,16]{1,0:T(8,128)S(1)} %copy.17, f32[1,8,96,256]{3,1,2,0:T(8,128)S(1)} %fusion.11, f32[1,8,96,256]{3,1,2,0:T(8,128)S(1)} %fusion.8, pred[96]{0:T(512)(128)(4,1)S(1)} %compare_and_fusion), kind=kOutput, calls=%fused_computation.43 | convolution fusion | flops 51118208 | bytes 3670624 | tf_op jit(solution)/shard_map/tk,ctrw->ckrw/dot_general | solution.py:102
  31.3 1.6 %add_add_fusion = f32[2,64,256,16]{2,3,1,0:T(8,128)S(1)} fusion(f32[2,64,256,16]{2,3,1,0:T(8,128)S(1)} %fusion.24, f32[2,64,256,16]{2,3,1,0:T(8,128)S(1)} %fusion.26, f32[2,64,256,16]{2,3,1,0:T(8,128)S(1)} %fusion.30, f32[2,64,256,16]{2,3,1,0:T(8,128)S(1)} %fusion.28, s32[8,16]{1,0:T(8,128)S(1)} %copy.17, f32[1,8,96,256]{3,1,2,0:T(8,128)S(1)} %fusion.11, ...), kind=kOutput, calls=%fused_computation.7 | convolution fusion | flops 53215360 | bytes 12059232 | tf_op jit(solution)/shard_map/tk,ctrw->ckrw/dot_general | solution.py:102
  32.9 0.1 dynamic-slice_bitcast_fusion
  33.1 2.6 %collective-permute-start.6 = (f32[2,8,16,128]{3,1,2,0:T(8,128)S(1)}, f32[2,8,16,128]{3,1,2,0:T(8,128)S(1)}, u32[]{:S(2)}, u32[]{:S(2)}) collective-permute-start(f32[2,8,16,128]{3,1,2,0:T(8,128)S(1)} %get-tuple-element.14), channel_id=1, source_target_pairs={{0,3},{1,0},{2,1},{3,2},{4,7},{5,4},{6,5},{7,6},{8,11},{9,8},{10,9... | collective-permute-start | bytes 393224 | tf_op jit(solution)/shard_map/ppermute | solution.py:47
  35.7 0.5 collective-permute-start.7
  36.2 0.9 %collective-permute-start.2 = (f32[2,8,16,128]{3,1,2,0:T(8,128)S(1)}, f32[2,8,16,128]{3,1,2,0:T(8,128)S(1)}, u32[]{:S(2)}, u32[]{:S(2)}) collective-permute-start(f32[2,8,16,128]{3,1,2,0:T(8,128)S(1)} %get-tuple-element.17), channel_id=1, source_target_pairs={{0,1},{1,2},{2,3},{3,0},{4,5},{5,6},{6,7},{7,4},{8,9},{9,10},{10,1... | collective-permute-start | bytes 393224 | tf_op jit(solution)/shard_map/ppermute | solution.py:47
  37.2 1.1 %collective-permute-done.6 = f32[2,8,16,128]{3,1,2,0:T(8,128)S(1)} collective-permute-done((f32[2,8,16,128]{3,1,2,0:T(8,128)S(1)}, f32[2,8,16,128]{3,1,2,0:T(8,128)S(1)}, u32[]{:S(2)}, u32[]{:S(2)}) %collective-permute-start.6) | collective-permute-done | bytes 131104 | tf_op jit(solution)/shard_map/ppermute | solution.py:47
  38.3 1.8 %collective-permute-done.7 = f32[2,8,16,128]{3,1,2,0:T(8,128)S(1)} collective-permute-done((f32[2,8,16,128]{3,1,2,0:T(8,128)S(1)}, f32[2,8,16,128]{3,1,2,0:T(8,128)S(1)}, u32[]{:S(2)}, u32[]{:S(2)}) %collective-permute-start.7) | collective-permute-done | bytes 131104 | tf_op jit(solution)/shard_map/ppermute | solution.py:47
  40.2 0.7 %fusion.16 = (f32[2,8,16,256]{3,1,2,0:T(8,128)}, f32[2,8,16,256]{3,1,2,0:T(8,128)S(1)}) fusion(f32[2,16,16,128]{3,1,2,0:T(8,128)S(1)} %get-tuple-element.12, f32[2,16,16,128]{3,1,2,0:T(8,128)S(1)} %get-tuple-element.13), kind=kLoop, calls=%fused_computation.30 | loop fusion | flops 131072 | bytes 1048576 | tf_op jit(solution)/shard_map/concatenate | solution.py:71
  40.9 2.7 %collective-permute-start.8 = (f32[2,8,16,256]{3,1,2,0:T(8,128)}, f32[2,8,16,256]{3,1,2,0:T(8,128)S(1)}, u32[]{:S(2)}, u32[]{:S(2)}) collective-permute-start(f32[2,8,16,256]{3,1,2,0:T(8,128)} %get-tuple-element.10), channel_id=1, source_target_pairs={{0,3},{1,0},{2,1},{3,2},{4,7},{5,4},{6,5},{7,6},{8,11},{9,8},{10,9... | collective-permute-start | bytes 786440 | tf_op jit(solution)/shard_map/ppermute | solution.py:47
  43.6 0.3 collective-permute-done.3
  44.0 0.8 %fusion.17 = (f32[2,8,16,256]{3,1,2,0:T(8,128)}, f32[2,8,16,256]{3,1,2,0:T(8,128)}) fusion(f32[2,16,16,128]{3,1,2,0:T(8,128)S(1)} %get-tuple-element.20, f32[2,16,16,128]{3,1,2,0:T(8,128)S(1)} %get-tuple-element.21), kind=kLoop, calls=%fused_computation.31 | loop fusion | flops 131072 | bytes 1048576 | tf_op jit(solution)/shard_map/concatenate | solution.py:69
  44.8 1.2 %collective-permute-start.4 = (f32[2,8,16,256]{3,1,2,0:T(8,128)}, f32[2,8,16,256]{3,1,2,0:T(8,128)S(1)}, u32[]{:S(2)}, u32[]{:S(2)}) collective-permute-start(f32[2,8,16,256]{3,1,2,0:T(8,128)} %get-tuple-element.18), channel_id=1, source_target_pairs={{0,1},{1,2},{2,3},{3,0},{4,5},{5,6},{6,7},{7,4},{8,9},{9,10},{10,1... | collective-permute-start | bytes 786440 | tf_op jit(solution)/shard_map/ppermute | solution.py:47
  46.0 4.1 %collective-permute-done.8 = f32[2,8,16,256]{3,1,2,0:T(8,128)S(1)} collective-permute-done((f32[2,8,16,256]{3,1,2,0:T(8,128)}, f32[2,8,16,256]{3,1,2,0:T(8,128)S(1)}, u32[]{:S(2)}, u32[]{:S(2)}) %collective-permute-start.8) | collective-permute-done | bytes 262176 | tf_op jit(solution)/shard_map/ppermute | solution.py:47
  50.0 4.7 %collective-permute-done.9 = f32[2,8,16,256]{3,1,2,0:T(8,128)S(1)} collective-permute-done((f32[2,8,16,256]{3,1,2,0:T(8,128)S(1)}, f32[2,8,16,256]{3,1,2,0:T(8,128)S(1)}, u32[]{:S(2)}, u32[]{:S(2)}) %collective-permute-start.9) | collective-permute-done | bytes 262176 | tf_op jit(solution)/shard_map/ppermute | solution.py:47
  54.8 4.6 %collective-permute-done.5 = f32[2,8,16,256]{3,1,2,0:T(8,128)S(1)} collective-permute-done((f32[2,8,16,256]{3,1,2,0:T(8,128)}, f32[2,8,16,256]{3,1,2,0:T(8,128)S(1)}, u32[]{:S(2)}, u32[]{:S(2)}) %collective-permute-start.5) | collective-permute-done | bytes 262176 | tf_op jit(solution)/shard_map/ppermute | solution.py:47
  59.4 0.1 fusion.14
  59.5 0.9 %copy.11 = f32[16,16,256]{2,1,0:T(8,128)} copy(f32[16,16,256]{2,0,1:T(8,128)S(1)} %fusion.19) | data formatting | bytes 524288 | tf_op jit(solution)/shard_map/div | solution.py:107
  (18 shorter events, 0.4 us)
Async XLA Ops:
  0.0 13.2 %copy-start = (s32[32,16]{0,1:T(8,128)S(1)}, s32[32,16]{0,1:T(8,128)}, u32[]{:S(2)}) copy-start(s32[32,16]{0,1:T(8,128)} %param.7) | copy-start | bytes 6148
  0.0 9.2 %copy-start.2 = (f32[11,11]{1,0:T(8,128)S(1)}, f32[11,11]{1,0:T(8,128)}, u32[]{:S(2)}) copy-start(f32[11,11]{1,0:T(8,128)} %param.6) | copy-start | bytes 1456
  1.9 13.0 %collective-permute-start = (f32[2,8,21,256]{3,1,2,0:T(8,128)S(1)}, f32[2,8,21,256]{3,1,2,0:T(8,128)S(1)}, u32[]{:S(2)}, u32[]{:S(2)}) collective-permute-start(f32[2,8,21,256]{3,1,2,0:T(8,128)S(1)} %get-tuple-element.8), channel_id=1, source_target_pairs={{0,4},{4,8},{8,12},{12,16},{16,20},{20,24},{24,28},{28,32},{32,36}... | collective-permute-start | bytes 1032200 | tf_op jit(solution)/shard_map/ppermute | solution.py:15
  7.2 9.8 %collective-permute-start.1 = (f32[2,8,21,256]{3,1,2,0:T(8,128)S(1)}, f32[2,8,21,256]{3,1,2,0:T(8,128)S(1)}, u32[]{:S(2)}, u32[]{:S(2)}) collective-permute-start(f32[2,8,21,256]{3,1,2,0:T(8,128)S(1)} %get-tuple-element.9), channel_id=1, source_target_pairs={{4,0},{8,4},{12,8},{16,12},{20,16},{24,20},{28,24},{32,28},{36,32}... | collective-permute-start | bytes 1032200 | tf_op jit(solution)/shard_map/ppermute | solution.py:18
  13.4 3.8 %copy-start.1 = (f32[256,256,11]{1,2,0:T(8,128)S(1)}, f32[256,256,11]{1,2,0:T(8,128)}, u32[]{:S(2)}) copy-start(f32[256,256,11]{1,2,0:T(8,128)} %fusion.1) | copy-start | bytes 8650756
  33.1 5.2 %collective-permute-start.6 = (f32[2,8,16,128]{3,1,2,0:T(8,128)S(1)}, f32[2,8,16,128]{3,1,2,0:T(8,128)S(1)}, u32[]{:S(2)}, u32[]{:S(2)}) collective-permute-start(f32[2,8,16,128]{3,1,2,0:T(8,128)S(1)} %get-tuple-element.14), channel_id=1, source_target_pairs={{0,3},{1,0},{2,1},{3,2},{4,7},{5,4},{6,5},{7,6},{8,11},{9,8},{10,9... | collective-permute-start | bytes 393224 | tf_op jit(solution)/shard_map/ppermute | solution.py:47
  35.7 4.4 %collective-permute-start.7 = (f32[2,8,16,128]{3,1,2,0:T(8,128)S(1)}, f32[2,8,16,128]{3,1,2,0:T(8,128)S(1)}, u32[]{:S(2)}, u32[]{:S(2)}) collective-permute-start(f32[2,8,16,128]{3,1,2,0:T(8,128)S(1)} %get-tuple-element.15), channel_id=1, source_target_pairs={{0,3},{1,0},{2,1},{3,2},{4,7},{5,4},{6,5},{7,6},{8,11},{9,8},{10,9... | collective-permute-start | bytes 393224 | tf_op jit(solution)/shard_map/ppermute | solution.py:47
  36.2 7.4 %collective-permute-start.2 = (f32[2,8,16,128]{3,1,2,0:T(8,128)S(1)}, f32[2,8,16,128]{3,1,2,0:T(8,128)S(1)}, u32[]{:S(2)}, u32[]{:S(2)}) collective-permute-start(f32[2,8,16,128]{3,1,2,0:T(8,128)S(1)} %get-tuple-element.17), channel_id=1, source_target_pairs={{0,1},{1,2},{2,3},{3,0},{4,5},{5,6},{6,7},{7,4},{8,9},{9,10},{10,1... | collective-permute-start | bytes 393224 | tf_op jit(solution)/shard_map/ppermute | solution.py:47
  37.1 6.8 %collective-permute-start.3 = (f32[2,8,16,128]{3,1,2,0:T(8,128)S(1)}, f32[2,8,16,128]{3,1,2,0:T(8,128)S(1)}, u32[]{:S(2)}, u32[]{:S(2)}) collective-permute-start(f32[2,8,16,128]{3,1,2,0:T(8,128)S(1)} %get-tuple-element.16), channel_id=1, source_target_pairs={{0,1},{1,2},{2,3},{3,0},{4,5},{5,6},{6,7},{7,4},{8,9},{9,10},{10,1... | collective-permute-start | bytes 393224 | tf_op jit(solution)/shard_map/ppermute | solution.py:47
  40.9 9.1 %collective-permute-start.8 = (f32[2,8,16,256]{3,1,2,0:T(8,128)}, f32[2,8,16,256]{3,1,2,0:T(8,128)S(1)}, u32[]{:S(2)}, u32[]{:S(2)}) collective-permute-start(f32[2,8,16,256]{3,1,2,0:T(8,128)} %get-tuple-element.10), channel_id=1, source_target_pairs={{0,3},{1,0},{2,1},{3,2},{4,7},{5,4},{6,5},{7,6},{8,11},{9,8},{10,9... | collective-permute-start | bytes 786440 | tf_op jit(solution)/shard_map/ppermute | solution.py:47
  43.6 11.2 %collective-permute-start.9 = (f32[2,8,16,256]{3,1,2,0:T(8,128)S(1)}, f32[2,8,16,256]{3,1,2,0:T(8,128)S(1)}, u32[]{:S(2)}, u32[]{:S(2)}) collective-permute-start(f32[2,8,16,256]{3,1,2,0:T(8,128)S(1)} %get-tuple-element.11), channel_id=1, source_target_pairs={{0,3},{1,0},{2,1},{3,2},{4,7},{5,4},{6,5},{7,6},{8,11},{9,8},{10,9... | collective-permute-start | bytes 786440 | tf_op jit(solution)/shard_map/ppermute | solution.py:47
  44.8 10.0 %collective-permute-start.4 = (f32[2,8,16,256]{3,1,2,0:T(8,128)}, f32[2,8,16,256]{3,1,2,0:T(8,128)S(1)}, u32[]{:S(2)}, u32[]{:S(2)}) collective-permute-start(f32[2,8,16,256]{3,1,2,0:T(8,128)} %get-tuple-element.18), channel_id=1, source_target_pairs={{0,1},{1,2},{2,3},{3,0},{4,5},{5,6},{6,7},{7,4},{8,9},{9,10},{10,1... | collective-permute-start | bytes 786440 | tf_op jit(solution)/shard_map/ppermute | solution.py:47
  45.9 13.4 %collective-permute-start.5 = (f32[2,8,16,256]{3,1,2,0:T(8,128)}, f32[2,8,16,256]{3,1,2,0:T(8,128)S(1)}, u32[]{:S(2)}, u32[]{:S(2)}) collective-permute-start(f32[2,8,16,256]{3,1,2,0:T(8,128)} %get-tuple-element.19), channel_id=1, source_target_pairs={{0,1},{1,2},{2,3},{3,0},{4,5},{5,6},{6,7},{7,4},{8,9},{9,10},{10,1... | collective-permute-start | bytes 786440 | tf_op jit(solution)/shard_map/ppermute | solution.py:47

commit v10 on v2

--- a/solution.py
+++ b/solution.py
@@ -86,14 +86,14 @@
     images = jnp.where(inside, images, 0.0)
 
     mine = lax.dynamic_slice_in_dim(offsets, lax.axis_index("visit") * visits, visits, 0)
-    partial = jnp.zeros((2, offsets.shape[1], rows, cols), jnp.float32)
-    for offset_value in range(-MAXOFF, MAXOFF + 1):
-        onehot = (mine == offset_value).astype(jnp.float32)
-        start = reach + offset_value * BR
-        window = images[:, :, start : start + rows, :]
-        partial = partial + jnp.einsum(
-            "tk,ctrw->ckrw", onehot, window, precision=lax.Precision.HIGHEST
-        )
+    shifts = range(-MAXOFF, MAXOFF + 1)
+    onehot = jnp.stack([(mine == value).astype(jnp.float32) for value in shifts])
+    windows = jnp.stack(
+        [images[:, :, reach + value * BR : reach + value * BR + rows, :] for value in shifts], axis=1
+    )
+    partial = jnp.einsum(
+        "otk,cotrw->ckrw", onehot, windows, precision=lax.Precision.HIGHEST
+    )
 
     stacked = ring_reduce_scatter(partial, "visit")
     return stacked[0] / jnp.sqrt(stacked[1])

time: 58.4 us -> 56.4 us (0.966)
  the two profiles are of different devices: /device:TPU:54 before, /device:TPU:119 now
where the time goes in v10:
time: 56.4 us; the launch traced here: 56.2 us
  waiting for transfers between devices  21.8 us (39%)
  matrix products  17.9 us (32%)
  starting transfers between devices  10.2 us (18%)
  other arithmetic  4.27 us (8%)
  local copies, waits for them, and re-layouts  1.75 us (3%)
    ppermute x1, waiting for transfers between devices, ring_reduce_scatter(): got_left = lax.ppermute(ahead, axis, right)  11.3 us
    conv_general_dilated x2, matrix products, correlate_rows(): lax.conv_general_dilated(bordered, kernel, window_strides=(1,), padding='...  9.6 us
    dot_general x2, matrix products, toeplitz(): jnp.einsum('ab,bwv->awv', taps, onehot, precision=lax.Precision.HIGHEST)  6.23 us
    ppermute x1, waiting for transfers between devices, ring_reduce_scatter(): from_left = lax.ppermute(far[..., :half], axis, right)  5.53 us
    ppermute x1, starting transfers between devices, bordered_rows(): lax.ppermute(lax.slice_in_dim(block, block.shape[dim] - width, None, axis...  5.32 us
    ppermute x1, waiting for transfers between devices, ring_reduce_scatter(): got_right = lax.ppermute(behind, axis, left)  3.68 us
    dot_general x1, matrix products, shards(): jnp.einsum('otk,cotrw->ckrw', onehot, windows, precision=lax.Precision.HI...  2.03 us
    ppermute x1, starting transfers between devices, bordered_rows(): lax.ppermute(lax.slice_in_dim(block, 0, width, axis=dim), axis, backward)  1.92 us
  transfers between devices with their start and end apart: 6, of which 4 were waited for; matrix products, arithmetic and copies ran while one was open for 15% of the time, Pallas kernels for 0%

profile of v10, /device:TPU:119, one launch (start us, length us, event | category | flops | bytes accessed | tf_op | source)
XLA Modules:
  0.0 56.2 jit_solution(14673754301693459438)
XLA Ops:
  0.0 1.8 %fusion.22 = (f32[1,8,64,256]{3,1,2,0:T(8,128)S(1)}, f32[1,8,64,256]{3,1,2,0:T(8,128)S(1)}) fusion(f32[8,64,256]{2,1,0:T(8,128)} %param.4, f32[8,64,256]{2,1,0:T(8,128)} %param.5), kind=kLoop, calls=%fused_computation.33 | loop fusion | flops 131072 | bytes 2097152 | tf_op jit(solution)/shard_map/stack | solution.py:76
  1.9 5.3 %collective-permute-start = (f32[2,8,21,256]{3,1,2,0:T(8,128)S(1)}, f32[2,8,21,256]{3,1,2,0:T(8,128)S(1)}, u32[]{:S(2)}, u32[]{:S(2)}) collective-permute-start(f32[2,8,21,256]{3,1,2,0:T(8,128)S(1)} %get-tuple-element.8), channel_id=1, source_target_pairs={{0,4},{4,8},{8,12},{12,16},{16,20},{20,24},{24,28},{28,32},{32,36}... | collective-permute-start | bytes 1032200 | tf_op jit(solution)/shard_map/ppermute | solution.py:15
  7.2 1.9 %collective-permute-start.1 = (f32[2,8,21,256]{3,1,2,0:T(8,128)S(1)}, f32[2,8,21,256]{3,1,2,0:T(8,128)S(1)}, u32[]{:S(2)}, u32[]{:S(2)}) collective-permute-start(f32[2,8,21,256]{3,1,2,0:T(8,128)S(1)} %get-tuple-element.9), channel_id=1, source_target_pairs={{4,0},{8,4},{12,8},{16,12},{20,16},{24,20},{28,24},{32,28},{36,32}... | collective-permute-start | bytes 1032200 | tf_op jit(solution)/shard_map/ppermute | solution.py:18
  9.2 4.8 %fusion.3 = f32[256,256,11]{1,2,0:T(8,128)} fusion(f32[11,11]{1,0:T(8,128)} %param.6), kind=kOutput, calls=%fused_computation.4 | convolution fusion | flops 97320960 | bytes 2884068 | tf_op jit(solution)/shard_map/ab,bwv->awv/dot_general | solution.py:29
  13.9 0.1 constant_dynamic-slice_fusion
  14.0 0.1 copy.17
  14.2 1.5 %fusion.2 = f32[11,256,256]{2,0,1:T(8,128)S(1)} fusion(f32[11,11]{1,0:T(8,128)S(1)} %copy-done.2), kind=kOutput, calls=%fused_computation.3 | convolution fusion | flops 97321080 | bytes 2884068 | tf_op jit(solution)/shard_map/ab,bwv->awv/dot_general | solution.py:29
  15.7 1.3 %collective-permute-done.1 = f32[2,8,21,256]{3,1,2,0:T(8,128)S(1)} collective-permute-done((f32[2,8,21,256]{3,1,2,0:T(8,128)S(1)}, f32[2,8,21,256]{3,1,2,0:T(8,128)S(1)}, u32[]{:S(2)}, u32[]{:S(2)}) %collective-permute-start.1) | collective-permute-done | bytes 344096 | tf_op jit(solution)/shard_map/ppermute | solution.py:18
  17.0 0.1 pad_maximum_fusion
  17.2 4.7 %fusion.10 = f32[1,8,96,256]{3,1,2,0:T(8,128)S(1)} fusion(f32[256,256,11]{1,2,0:T(8,128)S(1)} %copy-done.1, f32[2,8,106,256]{3,1,2,0:T(8,128)S(1)} %pad_maximum_fusion), kind=kOutput, calls=%fused_computation.14 | convolution fusion | flops 3321888768 | bytes 5849088 | tf_op jit(solution)/shard_map/conv_general_dilated | solution.py:33
  21.9 4.9 %fusion.13 = f32[1,8,96,256]{3,1,2,0:T(8,128)S(1)} fusion(f32[11,256,256]{2,0,1:T(8,128)S(1)} %fusion.2, f32[2,8,106,256]{3,1,2,0:T(8,128)S(1)} %pad_maximum_fusion), kind=kOutput, calls=%fused_computation.15 | convolution fusion | flops 3321888768 | bytes 5849088 | tf_op jit(solution)/shard_map/conv_general_dilated | solution.py:33
  26.8 0.2 maximum_select_fusion
  27.0 0.1 fusion.20
  27.1 0.1 fusion.19
  27.1 0.1 fusion.18
  27.2 0.1 fusion.17
  27.3 0.1 fusion.16
  27.4 2.0 %fusion = f32[2,64,256,16,1]{2,3,0,1,4:T(8,128)S(1)} fusion(f32[2,5,8,64,256]{4,2,3,0,1:T(8,128)S(1)} %fusion.16, pred[5,8,16]{2,1,0:T(8,128)(4,1)S(1)} %constant_dynamic-update-slice_fusion), kind=kOutput, calls=%fused_computation | convolution fusion | flops 251658240 | bytes 7340672 | tf_op jit(solution)/shard_map/otk,cotrw->ckrw/dot_general | solution.py:94
  29.4 0.2 copy.34
  29.6 0.1 dynamic-slice_bitcast_fusion.2
  29.8 0.3 collective-permute-start.2
  30.1 1.3 %collective-permute-start.4 = (f32[2,16,16,128]{3,1,2,0:T(8,128)S(1)}, f32[2,16,16,128]{3,1,2,0:T(8,128)S(1)}, u32[]{:S(2)}, u32[]{:S(2)}) collective-permute-start(f32[2,16,16,128]{3,1,2,0:T(8,128)S(1)} %get-tuple-element.13), channel_id=1, source_target_pairs={{0,3},{1,0},{2,1},{3,2},{4,7},{5,4},{6,5},{7,6},{8,11},{9,8},{10,9... | collective-permute-start | bytes 786440 | tf_op jit(solution)/shard_map/ppermute | solution.py:59
  31.4 5.5 %collective-permute-done.2 = f32[2,16,16,128]{3,1,2,0:T(8,128)S(1)} collective-permute-done((f32[2,16,16,128]{3,1,2,0:T(8,128)S(1)}, f32[2,16,16,128]{3,1,2,0:T(8,128)S(1)}, u32[]{:S(2)}, u32[]{:S(2)}) %collective-permute-start.2) | collective-permute-done | bytes 262176 | tf_op jit(solution)/shard_map/ppermute | solution.py:58
  36.9 0.1 slice_add_fusion.1
  37.0 0.8 %pad_maximum_fusion.1 = f32[2,16,16,256]{3,1,2,0:T(8,128)} fusion(f32[2,16,16,128]{3,1,2,0:T(8,128)S(1)} %get-tuple-element.11, f32[2,16,16,128]{3,1,2,0:T(8,128)S(1)} %get-tuple-element.10), kind=kLoop, calls=%fused_computation.28 | loop fusion | flops 131072 | bytes 1048576 | tf_op jit(solution)/shard_map/concatenate | solution.py:61
  37.8 1.1 %collective-permute-start.3 = (f32[2,16,16,256]{3,1,2,0:T(8,128)}, f32[2,16,16,256]{3,1,2,0:T(8,128)S(1)}, u32[]{:S(2)}, u32[]{:S(2)}) collective-permute-start(f32[2,16,16,256]{3,1,2,0:T(8,128)} %pad_maximum_fusion.1), channel_id=1, source_target_pairs={{0,1},{1,2},{2,3},{3,0},{4,5},{5,6},{6,7},{7,4},{8,9},{9,10},{10,1... | collective-permute-start | bytes 1572872 | tf_op jit(solution)/shard_map/ppermute | solution.py:64
  39.0 0.8 %pad_maximum_fusion.2 = f32[2,16,16,256]{3,1,2,0:T(8,128)} fusion(f32[2,16,16,128]{3,1,2,0:T(8,128)S(1)} %get-tuple-element.15, f32[2,16,16,128]{3,1,2,0:T(8,128)S(1)} %get-tuple-element.14), kind=kLoop, calls=%fused_computation.29 | loop fusion | flops 131072 | bytes 1048576 | tf_op jit(solution)/shard_map/concatenate | solution.py:63
  39.8 0.4 collective-permute-start.5
  40.2 11.3 %collective-permute-done.3 = f32[2,16,16,256]{3,1,2,0:T(8,128)S(1)} collective-permute-done((f32[2,16,16,256]{3,1,2,0:T(8,128)}, f32[2,16,16,256]{3,1,2,0:T(8,128)S(1)}, u32[]{:S(2)}, u32[]{:S(2)}) %collective-permute-start.3) | collective-permute-done | bytes 524320 | tf_op jit(solution)/shard_map/ppermute | solution.py:64
  51.4 3.7 %collective-permute-done.5 = f32[2,16,16,256]{3,1,2,0:T(8,128)S(1)} collective-permute-done((f32[2,16,16,256]{3,1,2,0:T(8,128)}, f32[2,16,16,256]{3,1,2,0:T(8,128)S(1)}, u32[]{:S(2)}, u32[]{:S(2)}) %collective-permute-start.5) | collective-permute-done | bytes 524320 | tf_op jit(solution)/shard_map/ppermute | solution.py:65
  55.1 0.1 fusion.21
  55.3 0.9 %copy.12 = f32[16,16,256]{2,1,0:T(8,128)} copy(f32[16,16,256]{2,0,1:T(8,128)S(1)} %fusion.24) | data formatting | bytes 524288 | tf_op jit(solution)/shard_map/div | solution.py:99
  (18 shorter events, 0.3 us)
Async XLA Ops:
  0.0 13.9 %copy-start = (s32[32,16]{0,1:T(8,128)S(1)}, s32[32,16]{0,1:T(8,128)}, u32[]{:S(2)}) copy-start(s32[32,16]{0,1:T(8,128)} %param.7) | copy-start | bytes 6148
  0.0 14.2 %copy-start.2 = (f32[11,11]{1,0:T(8,128)S(1)}, f32[11,11]{1,0:T(8,128)}, u32[]{:S(2)}) copy-start(f32[11,11]{1,0:T(8,128)} %param.6) | copy-start | bytes 1456
  1.9 13.8 %collective-permute-start = (f32[2,8,21,256]{3,1,2,0:T(8,128)S(1)}, f32[2,8,21,256]{3,1,2,0:T(8,128)S(1)}, u32[]{:S(2)}, u32[]{:S(2)}) collective-permute-start(f32[2,8,21,256]{3,1,2,0:T(8,128)S(1)} %get-tuple-element.8), channel_id=1, source_target_pairs={{0,4},{4,8},{8,12},{12,16},{16,20},{20,24},{24,28},{28,32},{32,36}... | collective-permute-start | bytes 1032200 | tf_op jit(solution)/shard_map/ppermute | solution.py:15
  7.2 9.8 %collective-permute-start.1 = (f32[2,8,21,256]{3,1,2,0:T(8,128)S(1)}, f32[2,8,21,256]{3,1,2,0:T(8,128)S(1)}, u32[]{:S(2)}, u32[]{:S(2)}) collective-permute-start(f32[2,8,21,256]{3,1,2,0:T(8,128)S(1)} %get-tuple-element.9), channel_id=1, source_target_pairs={{4,0},{8,4},{12,8},{16,12},{20,16},{24,20},{28,24},{32,28},{36,32}... | collective-permute-start | bytes 1032200 | tf_op jit(solution)/shard_map/ppermute | solution.py:18
  14.2 3.0 %copy-start.1 = (f32[256,256,11]{1,2,0:T(8,128)S(1)}, f32[256,256,11]{1,2,0:T(8,128)}, u32[]{:S(2)}) copy-start(f32[256,256,11]{1,2,0:T(8,128)} %fusion.3) | copy-start | bytes 8650756
  29.8 7.1 %collective-permute-start.2 = (f32[2,16,16,128]{3,1,2,0:T(8,128)S(1)}, f32[2,16,16,128]{3,1,2,0:T(8,128)S(1)}, u32[]{:S(2)}, u32[]{:S(2)}) collective-permute-start(f32[2,16,16,128]{3,1,2,0:T(8,128)S(1)} %get-tuple-element.12), channel_id=1, source_target_pairs={{0,1},{1,2},{2,3},{3,0},{4,5},{5,6},{6,7},{7,4},{8,9},{9,10},{10,1... | collective-permute-start | bytes 786440 | tf_op jit(solution)/shard_map/ppermute | solution.py:58
  30.1 8.8 %collective-permute-start.4 = (f32[2,16,16,128]{3,1,2,0:T(8,128)S(1)}, f32[2,16,16,128]{3,1,2,0:T(8,128)S(1)}, u32[]{:S(2)}, u32[]{:S(2)}) collective-permute-start(f32[2,16,16,128]{3,1,2,0:T(8,128)S(1)} %get-tuple-element.13), channel_id=1, source_target_pairs={{0,3},{1,0},{2,1},{3,2},{4,7},{5,4},{6,5},{7,6},{8,11},{9,8},{10,9... | collective-permute-start | bytes 786440 | tf_op jit(solution)/shard_map/ppermute | solution.py:59
  37.8 13.6 %collective-permute-start.3 = (f32[2,16,16,256]{3,1,2,0:T(8,128)}, f32[2,16,16,256]{3,1,2,0:T(8,128)S(1)}, u32[]{:S(2)}, u32[]{:S(2)}) collective-permute-start(f32[2,16,16,256]{3,1,2,0:T(8,128)} %pad_maximum_fusion.1), channel_id=1, source_target_pairs={{0,1},{1,2},{2,3},{3,0},{4,5},{5,6},{6,7},{7,4},{8,9},{9,10},{10,1... | collective-permute-start | bytes 1572872 | tf_op jit(solution)/shard_map/ppermute | solution.py:64
  39.8 15.3 %collective-permute-start.5 = (f32[2,16,16,256]{3,1,2,0:T(8,128)}, f32[2,16,16,256]{3,1,2,0:T(8,128)S(1)}, u32[]{:S(2)}, u32[]{:S(2)}) collective-permute-start(f32[2,16,16,256]{3,1,2,0:T(8,128)} %pad_maximum_fusion.2), channel_id=1, source_target_pairs={{0,3},{1,0},{2,1},{3,2},{4,7},{5,4},{6,5},{7,6},{8,11},{9,8},{10,9... | collective-permute-start | bytes 1572872 | tf_op jit(solution)/shard_map/ppermute | solution.py:65

commit v11 on v10

--- a/solution.py
+++ b/solution.py
@@ -54,16 +54,14 @@
     def block(step):
         return lax.dynamic_slice_in_dim(partial, ((me + step) % count) * rows, rows, axis=2)
 
-    far = block(2)
+    far, ahead, behind = block(2), block(1), block(count - 1)
     from_left = lax.ppermute(far[..., :half], axis, right)
+    own_high = lax.ppermute(ahead[..., half:], axis, right)
     from_right = lax.ppermute(far[..., half:], axis, left)
-    ahead = block(1)
-    ahead = jnp.concatenate([ahead[..., :half] + from_left, ahead[..., half:]], axis=-1)
-    behind = block(count - 1)
-    behind = jnp.concatenate([behind[..., :half], behind[..., half:] + from_right], axis=-1)
-    got_left = lax.ppermute(ahead, axis, right)
-    got_right = lax.ppermute(behind, axis, left)
-    return block(0) + got_left + got_right
+    own_low = lax.ppermute(behind[..., :half], axis, left)
+    got_low = lax.ppermute(ahead[..., :half] + from_left, axis, right)
+    got_high = lax.ppermute(behind[..., half:] + from_right, axis, left)
+    return block(0) + jnp.concatenate([got_low + own_low, got_high + own_high], axis=-1)
 
 
 def shards(science, inv_variance, psf_kernel, offsets):

time: 56.4 us -> 56.7 us (level)
  waiting for transfers between devices: 21.8 us -> 18.7 us
  starting transfers between devices: 10.2 us -> 12.6 us
  other arithmetic: 4.27 us -> 5.22 us
    ppermute x2 -> x4, waiting for transfers between devices: 15 us -> 11.7 us  [the longest x1 3.81 us: ring_reduce_scatter(): got_high = lax.ppermute(behind[..., half:] + from_right, axis, left)]
    ppermute x2 -> x4, starting transfers between devices: 1.47 us -> 3.87 us  [the longest x1 2.46 us: ring_reduce_scatter(): own_high = lax.ppermute(ahead[..., half:], axis, right)]
    add x2 -> x4, other arithmetic: 0.2 us -> 2.13 us  [the longest x1 1 us: ring_reduce_scatter(): got_low + own_low]
    concatenate x2 -> x0, other arithmetic: 1.68 us -> none  [the longest x1 0.85 us: ring_reduce_scatter(): jnp.concatenate([ahead[..., :half] + from_left, ahead[..., half:]], axis=-1)]
    slice x1, other arithmetic: 0.06 us -> 0.76 us  [ring_reduce_scatter(): own_low = lax.ppermute(behind[..., :half], axis, left)]
  transfers between devices with their start and end apart: 6 -> 8, of which waited for: 4 -> 7; matrix products, arithmetic and copies ran while one was open for 15% -> 15% of each run, Pallas kernels for 0% -> 0%
where the time goes in v11:
time: 56.7 us; the launch traced here: 56.4 us
  waiting for transfers between devices  18.7 us (33%)
  matrix products  17.9 us (32%)
  starting transfers between devices  12.6 us (22%)
  other arithmetic  5.22 us (9%)
  local copies, waits for them, and re-layouts  1.75 us (3%)
    conv_general_dilated x2, matrix products, correlate_rows(): lax.conv_general_dilated(bordered, kernel, window_strides=(1,), padding='...  9.6 us
    dot_general x2, matrix products, toeplitz(): jnp.einsum('ab,bwv->awv', taps, onehot, precision=lax.Precision.HIGHEST)  6.25 us
    ppermute x1, waiting for transfers between devices, ring_reduce_scatter(): from_left = lax.ppermute(far[..., :half], axis, right)  5.55 us
    ppermute x1, starting transfers between devices, bordered_rows(): lax.ppermute(lax.slice_in_dim(block, block.shape[dim] - width, None, axis...  5.32 us
    ppermute x1, waiting for transfers between devices, ring_reduce_scatter(): got_high = lax.ppermute(behind[..., half:] + from_right, axis, left)  3.81 us
    ppermute x1, waiting for transfers between devices, ring_reduce_scatter(): got_low = lax.ppermute(ahead[..., :half] + from_left, axis, right)  3.66 us
    ppermute x1, waiting for transfers between devices, ring_reduce_scatter(): own_low = lax.ppermute(behind[..., :half], axis, left)  3.39 us
    ppermute x1, starting transfers between devices, ring_reduce_scatter(): own_high = lax.ppermute(ahead[..., half:], axis, right)  2.46 us
  transfers between devices with their start and end apart: 8, of which 7 were waited for; matrix products, arithmetic and copies ran while one was open for 15% of the time, Pallas kernels for 0%

profile of v11, /device:TPU:119, one launch (start us, length us, event | category | flops | bytes accessed | tf_op | source)
XLA Modules:
  0.0 56.4 jit_solution(10814553207197827095)
XLA Ops:
  0.0 1.8 %fusion.21 = (f32[1,8,64,256]{3,1,2,0:T(8,128)S(1)}, f32[1,8,64,256]{3,1,2,0:T(8,128)S(1)}) fusion(f32[8,64,256]{2,1,0:T(8,128)} %param.4, f32[8,64,256]{2,1,0:T(8,128)} %param.5), kind=kLoop, calls=%fused_computation.30 | loop fusion | flops 131072 | bytes 2097152 | tf_op jit(solution)/shard_map/stack | solution.py:74
  1.9 5.3 %collective-permute-start = (f32[2,8,21,256]{3,1,2,0:T(8,128)S(1)}, f32[2,8,21,256]{3,1,2,0:T(8,128)S(1)}, u32[]{:S(2)}, u32[]{:S(2)}) collective-permute-start(f32[2,8,21,256]{3,1,2,0:T(8,128)S(1)} %get-tuple-element.8), channel_id=1, source_target_pairs={{0,4},{4,8},{8,12},{12,16},{16,20},{20,24},{24,28},{28,32},{32,36}... | collective-permute-start | bytes 1032200 | tf_op jit(solution)/shard_map/ppermute | solution.py:15
  7.2 1.9 %collective-permute-start.1 = (f32[2,8,21,256]{3,1,2,0:T(8,128)S(1)}, f32[2,8,21,256]{3,1,2,0:T(8,128)S(1)}, u32[]{:S(2)}, u32[]{:S(2)}) collective-permute-start(f32[2,8,21,256]{3,1,2,0:T(8,128)S(1)} %get-tuple-element.9), channel_id=1, source_target_pairs={{4,0},{8,4},{12,8},{16,12},{20,16},{24,20},{28,24},{32,28},{36,32}... | collective-permute-start | bytes 1032200 | tf_op jit(solution)/shard_map/ppermute | solution.py:18
  9.2 4.8 %fusion.3 = f32[256,256,11]{1,2,0:T(8,128)} fusion(f32[11,11]{1,0:T(8,128)} %param.6), kind=kOutput, calls=%fused_computation.4 | convolution fusion | flops 97320960 | bytes 2884068 | tf_op jit(solution)/shard_map/ab,bwv->awv/dot_general | solution.py:29
  13.9 0.1 constant_dynamic-slice_fusion
  14.0 0.1 copy.17
  14.2 1.5 %fusion.2 = f32[11,256,256]{2,0,1:T(8,128)S(1)} fusion(f32[11,11]{1,0:T(8,128)S(1)} %copy-done.2), kind=kOutput, calls=%fused_computation.3 | convolution fusion | flops 97321080 | bytes 2884068 | tf_op jit(solution)/shard_map/ab,bwv->awv/dot_general | solution.py:29
  15.7 1.3 %collective-permute-done.1 = f32[2,8,21,256]{3,1,2,0:T(8,128)S(1)} collective-permute-done((f32[2,8,21,256]{3,1,2,0:T(8,128)S(1)}, f32[2,8,21,256]{3,1,2,0:T(8,128)S(1)}, u32[]{:S(2)}, u32[]{:S(2)}) %collective-permute-start.1) | collective-permute-done | bytes 344096 | tf_op jit(solution)/shard_map/ppermute | solution.py:18
  17.0 0.1 pad_maximum_fusion
  17.2 4.7 %fusion.10 = f32[1,8,96,256]{3,1,2,0:T(8,128)S(1)} fusion(f32[256,256,11]{1,2,0:T(8,128)S(1)} %copy-done.1, f32[2,8,106,256]{3,1,2,0:T(8,128)S(1)} %pad_maximum_fusion), kind=kOutput, calls=%fused_computation.14 | convolution fusion | flops 3321888768 | bytes 5849088 | tf_op jit(solution)/shard_map/conv_general_dilated | solution.py:33
  21.9 4.9 %fusion.13 = f32[1,8,96,256]{3,1,2,0:T(8,128)S(1)} fusion(f32[11,256,256]{2,0,1:T(8,128)S(1)} %fusion.2, f32[2,8,106,256]{3,1,2,0:T(8,128)S(1)} %pad_maximum_fusion), kind=kOutput, calls=%fused_computation.15 | convolution fusion | flops 3321888768 | bytes 5849088 | tf_op jit(solution)/shard_map/conv_general_dilated | solution.py:33
  26.8 0.2 maximum_select_fusion
  27.1 0.1 fusion.18
  27.4 2.0 %fusion = f32[2,64,256,16,1]{2,3,0,1,4:T(8,128)S(1)} fusion(f32[2,5,8,64,256]{4,2,3,0,1:T(8,128)S(1)} %fusion.16, pred[5,8,16]{2,1,0:T(8,128)(4,1)S(1)} %constant_dynamic-update-slice_fusion), kind=kOutput, calls=%fused_computation | convolution fusion | flops 251658240 | bytes 7340672 | tf_op jit(solution)/shard_map/otk,cotrw->ckrw/dot_general | solution.py:92
  29.4 0.2 copy.34
  29.6 0.1 dynamic-slice_bitcast_fusion.2
  29.8 0.3 collective-permute-start.2
  30.1 1.3 %collective-permute-start.5 = (f32[2,16,16,128]{3,1,2,0:T(8,128)S(1)}, f32[2,16,16,128]{3,1,2,0:T(8,128)S(1)}, u32[]{:S(2)}, u32[]{:S(2)}) collective-permute-start(f32[2,16,16,128]{3,1,2,0:T(8,128)S(1)} %get-tuple-element.15), channel_id=1, source_target_pairs={{0,3},{1,0},{2,1},{3,2},{4,7},{5,4},{6,5},{7,6},{8,11},{9,8},{10,9... | collective-permute-start | bytes 786440 | tf_op jit(solution)/shard_map/ppermute | solution.py:60
  31.4 5.6 %collective-permute-done.2 = f32[2,16,16,128]{3,1,2,0:T(8,128)S(1)} collective-permute-done((f32[2,16,16,128]{3,1,2,0:T(8,128)S(1)}, f32[2,16,16,128]{3,1,2,0:T(8,128)S(1)}, u32[]{:S(2)}, u32[]{:S(2)}) %collective-permute-start.2) | collective-permute-done | bytes 262176 | tf_op jit(solution)/shard_map/ppermute | solution.py:58
  37.0 1.2 %collective-permute-start.3 = (f32[2,16,16,128]{3,1,2,0:T(8,128)S(1)}, f32[2,16,16,128]{3,1,2,0:T(8,128)S(1)}, u32[]{:S(2)}, u32[]{:S(2)}) collective-permute-start(f32[2,16,16,128]{3,1,2,0:T(8,128)S(1)} %get-tuple-element.12), channel_id=1, source_target_pairs={{0,1},{1,2},{2,3},{3,0},{4,5},{5,6},{6,7},{7,4},{8,9},{9,10},{10,1... | collective-permute-start | bytes 786440 | tf_op jit(solution)/shard_map/ppermute | solution.py:62
  38.2 0.1 collective-permute-done.5
  38.3 0.8 %fusion.30 = (f32[2,16,16,128]{3,1,2,0:T(8,128)}, f32[2,16,16,128]{3,1,2,0:T(8,128)S(1)}) fusion(f32[2,16,16,256]{3,1,2,0:T(8,128)S(1)} %get-tuple-element.6, f32[2,16,16,128]{3,1,2,0:T(8,128)S(1)} %collective-permute-done.5), kind=kLoop, calls=%fused_computation.55 | loop fusion | flops 65536 | bytes 1310720 | tf_op jit(solution)/shard_map/slice | solution.py:61
  39.1 0.2 collective-permute-start.4
  39.3 2.5 %collective-permute-start.7 = (f32[2,16,16,128]{3,1,2,0:T(8,128)S(1)}, f32[2,16,16,128]{3,1,2,0:T(8,128)S(1)}, u32[]{:S(2)}, u32[]{:S(2)}) collective-permute-start(f32[2,16,16,128]{3,1,2,0:T(8,128)S(1)} %get-tuple-element.13), channel_id=1, source_target_pairs={{0,1},{1,2},{2,3},{3,0},{4,5},{5,6},{6,7},{7,4},{8,9},{9,10},{10,1... | collective-permute-start | bytes 786440 | tf_op jit(solution)/shard_map/ppermute | solution.py:59
  41.7 3.7 %collective-permute-done.3 = f32[2,16,16,128]{3,1,2,0:T(8,128)S(1)} collective-permute-done((f32[2,16,16,128]{3,1,2,0:T(8,128)S(1)}, f32[2,16,16,128]{3,1,2,0:T(8,128)S(1)}, u32[]{:S(2)}, u32[]{:S(2)}) %collective-permute-start.3) | collective-permute-done | bytes 262176 | tf_op jit(solution)/shard_map/ppermute | solution.py:62
  45.4 3.4 %collective-permute-done.4 = f32[2,16,16,128]{3,1,2,0:T(8,128)} collective-permute-done((f32[2,16,16,128]{3,1,2,0:T(8,128)}, f32[2,16,16,128]{3,1,2,0:T(8,128)}, u32[]{:S(2)}, u32[]{:S(2)}) %collective-permute-start.4) | collective-permute-done | bytes 262176 | tf_op jit(solution)/shard_map/ppermute | solution.py:61
  48.8 1.0 %add.86 = f32[2,16,16,128]{3,1,2,0:T(8,128)S(1)} add(f32[2,16,16,128]{3,1,2,0:T(8,128)S(1)} %collective-permute-done.3, f32[2,16,16,128]{3,1,2,0:T(8,128)} %collective-permute-done.4) | non-fusion elementwise | flops 65536 | bytes 786432 | tf_op jit(solution)/shard_map/add | solution.py:64
  49.8 0.8 %collective-permute-done.7 = f32[2,16,16,128]{3,1,2,0:T(8,128)S(1)} collective-permute-done((f32[2,16,16,128]{3,1,2,0:T(8,128)S(1)}, f32[2,16,16,128]{3,1,2,0:T(8,128)S(1)}, u32[]{:S(2)}, u32[]{:S(2)}) %collective-permute-start.7) | collective-permute-done | bytes 262176 | tf_op jit(solution)/shard_map/ppermute | solution.py:59
  50.6 3.8 %collective-permute-done.6 = f32[2,16,16,128]{3,1,2,0:T(8,128)} collective-permute-done((f32[2,16,16,128]{3,1,2,0:T(8,128)S(1)}, f32[2,16,16,128]{3,1,2,0:T(8,128)}, u32[]{:S(2)}, u32[]{:S(2)}) %collective-permute-start.6) | collective-permute-done | bytes 262176 | tf_op jit(solution)/shard_map/ppermute | solution.py:63
  54.4 1.0 %add.88 = f32[2,16,16,128]{3,1,2,0:T(8,128)S(1)} add(f32[2,16,16,128]{3,1,2,0:T(8,128)} %collective-permute-done.6, f32[2,16,16,128]{3,1,2,0:T(8,128)S(1)} %collective-permute-done.7) | non-fusion elementwise | flops 65536 | bytes 786432 | tf_op jit(solution)/shard_map/add | solution.py:64
  55.4 0.1 maximum_add_fusion
  55.6 0.9 %copy.12 = f32[16,16,256]{2,1,0:T(8,128)} copy(f32[16,16,256]{2,0,1:T(8,128)S(1)} %fusion.23) | data formatting | bytes 524288 | tf_op jit(solution)/shard_map/div | solution.py:97
  (22 shorter events, 0.6 us)
Async XLA Ops:
  0.0 13.9 %copy-start = (s32[32,16]{0,1:T(8,128)S(1)}, s32[32,16]{0,1:T(8,128)}, u32[]{:S(2)}) copy-start(s32[32,16]{0,1:T(8,128)} %param.7) | copy-start | bytes 6148
  0.0 14.2 %copy-start.2 = (f32[11,11]{1,0:T(8,128)S(1)}, f32[11,11]{1,0:T(8,128)}, u32[]{:S(2)}) copy-start(f32[11,11]{1,0:T(8,128)} %param.6) | copy-start | bytes 1456
  1.9 13.8 %collective-permute-start = (f32[2,8,21,256]{3,1,2,0:T(8,128)S(1)}, f32[2,8,21,256]{3,1,2,0:T(8,128)S(1)}, u32[]{:S(2)}, u32[]{:S(2)}) collective-permute-start(f32[2,8,21,256]{3,1,2,0:T(8,128)S(1)} %get-tuple-element.8), channel_id=1, source_target_pairs={{0,4},{4,8},{8,12},{12,16},{16,20},{20,24},{24,28},{28,32},{32,36}... | collective-permute-start | bytes 1032200 | tf_op jit(solution)/shard_map/ppermute | solution.py:15
  7.2 9.8 %collective-permute-start.1 = (f32[2,8,21,256]{3,1,2,0:T(8,128)S(1)}, f32[2,8,21,256]{3,1,2,0:T(8,128)S(1)}, u32[]{:S(2)}, u32[]{:S(2)}) collective-permute-start(f32[2,8,21,256]{3,1,2,0:T(8,128)S(1)} %get-tuple-element.9), channel_id=1, source_target_pairs={{4,0},{8,4},{12,8},{16,12},{20,16},{24,20},{28,24},{32,28},{36,32}... | collective-permute-start | bytes 1032200 | tf_op jit(solution)/shard_map/ppermute | solution.py:18
  14.2 2.9 %copy-start.1 = (f32[256,256,11]{1,2,0:T(8,128)S(1)}, f32[256,256,11]{1,2,0:T(8,128)}, u32[]{:S(2)}) copy-start(f32[256,256,11]{1,2,0:T(8,128)} %fusion.3) | copy-start | bytes 8650756
  29.8 7.1 %collective-permute-start.2 = (f32[2,16,16,128]{3,1,2,0:T(8,128)S(1)}, f32[2,16,16,128]{3,1,2,0:T(8,128)S(1)}, u32[]{:S(2)}, u32[]{:S(2)}) collective-permute-start(f32[2,16,16,128]{3,1,2,0:T(8,128)S(1)} %get-tuple-element.14), channel_id=1, source_target_pairs={{0,1},{1,2},{2,3},{3,0},{4,5},{5,6},{6,7},{7,4},{8,9},{9,10},{10,1... | collective-permute-start | bytes 786440 | tf_op jit(solution)/shard_map/ppermute | solution.py:58
  30.1 8.2 %collective-permute-start.5 = (f32[2,16,16,128]{3,1,2,0:T(8,128)S(1)}, f32[2,16,16,128]{3,1,2,0:T(8,128)S(1)}, u32[]{:S(2)}, u32[]{:S(2)}) collective-permute-start(f32[2,16,16,128]{3,1,2,0:T(8,128)S(1)} %get-tuple-element.15), channel_id=1, source_target_pairs={{0,3},{1,0},{2,1},{3,2},{4,7},{5,4},{6,5},{7,6},{8,11},{9,8},{10,9... | collective-permute-start | bytes 786440 | tf_op jit(solution)/shard_map/ppermute | solution.py:60
  37.0 8.4 %collective-permute-start.3 = (f32[2,16,16,128]{3,1,2,0:T(8,128)S(1)}, f32[2,16,16,128]{3,1,2,0:T(8,128)S(1)}, u32[]{:S(2)}, u32[]{:S(2)}) collective-permute-start(f32[2,16,16,128]{3,1,2,0:T(8,128)S(1)} %get-tuple-element.12), channel_id=1, source_target_pairs={{0,1},{1,2},{2,3},{3,0},{4,5},{5,6},{6,7},{7,4},{8,9},{9,10},{10,1... | collective-permute-start | bytes 786440 | tf_op jit(solution)/shard_map/ppermute | solution.py:62
  39.1 9.7 %collective-permute-start.4 = (f32[2,16,16,128]{3,1,2,0:T(8,128)}, f32[2,16,16,128]{3,1,2,0:T(8,128)}, u32[]{:S(2)}, u32[]{:S(2)}) collective-permute-start(f32[2,16,16,128]{3,1,2,0:T(8,128)} %get-tuple-element.10), channel_id=1, source_target_pairs={{0,3},{1,0},{2,1},{3,2},{4,7},{5,4},{6,5},{7,6},{8,11},{9,8},{10,9... | collective-permute-start | bytes 786440 | tf_op jit(solution)/shard_map/ppermute | solution.py:61
  39.3 11.3 %collective-permute-start.7 = (f32[2,16,16,128]{3,1,2,0:T(8,128)S(1)}, f32[2,16,16,128]{3,1,2,0:T(8,128)S(1)}, u32[]{:S(2)}, u32[]{:S(2)}) collective-permute-start(f32[2,16,16,128]{3,1,2,0:T(8,128)S(1)} %get-tuple-element.13), channel_id=1, source_target_pairs={{0,1},{1,2},{2,3},{3,0},{4,5},{5,6},{6,7},{7,4},{8,9},{9,10},{10,1... | collective-permute-start | bytes 786440 | tf_op jit(solution)/shard_map/ppermute | solution.py:59
  41.7 12.7 %collective-permute-start.6 = (f32[2,16,16,128]{3,1,2,0:T(8,128)S(1)}, f32[2,16,16,128]{3,1,2,0:T(8,128)}, u32[]{:S(2)}, u32[]{:S(2)}) collective-permute-start(f32[2,16,16,128]{3,1,2,0:T(8,128)S(1)} %get-tuple-element.11), channel_id=1, source_target_pairs={{0,3},{1,0},{2,1},{3,2},{4,7},{5,4},{6,5},{7,6},{8,11},{9,8},{10,9... | collective-permute-start | bytes 786440 | tf_op jit(solution)/shard_map/ppermute | solution.py:63

commit v12 on v10

--- a/solution.py
+++ b/solution.py
@@ -22,11 +22,13 @@
 def toeplitz(taps, cols):
     size = taps.shape[1]
     radius = (size - 1) // 2
-    w = lax.broadcasted_iota(jnp.int32, (size, cols, cols), 1)
-    v = lax.broadcasted_iota(jnp.int32, (size, cols, cols), 2)
-    b = lax.broadcasted_iota(jnp.int32, (size, cols, cols), 0)
-    onehot = (w - v + radius == b).astype(jnp.float32)
-    return jnp.einsum("ab,bwv->awv", taps, onehot, precision=lax.Precision.HIGHEST)
+    w = lax.broadcasted_iota(jnp.int32, (1, cols, cols), 1)
+    v = lax.broadcasted_iota(jnp.int32, (1, cols, cols), 2)
+    tap = w - v + radius
+    out = jnp.zeros((taps.shape[0], cols, cols), jnp.float32)
+    for b in range(size):
+        out = jnp.where(tap == b, taps[:, b][:, None, None], out)
+    return out
 
 
 def correlate_rows(bordered, kernel):

time: 56.4 us -> 55.3 us (0.980)
  the two profiles are of different devices: /device:TPU:119 before, /device:TPU:54 now
where the time goes in v12:
time: 55.3 us; the launch traced here: 55.1 us
  waiting for transfers between devices  24.9 us (45%)
  matrix products  13 us (24%)
  starting transfers between devices  9.69 us (18%)
  other arithmetic  4.6 us (8%)
  local copies, waits for them, and re-layouts  2.49 us (5%)
    ppermute x1, waiting for transfers between devices, ring_reduce_scatter(): got_left = lax.ppermute(ahead, axis, right)  11.8 us
    conv_general_dilated x2, matrix products, correlate_rows(): lax.conv_general_dilated(bordered, kernel, window_strides=(1,), padding='...  11 us
    ppermute x1, waiting for transfers between devices, ring_reduce_scatter(): from_left = lax.ppermute(far[..., :half], axis, right)  5.9 us
    ppermute x1, waiting for transfers between devices, ring_reduce_scatter(): got_right = lax.ppermute(behind, axis, left)  3.93 us
    ppermute x1, starting transfers between devices, bordered_rows(): lax.ppermute(lax.slice_in_dim(block, 0, width, axis=dim), axis, backward)  3.64 us
    dot_general x1, matrix products, shards(): jnp.einsum('otk,cotrw->ckrw', onehot, windows, precision=lax.Precision.HI...  2.03 us
    ppermute x1, starting transfers between devices, bordered_rows(): lax.ppermute(lax.slice_in_dim(block, block.shape[dim] - width, None, axis...  1.92 us
    another operation x1, other arithmetic, shards(): both = jnp.stack([weighted, inv_variance])  1.84 us
  transfers between devices with their start and end apart: 6, of which 5 were waited for; matrix products, arithmetic and copies ran while one was open for 6% of the time, Pallas kernels for 0%

profile of v12, /device:TPU:54, one launch (start us, length us, event | category | flops | bytes accessed | tf_op | source)
XLA Modules:
  0.0 55.1 jit_solution(4369716960999394381)
XLA Ops:
  0.0 1.8 %fusion.84 = (f32[1,8,64,256]{3,1,2,0:T(8,128)S(1)}, f32[1,8,64,256]{3,1,2,0:T(8,128)S(1)}) fusion(f32[8,64,256]{2,1,0:T(8,128)} %param.4, f32[8,64,256]{2,1,0:T(8,128)} %param.5), kind=kLoop, calls=%fused_computation.94 | loop fusion | flops 131072 | bytes 2097152 | tf_op jit(solution)/shard_map/stack | solution.py:78
  1.9 1.9 %collective-permute-start = (f32[2,8,21,256]{3,1,2,0:T(8,128)S(1)}, f32[2,8,21,256]{3,1,2,0:T(8,128)S(1)}, u32[]{:S(2)}, u32[]{:S(2)}) collective-permute-start(f32[2,8,21,256]{3,1,2,0:T(8,128)S(1)} %get-tuple-element.30), channel_id=1, source_target_pairs={{0,4},{4,8},{8,12},{12,16},{16,20},{20,24},{24,28},{28,32},{32,36}... | collective-permute-start | bytes 1032200 | tf_op jit(solution)/shard_map/ppermute | solution.py:15
  3.8 3.6 %collective-permute-start.1 = (f32[2,8,21,256]{3,1,2,0:T(8,128)S(1)}, f32[2,8,21,256]{3,1,2,0:T(8,128)S(1)}, u32[]{:S(2)}, u32[]{:S(2)}) collective-permute-start(f32[2,8,21,256]{3,1,2,0:T(8,128)S(1)} %get-tuple-element.31), channel_id=1, source_target_pairs={{4,0},{8,4},{12,8},{16,12},{20,16},{24,20},{28,24},{32,28},{36,32}... | collective-permute-start | bytes 1032200 | tf_op jit(solution)/shard_map/ppermute | solution.py:18
  7.8 0.4 slice_reduce_fusion.21
  8.2 0.4 slice_reduce_fusion.10
  8.6 0.1 constant_dynamic-slice_fusion
  8.6 0.1 copy.21
  8.9 1.6 %collective-permute-done = f32[2,8,21,256]{3,1,2,0:T(8,128)S(1)} collective-permute-done((f32[2,8,21,256]{3,1,2,0:T(8,128)S(1)}, f32[2,8,21,256]{3,1,2,0:T(8,128)S(1)}, u32[]{:S(2)}, u32[]{:S(2)}) %collective-permute-start) | collective-permute-done | bytes 344096 | tf_op jit(solution)/shard_map/ppermute | solution.py:15
  10.5 1.8 %collective-permute-done.1 = f32[2,8,21,256]{3,1,2,0:T(8,128)S(1)} collective-permute-done((f32[2,8,21,256]{3,1,2,0:T(8,128)S(1)}, f32[2,8,21,256]{3,1,2,0:T(8,128)S(1)}, u32[]{:S(2)}, u32[]{:S(2)}) %collective-permute-start.1) | collective-permute-done | bytes 344096 | tf_op jit(solution)/shard_map/ppermute | solution.py:18
  12.2 0.1 pad_maximum_fusion
  12.4 5.4 %fusion.72 = f32[1,8,96,256]{3,1,2,0:T(8,128)S(1)} fusion(f32[11]{0:T(128)S(1)} %get-tuple-element.15, f32[11]{0:T(128)S(1)} %get-tuple-element.6, f32[11]{0:T(128)S(1)} %get-tuple-element.7, f32[11]{0:T(128)S(1)} %get-tuple-element.8, f32[11]{0:T(128)S(1)} %get-tuple-element.9, f32[11]{0:T(128)S(1)} %get-tuple-element.10, f32[11]{0:T(128)S(1)} %get-tuple-element.11, ...), kind=kOutput, calls=%fused_computation.75 | convolution fusion | flops 3329818624 | bytes 2381312 | tf_op jit(solution)/shard_map/conv_general_dilated | solution.py:35
  17.8 5.6 %fusion.75 = f32[1,8,96,256]{3,1,2,0:T(8,128)S(1)} fusion(f32[11]{0:T(128)S(1)} %get-tuple-element.17, f32[11]{0:T(128)S(1)} %get-tuple-element.18, f32[11]{0:T(128)S(1)} %get-tuple-element.19, f32[11]{0:T(128)S(1)} %get-tuple-element.20, f32[11]{0:T(128)S(1)} %get-tuple-element.21, f32[11]{0:T(128)S(1)} %get-tuple-element.22, ...), kind=kOutput, calls=%fused_computation.76 | convolution fusion | flops 3329818624 | bytes 2381312 | tf_op jit(solution)/shard_map/conv_general_dilated | solution.py:35
  23.4 0.2 maximum_select_fusion
  23.6 0.1 fusion.82
  23.7 0.1 fusion.81
  23.8 0.1 fusion.80
  23.8 0.1 fusion.79
  23.9 0.1 fusion.78
  24.0 2.0 %fusion = f32[2,64,256,16,1]{2,3,0,1,4:T(8,128)S(1)} fusion(f32[2,5,8,64,256]{4,2,3,0,1:T(8,128)S(1)} %fusion.78, pred[5,8,16]{2,1,0:T(8,128)(4,1)S(1)} %constant_dynamic-update-slice_fusion), kind=kOutput, calls=%fused_computation | convolution fusion | flops 251658240 | bytes 7340672 | tf_op jit(solution)/shard_map/otk,cotrw->ckrw/dot_general | solution.py:96
  26.0 0.2 copy.30
  26.2 0.1 dynamic-slice_bitcast_fusion.2
  26.4 0.6 %collective-permute-start.2 = (f32[2,16,16,128]{3,1,2,0:T(8,128)S(1)}, f32[2,16,16,128]{3,1,2,0:T(8,128)S(1)}, u32[]{:S(2)}, u32[]{:S(2)}) collective-permute-start(f32[2,16,16,128]{3,1,2,0:T(8,128)S(1)} %get-tuple-element.34), channel_id=1, source_target_pairs={{0,1},{1,2},{2,3},{3,0},{4,5},{5,6},{6,7},{7,4},{8,9},{9,10},{10,1... | collective-permute-start | bytes 786440 | tf_op jit(solution)/shard_map/ppermute | solution.py:60
  27.0 1.5 %collective-permute-start.4 = (f32[2,16,16,128]{3,1,2,0:T(8,128)S(1)}, f32[2,16,16,128]{3,1,2,0:T(8,128)S(1)}, u32[]{:S(2)}, u32[]{:S(2)}) collective-permute-start(f32[2,16,16,128]{3,1,2,0:T(8,128)S(1)} %get-tuple-element.35), channel_id=1, source_target_pairs={{0,3},{1,0},{2,1},{3,2},{4,7},{5,4},{6,5},{7,6},{8,11},{9,8},{10,9... | collective-permute-start | bytes 786440 | tf_op jit(solution)/shard_map/ppermute | solution.py:61
  28.5 5.9 %collective-permute-done.2 = f32[2,16,16,128]{3,1,2,0:T(8,128)S(1)} collective-permute-done((f32[2,16,16,128]{3,1,2,0:T(8,128)S(1)}, f32[2,16,16,128]{3,1,2,0:T(8,128)S(1)}, u32[]{:S(2)}, u32[]{:S(2)}) %collective-permute-start.2) | collective-permute-done | bytes 262176 | tf_op jit(solution)/shard_map/ppermute | solution.py:60
  34.5 0.9 %pad_maximum_fusion.1 = f32[2,16,16,256]{3,1,2,0:T(8,128)} fusion(f32[2,16,16,128]{3,1,2,0:T(8,128)S(1)} %get-tuple-element.33, f32[2,16,16,128]{3,1,2,0:T(8,128)S(1)} %get-tuple-element.32), kind=kLoop, calls=%fused_computation.89 | loop fusion | flops 131072 | bytes 1048576 | tf_op jit(solution)/shard_map/concatenate | solution.py:63
  35.4 1.7 %collective-permute-start.3 = (f32[2,16,16,256]{3,1,2,0:T(8,128)}, f32[2,16,16,256]{3,1,2,0:T(8,128)S(1)}, u32[]{:S(2)}, u32[]{:S(2)}) collective-permute-start(f32[2,16,16,256]{3,1,2,0:T(8,128)} %pad_maximum_fusion.1), channel_id=1, source_target_pairs={{0,1},{1,2},{2,3},{3,0},{4,5},{5,6},{6,7},{7,4},{8,9},{9,10},{10,1... | collective-permute-start | bytes 1572872 | tf_op jit(solution)/shard_map/ppermute | solution.py:66
  37.1 0.8 %pad_maximum_fusion.2 = f32[2,16,16,256]{3,1,2,0:T(8,128)} fusion(f32[2,16,16,128]{3,1,2,0:T(8,128)S(1)} %get-tuple-element.37, f32[2,16,16,128]{3,1,2,0:T(8,128)S(1)} %get-tuple-element.36), kind=kLoop, calls=%fused_computation.90 | loop fusion | flops 131072 | bytes 1048576 | tf_op jit(solution)/shard_map/concatenate | solution.py:65
  38.0 0.3 collective-permute-start.5
  38.3 11.8 %collective-permute-done.3 = f32[2,16,16,256]{3,1,2,0:T(8,128)S(1)} collective-permute-done((f32[2,16,16,256]{3,1,2,0:T(8,128)}, f32[2,16,16,256]{3,1,2,0:T(8,128)S(1)}, u32[]{:S(2)}, u32[]{:S(2)}) %collective-permute-start.3) | collective-permute-done | bytes 524320 | tf_op jit(solution)/shard_map/ppermute | solution.py:66
  50.1 3.9 %collective-permute-done.5 = f32[2,16,16,256]{3,1,2,0:T(8,128)S(1)} collective-permute-done((f32[2,16,16,256]{3,1,2,0:T(8,128)}, f32[2,16,16,256]{3,1,2,0:T(8,128)S(1)}, u32[]{:S(2)}, u32[]{:S(2)}) %collective-permute-start.5) | collective-permute-done | bytes 524320 | tf_op jit(solution)/shard_map/ppermute | solution.py:67
  54.0 0.1 fusion.83
  54.2 0.9 %copy.16 = f32[16,16,256]{2,1,0:T(8,128)} copy(f32[16,16,256]{2,0,1:T(8,128)S(1)} %fusion.86) | data formatting | bytes 524288 | tf_op jit(solution)/shard_map/div | solution.py:101
  (23 shorter events, 0.7 us)
Async XLA Ops:
  0.0 8.6 %copy-start = (s32[32,16]{0,1:T(8,128)S(1)}, s32[32,16]{0,1:T(8,128)}, u32[]{:S(2)}) copy-start(s32[32,16]{0,1:T(8,128)} %param.7) | copy-start | bytes 6148
  0.0 7.8 %copy-start.1 = (f32[11,11]{1,0:T(8,128)S(1)}, f32[11,11]{1,0:T(8,128)}, u32[]{:S(2)}) copy-start(f32[11,11]{1,0:T(8,128)} %param.6) | copy-start | bytes 1456
  1.9 8.6 %collective-permute-start = (f32[2,8,21,256]{3,1,2,0:T(8,128)S(1)}, f32[2,8,21,256]{3,1,2,0:T(8,128)S(1)}, u32[]{:S(2)}, u32[]{:S(2)}) collective-permute-start(f32[2,8,21,256]{3,1,2,0:T(8,128)S(1)} %get-tuple-element.30), channel_id=1, source_target_pairs={{0,4},{4,8},{8,12},{12,16},{16,20},{20,24},{24,28},{28,32},{32,36}... | collective-permute-start | bytes 1032200 | tf_op jit(solution)/shard_map/ppermute | solution.py:15
  3.8 8.4 %collective-permute-start.1 = (f32[2,8,21,256]{3,1,2,0:T(8,128)S(1)}, f32[2,8,21,256]{3,1,2,0:T(8,128)S(1)}, u32[]{:S(2)}, u32[]{:S(2)}) collective-permute-start(f32[2,8,21,256]{3,1,2,0:T(8,128)S(1)} %get-tuple-element.31), channel_id=1, source_target_pairs={{4,0},{8,4},{12,8},{16,12},{20,16},{24,20},{28,24},{32,28},{36,32}... | collective-permute-start | bytes 1032200 | tf_op jit(solution)/shard_map/ppermute | solution.py:18
  26.4 8.0 %collective-permute-start.2 = (f32[2,16,16,128]{3,1,2,0:T(8,128)S(1)}, f32[2,16,16,128]{3,1,2,0:T(8,128)S(1)}, u32[]{:S(2)}, u32[]{:S(2)}) collective-permute-start(f32[2,16,16,128]{3,1,2,0:T(8,128)S(1)} %get-tuple-element.34), channel_id=1, source_target_pairs={{0,1},{1,2},{2,3},{3,0},{4,5},{5,6},{6,7},{7,4},{8,9},{9,10},{10,1... | collective-permute-start | bytes 786440 | tf_op jit(solution)/shard_map/ppermute | solution.py:60
  27.0 10.1 %collective-permute-start.4 = (f32[2,16,16,128]{3,1,2,0:T(8,128)S(1)}, f32[2,16,16,128]{3,1,2,0:T(8,128)S(1)}, u32[]{:S(2)}, u32[]{:S(2)}) collective-permute-start(f32[2,16,16,128]{3,1,2,0:T(8,128)S(1)} %get-tuple-element.35), channel_id=1, source_target_pairs={{0,3},{1,0},{2,1},{3,2},{4,7},{5,4},{6,5},{7,6},{8,11},{9,8},{10,9... | collective-permute-start | bytes 786440 | tf_op jit(solution)/shard_map/ppermute | solution.py:61
  35.4 14.7 %collective-permute-start.3 = (f32[2,16,16,256]{3,1,2,0:T(8,128)}, f32[2,16,16,256]{3,1,2,0:T(8,128)S(1)}, u32[]{:S(2)}, u32[]{:S(2)}) collective-permute-start(f32[2,16,16,256]{3,1,2,0:T(8,128)} %pad_maximum_fusion.1), channel_id=1, source_target_pairs={{0,1},{1,2},{2,3},{3,0},{4,5},{5,6},{6,7},{7,4},{8,9},{9,10},{10,1... | collective-permute-start | bytes 1572872 | tf_op jit(solution)/shard_map/ppermute | solution.py:66
  38.0 16.0 %collective-permute-start.5 = (f32[2,16,16,256]{3,1,2,0:T(8,128)}, f32[2,16,16,256]{3,1,2,0:T(8,128)S(1)}, u32[]{:S(2)}, u32[]{:S(2)}) collective-permute-start(f32[2,16,16,256]{3,1,2,0:T(8,128)} %pad_maximum_fusion.2), channel_id=1, source_target_pairs={{0,3},{1,0},{2,1},{3,2},{4,7},{5,4},{6,5},{7,6},{8,11},{9,8},{10,9... | collective-permute-start | bytes 1572872 | tf_op jit(solution)/shard_map/ppermute | solution.py:67

commit v13 on v12

--- a/solution.py
+++ b/solution.py
@@ -74,9 +74,16 @@
     visits, rows, cols = science.shape
     total_rows = rows * lax.axis_size("sky")
 
-    weighted = science * inv_variance
-    both = jnp.stack([weighted, inv_variance])
-    bordered = bordered_rows(both, "sky", radius + reach)
+    width = radius + reach
+    count = lax.axis_size("sky")
+    forward = [(i, i + 1) for i in range(count - 1)]
+    backward = [(target, source) for source, target in forward]
+    low = lax.ppermute(jnp.stack([science[:, rows - width :], inv_variance[:, rows - width :]]), "sky", forward)
+    high = lax.ppermute(jnp.stack([science[:, :width], inv_variance[:, :width]]), "sky", backward)
+    bordered = [
+        jnp.concatenate([low[0] * low[1], science * inv_variance, high[0] * high[1]], axis=1),
+        jnp.concatenate([low[1], inv_variance, high[1]], axis=1),
+    ]
 
     psi = correlate_rows(bordered[0], toeplitz(psf_kernel, cols))
     phi = correlate_rows(bordered[1], toeplitz(psf_kernel * psf_kernel, cols))

time: 55.3 us -> 55.2 us (level)
    mul x0 -> x3, other arithmetic: none -> 1.88 us  [the longest x1 1.84 us: shards(): science * inv_variance]
    another operation x1 -> x2, other arithmetic: 1.84 us -> 0.07 us  [the longest x1 0.03 us: shards(): jnp.stack([science[:, rows - width:], inv_variance[:, rows - width:]])]
where the time goes in v13:
time: 55.2 us; the launch traced here: 55 us
  waiting for transfers between devices  24.9 us (45%)
  matrix products  13 us (24%)
  starting transfers between devices  9.69 us (18%)
  other arithmetic  4.51 us (8%)
  local copies, waits for them, and re-layouts  2.56 us (5%)
    ppermute x1, waiting for transfers between devices, ring_reduce_scatter(): got_left = lax.ppermute(ahead, axis, right)  11.8 us
    conv_general_dilated x2, matrix products, correlate_rows(): lax.conv_general_dilated(bordered, kernel, window_strides=(1,), padding='...  11 us
    ppermute x1, waiting for transfers between devices, ring_reduce_scatter(): from_left = lax.ppermute(far[..., :half], axis, right)  5.9 us
    ppermute x1, waiting for transfers between devices, ring_reduce_scatter(): got_right = lax.ppermute(behind, axis, left)  3.93 us
    ppermute x1, starting transfers between devices, shards(): lax.ppermute(jnp.stack([science[:, :width], inv_variance[:, :width]]), 's...  3.64 us
    dot_general x1, matrix products, shards(): jnp.einsum('otk,cotrw->ckrw', onehot, windows, precision=lax.Precision.HI...  2.03 us
    ppermute x1, starting transfers between devices, shards(): lax.ppermute(jnp.stack([science[:, rows - width:], inv_variance[:, rows -...  1.92 us
    mul x1, other arithmetic, shards(): science * inv_variance  1.84 us
  transfers between devices with their start and end apart: 6, of which 5 were waited for; matrix products, arithmetic and copies ran while one was open for 6% of the time, Pallas kernels for 0%

profile of v13, /device:TPU:54, one launch (start us, length us, event | category | flops | bytes accessed | tf_op | source)
XLA Modules:
  0.0 55.0 jit_solution(1701024058392113453)
XLA Ops:
  0.0 1.8 %copy_multiply_fusion = (f32[8,64,256]{2,0,1:T(8,128)S(1)}, f32[8,64,256]{2,0,1:T(8,128)S(1)}, f32[8,64,256]{2,0,1:T(8,128)S(1)}) fusion(f32[8,64,256]{2,1,0:T(8,128)} %param.5, f32[8,64,256]{2,1,0:T(8,128)} %param.4), kind=kLoop, calls=%fused_computation.166 | loop fusion | flops 131072 | bytes 2621440 | tf_op jit(solution)/shard_map/mul | solution.py:84
  1.9 1.9 %collective-permute-start = (f32[2,8,21,256]{3,1,2,0:T(8,128)S(1)}, f32[2,8,21,256]{3,1,2,0:T(8,128)S(1)}, u32[]{:S(2)}, u32[]{:S(2)}) collective-permute-start(f32[2,8,21,256]{3,1,2,0:T(8,128)S(1)} %pad_maximum_fusion.2), channel_id=1, source_target_pairs={{0,4},{4,8},{8,12},{12,16},{16,20},{20,24},{24,28},{28,32},{32,36}... | collective-permute-start | bytes 1032200 | tf_op jit(solution)/shard_map/ppermute | solution.py:81
  3.9 3.6 %collective-permute-start.1 = (f32[2,8,21,256]{3,1,2,0:T(8,128)S(1)}, f32[2,8,21,256]{3,1,2,0:T(8,128)S(1)}, u32[]{:S(2)}, u32[]{:S(2)}) collective-permute-start(f32[2,8,21,256]{3,1,2,0:T(8,128)S(1)} %pad_maximum_fusion.3), channel_id=1, source_target_pairs={{4,0},{8,4},{12,8},{16,12},{20,16},{24,20},{28,24},{32,28},{36,32}... | collective-permute-start | bytes 1032200 | tf_op jit(solution)/shard_map/ppermute | solution.py:82
  7.9 0.4 slice_reduce_fusion.21
  8.3 0.1 constant_dynamic-slice_fusion
  8.4 0.1 copy.29
  8.5 0.4 slice_reduce_fusion.10
  9.0 1.5 %collective-permute-done = f32[2,8,21,256]{3,1,2,0:T(8,128)S(1)} collective-permute-done((f32[2,8,21,256]{3,1,2,0:T(8,128)S(1)}, f32[2,8,21,256]{3,1,2,0:T(8,128)S(1)}, u32[]{:S(2)}, u32[]{:S(2)}) %collective-permute-start) | collective-permute-done | bytes 344096 | tf_op jit(solution)/shard_map/ppermute | solution.py:81
  10.5 1.8 %collective-permute-done.1 = f32[2,8,21,256]{3,1,2,0:T(8,128)S(1)} collective-permute-done((f32[2,8,21,256]{3,1,2,0:T(8,128)S(1)}, f32[2,8,21,256]{3,1,2,0:T(8,128)S(1)}, u32[]{:S(2)}, u32[]{:S(2)}) %collective-permute-start.1) | collective-permute-done | bytes 344096 | tf_op jit(solution)/shard_map/ppermute | solution.py:82
  12.3 5.4 %fusion.75 = f32[1,8,96,256]{3,1,2,0:T(8,128)S(1)} fusion(f32[11]{0:T(128)S(1)} %get-tuple-element.17, f32[11]{0:T(128)S(1)} %get-tuple-element.18, f32[11]{0:T(128)S(1)} %get-tuple-element.19, f32[11]{0:T(128)S(1)} %get-tuple-element.20, f32[11]{0:T(128)S(1)} %get-tuple-element.21, f32[11]{0:T(128)S(1)} %get-tuple-element.22, ...), kind=kOutput, calls=%fused_computation.75 | convolution fusion | flops 3330252800 | bytes 2376164 | tf_op jit(solution)/shard_map/conv_general_dilated | solution.py:35
  17.8 5.6 %fusion.72 = f32[1,8,96,256]{3,1,2,0:T(8,128)S(1)} fusion(f32[11]{0:T(128)S(1)} %get-tuple-element.15, f32[11]{0:T(128)S(1)} %get-tuple-element.6, f32[11]{0:T(128)S(1)} %get-tuple-element.7, f32[11]{0:T(128)S(1)} %get-tuple-element.8, f32[11]{0:T(128)S(1)} %get-tuple-element.9, f32[11]{0:T(128)S(1)} %get-tuple-element.10, f32[11]{0:T(128)S(1)} %get-tuple-element.11, ...), kind=kOutput, calls=%fused_computation.74 | convolution fusion | flops 3330252800 | bytes 2376164 | tf_op jit(solution)/shard_map/conv_general_dilated | solution.py:35
  23.3 0.2 maximum_select_fusion
  23.5 0.1 fusion.82
  23.6 0.1 fusion.81
  23.7 0.1 fusion.80
  23.8 0.1 fusion.79
  23.8 0.1 fusion.78
  23.9 2.0 %fusion = f32[2,64,256,16,1]{2,3,0,1,4:T(8,128)S(1)} fusion(f32[2,5,8,64,256]{4,2,3,0,1:T(8,128)S(1)} %fusion.78, pred[5,8,16]{2,1,0:T(8,128)(4,1)S(1)} %constant_dynamic-update-slice_fusion), kind=kOutput, calls=%fused_computation | convolution fusion | flops 251658240 | bytes 7340672 | tf_op jit(solution)/shard_map/otk,cotrw->ckrw/dot_general | solution.py:103
  26.0 0.2 copy.37
  26.2 0.1 dynamic-slice_bitcast_fusion.2
  26.4 0.6 %collective-permute-start.2 = (f32[2,16,16,128]{3,1,2,0:T(8,128)S(1)}, f32[2,16,16,128]{3,1,2,0:T(8,128)S(1)}, u32[]{:S(2)}, u32[]{:S(2)}) collective-permute-start(f32[2,16,16,128]{3,1,2,0:T(8,128)S(1)} %get-tuple-element.32), channel_id=1, source_target_pairs={{0,1},{1,2},{2,3},{3,0},{4,5},{5,6},{6,7},{7,4},{8,9},{9,10},{10,1... | collective-permute-start | bytes 786440 | tf_op jit(solution)/shard_map/ppermute | solution.py:60
  26.9 1.5 %collective-permute-start.4 = (f32[2,16,16,128]{3,1,2,0:T(8,128)S(1)}, f32[2,16,16,128]{3,1,2,0:T(8,128)S(1)}, u32[]{:S(2)}, u32[]{:S(2)}) collective-permute-start(f32[2,16,16,128]{3,1,2,0:T(8,128)S(1)} %get-tuple-element.33), channel_id=1, source_target_pairs={{0,3},{1,0},{2,1},{3,2},{4,7},{5,4},{6,5},{7,6},{8,11},{9,8},{10,9... | collective-permute-start | bytes 786440 | tf_op jit(solution)/shard_map/ppermute | solution.py:61
  28.5 5.9 %collective-permute-done.2 = f32[2,16,16,128]{3,1,2,0:T(8,128)S(1)} collective-permute-done((f32[2,16,16,128]{3,1,2,0:T(8,128)S(1)}, f32[2,16,16,128]{3,1,2,0:T(8,128)S(1)}, u32[]{:S(2)}, u32[]{:S(2)}) %collective-permute-start.2) | collective-permute-done | bytes 262176 | tf_op jit(solution)/shard_map/ppermute | solution.py:60
  34.4 0.1 slice_add_fusion.1
  34.4 0.9 %pad_maximum_fusion = f32[2,16,16,256]{3,1,2,0:T(8,128)} fusion(f32[2,16,16,128]{3,1,2,0:T(8,128)S(1)} %get-tuple-element.31, f32[2,16,16,128]{3,1,2,0:T(8,128)S(1)} %get-tuple-element.30), kind=kLoop, calls=%fused_computation.96 | loop fusion | flops 131072 | bytes 1048576 | tf_op jit(solution)/shard_map/concatenate | solution.py:63
  35.3 1.7 %collective-permute-start.3 = (f32[2,16,16,256]{3,1,2,0:T(8,128)}, f32[2,16,16,256]{3,1,2,0:T(8,128)S(1)}, u32[]{:S(2)}, u32[]{:S(2)}) collective-permute-start(f32[2,16,16,256]{3,1,2,0:T(8,128)} %pad_maximum_fusion), channel_id=1, source_target_pairs={{0,1},{1,2},{2,3},{3,0},{4,5},{5,6},{6,7},{7,4},{8,9},{9,10},{10,1... | collective-permute-start | bytes 1572872 | tf_op jit(solution)/shard_map/ppermute | solution.py:66
  37.0 0.8 %pad_maximum_fusion.1 = f32[2,16,16,256]{3,1,2,0:T(8,128)} fusion(f32[2,16,16,128]{3,1,2,0:T(8,128)S(1)} %get-tuple-element.35, f32[2,16,16,128]{3,1,2,0:T(8,128)S(1)} %get-tuple-element.34), kind=kLoop, calls=%fused_computation.97 | loop fusion | flops 131072 | bytes 1048576 | tf_op jit(solution)/shard_map/concatenate | solution.py:65
  37.9 0.3 collective-permute-start.5
  38.2 11.8 %collective-permute-done.3 = f32[2,16,16,256]{3,1,2,0:T(8,128)S(1)} collective-permute-done((f32[2,16,16,256]{3,1,2,0:T(8,128)}, f32[2,16,16,256]{3,1,2,0:T(8,128)S(1)}, u32[]{:S(2)}, u32[]{:S(2)}) %collective-permute-start.3) | collective-permute-done | bytes 524320 | tf_op jit(solution)/shard_map/ppermute | solution.py:66
  50.0 3.9 %collective-permute-done.5 = f32[2,16,16,256]{3,1,2,0:T(8,128)S(1)} collective-permute-done((f32[2,16,16,256]{3,1,2,0:T(8,128)}, f32[2,16,16,256]{3,1,2,0:T(8,128)S(1)}, u32[]{:S(2)}, u32[]{:S(2)}) %collective-permute-start.5) | collective-permute-done | bytes 524320 | tf_op jit(solution)/shard_map/ppermute | solution.py:67
  53.9 0.1 fusion.93
  54.1 0.9 %copy.24 = f32[16,16,256]{2,1,0:T(8,128)} copy(f32[16,16,256]{2,0,1:T(8,128)S(1)} %fusion.95) | data formatting | bytes 524288 | tf_op jit(solution)/shard_map/div | solution.py:108
  (28 shorter events, 0.7 us)
Async XLA Ops:
  0.0 8.3 %copy-start = (s32[32,16]{0,1:T(8,128)S(1)}, s32[32,16]{0,1:T(8,128)}, u32[]{:S(2)}) copy-start(s32[32,16]{0,1:T(8,128)} %param.7) | copy-start | bytes 6148
  0.0 7.9 %copy-start.1 = (f32[11,11]{1,0:T(8,128)S(1)}, f32[11,11]{1,0:T(8,128)}, u32[]{:S(2)}) copy-start(f32[11,11]{1,0:T(8,128)} %param.6) | copy-start | bytes 1456
  1.9 8.6 %collective-permute-start = (f32[2,8,21,256]{3,1,2,0:T(8,128)S(1)}, f32[2,8,21,256]{3,1,2,0:T(8,128)S(1)}, u32[]{:S(2)}, u32[]{:S(2)}) collective-permute-start(f32[2,8,21,256]{3,1,2,0:T(8,128)S(1)} %pad_maximum_fusion.2), channel_id=1, source_target_pairs={{0,4},{4,8},{8,12},{12,16},{16,20},{20,24},{24,28},{28,32},{32,36}... | collective-permute-start | bytes 1032200 | tf_op jit(solution)/shard_map/ppermute | solution.py:81
  3.9 8.4 %collective-permute-start.1 = (f32[2,8,21,256]{3,1,2,0:T(8,128)S(1)}, f32[2,8,21,256]{3,1,2,0:T(8,128)S(1)}, u32[]{:S(2)}, u32[]{:S(2)}) collective-permute-start(f32[2,8,21,256]{3,1,2,0:T(8,128)S(1)} %pad_maximum_fusion.3), channel_id=1, source_target_pairs={{4,0},{8,4},{12,8},{16,12},{20,16},{24,20},{28,24},{32,28},{36,32}... | collective-permute-start | bytes 1032200 | tf_op jit(solution)/shard_map/ppermute | solution.py:82
  26.4 8.0 %collective-permute-start.2 = (f32[2,16,16,128]{3,1,2,0:T(8,128)S(1)}, f32[2,16,16,128]{3,1,2,0:T(8,128)S(1)}, u32[]{:S(2)}, u32[]{:S(2)}) collective-permute-start(f32[2,16,16,128]{3,1,2,0:T(8,128)S(1)} %get-tuple-element.32), channel_id=1, source_target_pairs={{0,1},{1,2},{2,3},{3,0},{4,5},{5,6},{6,7},{7,4},{8,9},{9,10},{10,1... | collective-permute-start | bytes 786440 | tf_op jit(solution)/shard_map/ppermute | solution.py:60
  26.9 10.1 %collective-permute-start.4 = (f32[2,16,16,128]{3,1,2,0:T(8,128)S(1)}, f32[2,16,16,128]{3,1,2,0:T(8,128)S(1)}, u32[]{:S(2)}, u32[]{:S(2)}) collective-permute-start(f32[2,16,16,128]{3,1,2,0:T(8,128)S(1)} %get-tuple-element.33), channel_id=1, source_target_pairs={{0,3},{1,0},{2,1},{3,2},{4,7},{5,4},{6,5},{7,6},{8,11},{9,8},{10,9... | collective-permute-start | bytes 786440 | tf_op jit(solution)/shard_map/ppermute | solution.py:61
  35.3 14.7 %collective-permute-start.3 = (f32[2,16,16,256]{3,1,2,0:T(8,128)}, f32[2,16,16,256]{3,1,2,0:T(8,128)S(1)}, u32[]{:S(2)}, u32[]{:S(2)}) collective-permute-start(f32[2,16,16,256]{3,1,2,0:T(8,128)} %pad_maximum_fusion), channel_id=1, source_target_pairs={{0,1},{1,2},{2,3},{3,0},{4,5},{5,6},{6,7},{7,4},{8,9},{9,10},{10,1... | collective-permute-start | bytes 1572872 | tf_op jit(solution)/shard_map/ppermute | solution.py:66
  37.9 16.0 %collective-permute-start.5 = (f32[2,16,16,256]{3,1,2,0:T(8,128)}, f32[2,16,16,256]{3,1,2,0:T(8,128)S(1)}, u32[]{:S(2)}, u32[]{:S(2)}) collective-permute-start(f32[2,16,16,256]{3,1,2,0:T(8,128)} %pad_maximum_fusion.1), channel_id=1, source_target_pairs={{0,3},{1,0},{2,1},{3,2},{4,7},{5,4},{6,5},{7,6},{8,11},{9,8},{10,9... | collective-permute-start | bytes 1572872 | tf_op jit(solution)/shard_map/ppermute | solution.py:67

commit v14 on v13

--- a/solution.py
+++ b/solution.py
@@ -80,13 +80,19 @@
     backward = [(target, source) for source, target in forward]
     low = lax.ppermute(jnp.stack([science[:, rows - width :], inv_variance[:, rows - width :]]), "sky", forward)
     high = lax.ppermute(jnp.stack([science[:, :width], inv_variance[:, :width]]), "sky", backward)
-    bordered = [
-        jnp.concatenate([low[0] * low[1], science * inv_variance, high[0] * high[1]], axis=1),
-        jnp.concatenate([low[1], inv_variance, high[1]], axis=1),
-    ]
+    own = [science * inv_variance, inv_variance]
+    lows = [low[0] * low[1], low[1]]
+    highs = [high[0] * high[1], high[1]]
+    reach_in = 2 * radius
 
-    psi = correlate_rows(bordered[0], toeplitz(psf_kernel, cols))
-    phi = correlate_rows(bordered[1], toeplitz(psf_kernel * psf_kernel, cols))
+    def correlated(c, kernel):
+        interior = correlate_rows(own[c], kernel)
+        top = correlate_rows(jnp.concatenate([lows[c], own[c][:, :reach_in]], axis=1), kernel)
+        bottom = correlate_rows(jnp.concatenate([own[c][:, rows - reach_in :], highs[c]], axis=1), kernel)
+        return jnp.concatenate([top, interior, bottom], axis=1)
+
+    psi = correlated(0, toeplitz(psf_kernel, cols))
+    phi = correlated(1, toeplitz(psf_kernel * psf_kernel, cols))
     images = jnp.stack([psi, phi])
 
     first = lax.axis_index("sky") * rows - reach

time: 55.2 us -> 71.9 us (1.30); the launches traced: 55 us -> 70.6 us
  matrix products: 13 us -> 25.8 us
  waiting for transfers between devices: 24.9 us -> 20.6 us
  other arithmetic: 4.51 us -> 8.7 us
  local copies, waits for them, and re-layouts: 2.56 us -> 5.14 us
    conv_general_dilated x2 -> x6, matrix products: 11 us -> 22.9 us  [correlate_rows(): lax.conv_general_dilated(bordered, kernel, window_strides=(1,), padding='...]
    unnamed x4, other arithmetic: 0.04 us -> 2.29 us
    ppermute x1, waiting for transfers between devices: 1.77 us -> 0.01 us  [shards(): lax.ppermute(jnp.stack([science[:, :width], inv_variance[:, :width]]), 's...]
    ppermute x1, waiting for transfers between devices: 1.55 us -> 0.01 us  [shards(): lax.ppermute(jnp.stack([science[:, rows - width:], inv_variance[:, rows -...]
    eq x6, other arithmetic: 0.32 us -> 1.57 us  [toeplitz(): out = jnp.where(tap == b, taps[:, b][:, None, None], out)]
    ppermute x1, waiting for transfers between devices: 11.8 us -> 10.6 us  [ring_reduce_scatter(): got_left = lax.ppermute(ahead, axis, right)]
    slice x2, local copies, waits for them, and re-layouts: 0.74 us -> 1.89 us  [toeplitz(): out = jnp.where(tap == b, taps[:, b][:, None, None], out)]
    dot_general x1, matrix products: 2.03 us -> 2.86 us  [shards(): jnp.einsum('otk,cotrw->ckrw', onehot, windows, precision=lax.Precision.HI...]
  transfers between devices with their start and end apart: 6 -> 6, of which waited for: 5 -> 3; matrix products, arithmetic and copies ran while one was open for 6% -> 32% of each run, Pallas kernels for 0% -> 0%
where the time goes in v14:
time: 71.9 us; the launch traced here: 70.6 us
  matrix products  25.8 us (36%)
  waiting for transfers between devices  20.6 us (29%)
  starting transfers between devices  9.69 us (13%)
  other arithmetic  8.7 us (12%)
  local copies, waits for them, and re-layouts  5.14 us (7%)
    conv_general_dilated x6, matrix products, correlate_rows(): lax.conv_general_dilated(bordered, kernel, window_strides=(1,), padding='...  22.9 us
    ppermute x1, waiting for transfers between devices, ring_reduce_scatter(): got_left = lax.ppermute(ahead, axis, right)  10.6 us
    ppermute x1, waiting for transfers between devices, ring_reduce_scatter(): from_left = lax.ppermute(far[..., :half], axis, right)  6.48 us
    ppermute x1, starting transfers between devices, shards(): lax.ppermute(jnp.stack([science[:, :width], inv_variance[:, :width]]), 's...  3.64 us
    ppermute x1, waiting for transfers between devices, ring_reduce_scatter(): got_right = lax.ppermute(behind, axis, left)  3.51 us
    dot_general x1, matrix products, shards(): jnp.einsum('otk,cotrw->ckrw', onehot, windows, precision=lax.Precision.HI...  2.86 us
    unnamed x4, other arithmetic  2.29 us
    ppermute x1, starting transfers between devices, shards(): lax.ppermute(jnp.stack([science[:, rows - width:], inv_variance[:, rows -...  1.92 us
  transfers between devices with their start and end apart: 6, of which 3 were waited for; matrix products, arithmetic and copies ran while one was open for 32% of the time, Pallas kernels for 0%

profile of v14, /device:TPU:54, one launch (start us, length us, event | category | flops | bytes accessed | tf_op | source)
XLA Modules:
  0.0 70.6 jit_solution(11635505249650721354)
XLA Ops:
  0.0 1.9 %copy_multiply_fusion = (f32[8,64,256]{2,0,1:T(8,128)S(1)}, f32[8,64,256]{2,0,1:T(8,128)S(1)}, f32[8,64,256]{2,0,1:T(8,128)S(1)}) fusion(f32[8,64,256]{2,1,0:T(8,128)} %param.4, f32[8,64,256]{2,1,0:T(8,128)} %param.5), kind=kLoop, calls=%fused_computation.250 | loop fusion | flops 131072 | bytes 2621440 | tf_op jit(solution)/shard_map/mul | solution.py:83
  2.0 1.9 %collective-permute-start = (f32[2,8,21,256]{3,1,2,0:T(8,128)S(1)}, f32[2,8,21,256]{3,1,2,0:T(8,128)S(1)}, u32[]{:S(2)}, u32[]{:S(2)}) collective-permute-start(f32[2,8,21,256]{3,1,2,0:T(8,128)S(1)} %pad_maximum_fusion.2), channel_id=1, source_target_pairs={{0,4},{4,8},{8,12},{12,16},{16,20},{20,24},{24,28},{28,32},{32,36}... | collective-permute-start | bytes 1032200 | tf_op jit(solution)/shard_map/ppermute | solution.py:81
  4.0 3.6 %collective-permute-start.1 = (f32[2,8,21,256]{3,1,2,0:T(8,128)S(1)}, f32[2,8,21,256]{3,1,2,0:T(8,128)S(1)}, u32[]{:S(2)}, u32[]{:S(2)}) collective-permute-start(f32[2,8,21,256]{3,1,2,0:T(8,128)S(1)} %pad_maximum_fusion.3), channel_id=1, source_target_pairs={{4,0},{8,4},{12,8},{16,12},{20,16},{24,20},{28,24},{32,28},{36,32}... | collective-permute-start | bytes 1032200 | tf_op jit(solution)/shard_map/ppermute | solution.py:82
  7.9 0.7 fusion.162
  8.5 0.7 fusion.164
  9.2 1.0 %slice_reduce_fusion.21 = (f32[11]{0:T(128)}, f32[11]{0:T(128)}, f32[11]{0:T(128)}, f32[11]{0:T(128)}, f32[11]{0:T(128)}, /*index=5*/f32[11]{0:T(128)}, f32[11]{...) fusion(f32[11,11]{1,0:T(8,128)S(1)} %copy-done.1), kind=kLoop, calls=%fused_computation.237 | loop fusion | bytes 968 | tf_op jit(solution)/shard_map/slice | solution.py:30
  10.2 0.9 %slice_reduce_fusion.10 = (f32[11]{0:T(128)}, f32[11]{0:T(128)}, f32[11]{0:T(128)}, f32[11]{0:T(128)}, f32[11]{0:T(128)}, /*index=5*/f32[11]{0:T(128)}, f32[11]{...) fusion(f32[11,11]{1,0:T(8,128)S(1)} %mul.34), kind=kLoop, calls=%fused_computation.226 | loop fusion | bytes 968 | tf_op jit(solution)/shard_map/slice | solution.py:30
  11.1 0.7 constant_dynamic-slice_fusion
  11.8 0.8 %copy.33 = s32[8,16]{1,0:T(8,128)S(1)} copy(s32[8,16]{0,1:T(8,128)} %constant_dynamic-slice_fusion) | data formatting | bytes 1024
  12.5 0.5 constant_dynamic-update-slice_fusion.4
  13.1 0.6 constant_dynamic-update-slice_fusion.3
  13.6 0.6 constant_dynamic-update-slice_fusion.2
  14.2 0.6 constant_dynamic-update-slice_fusion.1
  14.8 0.6 constant_dynamic-update-slice_fusion
  15.5 5.3 %fusion.6 = f32[8,54,256]{2,0,1:T(8,128)S(1)} fusion(f32[11]{0:T(128)} %get-tuple-element.17, f32[11]{0:T(128)} %get-tuple-element.18, f32[11]{0:T(128)} %get-tuple-element.19, f32[11]{0:T(128)} %get-tuple-element.20, f32[11]{0:T(128)} %get-tuple-element.21, f32[11]{0:T(128)} %get-tuple-element.22, f32[11]{0:T(128)} %get-tuple-element.23, ...), kind=kOutput, calls=%fused_computation.9 | convolution fusion | flops 1876492288 | bytes 1688036 | tf_op jit(solution)/shard_map/conv_general_dilated | solution.py:35
  21.0 4.2 %fusion.3 = f32[8,54,256]{2,0,1:T(8,128)S(1)} fusion(f32[8,64,256]{2,0,1:T(8,128)S(1)} %get-tuple-element.38, f32[11]{0:T(128)S(1)} %copy-done.15, f32[11]{0:T(128)S(1)} %copy-done.6, f32[11]{0:T(128)S(1)} %copy-done.7, f32[11]{0:T(128)S(1)} %copy-done.8, f32[11]{0:T(128)S(1)} %copy-done.9, f32[11]{0:T(128)S(1)} %copy-done.10, f32[11]{0:T(128)S(1)} %copy-done.11, ...), kind=kOutput, calls=%fused_computation.6 | convolution fusion | flops 1876492288 | bytes 1688036 | tf_op jit(solution)/shard_map/conv_general_dilated | solution.py:35
  25.2 3.5 %fusion.4 = f32[8,21,256]{2,0,1:T(8,128)S(1)} fusion(f32[11]{0:T(128)S(1)} %copy-done.15, f32[11]{0:T(128)S(1)} %copy-done.6, f32[11]{0:T(128)S(1)} %copy-done.7, f32[11]{0:T(128)S(1)} %copy-done.8, f32[11]{0:T(128)S(1)} %copy-done.9, f32[11]{0:T(128)S(1)} %copy-done.10, f32[11]{0:T(128)S(1)} %copy-done.11, f32[11]{0:T(128)S(1)} %copy-done.12, ...), kind=kOutput, calls=%fused_computation.7 | convolution fusion | flops 734656512 | bytes 1147364 | tf_op jit(solution)/shard_map/conv_general_dilated | solution.py:35
  28.9 3.3 %fusion.2 = f32[8,21,256]{2,0,1:T(8,128)S(1)} fusion(f32[11]{0:T(128)S(1)} %copy-done.15, f32[11]{0:T(128)S(1)} %copy-done.6, f32[11]{0:T(128)S(1)} %copy-done.7, f32[11]{0:T(128)S(1)} %copy-done.8, f32[11]{0:T(128)S(1)} %copy-done.9, f32[11]{0:T(128)S(1)} %copy-done.10, f32[11]{0:T(128)S(1)} %copy-done.11, f32[11]{0:T(128)S(1)} %copy-done.12, ...), kind=kOutput, calls=%fused_computation.5 | convolution fusion | flops 734656512 | bytes 1147364 | tf_op jit(solution)/shard_map/conv_general_dilated | solution.py:35
  32.3 3.3 %fusion.7 = f32[8,21,256]{2,0,1:T(8,128)S(1)} fusion(f32[11]{0:T(128)S(1)} %copy-done.17, f32[11]{0:T(128)S(1)} %copy-done.18, f32[11]{0:T(128)S(1)} %copy-done.19, f32[11]{0:T(128)S(1)} %copy-done.20, f32[11]{0:T(128)S(1)} %copy-done.21, f32[11]{0:T(128)S(1)} %copy-done.22, f32[11]{0:T(128)S(1)} %copy-done.23, f32[11]{0:T(128)S(1)} %copy-done.24, ...), kind=kOutput, calls=%fused_computation.10 | convolution fusion | flops 734656512 | bytes 1147364 | tf_op jit(solution)/shard_map/conv_general_dilated | solution.py:35
  35.7 3.3 %fusion.5 = f32[8,21,256]{2,0,1:T(8,128)S(1)} fusion(f32[11]{0:T(128)S(1)} %copy-done.17, f32[11]{0:T(128)S(1)} %copy-done.18, f32[11]{0:T(128)S(1)} %copy-done.19, f32[11]{0:T(128)S(1)} %copy-done.20, f32[11]{0:T(128)S(1)} %copy-done.21, f32[11]{0:T(128)S(1)} %copy-done.22, f32[11]{0:T(128)S(1)} %copy-done.23, f32[11]{0:T(128)S(1)} %copy-done.24, ...), kind=kOutput, calls=%fused_computation.8 | convolution fusion | flops 734656512 | bytes 1147364 | tf_op jit(solution)/shard_map/conv_general_dilated | solution.py:35
  39.7 2.9 %fusion = f32[2,64,256,16,1]{2,3,0,1,4:T(8,128)S(1)} fusion(f32[2,5,8,64,256]{4,2,3,0,1:T(8,128)S(1)} %fusion.146, pred[5,8,16]{2,1,0:T(8,128)(4,1)} %constant_dynamic-update-slice_fusion), kind=kOutput, calls=%fused_computation | convolution fusion | flops 251658240 | bytes 7340672 | tf_op jit(solution)/shard_map/otk,cotrw->ckrw/dot_general | solution.py:109
  42.6 0.2 copy.43
  43.0 0.6 collective-permute-start.2
  43.5 1.5 %collective-permute-start.4 = (f32[2,16,16,128]{3,1,2,0:T(8,128)S(1)}, f32[2,16,16,128]{3,1,2,0:T(8,128)S(1)}, u32[]{:S(2)}, u32[]{:S(2)}) collective-permute-start(f32[2,16,16,128]{3,1,2,0:T(8,128)S(1)} %get-tuple-element.33), channel_id=1, source_target_pairs={{0,3},{1,0},{2,1},{3,2},{4,7},{5,4},{6,5},{7,6},{8,11},{9,8},{10,9... | collective-permute-start | bytes 786440 | tf_op jit(solution)/shard_map/ppermute | solution.py:61
  45.1 6.5 %collective-permute-done.2 = f32[2,16,16,128]{3,1,2,0:T(8,128)S(1)} collective-permute-done((f32[2,16,16,128]{3,1,2,0:T(8,128)S(1)}, f32[2,16,16,128]{3,1,2,0:T(8,128)S(1)}, u32[]{:S(2)}, u32[]{:S(2)}) %collective-permute-start.2) | collective-permute-done | bytes 262176 | tf_op jit(solution)/shard_map/ppermute | solution.py:60
  51.6 0.9 %pad_maximum_fusion = f32[2,16,16,256]{3,1,2,0:T(8,128)} fusion(f32[2,16,16,128]{3,1,2,0:T(8,128)S(1)} %get-tuple-element.31, f32[2,16,16,128]{3,1,2,0:T(8,128)S(1)} %get-tuple-element.30), kind=kLoop, calls=%fused_computation.162 | loop fusion | flops 131072 | bytes 1048576 | tf_op jit(solution)/shard_map/concatenate | solution.py:63
  52.5 1.7 %collective-permute-start.3 = (f32[2,16,16,256]{3,1,2,0:T(8,128)}, f32[2,16,16,256]{3,1,2,0:T(8,128)S(1)}, u32[]{:S(2)}, u32[]{:S(2)}) collective-permute-start(f32[2,16,16,256]{3,1,2,0:T(8,128)} %pad_maximum_fusion), channel_id=1, source_target_pairs={{0,1},{1,2},{2,3},{3,0},{4,5},{5,6},{6,7},{7,4},{8,9},{9,10},{10,1... | collective-permute-start | bytes 1572872 | tf_op jit(solution)/shard_map/ppermute | solution.py:66
  54.2 0.8 %pad_maximum_fusion.1 = f32[2,16,16,256]{3,1,2,0:T(8,128)} fusion(f32[2,16,16,128]{3,1,2,0:T(8,128)S(1)} %get-tuple-element.35, f32[2,16,16,128]{3,1,2,0:T(8,128)S(1)} %get-tuple-element.34), kind=kLoop, calls=%fused_computation.163 | loop fusion | flops 131072 | bytes 1048576 | tf_op jit(solution)/shard_map/concatenate | solution.py:65
  55.1 0.3 collective-permute-start.5
  55.4 10.6 %collective-permute-done.3 = f32[2,16,16,256]{3,1,2,0:T(8,128)S(1)} collective-permute-done((f32[2,16,16,256]{3,1,2,0:T(8,128)}, f32[2,16,16,256]{3,1,2,0:T(8,128)S(1)}, u32[]{:S(2)}, u32[]{:S(2)}) %collective-permute-start.3) | collective-permute-done | bytes 524320 | tf_op jit(solution)/shard_map/ppermute | solution.py:66
  66.0 3.5 %collective-permute-done.5 = f32[2,16,16,256]{3,1,2,0:T(8,128)S(1)} collective-permute-done((f32[2,16,16,256]{3,1,2,0:T(8,128)}, f32[2,16,16,256]{3,1,2,0:T(8,128)S(1)}, u32[]{:S(2)}, u32[]{:S(2)}) %collective-permute-start.5) | collective-permute-done | bytes 524320 | tf_op jit(solution)/shard_map/ppermute | solution.py:67
  69.7 0.9 %copy.28 = f32[16,16,256]{2,1,0:T(8,128)} copy(f32[16,16,256]{2,0,1:T(8,128)S(1)} %fusion.153) | data formatting | bytes 524288 | tf_op jit(solution)/shard_map/div | solution.py:114
  (85 shorter events, 1.7 us)
Async XLA Ops:
  0.0 11.1 %copy-start = (s32[32,16]{0,1:T(8,128)S(1)}, s32[32,16]{0,1:T(8,128)}, u32[]{:S(2)}) copy-start(s32[32,16]{0,1:T(8,128)} %param.7) | copy-start | bytes 6148
  0.0 15.4 %copy-start.2 = (f32[8,64,256]{2,1,0:T(8,128)S(1)}, f32[8,64,256]{2,1,0:T(8,128)}, u32[]{:S(2)}) copy-start(f32[8,64,256]{2,1,0:T(8,128)} %param.5) | copy-start | bytes 1572868
  0.0 9.2 %copy-start.1 = (f32[11,11]{1,0:T(8,128)S(1)}, f32[11,11]{1,0:T(8,128)}, u32[]{:S(2)}) copy-start(f32[11,11]{1,0:T(8,128)} %param.6) | copy-start | bytes 1456
  2.0 23.2 %collective-permute-start = (f32[2,8,21,256]{3,1,2,0:T(8,128)S(1)}, f32[2,8,21,256]{3,1,2,0:T(8,128)S(1)}, u32[]{:S(2)}, u32[]{:S(2)}) collective-permute-start(f32[2,8,21,256]{3,1,2,0:T(8,128)S(1)} %pad_maximum_fusion.2), channel_id=1, source_target_pairs={{0,4},{4,8},{8,12},{12,16},{16,20},{20,24},{24,28},{28,32},{32,36}... | collective-permute-start | bytes 1032200 | tf_op jit(solution)/shard_map/ppermute | solution.py:81
  4.0 24.8 %collective-permute-start.1 = (f32[2,8,21,256]{3,1,2,0:T(8,128)S(1)}, f32[2,8,21,256]{3,1,2,0:T(8,128)S(1)}, u32[]{:S(2)}, u32[]{:S(2)}) collective-permute-start(f32[2,8,21,256]{3,1,2,0:T(8,128)S(1)} %pad_maximum_fusion.3), channel_id=1, source_target_pairs={{4,0},{8,4},{12,8},{16,12},{20,16},{24,20},{28,24},{32,28},{36,32}... | collective-permute-start | bytes 1032200 | tf_op jit(solution)/shard_map/ppermute | solution.py:82
  15.4 5.4 %copy-start.3 = (pred[256,256]{1,0:T(8,128)(4,1)S(1)}, pred[256,256]{1,0:T(8,128)(4,1)}, u32[]{:S(2)}) copy-start(pred[256,256]{1,0:T(8,128)(4,1)} %get-tuple-element.60) | copy-start | bytes 196612
  15.4 5.4 %copy-start.4 = (pred[256,256]{1,0:T(8,128)(4,1)S(1)}, pred[256,256]{1,0:T(8,128)(4,1)}, u32[]{:S(2)}) copy-start(pred[256,256]{1,0:T(8,128)(4,1)} %fusion.164) | copy-start | bytes 196612
  15.4 5.5 %copy-start.5 = (f32[11]{0:T(128)S(1)}, f32[11]{0:T(128)}, u32[]{:S(2)}) copy-start(f32[11]{0:T(128)} %get-tuple-element.5) | copy-start | bytes 136
  15.4 5.5 %copy-start.6 = (f32[11]{0:T(128)S(1)}, f32[11]{0:T(128)}, u32[]{:S(2)}) copy-start(f32[11]{0:T(128)} %get-tuple-element.6) | copy-start | bytes 136
  15.4 5.5 %copy-start.7 = (f32[11]{0:T(128)S(1)}, f32[11]{0:T(128)}, u32[]{:S(2)}) copy-start(f32[11]{0:T(128)} %get-tuple-element.7) | copy-start | bytes 136
  15.4 5.5 %copy-start.8 = (f32[11]{0:T(128)S(1)}, f32[11]{0:T(128)}, u32[]{:S(2)}) copy-start(f32[11]{0:T(128)} %get-tuple-element.8) | copy-start | bytes 136
  15.4 5.5 %copy-start.9 = (f32[11]{0:T(128)S(1)}, f32[11]{0:T(128)}, u32[]{:S(2)}) copy-start(f32[11]{0:T(128)} %get-tuple-element.9) | copy-start | bytes 136
  15.4 5.5 %copy-start.10 = (f32[11]{0:T(128)S(1)}, f32[11]{0:T(128)}, u32[]{:S(2)}) copy-start(f32[11]{0:T(128)} %get-tuple-element.10) | copy-start | bytes 136
  15.4 5.5 %copy-start.11 = (f32[11]{0:T(128)S(1)}, f32[11]{0:T(128)}, u32[]{:S(2)}) copy-start(f32[11]{0:T(128)} %get-tuple-element.11) | copy-start | bytes 136
  15.5 5.5 %copy-start.12 = (f32[11]{0:T(128)S(1)}, f32[11]{0:T(128)}, u32[]{:S(2)}) copy-start(f32[11]{0:T(128)} %get-tuple-element.12) | copy-start | bytes 136
  15.5 5.5 %copy-start.13 = (f32[11]{0:T(128)S(1)}, f32[11]{0:T(128)}, u32[]{:S(2)}) copy-start(f32[11]{0:T(128)} %get-tuple-element.13) | copy-start | bytes 136
  15.5 5.5 %copy-start.14 = (f32[11]{0:T(128)S(1)}, f32[11]{0:T(128)}, u32[]{:S(2)}) copy-start(f32[11]{0:T(128)} %get-tuple-element.14) | copy-start | bytes 136
  15.5 5.5 %copy-start.15 = (f32[11]{0:T(128)S(1)}, f32[11]{0:T(128)}, u32[]{:S(2)}) copy-start(f32[11]{0:T(128)} %get-tuple-element.15) | copy-start | bytes 136
  28.8 3.4 %copy-start.16 = (f32[11]{0:T(128)S(1)}, f32[11]{0:T(128)}, u32[]{:S(2)}) copy-start(f32[11]{0:T(128)} %get-tuple-element.16) | copy-start | bytes 136
  28.8 3.4 %copy-start.17 = (f32[11]{0:T(128)S(1)}, f32[11]{0:T(128)}, u32[]{:S(2)}) copy-start(f32[11]{0:T(128)} %get-tuple-element.17) | copy-start | bytes 136
  28.8 3.4 %copy-start.18 = (f32[11]{0:T(128)S(1)}, f32[11]{0:T(128)}, u32[]{:S(2)}) copy-start(f32[11]{0:T(128)} %get-tuple-element.18) | copy-start | bytes 136
  28.8 3.4 %copy-start.19 = (f32[11]{0:T(128)S(1)}, f32[11]{0:T(128)}, u32[]{:S(2)}) copy-start(f32[11]{0:T(128)} %get-tuple-element.19) | copy-start | bytes 136
  28.8 3.4 %copy-start.20 = (f32[11]{0:T(128)S(1)}, f32[11]{0:T(128)}, u32[]{:S(2)}) copy-start(f32[11]{0:T(128)} %get-tuple-element.20) | copy-start | bytes 136
  28.8 3.4 %copy-start.21 = (f32[11]{0:T(128)S(1)}, f32[11]{0:T(128)}, u32[]{:S(2)}) copy-start(f32[11]{0:T(128)} %get-tuple-element.21) | copy-start | bytes 136
  28.8 3.4 %copy-start.22 = (f32[11]{0:T(128)S(1)}, f32[11]{0:T(128)}, u32[]{:S(2)}) copy-start(f32[11]{0:T(128)} %get-tuple-element.22) | copy-start | bytes 136
  28.8 3.4 %copy-start.23 = (f32[11]{0:T(128)S(1)}, f32[11]{0:T(128)}, u32[]{:S(2)}) copy-start(f32[11]{0:T(128)} %get-tuple-element.23) | copy-start | bytes 136
  28.9 3.4 %copy-start.24 = (f32[11]{0:T(128)S(1)}, f32[11]{0:T(128)}, u32[]{:S(2)}) copy-start(f32[11]{0:T(128)} %get-tuple-element.24) | copy-start | bytes 136
  28.9 3.4 %copy-start.25 = (f32[11]{0:T(128)S(1)}, f32[11]{0:T(128)}, u32[]{:S(2)}) copy-start(f32[11]{0:T(128)} %get-tuple-element.25) | copy-start | bytes 136
  43.0 8.6 %collective-permute-start.2 = (f32[2,16,16,128]{3,1,2,0:T(8,128)S(1)}, f32[2,16,16,128]{3,1,2,0:T(8,128)S(1)}, u32[]{:S(2)}, u32[]{:S(2)}) collective-permute-start(f32[2,16,16,128]{3,1,2,0:T(8,128)S(1)} %get-tuple-element.32), channel_id=1, source_target_pairs={{0,1},{1,2},{2,3},{3,0},{4,5},{5,6},{6,7},{7,4},{8,9},{9,10},{10,1... | collective-permute-start | bytes 786440 | tf_op jit(solution)/shard_map/ppermute | solution.py:60
  43.5 10.6 %collective-permute-start.4 = (f32[2,16,16,128]{3,1,2,0:T(8,128)S(1)}, f32[2,16,16,128]{3,1,2,0:T(8,128)S(1)}, u32[]{:S(2)}, u32[]{:S(2)}) collective-permute-start(f32[2,16,16,128]{3,1,2,0:T(8,128)S(1)} %get-tuple-element.33), channel_id=1, source_target_pairs={{0,3},{1,0},{2,1},{3,2},{4,7},{5,4},{6,5},{7,6},{8,11},{9,8},{10,9... | collective-permute-start | bytes 786440 | tf_op jit(solution)/shard_map/ppermute | solution.py:61
  52.5 13.5 %collective-permute-start.3 = (f32[2,16,16,256]{3,1,2,0:T(8,128)}, f32[2,16,16,256]{3,1,2,0:T(8,128)S(1)}, u32[]{:S(2)}, u32[]{:S(2)}) collective-permute-start(f32[2,16,16,256]{3,1,2,0:T(8,128)} %pad_maximum_fusion), channel_id=1, source_target_pairs={{0,1},{1,2},{2,3},{3,0},{4,5},{5,6},{6,7},{7,4},{8,9},{9,10},{10,1... | collective-permute-start | bytes 1572872 | tf_op jit(solution)/shard_map/ppermute | solution.py:66
  55.1 14.5 %collective-permute-start.5 = (f32[2,16,16,256]{3,1,2,0:T(8,128)}, f32[2,16,16,256]{3,1,2,0:T(8,128)S(1)}, u32[]{:S(2)}, u32[]{:S(2)}) collective-permute-start(f32[2,16,16,256]{3,1,2,0:T(8,128)} %pad_maximum_fusion.1), channel_id=1, source_target_pairs={{0,3},{1,0},{2,1},{3,2},{4,7},{5,4},{6,5},{7,6},{8,11},{9,8},{10,9... | collective-permute-start | bytes 1572872 | tf_op jit(solution)/shard_map/ppermute | solution.py:67
  (1 other events, 3.4 us)

commit v15 on v13

--- a/solution.py
+++ b/solution.py
@@ -59,13 +59,12 @@
     far = block(2)
     from_left = lax.ppermute(far[..., :half], axis, right)
     from_right = lax.ppermute(far[..., half:], axis, left)
-    ahead = block(1)
-    ahead = jnp.concatenate([ahead[..., :half] + from_left, ahead[..., half:]], axis=-1)
-    behind = block(count - 1)
-    behind = jnp.concatenate([behind[..., :half], behind[..., half:] + from_right], axis=-1)
-    got_left = lax.ppermute(ahead, axis, right)
-    got_right = lax.ppermute(behind, axis, left)
-    return block(0) + got_left + got_right
+    ahead, behind = block(1), block(count - 1)
+    left_low = lax.ppermute(ahead[..., :half] + from_left, axis, right)
+    left_high = lax.ppermute(ahead[..., half:], axis, right)
+    right_low = lax.ppermute(behind[..., :half], axis, left)
+    right_high = lax.ppermute(behind[..., half:] + from_right, axis, left)
+    return block(0) + jnp.concatenate([left_low + right_low, left_high + right_high], axis=-1)
 
 
 def shards(science, inv_variance, psf_kernel, offsets):

time: 55.2 us -> 58 us (1.051)
  the two profiles are of different devices: /device:TPU:54 before, /device:TPU:168 now
where the time goes in v15:
time: 58 us; the launch traced here: 57.8 us
  waiting for transfers between devices  21.1 us (36%)
  starting transfers between devices  15.4 us (27%)
  matrix products  13 us (22%)
  other arithmetic  5.46 us (9%)
  local copies, waits for them, and re-layouts  2.56 us (4%)
    conv_general_dilated x2, matrix products, correlate_rows(): lax.conv_general_dilated(bordered, kernel, window_strides=(1,), padding='...  10.9 us
    ppermute x1, waiting for transfers between devices, ring_reduce_scatter(): from_right = lax.ppermute(far[..., half:], axis, left)  6.37 us
    ppermute x1, waiting for transfers between devices, ring_reduce_scatter(): left_low = lax.ppermute(ahead[..., :half] + from_left, axis, right)  4.91 us
    ppermute x1, waiting for transfers between devices, ring_reduce_scatter(): left_high = lax.ppermute(ahead[..., half:], axis, right)  3.79 us
    ppermute x1, starting transfers between devices, ring_reduce_scatter(): right_low = lax.ppermute(behind[..., :half], axis, left)  3.77 us
    ppermute x1, starting transfers between devices, shards(): lax.ppermute(jnp.stack([science[:, :width], inv_variance[:, :width]]), 's...  3.64 us
    ppermute x1, starting transfers between devices, ring_reduce_scatter(): right_high = lax.ppermute(behind[..., half:] + from_right, axis, left)  3.23 us
    ppermute x1, starting transfers between devices, ring_reduce_scatter(): from_right = lax.ppermute(far[..., half:], axis, left)  2.84 us
  transfers between devices with their start and end apart: 8, of which 7 were waited for; matrix products, arithmetic and copies ran while one was open for 5% of the time, Pallas kernels for 0%

profile of v15, /device:TPU:168, one launch (start us, length us, event | category | flops | bytes accessed | tf_op | source)
XLA Modules:
  0.0 57.8 jit_solution(4834828156816694958)
XLA Ops:
  0.0 1.8 %copy_multiply_fusion = (f32[8,64,256]{2,0,1:T(8,128)S(1)}, f32[8,64,256]{2,0,1:T(8,128)S(1)}, f32[8,64,256]{2,0,1:T(8,128)S(1)}) fusion(f32[8,64,256]{2,1,0:T(8,128)} %param.5, f32[8,64,256]{2,1,0:T(8,128)} %param.4), kind=kLoop, calls=%fused_computation.163 | loop fusion | flops 131072 | bytes 2621440 | tf_op jit(solution)/shard_map/mul | solution.py:83
  1.9 1.9 %collective-permute-start = (f32[2,8,21,256]{3,1,2,0:T(8,128)S(1)}, f32[2,8,21,256]{3,1,2,0:T(8,128)S(1)}, u32[]{:S(2)}, u32[]{:S(2)}) collective-permute-start(f32[2,8,21,256]{3,1,2,0:T(8,128)S(1)} %pad_maximum_fusion), channel_id=1, source_target_pairs={{0,4},{4,8},{8,12},{12,16},{16,20},{20,24},{24,28},{28,32},{32,36}... | collective-permute-start | bytes 1032200 | tf_op jit(solution)/shard_map/ppermute | solution.py:80
  3.9 3.6 %collective-permute-start.1 = (f32[2,8,21,256]{3,1,2,0:T(8,128)S(1)}, f32[2,8,21,256]{3,1,2,0:T(8,128)S(1)}, u32[]{:S(2)}, u32[]{:S(2)}) collective-permute-start(f32[2,8,21,256]{3,1,2,0:T(8,128)S(1)} %pad_maximum_fusion.1), channel_id=1, source_target_pairs={{4,0},{8,4},{12,8},{16,12},{20,16},{24,20},{28,24},{32,28},{36,32}... | collective-permute-start | bytes 1032200 | tf_op jit(solution)/shard_map/ppermute | solution.py:81
  7.9 0.4 slice_reduce_fusion.21
  8.3 0.1 constant_dynamic-slice_fusion
  8.4 0.1 copy.29
  8.5 0.4 slice_reduce_fusion.10
  9.0 1.5 %collective-permute-done = f32[2,8,21,256]{3,1,2,0:T(8,128)S(1)} collective-permute-done((f32[2,8,21,256]{3,1,2,0:T(8,128)S(1)}, f32[2,8,21,256]{3,1,2,0:T(8,128)S(1)}, u32[]{:S(2)}, u32[]{:S(2)}) %collective-permute-start) | collective-permute-done | bytes 344096 | tf_op jit(solution)/shard_map/ppermute | solution.py:80
  10.5 1.8 %collective-permute-done.1 = f32[2,8,21,256]{3,1,2,0:T(8,128)S(1)} collective-permute-done((f32[2,8,21,256]{3,1,2,0:T(8,128)S(1)}, f32[2,8,21,256]{3,1,2,0:T(8,128)S(1)}, u32[]{:S(2)}, u32[]{:S(2)}) %collective-permute-start.1) | collective-permute-done | bytes 344096 | tf_op jit(solution)/shard_map/ppermute | solution.py:81
  12.3 5.4 %fusion.75 = f32[1,8,96,256]{3,1,2,0:T(8,128)S(1)} fusion(f32[11]{0:T(128)S(1)} %get-tuple-element.17, f32[11]{0:T(128)S(1)} %get-tuple-element.18, f32[11]{0:T(128)S(1)} %get-tuple-element.19, f32[11]{0:T(128)S(1)} %get-tuple-element.20, f32[11]{0:T(128)S(1)} %get-tuple-element.21, f32[11]{0:T(128)S(1)} %get-tuple-element.22, ...), kind=kOutput, calls=%fused_computation.75 | convolution fusion | flops 3330252800 | bytes 2376164 | tf_op jit(solution)/shard_map/conv_general_dilated | solution.py:35
  17.8 5.6 %fusion.72 = f32[1,8,96,256]{3,1,2,0:T(8,128)S(1)} fusion(f32[11]{0:T(128)S(1)} %get-tuple-element.15, f32[11]{0:T(128)S(1)} %get-tuple-element.6, f32[11]{0:T(128)S(1)} %get-tuple-element.7, f32[11]{0:T(128)S(1)} %get-tuple-element.8, f32[11]{0:T(128)S(1)} %get-tuple-element.9, f32[11]{0:T(128)S(1)} %get-tuple-element.10, f32[11]{0:T(128)S(1)} %get-tuple-element.11, ...), kind=kOutput, calls=%fused_computation.74 | convolution fusion | flops 3330252800 | bytes 2376164 | tf_op jit(solution)/shard_map/conv_general_dilated | solution.py:35
  23.3 0.2 maximum_select_fusion
  23.6 0.1 fusion.81
  23.7 0.1 fusion.80
  23.8 0.1 fusion.79
  23.8 0.1 fusion.78
  23.9 2.0 %fusion = f32[2,64,256,16,1]{2,3,0,1,4:T(8,128)S(1)} fusion(f32[2,5,8,64,256]{4,2,3,0,1:T(8,128)S(1)} %fusion.78, pred[5,8,16]{2,1,0:T(8,128)(4,1)S(1)} %constant_dynamic-update-slice_fusion), kind=kOutput, calls=%fused_computation | convolution fusion | flops 251658240 | bytes 7340672 | tf_op jit(solution)/shard_map/otk,cotrw->ckrw/dot_general | solution.py:102
  26.0 0.2 copy.37
  26.2 0.1 dynamic-slice_bitcast_fusion
  26.4 2.8 %collective-permute-start.6 = (f32[2,16,16,128]{3,1,2,0:T(8,128)S(1)}, f32[2,16,16,128]{3,1,2,0:T(8,128)S(1)}, u32[]{:S(2)}, u32[]{:S(2)}) collective-permute-start(f32[2,16,16,128]{3,1,2,0:T(8,128)S(1)} %get-tuple-element.35), channel_id=1, source_target_pairs={{0,3},{1,0},{2,1},{3,2},{4,7},{5,4},{6,5},{7,6},{8,11},{9,8},{10,9... | collective-permute-start | bytes 786440 | tf_op jit(solution)/shard_map/ppermute | solution.py:61
  29.2 6.4 %collective-permute-done.6 = f32[2,16,16,128]{3,1,2,0:T(8,128)S(1)} collective-permute-done((f32[2,16,16,128]{3,1,2,0:T(8,128)S(1)}, f32[2,16,16,128]{3,1,2,0:T(8,128)S(1)}, u32[]{:S(2)}, u32[]{:S(2)}) %collective-permute-start.6) | collective-permute-done | bytes 262176 | tf_op jit(solution)/shard_map/ppermute | solution.py:61
  35.6 3.8 %collective-permute-start.4 = (f32[2,16,16,128]{3,1,2,0:T(8,128)S(1)}, f32[2,16,16,128]{3,1,2,0:T(8,128)S(1)}, u32[]{:S(2)}, u32[]{:S(2)}) collective-permute-start(f32[2,16,16,128]{3,1,2,0:T(8,128)S(1)} %get-tuple-element.30), channel_id=1, source_target_pairs={{0,3},{1,0},{2,1},{3,2},{4,7},{5,4},{6,5},{7,6},{8,11},{9,8},{10,9... | collective-permute-start | bytes 786440 | tf_op jit(solution)/shard_map/ppermute | solution.py:65
  39.4 0.1 collective-permute-done.2
  39.5 0.8 %slice_add_fusion.1 = (f32[2,16,16,128]{3,1,2,0:T(8,128)}, f32[2,16,16,128]{3,1,2,0:T(8,128)S(1)}) fusion(f32[2,16,16,128]{3,1,2,0:T(8,128)S(1)} %collective-permute-done.2, f32[2,16,16,256]{3,1,2,0:T(8,128)S(1)} %get-tuple-element.29), kind=kLoop, calls=%fused_computation.106 | loop fusion | flops 65536 | bytes 1310720 | tf_op jit(solution)/shard_map/add | solution.py:63
  40.3 3.2 %collective-permute-start.7 = (f32[2,16,16,128]{3,1,2,0:T(8,128)S(1)}, f32[2,16,16,128]{3,1,2,0:T(8,128)S(1)}, u32[]{:S(2)}, u32[]{:S(2)}) collective-permute-start(f32[2,16,16,128]{3,1,2,0:T(8,128)S(1)} %get-tuple-element.31), channel_id=1, source_target_pairs={{0,3},{1,0},{2,1},{3,2},{4,7},{5,4},{6,5},{7,6},{8,11},{9,8},{10,9... | collective-permute-start | bytes 786440 | tf_op jit(solution)/shard_map/ppermute | solution.py:66
  43.5 2.5 %collective-permute-done.4 = f32[2,16,16,128]{3,1,2,0:T(8,128)S(1)} collective-permute-done((f32[2,16,16,128]{3,1,2,0:T(8,128)S(1)}, f32[2,16,16,128]{3,1,2,0:T(8,128)S(1)}, u32[]{:S(2)}, u32[]{:S(2)}) %collective-permute-start.4) | collective-permute-done | bytes 262176 | tf_op jit(solution)/shard_map/ppermute | solution.py:65
  46.1 4.9 %collective-permute-done.3 = f32[2,16,16,128]{3,1,2,0:T(8,128)} collective-permute-done((f32[2,16,16,128]{3,1,2,0:T(8,128)}, f32[2,16,16,128]{3,1,2,0:T(8,128)}, u32[]{:S(2)}, u32[]{:S(2)}) %collective-permute-start.3) | collective-permute-done | bytes 262176 | tf_op jit(solution)/shard_map/ppermute | solution.py:63
  51.0 1.0 %add.161 = f32[2,16,16,128]{3,1,2,0:T(8,128)S(1)} add(f32[2,16,16,128]{3,1,2,0:T(8,128)} %collective-permute-done.3, f32[2,16,16,128]{3,1,2,0:T(8,128)S(1)} %collective-permute-done.4) | non-fusion elementwise | flops 65536 | bytes 786432 | tf_op jit(solution)/shard_map/add | solution.py:67
  52.0 3.8 %collective-permute-done.5 = f32[2,16,16,128]{3,1,2,0:T(8,128)} collective-permute-done((f32[2,16,16,128]{3,1,2,0:T(8,128)S(1)}, f32[2,16,16,128]{3,1,2,0:T(8,128)}, u32[]{:S(2)}, u32[]{:S(2)}) %collective-permute-start.5) | collective-permute-done | bytes 262176 | tf_op jit(solution)/shard_map/ppermute | solution.py:64
  55.8 1.0 %add.163 = f32[2,16,16,128]{3,1,2,0:T(8,128)S(1)} add(f32[2,16,16,128]{3,1,2,0:T(8,128)} %collective-permute-done.5, f32[2,16,16,128]{3,1,2,0:T(8,128)S(1)} %collective-permute-done.7) | non-fusion elementwise | flops 65536 | bytes 786432 | tf_op jit(solution)/shard_map/add | solution.py:67
  56.8 0.1 maximum_add_fusion
  56.9 0.9 %copy.24 = f32[16,16,256]{2,1,0:T(8,128)} copy(f32[16,16,256]{2,0,1:T(8,128)S(1)} %fusion.94) | data formatting | bytes 524288 | tf_op jit(solution)/shard_map/div | solution.py:107
  (32 shorter events, 0.8 us)
Async XLA Ops:
  0.0 8.3 %copy-start = (s32[32,16]{0,1:T(8,128)S(1)}, s32[32,16]{0,1:T(8,128)}, u32[]{:S(2)}) copy-start(s32[32,16]{0,1:T(8,128)} %param.7) | copy-start | bytes 6148
  0.0 7.9 %copy-start.1 = (f32[11,11]{1,0:T(8,128)S(1)}, f32[11,11]{1,0:T(8,128)}, u32[]{:S(2)}) copy-start(f32[11,11]{1,0:T(8,128)} %param.6) | copy-start | bytes 1456
  1.9 8.6 %collective-permute-start = (f32[2,8,21,256]{3,1,2,0:T(8,128)S(1)}, f32[2,8,21,256]{3,1,2,0:T(8,128)S(1)}, u32[]{:S(2)}, u32[]{:S(2)}) collective-permute-start(f32[2,8,21,256]{3,1,2,0:T(8,128)S(1)} %pad_maximum_fusion), channel_id=1, source_target_pairs={{0,4},{4,8},{8,12},{12,16},{16,20},{20,24},{24,28},{28,32},{32,36}... | collective-permute-start | bytes 1032200 | tf_op jit(solution)/shard_map/ppermute | solution.py:80
  3.9 8.4 %collective-permute-start.1 = (f32[2,8,21,256]{3,1,2,0:T(8,128)S(1)}, f32[2,8,21,256]{3,1,2,0:T(8,128)S(1)}, u32[]{:S(2)}, u32[]{:S(2)}) collective-permute-start(f32[2,8,21,256]{3,1,2,0:T(8,128)S(1)} %pad_maximum_fusion.1), channel_id=1, source_target_pairs={{4,0},{8,4},{12,8},{16,12},{20,16},{24,20},{28,24},{32,28},{36,32}... | collective-permute-start | bytes 1032200 | tf_op jit(solution)/shard_map/ppermute | solution.py:81
  26.4 9.2 %collective-permute-start.6 = (f32[2,16,16,128]{3,1,2,0:T(8,128)S(1)}, f32[2,16,16,128]{3,1,2,0:T(8,128)S(1)}, u32[]{:S(2)}, u32[]{:S(2)}) collective-permute-start(f32[2,16,16,128]{3,1,2,0:T(8,128)S(1)} %get-tuple-element.35), channel_id=1, source_target_pairs={{0,3},{1,0},{2,1},{3,2},{4,7},{5,4},{6,5},{7,6},{8,11},{9,8},{10,9... | collective-permute-start | bytes 786440 | tf_op jit(solution)/shard_map/ppermute | solution.py:61
  29.2 10.3 %collective-permute-start.2 = (f32[2,16,16,128]{3,1,2,0:T(8,128)S(1)}, f32[2,16,16,128]{3,1,2,0:T(8,128)S(1)}, u32[]{:S(2)}, u32[]{:S(2)}) collective-permute-start(f32[2,16,16,128]{3,1,2,0:T(8,128)S(1)} %get-tuple-element.34), channel_id=1, source_target_pairs={{0,1},{1,2},{2,3},{3,0},{4,5},{5,6},{6,7},{7,4},{8,9},{9,10},{10,1... | collective-permute-start | bytes 786440 | tf_op jit(solution)/shard_map/ppermute | solution.py:60
  35.6 10.4 %collective-permute-start.4 = (f32[2,16,16,128]{3,1,2,0:T(8,128)S(1)}, f32[2,16,16,128]{3,1,2,0:T(8,128)S(1)}, u32[]{:S(2)}, u32[]{:S(2)}) collective-permute-start(f32[2,16,16,128]{3,1,2,0:T(8,128)S(1)} %get-tuple-element.30), channel_id=1, source_target_pairs={{0,3},{1,0},{2,1},{3,2},{4,7},{5,4},{6,5},{7,6},{8,11},{9,8},{10,9... | collective-permute-start | bytes 786440 | tf_op jit(solution)/shard_map/ppermute | solution.py:65
  40.3 10.7 %collective-permute-start.3 = (f32[2,16,16,128]{3,1,2,0:T(8,128)}, f32[2,16,16,128]{3,1,2,0:T(8,128)}, u32[]{:S(2)}, u32[]{:S(2)}) collective-permute-start(f32[2,16,16,128]{3,1,2,0:T(8,128)} %get-tuple-element.32), channel_id=1, source_target_pairs={{0,1},{1,2},{2,3},{3,0},{4,5},{5,6},{6,7},{7,4},{8,9},{9,10},{10,1... | collective-permute-start | bytes 786440 | tf_op jit(solution)/shard_map/ppermute | solution.py:63
  40.3 11.7 %collective-permute-start.7 = (f32[2,16,16,128]{3,1,2,0:T(8,128)S(1)}, f32[2,16,16,128]{3,1,2,0:T(8,128)S(1)}, u32[]{:S(2)}, u32[]{:S(2)}) collective-permute-start(f32[2,16,16,128]{3,1,2,0:T(8,128)S(1)} %get-tuple-element.31), channel_id=1, source_target_pairs={{0,3},{1,0},{2,1},{3,2},{4,7},{5,4},{6,5},{7,6},{8,11},{9,8},{10,9... | collective-permute-start | bytes 786440 | tf_op jit(solution)/shard_map/ppermute | solution.py:66
  43.5 12.2 %collective-permute-start.5 = (f32[2,16,16,128]{3,1,2,0:T(8,128)S(1)}, f32[2,16,16,128]{3,1,2,0:T(8,128)}, u32[]{:S(2)}, u32[]{:S(2)}) collective-permute-start(f32[2,16,16,128]{3,1,2,0:T(8,128)S(1)} %get-tuple-element.33), channel_id=1, source_target_pairs={{0,1},{1,2},{2,3},{3,0},{4,5},{5,6},{6,7},{7,4},{8,9},{9,10},{10,1... | collective-permute-start | bytes 786440 | tf_op jit(solution)/shard_map/ppermute | solution.py:64

commit v16 on v13

--- a/solution.py
+++ b/solution.py
@@ -32,15 +32,18 @@
 
 
 def correlate_rows(bordered, kernel):
-    return lax.conv_general_dilated(
-        bordered,
+    n, extended, cols = bordered.shape
+    out_rows = extended - kernel.shape[0] + 1
+    joined = lax.conv_general_dilated(
+        bordered.reshape(1, n * extended, cols),
         kernel,
         window_strides=(1,),
-        padding="VALID",
+        padding=((0, kernel.shape[0] - 1),),
         dimension_numbers=("NHC", "HIO", "NHC"),
         precision=lax.Precision.HIGH,
         preferred_element_type=jnp.float32,
     )
+    return joined.reshape(n, extended, cols)[:, :out_rows, :]
 
 
 def ring_reduce_scatter(partial, axis):

time: 55.2 us -> 63.9 us (1.16)
  local copies, waits for them, and re-layouts: 2.56 us -> 10.4 us
  waiting for transfers between devices: 24.9 us -> 20.7 us
  other arithmetic: 4.51 us -> 7.34 us
  matrix products: 13 us -> 13.9 us
  between operations: 0.31 us -> 1.03 us
    eq x6, other arithmetic: 0.32 us -> 4.23 us  [toeplitz(): out = jnp.where(tap == b, taps[:, b][:, None, None], out)]
    unnamed x9 -> x115, local copies, waits for them, and re-layouts: 0.36 us -> 3.23 us
    conv_general_dilated x0 -> x12, local copies, waits for them, and re-layouts: none -> 2.1 us  [correlate_rows(): lax.conv_general_dilated(bordered.reshape(1, n * extended, cols), kernel,...]
    ppermute x1, waiting for transfers between devices: 1.77 us -> 0.01 us  [shards(): lax.ppermute(jnp.stack([science[:, :width], inv_variance[:, :width]]), 's...]
    mul x1, other arithmetic: 1.84 us -> 0.07 us  [shards(): science * inv_variance]
    ppermute x1, waiting for transfers between devices: 1.55 us -> 0.01 us  [shards(): lax.ppermute(jnp.stack([science[:, rows - width:], inv_variance[:, rows -...]
    another operation x1, local copies, waits for them, and re-layouts: 0.05 us -> 1.36 us  [shards(): jnp.stack([science[:, rows - width:], inv_variance[:, rows - width:]])]
    slice x2, local copies, waits for them, and re-layouts: 0.74 us -> 1.89 us  [toeplitz(): out = jnp.where(tap == b, taps[:, b][:, None, None], out)]
  transfers between devices with their start and end apart: 6 -> 6, of which waited for: 5 -> 3; matrix products, arithmetic and copies ran while one was open for 6% -> 14% of each run, Pallas kernels for 0% -> 0%
where the time goes in v16:
time: 63.9 us; the launch traced here: 63.1 us
  waiting for transfers between devices  20.7 us (32%)
  matrix products  13.9 us (22%)
  local copies, waits for them, and re-layouts  10.4 us (16%)
  starting transfers between devices  9.69 us (15%)
  other arithmetic  7.34 us (11%)
  between operations  1.03 us (2%)
    conv_general_dilated x2, matrix products, correlate_rows(): lax.conv_general_dilated(bordered.reshape(1, n * extended, cols), kernel,...  11.9 us
    ppermute x1, waiting for transfers between devices, ring_reduce_scatter(): got_left = lax.ppermute(ahead, axis, right)  10.6 us
    ppermute x1, waiting for transfers between devices, ring_reduce_scatter(): from_left = lax.ppermute(far[..., :half], axis, right)  6.51 us
    eq x6, other arithmetic, toeplitz(): out = jnp.where(tap == b, taps[:, b][:, None, None], out)  4.23 us
    ppermute x1, starting transfers between devices, shards(): lax.ppermute(jnp.stack([science[:, :width], inv_variance[:, :width]]), 's...  3.64 us
    ppermute x1, waiting for transfers between devices, ring_reduce_scatter(): got_right = lax.ppermute(behind, axis, left)  3.52 us
    unnamed x115, local copies, waits for them, and re-layouts  3.23 us
    conv_general_dilated x12, local copies, waits for them, and re-layouts, correlate_rows(): lax.conv_general_dilated(bordered.reshape(1, n * extended, cols), kernel,...  2.1 us
  transfers between devices with their start and end apart: 6, of which 3 were waited for; matrix products, arithmetic and copies ran while one was open for 14% of the time, Pallas kernels for 0%

profile of v16, /device:TPU:54, one launch (start us, length us, event | category | flops | bytes accessed | tf_op | source)
XLA Modules:
  0.0 63.1 jit_solution(6653856191678140889)
XLA Ops:
  0.0 1.4 %slice_bitcast_fusion.11 = (f32[1,8,21,256]{3,2,1,0:T(8,128)S(1)}, f32[1,8,21,256]{3,2,1,0:T(8,128)S(1)}, f32[1,8,21,256]{3,2,1,0:T(8,128)S(1)}, f32[1,8,21,256]{3,2,1,0:T(8,128)S(1)}) fusion(f32[8,64,256]{2,1,0:T(8,128)} %param.5, f32[8,64,256]{2,1,0:T(8,128)} %param.4), kind=kLoop, calls=%fused_computation.135 | loop fusion | bytes 1376256 | tf_op jit(solution)/shard_map/stack | solution.py:84
  1.4 1.9 %collective-permute-start = (f32[2,8,21,256]{3,2,1,0:T(8,128)S(1)}, f32[2,8,21,256]{3,2,1,0:T(8,128)S(1)}, u32[]{:S(2)}, u32[]{:S(2)}) collective-permute-start(f32[2,8,21,256]{3,2,1,0:T(8,128)S(1)} %pad_maximum_fusion.4), channel_id=1, source_target_pairs={{0,4},{4,8},{8,12},{12,16},{16,20},{20,24},{24,28},{28,32},{32,36}... | collective-permute-start | bytes 1032200 | tf_op jit(solution)/shard_map/ppermute | solution.py:84
  3.4 3.6 %collective-permute-start.1 = (f32[2,8,21,256]{3,2,1,0:T(8,128)S(1)}, f32[2,8,21,256]{3,2,1,0:T(8,128)S(1)}, u32[]{:S(2)}, u32[]{:S(2)}) collective-permute-start(f32[2,8,21,256]{3,2,1,0:T(8,128)S(1)} %pad_maximum_fusion.5), channel_id=1, source_target_pairs={{4,0},{8,4},{12,8},{16,12},{20,16},{24,20},{28,24},{32,28},{36,32}... | collective-permute-start | bytes 1032200 | tf_op jit(solution)/shard_map/ppermute | solution.py:85
  7.0 0.7 %fusion.96 = (pred[256,256]{1,0:T(8,128)(4,1)}, pred[256,256]{1,0:T(8,128)(4,1)}) fusion(), kind=kLoop, calls=%fused_computation.116 | loop fusion | flops 262144 | bytes 131072 | tf_op jit(solution)/shard_map/eq | solution.py:30
  7.7 0.7 %fusion.98 = (pred[256,256]{1,0:T(8,128)(4,1)}, pred[256,256]{1,0:T(8,128)(4,1)}) fusion(), kind=kLoop, calls=%fused_computation.118 | loop fusion | flops 262144 | bytes 131072 | tf_op jit(solution)/shard_map/eq | solution.py:30
  8.5 0.7 %fusion.100 = (pred[256,256]{1,0:T(8,128)(4,1)}, pred[256,256]{1,0:T(8,128)(4,1)}) fusion(), kind=kLoop, calls=%fused_computation.120 | loop fusion | flops 262144 | bytes 131072 | tf_op jit(solution)/shard_map/eq | solution.py:30
  9.2 0.7 %fusion.102 = (pred[256,256]{1,0:T(8,128)(4,1)}, pred[256,256]{1,0:T(8,128)(4,1)}) fusion(), kind=kLoop, calls=%fused_computation.122 | loop fusion | flops 262144 | bytes 131072 | tf_op jit(solution)/shard_map/eq | solution.py:30
  9.9 0.7 %fusion.104 = (pred[256,256]{1,0:T(8,128)(4,1)}, pred[256,256]{1,0:T(8,128)(4,1)}) fusion(), kind=kLoop, calls=%fused_computation.124 | loop fusion | flops 262144 | bytes 131072 | tf_op jit(solution)/shard_map/eq | solution.py:30
  10.6 0.7 %fusion.106 = pred[256,256]{1,0:T(8,128)(4,1)} fusion(), kind=kLoop, calls=%fused_computation.126 | loop fusion | flops 196608 | bytes 65536 | tf_op jit(solution)/shard_map/eq | solution.py:30
  11.3 0.9 %slice_reduce_fusion.21 = (f32[11]{0:T(128)}, f32[11]{0:T(128)}, f32[11]{0:T(128)}, f32[11]{0:T(128)}, f32[11]{0:T(128)}, /*index=5*/f32[11]{0:T(128)}, f32[11]{...) fusion(f32[11,11]{1,0:T(8,128)S(1)} %copy-done.3), kind=kLoop, calls=%fused_computation.164 | loop fusion | bytes 968 | tf_op jit(solution)/shard_map/slice | solution.py:30
  12.4 1.0 %slice_reduce_fusion.10 = (f32[11]{0:T(128)}, f32[11]{0:T(128)}, f32[11]{0:T(128)}, f32[11]{0:T(128)}, f32[11]{0:T(128)}, /*index=5*/f32[11]{0:T(128)}, f32[11]{...) fusion(f32[11,11]{1,0:T(8,128)S(1)} %mul.34), kind=kLoop, calls=%fused_computation.153 | loop fusion | bytes 968 | tf_op jit(solution)/shard_map/slice | solution.py:30
  13.5 0.5 compare_and_fusion
  14.1 0.7 %copy-done.4 = f32[2,8,21,256]{3,2,1,0:T(8,128)} copy-done((f32[2,8,21,256]{3,2,1,0:T(8,128)}, f32[2,8,21,256]{3,2,1,0:T(8,128)S(1)}, u32[]{:S(2)}) %copy-start.4) | copy-done | bytes 344088
  15.5 0.5 copy.12
  16.4 5.8 %fusion.70 = f32[8,108,256]{2,0,1:T(8,128)S(1)} fusion(f32[11]{0:T(128)S(1)} %copy-done.50, f32[11]{0:T(128)S(1)} %copy-done.41, f32[11]{0:T(128)S(1)} %copy-done.42, f32[11]{0:T(128)S(1)} %copy-done.43, f32[11]{0:T(128)S(1)} %copy-done.44, f32[11]{0:T(128)S(1)} %copy-done.45, f32[11]{0:T(128)S(1)} %copy-done.46, f32[11]{0:T(128)S(1)} %copy-done.47, ...), kind=kOutput, calls=%fused_computation.72 | convolution fusion | flops 3746000896 | bytes 2563396 | tf_op jit(solution)/shard_map/conv_general_dilated | solution.py:37
  22.2 0.3 copy.13
  22.9 0.5 copy.33
  23.3 0.4 copy-done.5
  24.5 0.5 copy.16
  25.4 6.0 %fusion.73 = f32[8,108,256]{2,0,1:T(8,128)S(1)} fusion(f32[11]{0:T(128)S(1)} %copy-done.30, f32[11]{0:T(128)S(1)} %copy-done.31, f32[11]{0:T(128)S(1)} %copy-done.32, f32[11]{0:T(128)S(1)} %copy-done.33, f32[11]{0:T(128)S(1)} %copy-done.34, f32[11]{0:T(128)S(1)} %copy-done.35, f32[11]{0:T(128)S(1)} %copy-done.36, f32[11]{0:T(128)S(1)} %copy-done.37, ...), kind=kOutput, calls=%fused_computation.73 | convolution fusion | flops 3746000896 | bytes 2563396 | tf_op jit(solution)/shard_map/conv_general_dilated | solution.py:37
  32.1 0.5 copy.32
  33.2 2.0 %convolution_bitcast_fusion = f32[2,64,256,16]{2,3,1,0:T(8,128)S(1)} fusion(f32[2,5,8,64,256]{4,2,1,3,0:T(8,128)S(1)} %fusion.76, pred[5,8,16]{2,1,0:T(8,128)(4,1)S(1)} %constant_dynamic-update-slice_fusion), kind=kOutput, calls=%fused_computation.24 | convolution fusion | flops 251658240 | bytes 7340672 | tf_op jit(solution)/shard_map/otk,cotrw->ckrw/dot_general | solution.py:106
  35.4 0.6 collective-permute-start.2
  35.9 1.5 %collective-permute-start.4 = (f32[2,16,16,128]{3,1,2,0:T(8,128)S(1)}, f32[2,16,16,128]{3,1,2,0:T(8,128)S(1)}, u32[]{:S(2)}, u32[]{:S(2)}) collective-permute-start(f32[2,16,16,128]{3,1,2,0:T(8,128)S(1)} %get-tuple-element.33), channel_id=1, source_target_pairs={{0,3},{1,0},{2,1},{3,2},{4,7},{5,4},{6,5},{7,6},{8,11},{9,8},{10,9... | collective-permute-start | bytes 786440 | tf_op jit(solution)/shard_map/ppermute | solution.py:64
  37.5 6.5 %collective-permute-done.2 = f32[2,16,16,128]{3,1,2,0:T(8,128)S(1)} collective-permute-done((f32[2,16,16,128]{3,1,2,0:T(8,128)S(1)}, f32[2,16,16,128]{3,1,2,0:T(8,128)S(1)}, u32[]{:S(2)}, u32[]{:S(2)}) %collective-permute-start.2) | collective-permute-done | bytes 262176 | tf_op jit(solution)/shard_map/ppermute | solution.py:63
  44.1 0.8 %pad_maximum_fusion.2 = f32[2,16,16,256]{3,1,2,0:T(8,128)} fusion(f32[2,16,16,128]{3,1,2,0:T(8,128)S(1)} %get-tuple-element.31, f32[2,16,16,128]{3,1,2,0:T(8,128)S(1)} %get-tuple-element.30), kind=kLoop, calls=%fused_computation.97 | loop fusion | flops 131072 | bytes 1048576 | tf_op jit(solution)/shard_map/concatenate | solution.py:66
  44.9 1.7 %collective-permute-start.3 = (f32[2,16,16,256]{3,1,2,0:T(8,128)}, f32[2,16,16,256]{3,1,2,0:T(8,128)S(1)}, u32[]{:S(2)}, u32[]{:S(2)}) collective-permute-start(f32[2,16,16,256]{3,1,2,0:T(8,128)} %pad_maximum_fusion.2), channel_id=1, source_target_pairs={{0,1},{1,2},{2,3},{3,0},{4,5},{5,6},{6,7},{7,4},{8,9},{9,10},{10,1... | collective-permute-start | bytes 1572872 | tf_op jit(solution)/shard_map/ppermute | solution.py:69
  46.7 0.8 %pad_maximum_fusion.3 = f32[2,16,16,256]{3,1,2,0:T(8,128)} fusion(f32[2,16,16,128]{3,1,2,0:T(8,128)S(1)} %get-tuple-element.35, f32[2,16,16,128]{3,1,2,0:T(8,128)S(1)} %get-tuple-element.34), kind=kLoop, calls=%fused_computation.98 | loop fusion | flops 131072 | bytes 1048576 | tf_op jit(solution)/shard_map/concatenate | solution.py:68
  47.5 0.3 collective-permute-start.5
  47.8 10.6 %collective-permute-done.3 = f32[2,16,16,256]{3,1,2,0:T(8,128)S(1)} collective-permute-done((f32[2,16,16,256]{3,1,2,0:T(8,128)}, f32[2,16,16,256]{3,1,2,0:T(8,128)S(1)}, u32[]{:S(2)}, u32[]{:S(2)}) %collective-permute-start.3) | collective-permute-done | bytes 524320 | tf_op jit(solution)/shard_map/ppermute | solution.py:69
  58.5 3.5 %collective-permute-done.5 = f32[2,16,16,256]{3,1,2,0:T(8,128)S(1)} collective-permute-done((f32[2,16,16,256]{3,1,2,0:T(8,128)}, f32[2,16,16,256]{3,1,2,0:T(8,128)S(1)}, u32[]{:S(2)}, u32[]{:S(2)}) %collective-permute-start.5) | collective-permute-done | bytes 524320 | tf_op jit(solution)/shard_map/ppermute | solution.py:70
  62.2 0.9 %copy.24 = f32[16,16,256]{2,1,0:T(8,128)} copy(f32[16,16,256]{2,0,1:T(8,128)S(1)} %fusion.95) | data formatting | bytes 524288 | tf_op jit(solution)/shard_map/div | solution.py:111
  (155 shorter events, 3.9 us)
Async XLA Ops:
  0.0 12.2 %copy-start = (s32[32,16]{0,1:T(8,128)S(1)}, s32[32,16]{0,1:T(8,128)}, u32[]{:S(2)}) copy-start(s32[32,16]{0,1:T(8,128)} %param.7) | copy-start | bytes 6148
  0.0 13.4 %copy-start.2 = (f32[8,64,256]{2,1,0:T(8,128)S(1)}, f32[8,64,256]{2,1,0:T(8,128)}, u32[]{:S(2)}) copy-start(f32[8,64,256]{2,1,0:T(8,128)} %param.4) | copy-start | bytes 1572868
  0.0 13.4 %copy-start.1 = (f32[8,64,256]{2,1,0:T(8,128)S(1)}, f32[8,64,256]{2,1,0:T(8,128)}, u32[]{:S(2)}) copy-start(f32[8,64,256]{2,1,0:T(8,128)} %param.5) | copy-start | bytes 1572868
  0.0 11.3 %copy-start.3 = (f32[11,11]{1,0:T(8,128)S(1)}, f32[11,11]{1,0:T(8,128)}, u32[]{:S(2)}) copy-start(f32[11,11]{1,0:T(8,128)} %param.6) | copy-start | bytes 1456
  1.4 12.6 %collective-permute-start = (f32[2,8,21,256]{3,2,1,0:T(8,128)S(1)}, f32[2,8,21,256]{3,2,1,0:T(8,128)S(1)}, u32[]{:S(2)}, u32[]{:S(2)}) collective-permute-start(f32[2,8,21,256]{3,2,1,0:T(8,128)S(1)} %pad_maximum_fusion.4), channel_id=1, source_target_pairs={{0,4},{4,8},{8,12},{12,16},{16,20},{20,24},{24,28},{28,32},{32,36}... | collective-permute-start | bytes 1032200 | tf_op jit(solution)/shard_map/ppermute | solution.py:84
  3.4 10.7 %collective-permute-start.1 = (f32[2,8,21,256]{3,2,1,0:T(8,128)S(1)}, f32[2,8,21,256]{3,2,1,0:T(8,128)S(1)}, u32[]{:S(2)}, u32[]{:S(2)}) collective-permute-start(f32[2,8,21,256]{3,2,1,0:T(8,128)S(1)} %pad_maximum_fusion.5), channel_id=1, source_target_pairs={{4,0},{8,4},{12,8},{16,12},{20,16},{24,20},{28,24},{32,28},{36,32}... | collective-permute-start | bytes 1032200 | tf_op jit(solution)/shard_map/ppermute | solution.py:85
  15.3 1.0 %copy-start.23 = (pred[256,256]{1,0:T(8,128)(4,1)S(1)}, pred[256,256]{1,0:T(8,128)(4,1)}, u32[]{:S(2)}) copy-start(pred[256,256]{1,0:T(8,128)(4,1)} %get-tuple-element.50) | copy-start | bytes 196612
  15.3 1.0 %copy-start.25 = (pred[256,256]{1,0:T(8,128)(4,1)S(1)}, pred[256,256]{1,0:T(8,128)(4,1)}, u32[]{:S(2)}) copy-start(pred[256,256]{1,0:T(8,128)(4,1)} %get-tuple-element.51) | copy-start | bytes 196612
  15.4 1.0 %copy-start.27 = (pred[256,256]{1,0:T(8,128)(4,1)S(1)}, pred[256,256]{1,0:T(8,128)(4,1)}, u32[]{:S(2)}) copy-start(pred[256,256]{1,0:T(8,128)(4,1)} %fusion.106) | copy-start | bytes 196612
  15.4 1.0 %copy-start.44 = (f32[11]{0:T(128)S(1)}, f32[11]{0:T(128)}, u32[]{:S(2)}) copy-start(f32[11]{0:T(128)} %get-tuple-element.9) | copy-start | bytes 136
  15.4 1.0 %copy-start.45 = (f32[11]{0:T(128)S(1)}, f32[11]{0:T(128)}, u32[]{:S(2)}) copy-start(f32[11]{0:T(128)} %get-tuple-element.10) | copy-start | bytes 136
  15.4 1.0 %copy-start.46 = (f32[11]{0:T(128)S(1)}, f32[11]{0:T(128)}, u32[]{:S(2)}) copy-start(f32[11]{0:T(128)} %get-tuple-element.11) | copy-start | bytes 136
  15.4 0.9 %copy-start.47 = (f32[11]{0:T(128)S(1)}, f32[11]{0:T(128)}, u32[]{:S(2)}) copy-start(f32[11]{0:T(128)} %get-tuple-element.12) | copy-start | bytes 136
  22.8 1.0 %copy-start.5 = (f32[2,8,21,256]{3,2,1,0:T(8,128)S(1)}, f32[2,8,21,256]{3,2,1,0:T(8,128)}, u32[]{:S(2)}) copy-start(f32[2,8,21,256]{3,2,1,0:T(8,128)} %copy-done.4) | copy-start | bytes 1032196
  22.8 1.1 %copy-start.7 = (f32[2,8,21,256]{3,2,1,0:T(8,128)S(1)}, f32[2,8,21,256]{3,2,1,0:T(8,128)}, u32[]{:S(2)}) copy-start(f32[2,8,21,256]{3,2,1,0:T(8,128)} %copy-done.6) | copy-start | bytes 1032196
  24.3 1.0 %copy-start.20 = (pred[256,256]{1,0:T(8,128)(4,1)S(1)}, pred[256,256]{1,0:T(8,128)(4,1)}, u32[]{:S(2)}) copy-start(pred[256,256]{1,0:T(8,128)(4,1)} %get-tuple-element.48) | copy-start | bytes 196612
  24.3 1.0 %copy-start.22 = (pred[256,256]{1,0:T(8,128)(4,1)S(1)}, pred[256,256]{1,0:T(8,128)(4,1)}, u32[]{:S(2)}) copy-start(pred[256,256]{1,0:T(8,128)(4,1)} %get-tuple-element.49) | copy-start | bytes 196612
  24.3 1.0 %copy-start.24 = (pred[256,256]{1,0:T(8,128)(4,1)S(1)}, pred[256,256]{1,0:T(8,128)(4,1)}, u32[]{:S(2)}) copy-start(pred[256,256]{1,0:T(8,128)(4,1)} %get-tuple-element.50) | copy-start | bytes 196612
  24.3 1.0 %copy-start.26 = (pred[256,256]{1,0:T(8,128)(4,1)S(1)}, pred[256,256]{1,0:T(8,128)(4,1)}, u32[]{:S(2)}) copy-start(pred[256,256]{1,0:T(8,128)(4,1)} %get-tuple-element.51) | copy-start | bytes 196612
  24.3 1.0 %copy-start.28 = (pred[256,256]{1,0:T(8,128)(4,1)S(1)}, pred[256,256]{1,0:T(8,128)(4,1)}, u32[]{:S(2)}) copy-start(pred[256,256]{1,0:T(8,128)(4,1)} %fusion.106) | copy-start | bytes 196612
  24.3 1.0 %copy-start.33 = (f32[11]{0:T(128)S(1)}, f32[11]{0:T(128)}, u32[]{:S(2)}) copy-start(f32[11]{0:T(128)} %get-tuple-element.20) | copy-start | bytes 136
  24.4 1.0 %copy-start.34 = (f32[11]{0:T(128)S(1)}, f32[11]{0:T(128)}, u32[]{:S(2)}) copy-start(f32[11]{0:T(128)} %get-tuple-element.21) | copy-start | bytes 136
  24.4 1.0 %copy-start.35 = (f32[11]{0:T(128)S(1)}, f32[11]{0:T(128)}, u32[]{:S(2)}) copy-start(f32[11]{0:T(128)} %get-tuple-element.22) | copy-start | bytes 136
  24.4 1.0 %copy-start.36 = (f32[11]{0:T(128)S(1)}, f32[11]{0:T(128)}, u32[]{:S(2)}) copy-start(f32[11]{0:T(128)} %get-tuple-element.23) | copy-start | bytes 136
  24.4 1.0 %copy-start.37 = (f32[11]{0:T(128)S(1)}, f32[11]{0:T(128)}, u32[]{:S(2)}) copy-start(f32[11]{0:T(128)} %get-tuple-element.24) | copy-start | bytes 136
  24.4 1.0 %copy-start.38 = (f32[11]{0:T(128)S(1)}, f32[11]{0:T(128)}, u32[]{:S(2)}) copy-start(f32[11]{0:T(128)} %get-tuple-element.25) | copy-start | bytes 136
  24.4 1.0 %copy-start.39 = (f32[11]{0:T(128)S(1)}, f32[11]{0:T(128)}, u32[]{:S(2)}) copy-start(f32[11]{0:T(128)} %get-tuple-element.26) | copy-start | bytes 136
  24.4 1.0 %copy-start.53 = (pred[8,108]{0,1:T(8,128)(4,1)S(1)}, pred[8,108]{0,1:T(8,128)(4,1)}, u32[]{:S(2)}) copy-start(pred[8,108]{0,1:T(8,128)(4,1)} %constant.87) | copy-start | bytes 2596
  35.4 8.6 %collective-permute-start.2 = (f32[2,16,16,128]{3,1,2,0:T(8,128)S(1)}, f32[2,16,16,128]{3,1,2,0:T(8,128)S(1)}, u32[]{:S(2)}, u32[]{:S(2)}) collective-permute-start(f32[2,16,16,128]{3,1,2,0:T(8,128)S(1)} %get-tuple-element.32), channel_id=1, source_target_pairs={{0,1},{1,2},{2,3},{3,0},{4,5},{5,6},{6,7},{7,4},{8,9},{9,10},{10,1... | collective-permute-start | bytes 786440 | tf_op jit(solution)/shard_map/ppermute | solution.py:63
  35.9 10.7 %collective-permute-start.4 = (f32[2,16,16,128]{3,1,2,0:T(8,128)S(1)}, f32[2,16,16,128]{3,1,2,0:T(8,128)S(1)}, u32[]{:S(2)}, u32[]{:S(2)}) collective-permute-start(f32[2,16,16,128]{3,1,2,0:T(8,128)S(1)} %get-tuple-element.33), channel_id=1, source_target_pairs={{0,3},{1,0},{2,1},{3,2},{4,7},{5,4},{6,5},{7,6},{8,11},{9,8},{10,9... | collective-permute-start | bytes 786440 | tf_op jit(solution)/shard_map/ppermute | solution.py:64
  44.9 13.6 %collective-permute-start.3 = (f32[2,16,16,256]{3,1,2,0:T(8,128)}, f32[2,16,16,256]{3,1,2,0:T(8,128)S(1)}, u32[]{:S(2)}, u32[]{:S(2)}) collective-permute-start(f32[2,16,16,256]{3,1,2,0:T(8,128)} %pad_maximum_fusion.2), channel_id=1, source_target_pairs={{0,1},{1,2},{2,3},{3,0},{4,5},{5,6},{6,7},{7,4},{8,9},{9,10},{10,1... | collective-permute-start | bytes 1572872 | tf_op jit(solution)/shard_map/ppermute | solution.py:69
  47.5 14.5 %collective-permute-start.5 = (f32[2,16,16,256]{3,1,2,0:T(8,128)}, f32[2,16,16,256]{3,1,2,0:T(8,128)S(1)}, u32[]{:S(2)}, u32[]{:S(2)}) collective-permute-start(f32[2,16,16,256]{3,1,2,0:T(8,128)} %pad_maximum_fusion.3), channel_id=1, source_target_pairs={{0,3},{1,0},{2,1},{3,2},{4,7},{5,4},{6,5},{7,6},{8,11},{9,8},{10,9... | collective-permute-start | bytes 1572872 | tf_op jit(solution)/shard_map/ppermute | solution.py:70
  (28 other events, 25.4 us)

commit v17 on v13

--- a/solution.py
+++ b/solution.py
@@ -101,7 +101,7 @@
         [images[:, :, reach + value * BR : reach + value * BR + rows, :] for value in shifts], axis=1
     )
     partial = jnp.einsum(
-        "otk,cotrw->ckrw", onehot, windows, precision=lax.Precision.HIGHEST
+        "otk,cotrw->ckrw", onehot, windows, precision=lax.Precision.HIGH
     )
 
     stacked = ring_reduce_scatter(partial, "visit")

time: 55.2 us -> 54.6 us (0.989)
  matrix products: 13 us -> 12.3 us
    dot_general x1, matrix products: 2.03 us -> 1.38 us  [shards(): jnp.einsum('otk,cotrw->ckrw', onehot, windows, precision=lax.Precision.HIGH)]
where the time goes in v17:
time: 54.6 us; the launch traced here: 54.3 us
  waiting for transfers between devices  24.9 us (46%)
  matrix products  12.3 us (23%)
  starting transfers between devices  9.69 us (18%)
  other arithmetic  4.51 us (8%)
  local copies, waits for them, and re-layouts  2.56 us (5%)
    ppermute x1, waiting for transfers between devices, ring_reduce_scatter(): got_left = lax.ppermute(ahead, axis, right)  11.8 us
    conv_general_dilated x2, matrix products, correlate_rows(): lax.conv_general_dilated(bordered, kernel, window_strides=(1,), padding='...  11 us
    ppermute x1, waiting for transfers between devices, ring_reduce_scatter(): from_left = lax.ppermute(far[..., :half], axis, right)  5.9 us
    ppermute x1, waiting for transfers between devices, ring_reduce_scatter(): got_right = lax.ppermute(behind, axis, left)  3.93 us
    ppermute x1, starting transfers between devices, shards(): lax.ppermute(jnp.stack([science[:, :width], inv_variance[:, :width]]), 's...  3.64 us
    ppermute x1, starting transfers between devices, shards(): lax.ppermute(jnp.stack([science[:, rows - width:], inv_variance[:, rows -...  1.92 us
    mul x1, other arithmetic, shards(): science * inv_variance  1.84 us
    ppermute x1, waiting for transfers between devices, shards(): lax.ppermute(jnp.stack([science[:, :width], inv_variance[:, :width]]), 's...  1.77 us
  transfers between devices with their start and end apart: 6, of which 5 were waited for; matrix products, arithmetic and copies ran while one was open for 6% of the time, Pallas kernels for 0%

profile of v17, /device:TPU:54, one launch (start us, length us, event | category | flops | bytes accessed | tf_op | source)
XLA Modules:
  0.0 54.3 jit_solution(2229847228132128084)
XLA Ops:
  0.0 1.8 %copy_multiply_fusion = (f32[8,64,256]{2,0,1:T(8,128)S(1)}, f32[8,64,256]{2,0,1:T(8,128)S(1)}, f32[8,64,256]{2,0,1:T(8,128)S(1)}) fusion(f32[8,64,256]{2,1,0:T(8,128)} %param.5, f32[8,64,256]{2,1,0:T(8,128)} %param.4), kind=kLoop, calls=%fused_computation.166 | loop fusion | flops 131072 | bytes 2621440 | tf_op jit(solution)/shard_map/mul | solution.py:84
  1.9 1.9 %collective-permute-start = (f32[2,8,21,256]{3,1,2,0:T(8,128)S(1)}, f32[2,8,21,256]{3,1,2,0:T(8,128)S(1)}, u32[]{:S(2)}, u32[]{:S(2)}) collective-permute-start(f32[2,8,21,256]{3,1,2,0:T(8,128)S(1)} %pad_maximum_fusion.2), channel_id=1, source_target_pairs={{0,4},{4,8},{8,12},{12,16},{16,20},{20,24},{24,28},{28,32},{32,36}... | collective-permute-start | bytes 1032200 | tf_op jit(solution)/shard_map/ppermute | solution.py:81
  3.9 3.6 %collective-permute-start.1 = (f32[2,8,21,256]{3,1,2,0:T(8,128)S(1)}, f32[2,8,21,256]{3,1,2,0:T(8,128)S(1)}, u32[]{:S(2)}, u32[]{:S(2)}) collective-permute-start(f32[2,8,21,256]{3,1,2,0:T(8,128)S(1)} %pad_maximum_fusion.3), channel_id=1, source_target_pairs={{4,0},{8,4},{12,8},{16,12},{20,16},{24,20},{28,24},{32,28},{36,32}... | collective-permute-start | bytes 1032200 | tf_op jit(solution)/shard_map/ppermute | solution.py:82
  7.9 0.4 slice_reduce_fusion.21
  8.3 0.1 constant_dynamic-slice_fusion
  8.4 0.1 copy.29
  8.5 0.4 slice_reduce_fusion.10
  9.0 1.5 %collective-permute-done = f32[2,8,21,256]{3,1,2,0:T(8,128)S(1)} collective-permute-done((f32[2,8,21,256]{3,1,2,0:T(8,128)S(1)}, f32[2,8,21,256]{3,1,2,0:T(8,128)S(1)}, u32[]{:S(2)}, u32[]{:S(2)}) %collective-permute-start) | collective-permute-done | bytes 344096 | tf_op jit(solution)/shard_map/ppermute | solution.py:81
  10.5 1.8 %collective-permute-done.1 = f32[2,8,21,256]{3,1,2,0:T(8,128)S(1)} collective-permute-done((f32[2,8,21,256]{3,1,2,0:T(8,128)S(1)}, f32[2,8,21,256]{3,1,2,0:T(8,128)S(1)}, u32[]{:S(2)}, u32[]{:S(2)}) %collective-permute-start.1) | collective-permute-done | bytes 344096 | tf_op jit(solution)/shard_map/ppermute | solution.py:82
  12.3 5.4 %fusion.75 = f32[1,8,96,256]{3,1,2,0:T(8,128)S(1)} fusion(f32[11]{0:T(128)S(1)} %get-tuple-element.17, f32[11]{0:T(128)S(1)} %get-tuple-element.18, f32[11]{0:T(128)S(1)} %get-tuple-element.19, f32[11]{0:T(128)S(1)} %get-tuple-element.20, f32[11]{0:T(128)S(1)} %get-tuple-element.21, f32[11]{0:T(128)S(1)} %get-tuple-element.22, ...), kind=kOutput, calls=%fused_computation.75 | convolution fusion | flops 3330252800 | bytes 2376164 | tf_op jit(solution)/shard_map/conv_general_dilated | solution.py:35
  17.8 5.6 %fusion.72 = f32[1,8,96,256]{3,1,2,0:T(8,128)S(1)} fusion(f32[11]{0:T(128)S(1)} %get-tuple-element.15, f32[11]{0:T(128)S(1)} %get-tuple-element.6, f32[11]{0:T(128)S(1)} %get-tuple-element.7, f32[11]{0:T(128)S(1)} %get-tuple-element.8, f32[11]{0:T(128)S(1)} %get-tuple-element.9, f32[11]{0:T(128)S(1)} %get-tuple-element.10, f32[11]{0:T(128)S(1)} %get-tuple-element.11, ...), kind=kOutput, calls=%fused_computation.74 | convolution fusion | flops 3330252800 | bytes 2376164 | tf_op jit(solution)/shard_map/conv_general_dilated | solution.py:35
  23.3 0.2 maximum_select_fusion
  23.5 0.1 fusion.82
  23.6 0.1 fusion.81
  23.7 0.1 fusion.80
  23.8 0.1 fusion.79
  23.8 0.1 fusion.78
  23.9 1.4 %fusion = f32[2,64,256,16,1]{2,3,0,1,4:T(8,128)S(1)} fusion(f32[2,5,8,64,256]{4,2,3,0,1:T(8,128)S(1)} %fusion.78, pred[5,8,16]{2,1,0:T(8,128)(4,1)S(1)} %constant_dynamic-update-slice_fusion), kind=kOutput, calls=%fused_computation | convolution fusion | flops 125829120 | bytes 7340672 | tf_op jit(solution)/shard_map/otk,cotrw->ckrw/dot_general | solution.py:103
  25.3 0.2 copy.37
  25.5 0.1 dynamic-slice_bitcast_fusion.2
  25.7 0.6 %collective-permute-start.2 = (f32[2,16,16,128]{3,1,2,0:T(8,128)S(1)}, f32[2,16,16,128]{3,1,2,0:T(8,128)S(1)}, u32[]{:S(2)}, u32[]{:S(2)}) collective-permute-start(f32[2,16,16,128]{3,1,2,0:T(8,128)S(1)} %get-tuple-element.32), channel_id=1, source_target_pairs={{0,1},{1,2},{2,3},{3,0},{4,5},{5,6},{6,7},{7,4},{8,9},{9,10},{10,1... | collective-permute-start | bytes 786440 | tf_op jit(solution)/shard_map/ppermute | solution.py:60
  26.3 1.5 %collective-permute-start.4 = (f32[2,16,16,128]{3,1,2,0:T(8,128)S(1)}, f32[2,16,16,128]{3,1,2,0:T(8,128)S(1)}, u32[]{:S(2)}, u32[]{:S(2)}) collective-permute-start(f32[2,16,16,128]{3,1,2,0:T(8,128)S(1)} %get-tuple-element.33), channel_id=1, source_target_pairs={{0,3},{1,0},{2,1},{3,2},{4,7},{5,4},{6,5},{7,6},{8,11},{9,8},{10,9... | collective-permute-start | bytes 786440 | tf_op jit(solution)/shard_map/ppermute | solution.py:61
  27.8 5.9 %collective-permute-done.2 = f32[2,16,16,128]{3,1,2,0:T(8,128)S(1)} collective-permute-done((f32[2,16,16,128]{3,1,2,0:T(8,128)S(1)}, f32[2,16,16,128]{3,1,2,0:T(8,128)S(1)}, u32[]{:S(2)}, u32[]{:S(2)}) %collective-permute-start.2) | collective-permute-done | bytes 262176 | tf_op jit(solution)/shard_map/ppermute | solution.py:60
  33.7 0.1 slice_add_fusion.1
  33.8 0.9 %pad_maximum_fusion = f32[2,16,16,256]{3,1,2,0:T(8,128)} fusion(f32[2,16,16,128]{3,1,2,0:T(8,128)S(1)} %get-tuple-element.31, f32[2,16,16,128]{3,1,2,0:T(8,128)S(1)} %get-tuple-element.30), kind=kLoop, calls=%fused_computation.96 | loop fusion | flops 131072 | bytes 1048576 | tf_op jit(solution)/shard_map/concatenate | solution.py:63
  34.6 1.7 %collective-permute-start.3 = (f32[2,16,16,256]{3,1,2,0:T(8,128)}, f32[2,16,16,256]{3,1,2,0:T(8,128)S(1)}, u32[]{:S(2)}, u32[]{:S(2)}) collective-permute-start(f32[2,16,16,256]{3,1,2,0:T(8,128)} %pad_maximum_fusion), channel_id=1, source_target_pairs={{0,1},{1,2},{2,3},{3,0},{4,5},{5,6},{6,7},{7,4},{8,9},{9,10},{10,1... | collective-permute-start | bytes 1572872 | tf_op jit(solution)/shard_map/ppermute | solution.py:66
  36.4 0.8 %pad_maximum_fusion.1 = f32[2,16,16,256]{3,1,2,0:T(8,128)} fusion(f32[2,16,16,128]{3,1,2,0:T(8,128)S(1)} %get-tuple-element.35, f32[2,16,16,128]{3,1,2,0:T(8,128)S(1)} %get-tuple-element.34), kind=kLoop, calls=%fused_computation.97 | loop fusion | flops 131072 | bytes 1048576 | tf_op jit(solution)/shard_map/concatenate | solution.py:65
  37.2 0.3 collective-permute-start.5
  37.6 11.8 %collective-permute-done.3 = f32[2,16,16,256]{3,1,2,0:T(8,128)S(1)} collective-permute-done((f32[2,16,16,256]{3,1,2,0:T(8,128)}, f32[2,16,16,256]{3,1,2,0:T(8,128)S(1)}, u32[]{:S(2)}, u32[]{:S(2)}) %collective-permute-start.3) | collective-permute-done | bytes 524320 | tf_op jit(solution)/shard_map/ppermute | solution.py:66
  49.3 3.9 %collective-permute-done.5 = f32[2,16,16,256]{3,1,2,0:T(8,128)S(1)} collective-permute-done((f32[2,16,16,256]{3,1,2,0:T(8,128)}, f32[2,16,16,256]{3,1,2,0:T(8,128)S(1)}, u32[]{:S(2)}, u32[]{:S(2)}) %collective-permute-start.5) | collective-permute-done | bytes 524320 | tf_op jit(solution)/shard_map/ppermute | solution.py:67
  53.3 0.1 fusion.93
  53.5 0.9 %copy.24 = f32[16,16,256]{2,1,0:T(8,128)} copy(f32[16,16,256]{2,0,1:T(8,128)S(1)} %fusion.95) | data formatting | bytes 524288 | tf_op jit(solution)/shard_map/div | solution.py:108
  (28 shorter events, 0.7 us)
Async XLA Ops:
  0.0 8.3 %copy-start = (s32[32,16]{0,1:T(8,128)S(1)}, s32[32,16]{0,1:T(8,128)}, u32[]{:S(2)}) copy-start(s32[32,16]{0,1:T(8,128)} %param.7) | copy-start | bytes 6148
  0.0 7.9 %copy-start.1 = (f32[11,11]{1,0:T(8,128)S(1)}, f32[11,11]{1,0:T(8,128)}, u32[]{:S(2)}) copy-start(f32[11,11]{1,0:T(8,128)} %param.6) | copy-start | bytes 1456
  1.9 8.6 %collective-permute-start = (f32[2,8,21,256]{3,1,2,0:T(8,128)S(1)}, f32[2,8,21,256]{3,1,2,0:T(8,128)S(1)}, u32[]{:S(2)}, u32[]{:S(2)}) collective-permute-start(f32[2,8,21,256]{3,1,2,0:T(8,128)S(1)} %pad_maximum_fusion.2), channel_id=1, source_target_pairs={{0,4},{4,8},{8,12},{12,16},{16,20},{20,24},{24,28},{28,32},{32,36}... | collective-permute-start | bytes 1032200 | tf_op jit(solution)/shard_map/ppermute | solution.py:81
  3.9 8.4 %collective-permute-start.1 = (f32[2,8,21,256]{3,1,2,0:T(8,128)S(1)}, f32[2,8,21,256]{3,1,2,0:T(8,128)S(1)}, u32[]{:S(2)}, u32[]{:S(2)}) collective-permute-start(f32[2,8,21,256]{3,1,2,0:T(8,128)S(1)} %pad_maximum_fusion.3), channel_id=1, source_target_pairs={{4,0},{8,4},{12,8},{16,12},{20,16},{24,20},{28,24},{32,28},{36,32}... | collective-permute-start | bytes 1032200 | tf_op jit(solution)/shard_map/ppermute | solution.py:82
  25.7 8.0 %collective-permute-start.2 = (f32[2,16,16,128]{3,1,2,0:T(8,128)S(1)}, f32[2,16,16,128]{3,1,2,0:T(8,128)S(1)}, u32[]{:S(2)}, u32[]{:S(2)}) collective-permute-start(f32[2,16,16,128]{3,1,2,0:T(8,128)S(1)} %get-tuple-element.32), channel_id=1, source_target_pairs={{0,1},{1,2},{2,3},{3,0},{4,5},{5,6},{6,7},{7,4},{8,9},{9,10},{10,1... | collective-permute-start | bytes 786440 | tf_op jit(solution)/shard_map/ppermute | solution.py:60
  26.3 10.1 %collective-permute-start.4 = (f32[2,16,16,128]{3,1,2,0:T(8,128)S(1)}, f32[2,16,16,128]{3,1,2,0:T(8,128)S(1)}, u32[]{:S(2)}, u32[]{:S(2)}) collective-permute-start(f32[2,16,16,128]{3,1,2,0:T(8,128)S(1)} %get-tuple-element.33), channel_id=1, source_target_pairs={{0,3},{1,0},{2,1},{3,2},{4,7},{5,4},{6,5},{7,6},{8,11},{9,8},{10,9... | collective-permute-start | bytes 786440 | tf_op jit(solution)/shard_map/ppermute | solution.py:61
  34.6 14.7 %collective-permute-start.3 = (f32[2,16,16,256]{3,1,2,0:T(8,128)}, f32[2,16,16,256]{3,1,2,0:T(8,128)S(1)}, u32[]{:S(2)}, u32[]{:S(2)}) collective-permute-start(f32[2,16,16,256]{3,1,2,0:T(8,128)} %pad_maximum_fusion), channel_id=1, source_target_pairs={{0,1},{1,2},{2,3},{3,0},{4,5},{5,6},{6,7},{7,4},{8,9},{9,10},{10,1... | collective-permute-start | bytes 1572872 | tf_op jit(solution)/shard_map/ppermute | solution.py:66
  37.2 16.0 %collective-permute-start.5 = (f32[2,16,16,256]{3,1,2,0:T(8,128)}, f32[2,16,16,256]{3,1,2,0:T(8,128)S(1)}, u32[]{:S(2)}, u32[]{:S(2)}) collective-permute-start(f32[2,16,16,256]{3,1,2,0:T(8,128)} %pad_maximum_fusion.1), channel_id=1, source_target_pairs={{0,3},{1,0},{2,1},{3,2},{4,7},{5,4},{6,5},{7,6},{8,11},{9,8},{10,9... | collective-permute-start | bytes 1572872 | tf_op jit(solution)/shard_map/ppermute | solution.py:67

commit v18 on v17

--- a/solution.py
+++ b/solution.py
@@ -49,7 +49,7 @@
         return lax.psum_scatter(partial, axis, scatter_dimension=2, tiled=True)
     me = lax.axis_index(axis)
     rows = partial.shape[2] // count
-    half = partial.shape[3] // 2
+    half = partial.shape[1] // 2
     right = [(i, (i + 1) % count) for i in range(count)]
     left = [(i, (i - 1) % count) for i in range(count)]
 
@@ -57,12 +57,12 @@
         return lax.dynamic_slice_in_dim(partial, ((me + step) % count) * rows, rows, axis=2)
 
     far = block(2)
-    from_left = lax.ppermute(far[..., :half], axis, right)
-    from_right = lax.ppermute(far[..., half:], axis, left)
+    from_left = lax.ppermute(far[:, :half], axis, right)
+    from_right = lax.ppermute(far[:, half:], axis, left)
     ahead = block(1)
-    ahead = jnp.concatenate([ahead[..., :half] + from_left, ahead[..., half:]], axis=-1)
+    ahead = jnp.concatenate([ahead[:, :half] + from_left, ahead[:, half:]], axis=1)
     behind = block(count - 1)
-    behind = jnp.concatenate([behind[..., :half], behind[..., half:] + from_right], axis=-1)
+    behind = jnp.concatenate([behind[:, :half], behind[:, half:] + from_right], axis=1)
     got_left = lax.ppermute(ahead, axis, right)
     got_right = lax.ppermute(behind, axis, left)
     return block(0) + got_left + got_right

time: 54.6 us -> 54.5 us (level)
  no operation moved by 1% of the time
where the time goes in v18:
time: 54.5 us; the launch traced here: 54.3 us
  waiting for transfers between devices  24.9 us (46%)
  matrix products  12.3 us (23%)
  starting transfers between devices  9.69 us (18%)
  other arithmetic  4.48 us (8%)
  local copies, waits for them, and re-layouts  2.56 us (5%)
    ppermute x1, waiting for transfers between devices, ring_reduce_scatter(): got_left = lax.ppermute(ahead, axis, right)  11.8 us
    conv_general_dilated x2, matrix products, correlate_rows(): lax.conv_general_dilated(bordered, kernel, window_strides=(1,), padding='...  11 us
    ppermute x1, waiting for transfers between devices, ring_reduce_scatter(): from_left = lax.ppermute(far[:, :half], axis, right)  5.9 us
    ppermute x1, waiting for transfers between devices, ring_reduce_scatter(): got_right = lax.ppermute(behind, axis, left)  3.92 us
    ppermute x1, starting transfers between devices, shards(): lax.ppermute(jnp.stack([science[:, :width], inv_variance[:, :width]]), 's...  3.64 us
    ppermute x1, starting transfers between devices, shards(): lax.ppermute(jnp.stack([science[:, rows - width:], inv_variance[:, rows -...  1.92 us
    mul x1, other arithmetic, shards(): science * inv_variance  1.84 us
    ppermute x1, waiting for transfers between devices, shards(): lax.ppermute(jnp.stack([science[:, :width], inv_variance[:, :width]]), 's...  1.77 us
  transfers between devices with their start and end apart: 6, of which 5 were waited for; matrix products, arithmetic and copies ran while one was open for 6% of the time, Pallas kernels for 0%

profile of v18, /device:TPU:54, one launch (start us, length us, event | category | flops | bytes accessed | tf_op | source)
XLA Modules:
  0.0 54.3 jit_solution(2933688114236666856)
XLA Ops:
  0.0 1.8 %copy_multiply_fusion = (f32[8,64,256]{2,0,1:T(8,128)S(1)}, f32[8,64,256]{2,0,1:T(8,128)S(1)}, f32[8,64,256]{2,0,1:T(8,128)S(1)}) fusion(f32[8,64,256]{2,1,0:T(8,128)} %param.5, f32[8,64,256]{2,1,0:T(8,128)} %param.4), kind=kLoop, calls=%fused_computation.166 | loop fusion | flops 131072 | bytes 2621440 | tf_op jit(solution)/shard_map/mul | solution.py:84
  1.9 1.9 %collective-permute-start = (f32[2,8,21,256]{3,1,2,0:T(8,128)S(1)}, f32[2,8,21,256]{3,1,2,0:T(8,128)S(1)}, u32[]{:S(2)}, u32[]{:S(2)}) collective-permute-start(f32[2,8,21,256]{3,1,2,0:T(8,128)S(1)} %pad_maximum_fusion.2), channel_id=1, source_target_pairs={{0,4},{4,8},{8,12},{12,16},{16,20},{20,24},{24,28},{28,32},{32,36}... | collective-permute-start | bytes 1032200 | tf_op jit(solution)/shard_map/ppermute | solution.py:81
  3.9 3.6 %collective-permute-start.1 = (f32[2,8,21,256]{3,1,2,0:T(8,128)S(1)}, f32[2,8,21,256]{3,1,2,0:T(8,128)S(1)}, u32[]{:S(2)}, u32[]{:S(2)}) collective-permute-start(f32[2,8,21,256]{3,1,2,0:T(8,128)S(1)} %pad_maximum_fusion.3), channel_id=1, source_target_pairs={{4,0},{8,4},{12,8},{16,12},{20,16},{24,20},{28,24},{32,28},{36,32}... | collective-permute-start | bytes 1032200 | tf_op jit(solution)/shard_map/ppermute | solution.py:82
  7.5 0.1 fusion.96
  7.9 0.4 slice_reduce_fusion.21
  8.3 0.1 constant_dynamic-slice_fusion
  8.4 0.1 copy.29
  8.5 0.4 slice_reduce_fusion.10
  9.0 1.5 %collective-permute-done = f32[2,8,21,256]{3,1,2,0:T(8,128)S(1)} collective-permute-done((f32[2,8,21,256]{3,1,2,0:T(8,128)S(1)}, f32[2,8,21,256]{3,1,2,0:T(8,128)S(1)}, u32[]{:S(2)}, u32[]{:S(2)}) %collective-permute-start) | collective-permute-done | bytes 344096 | tf_op jit(solution)/shard_map/ppermute | solution.py:81
  10.5 1.8 %collective-permute-done.1 = f32[2,8,21,256]{3,1,2,0:T(8,128)S(1)} collective-permute-done((f32[2,8,21,256]{3,1,2,0:T(8,128)S(1)}, f32[2,8,21,256]{3,1,2,0:T(8,128)S(1)}, u32[]{:S(2)}, u32[]{:S(2)}) %collective-permute-start.1) | collective-permute-done | bytes 344096 | tf_op jit(solution)/shard_map/ppermute | solution.py:82
  12.3 5.4 %fusion.75 = f32[1,8,96,256]{3,1,2,0:T(8,128)S(1)} fusion(f32[11]{0:T(128)S(1)} %get-tuple-element.17, f32[11]{0:T(128)S(1)} %get-tuple-element.18, f32[11]{0:T(128)S(1)} %get-tuple-element.19, f32[11]{0:T(128)S(1)} %get-tuple-element.20, f32[11]{0:T(128)S(1)} %get-tuple-element.21, f32[11]{0:T(128)S(1)} %get-tuple-element.22, ...), kind=kOutput, calls=%fused_computation.75 | convolution fusion | flops 3330252800 | bytes 2376164 | tf_op jit(solution)/shard_map/conv_general_dilated | solution.py:35
  17.8 5.6 %fusion.72 = f32[1,8,96,256]{3,1,2,0:T(8,128)S(1)} fusion(f32[11]{0:T(128)S(1)} %get-tuple-element.15, f32[11]{0:T(128)S(1)} %get-tuple-element.6, f32[11]{0:T(128)S(1)} %get-tuple-element.7, f32[11]{0:T(128)S(1)} %get-tuple-element.8, f32[11]{0:T(128)S(1)} %get-tuple-element.9, f32[11]{0:T(128)S(1)} %get-tuple-element.10, f32[11]{0:T(128)S(1)} %get-tuple-element.11, ...), kind=kOutput, calls=%fused_computation.74 | convolution fusion | flops 3330252800 | bytes 2376164 | tf_op jit(solution)/shard_map/conv_general_dilated | solution.py:35
  23.3 0.2 maximum_select_fusion
  23.5 0.1 fusion.82
  23.6 0.1 fusion.81
  23.7 0.1 fusion.80
  23.8 0.1 fusion.79
  23.8 0.1 fusion.78
  23.9 1.4 %fusion = f32[2,64,256,16,1]{2,3,0,1,4:T(8,128)S(1)} fusion(f32[2,5,8,64,256]{4,2,3,0,1:T(8,128)S(1)} %fusion.78, pred[5,8,16]{2,1,0:T(8,128)(4,1)S(1)} %constant_dynamic-update-slice_fusion), kind=kOutput, calls=%fused_computation | convolution fusion | flops 125829120 | bytes 7340672 | tf_op jit(solution)/shard_map/otk,cotrw->ckrw/dot_general | solution.py:103
  25.3 0.2 copy.37
  25.5 0.1 dynamic-slice_bitcast_fusion.2
  25.7 0.6 %collective-permute-start.2 = (f32[2,8,16,256]{3,1,2,0:T(8,128)S(1)}, f32[2,8,16,256]{3,1,2,0:T(8,128)S(1)}, u32[]{:S(2)}, u32[]{:S(2)}) collective-permute-start(f32[2,8,16,256]{3,1,2,0:T(8,128)S(1)} %get-tuple-element.32), channel_id=1, source_target_pairs={{0,1},{1,2},{2,3},{3,0},{4,5},{5,6},{6,7},{7,4},{8,9},{9,10},{10,1... | collective-permute-start | bytes 786440 | tf_op jit(solution)/shard_map/ppermute | solution.py:60
  26.3 1.5 %collective-permute-start.4 = (f32[2,8,16,256]{3,1,2,0:T(8,128)S(1)}, f32[2,8,16,256]{3,1,2,0:T(8,128)S(1)}, u32[]{:S(2)}, u32[]{:S(2)}) collective-permute-start(f32[2,8,16,256]{3,1,2,0:T(8,128)S(1)} %get-tuple-element.33), channel_id=1, source_target_pairs={{0,3},{1,0},{2,1},{3,2},{4,7},{5,4},{6,5},{7,6},{8,11},{9,8},{10,9... | collective-permute-start | bytes 786440 | tf_op jit(solution)/shard_map/ppermute | solution.py:61
  27.8 5.9 %collective-permute-done.2 = f32[2,8,16,256]{3,1,2,0:T(8,128)S(1)} collective-permute-done((f32[2,8,16,256]{3,1,2,0:T(8,128)S(1)}, f32[2,8,16,256]{3,1,2,0:T(8,128)S(1)}, u32[]{:S(2)}, u32[]{:S(2)}) %collective-permute-start.2) | collective-permute-done | bytes 262176 | tf_op jit(solution)/shard_map/ppermute | solution.py:60
  33.8 0.8 %pad_maximum_fusion = f32[2,16,16,256]{3,1,2,0:T(8,128)} fusion(f32[2,8,16,256]{3,1,2,0:T(8,128)S(1)} %get-tuple-element.31, f32[2,8,16,256]{3,1,2,0:T(8,128)S(1)} %get-tuple-element.30), kind=kLoop, calls=%fused_computation.96 | loop fusion | flops 131072 | bytes 1048576 | tf_op jit(solution)/shard_map/concatenate | solution.py:63
  34.6 1.7 %collective-permute-start.3 = (f32[2,16,16,256]{3,1,2,0:T(8,128)}, f32[2,16,16,256]{3,1,2,0:T(8,128)S(1)}, u32[]{:S(2)}, u32[]{:S(2)}) collective-permute-start(f32[2,16,16,256]{3,1,2,0:T(8,128)} %pad_maximum_fusion), channel_id=1, source_target_pairs={{0,1},{1,2},{2,3},{3,0},{4,5},{5,6},{6,7},{7,4},{8,9},{9,10},{10,1... | collective-permute-start | bytes 1572872 | tf_op jit(solution)/shard_map/ppermute | solution.py:66
  36.4 0.8 %pad_maximum_fusion.1 = f32[2,16,16,256]{3,1,2,0:T(8,128)} fusion(f32[2,8,16,256]{3,1,2,0:T(8,128)S(1)} %get-tuple-element.35, f32[2,8,16,256]{3,1,2,0:T(8,128)S(1)} %get-tuple-element.34), kind=kLoop, calls=%fused_computation.97 | loop fusion | flops 131072 | bytes 1048576 | tf_op jit(solution)/shard_map/concatenate | solution.py:65
  37.2 0.3 collective-permute-start.5
  37.5 11.8 %collective-permute-done.3 = f32[2,16,16,256]{3,1,2,0:T(8,128)S(1)} collective-permute-done((f32[2,16,16,256]{3,1,2,0:T(8,128)}, f32[2,16,16,256]{3,1,2,0:T(8,128)S(1)}, u32[]{:S(2)}, u32[]{:S(2)}) %collective-permute-start.3) | collective-permute-done | bytes 524320 | tf_op jit(solution)/shard_map/ppermute | solution.py:66
  49.3 3.9 %collective-permute-done.5 = f32[2,16,16,256]{3,1,2,0:T(8,128)S(1)} collective-permute-done((f32[2,16,16,256]{3,1,2,0:T(8,128)}, f32[2,16,16,256]{3,1,2,0:T(8,128)S(1)}, u32[]{:S(2)}, u32[]{:S(2)}) %collective-permute-start.5) | collective-permute-done | bytes 524320 | tf_op jit(solution)/shard_map/ppermute | solution.py:67
  53.2 0.1 fusion.93
  53.4 0.9 %copy.24 = f32[16,16,256]{2,1,0:T(8,128)} copy(f32[16,16,256]{2,0,1:T(8,128)S(1)} %fusion.95) | data formatting | bytes 524288 | tf_op jit(solution)/shard_map/div | solution.py:108
  (28 shorter events, 0.7 us)
Async XLA Ops:
  0.0 8.3 %copy-start = (s32[32,16]{0,1:T(8,128)S(1)}, s32[32,16]{0,1:T(8,128)}, u32[]{:S(2)}) copy-start(s32[32,16]{0,1:T(8,128)} %param.7) | copy-start | bytes 6148
  0.0 7.9 %copy-start.1 = (f32[11,11]{1,0:T(8,128)S(1)}, f32[11,11]{1,0:T(8,128)}, u32[]{:S(2)}) copy-start(f32[11,11]{1,0:T(8,128)} %param.6) | copy-start | bytes 1456
  1.9 8.6 %collective-permute-start = (f32[2,8,21,256]{3,1,2,0:T(8,128)S(1)}, f32[2,8,21,256]{3,1,2,0:T(8,128)S(1)}, u32[]{:S(2)}, u32[]{:S(2)}) collective-permute-start(f32[2,8,21,256]{3,1,2,0:T(8,128)S(1)} %pad_maximum_fusion.2), channel_id=1, source_target_pairs={{0,4},{4,8},{8,12},{12,16},{16,20},{20,24},{24,28},{28,32},{32,36}... | collective-permute-start | bytes 1032200 | tf_op jit(solution)/shard_map/ppermute | solution.py:81
  3.9 8.4 %collective-permute-start.1 = (f32[2,8,21,256]{3,1,2,0:T(8,128)S(1)}, f32[2,8,21,256]{3,1,2,0:T(8,128)S(1)}, u32[]{:S(2)}, u32[]{:S(2)}) collective-permute-start(f32[2,8,21,256]{3,1,2,0:T(8,128)S(1)} %pad_maximum_fusion.3), channel_id=1, source_target_pairs={{4,0},{8,4},{12,8},{16,12},{20,16},{24,20},{28,24},{32,28},{36,32}... | collective-permute-start | bytes 1032200 | tf_op jit(solution)/shard_map/ppermute | solution.py:82
  25.7 8.0 %collective-permute-start.2 = (f32[2,8,16,256]{3,1,2,0:T(8,128)S(1)}, f32[2,8,16,256]{3,1,2,0:T(8,128)S(1)}, u32[]{:S(2)}, u32[]{:S(2)}) collective-permute-start(f32[2,8,16,256]{3,1,2,0:T(8,128)S(1)} %get-tuple-element.32), channel_id=1, source_target_pairs={{0,1},{1,2},{2,3},{3,0},{4,5},{5,6},{6,7},{7,4},{8,9},{9,10},{10,1... | collective-permute-start | bytes 786440 | tf_op jit(solution)/shard_map/ppermute | solution.py:60
  26.3 10.0 %collective-permute-start.4 = (f32[2,8,16,256]{3,1,2,0:T(8,128)S(1)}, f32[2,8,16,256]{3,1,2,0:T(8,128)S(1)}, u32[]{:S(2)}, u32[]{:S(2)}) collective-permute-start(f32[2,8,16,256]{3,1,2,0:T(8,128)S(1)} %get-tuple-element.33), channel_id=1, source_target_pairs={{0,3},{1,0},{2,1},{3,2},{4,7},{5,4},{6,5},{7,6},{8,11},{9,8},{10,9... | collective-permute-start | bytes 786440 | tf_op jit(solution)/shard_map/ppermute | solution.py:61
  34.6 14.7 %collective-permute-start.3 = (f32[2,16,16,256]{3,1,2,0:T(8,128)}, f32[2,16,16,256]{3,1,2,0:T(8,128)S(1)}, u32[]{:S(2)}, u32[]{:S(2)}) collective-permute-start(f32[2,16,16,256]{3,1,2,0:T(8,128)} %pad_maximum_fusion), channel_id=1, source_target_pairs={{0,1},{1,2},{2,3},{3,0},{4,5},{5,6},{6,7},{7,4},{8,9},{9,10},{10,1... | collective-permute-start | bytes 1572872 | tf_op jit(solution)/shard_map/ppermute | solution.py:66
  37.2 16.0 %collective-permute-start.5 = (f32[2,16,16,256]{3,1,2,0:T(8,128)}, f32[2,16,16,256]{3,1,2,0:T(8,128)S(1)}, u32[]{:S(2)}, u32[]{:S(2)}) collective-permute-start(f32[2,16,16,256]{3,1,2,0:T(8,128)} %pad_maximum_fusion.1), channel_id=1, source_target_pairs={{0,3},{1,0},{2,1},{3,2},{4,7},{5,4},{6,5},{7,6},{8,11},{9,8},{10,9... | collective-permute-start | bytes 1572872 | tf_op jit(solution)/shard_map/ppermute | solution.py:67

commit v19 on v18

--- a/solution.py
+++ b/solution.py
@@ -59,10 +59,11 @@
     far = block(2)
     from_left = lax.ppermute(far[:, :half], axis, right)
     from_right = lax.ppermute(far[:, half:], axis, left)
-    ahead = block(1)
-    ahead = jnp.concatenate([ahead[:, :half] + from_left, ahead[:, half:]], axis=1)
-    behind = block(count - 1)
-    behind = jnp.concatenate([behind[:, :half], behind[:, half:] + from_right], axis=1)
+    ahead, behind, from_left, from_right = lax.optimization_barrier(
+        (block(1), block(count - 1), from_left, from_right)
+    )
+    ahead = lax.dynamic_update_slice_in_dim(ahead, ahead[:, :half] + from_left, 0, axis=1)
+    behind = lax.dynamic_update_slice_in_dim(behind, behind[:, half:] + from_right, half, axis=1)
     got_left = lax.ppermute(ahead, axis, right)
     got_right = lax.ppermute(behind, axis, left)
     return block(0) + got_left + got_right

time: 54.5 us -> 54.7 us (level)
    ppermute x1, waiting for transfers between devices: 3.92 us -> 1.38 us  [ring_reduce_scatter(): got_right = lax.ppermute(behind, axis, left)]
    ppermute x1, waiting for transfers between devices: 0.01 us -> 2.01 us  [ring_reduce_scatter(): from_right = lax.ppermute(far[:, half:], axis, left)]
    concatenate x2 -> x0, other arithmetic: 1.67 us -> none  [the longest x1 0.85 us: ring_reduce_scatter(): jnp.concatenate([ahead[:, :half] + from_left, ahead[:, half:]], axis=1)]
    ppermute x1, starting transfers between devices: 0.34 us -> 1.83 us  [ring_reduce_scatter(): got_right = lax.ppermute(behind, axis, left)]
    ppermute x1, starting transfers between devices: 1.69 us -> 0.35 us  [ring_reduce_scatter(): got_left = lax.ppermute(ahead, axis, right)]
    add x1, other arithmetic: 0.14 us -> 1.37 us  [ring_reduce_scatter(): return block(0) + got_left + got_right]
    ppermute x1, waiting for transfers between devices: 11.8 us -> 12.5 us  [ring_reduce_scatter(): got_left = lax.ppermute(ahead, axis, right)]
  transfers between devices with their start and end apart: 6 -> 6, of which waited for: 5 -> 6; matrix products, arithmetic and copies ran while one was open for 6% -> 3% of each run, Pallas kernels for 0% -> 0%
where the time goes in v19:
time: 54.7 us; the launch traced here: 54.3 us
  waiting for transfers between devices  25.1 us (46%)
  matrix products  12.3 us (22%)
  starting transfers between devices  9.84 us (18%)
  other arithmetic  4.07 us (7%)
  local copies, waits for them, and re-layouts  2.59 us (5%)
    ppermute x1, waiting for transfers between devices, ring_reduce_scatter(): got_left = lax.ppermute(ahead, axis, right)  12.5 us
    conv_general_dilated x2, matrix products, correlate_rows(): lax.conv_general_dilated(bordered, kernel, window_strides=(1,), padding='...  11 us
    ppermute x1, waiting for transfers between devices, ring_reduce_scatter(): from_left = lax.ppermute(far[:, :half], axis, right)  5.9 us
    ppermute x1, starting transfers between devices, shards(): lax.ppermute(jnp.stack([science[:, :width], inv_variance[:, :width]]), 's...  3.64 us
    ppermute x1, waiting for transfers between devices, ring_reduce_scatter(): from_right = lax.ppermute(far[:, half:], axis, left)  2.01 us
    ppermute x1, starting transfers between devices, shards(): lax.ppermute(jnp.stack([science[:, rows - width:], inv_variance[:, rows -...  1.92 us
    mul x1, other arithmetic, shards(): science * inv_variance  1.84 us
    ppermute x1, starting transfers between devices, ring_reduce_scatter(): got_right = lax.ppermute(behind, axis, left)  1.83 us
  transfers between devices with their start and end apart: 6, of which 6 were waited for; matrix products, arithmetic and copies ran while one was open for 3% of the time, Pallas kernels for 0%

profile of v19, /device:TPU:54, one launch (start us, length us, event | category | flops | bytes accessed | tf_op | source)
XLA Modules:
  0.0 54.3 jit_solution(6417615700972884798)
XLA Ops:
  0.0 1.8 %copy_multiply_fusion = (f32[8,64,256]{2,0,1:T(8,128)S(1)}, f32[8,64,256]{2,0,1:T(8,128)S(1)}, f32[8,64,256]{2,0,1:T(8,128)S(1)}) fusion(f32[8,64,256]{2,1,0:T(8,128)} %param.5, f32[8,64,256]{2,1,0:T(8,128)} %param.4), kind=kLoop, calls=%fused_computation.164 | loop fusion | flops 131072 | bytes 2621440 | tf_op jit(solution)/shard_map/mul | solution.py:85
  1.9 1.9 %collective-permute-start = (f32[2,8,21,256]{3,1,2,0:T(8,128)S(1)}, f32[2,8,21,256]{3,1,2,0:T(8,128)S(1)}, u32[]{:S(2)}, u32[]{:S(2)}) collective-permute-start(f32[2,8,21,256]{3,1,2,0:T(8,128)S(1)} %pad_maximum_fusion), channel_id=1, source_target_pairs={{0,4},{4,8},{8,12},{12,16},{16,20},{20,24},{24,28},{28,32},{32,36}... | collective-permute-start | bytes 1032200 | tf_op jit(solution)/shard_map/ppermute | solution.py:82
  3.9 3.6 %collective-permute-start.1 = (f32[2,8,21,256]{3,1,2,0:T(8,128)S(1)}, f32[2,8,21,256]{3,1,2,0:T(8,128)S(1)}, u32[]{:S(2)}, u32[]{:S(2)}) collective-permute-start(f32[2,8,21,256]{3,1,2,0:T(8,128)S(1)} %pad_maximum_fusion.1), channel_id=1, source_target_pairs={{4,0},{8,4},{12,8},{16,12},{20,16},{24,20},{28,24},{32,28},{36,32}... | collective-permute-start | bytes 1032200 | tf_op jit(solution)/shard_map/ppermute | solution.py:83
  7.9 0.4 slice_reduce_fusion.21
  8.3 0.1 constant_dynamic-slice_fusion
  8.4 0.1 copy.29
  8.5 0.4 slice_reduce_fusion.10
  9.0 1.5 %collective-permute-done = f32[2,8,21,256]{3,1,2,0:T(8,128)S(1)} collective-permute-done((f32[2,8,21,256]{3,1,2,0:T(8,128)S(1)}, f32[2,8,21,256]{3,1,2,0:T(8,128)S(1)}, u32[]{:S(2)}, u32[]{:S(2)}) %collective-permute-start) | collective-permute-done | bytes 344096 | tf_op jit(solution)/shard_map/ppermute | solution.py:82
  10.5 1.8 %collective-permute-done.1 = f32[2,8,21,256]{3,1,2,0:T(8,128)S(1)} collective-permute-done((f32[2,8,21,256]{3,1,2,0:T(8,128)S(1)}, f32[2,8,21,256]{3,1,2,0:T(8,128)S(1)}, u32[]{:S(2)}, u32[]{:S(2)}) %collective-permute-start.1) | collective-permute-done | bytes 344096 | tf_op jit(solution)/shard_map/ppermute | solution.py:83
  12.3 5.4 %fusion.75 = f32[1,8,96,256]{3,1,2,0:T(8,128)S(1)} fusion(f32[11]{0:T(128)S(1)} %get-tuple-element.25, f32[11]{0:T(128)S(1)} %get-tuple-element.26, f32[11]{0:T(128)S(1)} %get-tuple-element.27, f32[11]{0:T(128)S(1)} %get-tuple-element.28, f32[11]{0:T(128)S(1)} %get-tuple-element.29, f32[11]{0:T(128)S(1)} %get-tuple-element.30, ...), kind=kOutput, calls=%fused_computation.75 | convolution fusion | flops 3330252800 | bytes 2376164 | tf_op jit(solution)/shard_map/conv_general_dilated | solution.py:35
  17.8 5.6 %fusion.72 = f32[1,8,96,256]{3,1,2,0:T(8,128)S(1)} fusion(f32[11]{0:T(128)S(1)} %get-tuple-element.23, f32[11]{0:T(128)S(1)} %get-tuple-element.14, f32[11]{0:T(128)S(1)} %get-tuple-element.15, f32[11]{0:T(128)S(1)} %get-tuple-element.16, f32[11]{0:T(128)S(1)} %get-tuple-element.17, f32[11]{0:T(128)S(1)} %get-tuple-element.18, ...), kind=kOutput, calls=%fused_computation.74 | convolution fusion | flops 3330252800 | bytes 2376164 | tf_op jit(solution)/shard_map/conv_general_dilated | solution.py:35
  23.3 0.2 maximum_select_fusion
  23.5 0.1 fusion.82
  23.6 0.1 fusion.81
  23.7 0.1 fusion.80
  23.8 0.1 fusion.79
  23.8 0.1 fusion.78
  23.9 1.4 %fusion = f32[2,64,256,16,1]{2,3,0,1,4:T(8,128)S(1)} fusion(f32[2,5,8,64,256]{4,2,3,0,1:T(8,128)S(1)} %fusion.78, pred[5,8,16]{2,1,0:T(8,128)(4,1)S(1)} %constant_dynamic-update-slice_fusion), kind=kOutput, calls=%fused_computation | convolution fusion | flops 125829120 | bytes 7340672 | tf_op jit(solution)/shard_map/otk,cotrw->ckrw/dot_general | solution.py:104
  25.3 0.2 copy.37
  25.5 0.2 dynamic-slice_bitcast_fusion
  25.7 0.6 %collective-permute-start.2 = (f32[2,8,16,256]{3,1,2,0:T(8,128)S(1)}, f32[2,8,16,256]{3,1,2,0:T(8,128)S(1)}, u32[]{:S(2)}, u32[]{:S(2)}) collective-permute-start(f32[2,8,16,256]{3,1,2,0:T(8,128)S(1)} %get-tuple-element.39), channel_id=1, source_target_pairs={{0,1},{1,2},{2,3},{3,0},{4,5},{5,6},{6,7},{7,4},{8,9},{9,10},{10,1... | collective-permute-start | bytes 786440 | tf_op jit(solution)/shard_map/ppermute | solution.py:60
  26.3 1.5 %collective-permute-start.3 = (f32[2,8,16,256]{3,1,2,0:T(8,128)S(1)}, f32[2,8,16,256]{3,1,2,0:T(8,128)S(1)}, u32[]{:S(2)}, u32[]{:S(2)}) collective-permute-start(f32[2,8,16,256]{3,1,2,0:T(8,128)S(1)} %get-tuple-element.38), channel_id=1, source_target_pairs={{0,3},{1,0},{2,1},{3,2},{4,7},{5,4},{6,5},{7,6},{8,11},{9,8},{10,9... | collective-permute-start | bytes 786440 | tf_op jit(solution)/shard_map/ppermute | solution.py:61
  27.8 5.9 %collective-permute-done.2 = f32[2,8,16,256]{3,1,2,0:T(8,128)S(1)} collective-permute-done((f32[2,8,16,256]{3,1,2,0:T(8,128)S(1)}, f32[2,8,16,256]{3,1,2,0:T(8,128)S(1)}, u32[]{:S(2)}, u32[]{:S(2)}) %collective-permute-start.2) | collective-permute-done | bytes 262176 | tf_op jit(solution)/shard_map/ppermute | solution.py:60
  33.7 2.0 %collective-permute-done.3 = f32[2,8,16,256]{3,1,2,0:T(8,128)S(1)} collective-permute-done((f32[2,8,16,256]{3,1,2,0:T(8,128)S(1)}, f32[2,8,16,256]{3,1,2,0:T(8,128)S(1)}, u32[]{:S(2)}, u32[]{:S(2)}) %collective-permute-start.3) | collective-permute-done | bytes 262176 | tf_op jit(solution)/shard_map/ppermute | solution.py:61
  35.7 0.1 add_dynamic-update-slice_fusion.1
  35.8 0.4 collective-permute-start.4
  36.2 0.1 add_dynamic-update-slice_fusion
  36.2 1.8 %collective-permute-start.5 = (f32[2,16,16,256]{3,1,2,0:T(8,128)S(1)}, f32[2,16,16,256]{3,1,2,0:T(8,128)}, u32[]{:S(2)}, u32[]{:S(2)}) collective-permute-start(f32[2,16,16,256]{3,1,2,0:T(8,128)S(1)} %add_dynamic-update-slice_fusion), channel_id=1, source_target_pairs={{0,3},{1,0},{2,1},{3,2},{4,7},{5,4},{6,5},{7,6},{8,11},{9,8},{10,9... | collective-permute-start | bytes 1572872 | tf_op jit(solution)/shard_map/ppermute | solution.py:68
  38.1 12.5 %collective-permute-done.4 = f32[2,16,16,256]{3,1,2,0:T(8,128)} collective-permute-done((f32[2,16,16,256]{3,1,2,0:T(8,128)S(1)}, f32[2,16,16,256]{3,1,2,0:T(8,128)}, u32[]{:S(2)}, u32[]{:S(2)}) %collective-permute-start.4) | collective-permute-done | bytes 524320 | tf_op jit(solution)/shard_map/ppermute | solution.py:67
  50.6 1.4 %collective-permute-done.5 = f32[2,16,16,256]{3,1,2,0:T(8,128)} collective-permute-done((f32[2,16,16,256]{3,1,2,0:T(8,128)S(1)}, f32[2,16,16,256]{3,1,2,0:T(8,128)}, u32[]{:S(2)}, u32[]{:S(2)}) %collective-permute-start.5) | collective-permute-done | bytes 524320 | tf_op jit(solution)/shard_map/ppermute | solution.py:68
  52.0 1.4 %fusion.93 = f32[2,16,16,256]{3,1,2,0:T(8,128)S(1)} fusion(f32[2,16,16,256]{3,1,2,0:T(8,128)} %collective-permute-done.5, f32[2,16,16,256]{3,1,2,0:T(8,128)} %collective-permute-done.4, f32[2,64,256,16]{2,3,1,0:T(8,128)S(1)} %bitcast.79, s32[]{:T(128)S(6)} %select_n.130), kind=kLoop, calls=%fused_computation.97 | loop fusion | flops 262144 | bytes 2097156 | tf_op jit(solution)/shard_map/add | solution.py:69
  53.4 0.9 %copy.24 = f32[16,16,256]{2,1,0:T(8,128)} copy(f32[16,16,256]{2,0,1:T(8,128)S(1)} %fusion.95) | data formatting | bytes 524288 | tf_op jit(solution)/shard_map/div | solution.py:109
  (26 shorter events, 0.7 us)
Async XLA Ops:
  0.0 8.3 %copy-start = (s32[32,16]{0,1:T(8,128)S(1)}, s32[32,16]{0,1:T(8,128)}, u32[]{:S(2)}) copy-start(s32[32,16]{0,1:T(8,128)} %param.7) | copy-start | bytes 6148
  0.0 7.9 %copy-start.1 = (f32[11,11]{1,0:T(8,128)S(1)}, f32[11,11]{1,0:T(8,128)}, u32[]{:S(2)}) copy-start(f32[11,11]{1,0:T(8,128)} %param.6) | copy-start | bytes 1456
  1.9 8.6 %collective-permute-start = (f32[2,8,21,256]{3,1,2,0:T(8,128)S(1)}, f32[2,8,21,256]{3,1,2,0:T(8,128)S(1)}, u32[]{:S(2)}, u32[]{:S(2)}) collective-permute-start(f32[2,8,21,256]{3,1,2,0:T(8,128)S(1)} %pad_maximum_fusion), channel_id=1, source_target_pairs={{0,4},{4,8},{8,12},{12,16},{16,20},{20,24},{24,28},{28,32},{32,36}... | collective-permute-start | bytes 1032200 | tf_op jit(solution)/shard_map/ppermute | solution.py:82
  3.9 8.4 %collective-permute-start.1 = (f32[2,8,21,256]{3,1,2,0:T(8,128)S(1)}, f32[2,8,21,256]{3,1,2,0:T(8,128)S(1)}, u32[]{:S(2)}, u32[]{:S(2)}) collective-permute-start(f32[2,8,21,256]{3,1,2,0:T(8,128)S(1)} %pad_maximum_fusion.1), channel_id=1, source_target_pairs={{4,0},{8,4},{12,8},{16,12},{20,16},{24,20},{28,24},{32,28},{36,32}... | collective-permute-start | bytes 1032200 | tf_op jit(solution)/shard_map/ppermute | solution.py:83
  25.7 8.0 %collective-permute-start.2 = (f32[2,8,16,256]{3,1,2,0:T(8,128)S(1)}, f32[2,8,16,256]{3,1,2,0:T(8,128)S(1)}, u32[]{:S(2)}, u32[]{:S(2)}) collective-permute-start(f32[2,8,16,256]{3,1,2,0:T(8,128)S(1)} %get-tuple-element.39), channel_id=1, source_target_pairs={{0,1},{1,2},{2,3},{3,0},{4,5},{5,6},{6,7},{7,4},{8,9},{9,10},{10,1... | collective-permute-start | bytes 786440 | tf_op jit(solution)/shard_map/ppermute | solution.py:60
  26.3 9.5 %collective-permute-start.3 = (f32[2,8,16,256]{3,1,2,0:T(8,128)S(1)}, f32[2,8,16,256]{3,1,2,0:T(8,128)S(1)}, u32[]{:S(2)}, u32[]{:S(2)}) collective-permute-start(f32[2,8,16,256]{3,1,2,0:T(8,128)S(1)} %get-tuple-element.38), channel_id=1, source_target_pairs={{0,3},{1,0},{2,1},{3,2},{4,7},{5,4},{6,5},{7,6},{8,11},{9,8},{10,9... | collective-permute-start | bytes 786440 | tf_op jit(solution)/shard_map/ppermute | solution.py:61
  35.8 14.8 %collective-permute-start.4 = (f32[2,16,16,256]{3,1,2,0:T(8,128)S(1)}, f32[2,16,16,256]{3,1,2,0:T(8,128)}, u32[]{:S(2)}, u32[]{:S(2)}) collective-permute-start(f32[2,16,16,256]{3,1,2,0:T(8,128)S(1)} %add_dynamic-update-slice_fusion.1), channel_id=1, source_target_pairs={{0,1},{1,2},{2,3},{3,0},{4,5},{5,6},{6,7},{7,4},{8,9},{9,10},{10,1... | collective-permute-start | bytes 1572872 | tf_op jit(solution)/shard_map/ppermute | solution.py:67
  36.2 15.7 %collective-permute-start.5 = (f32[2,16,16,256]{3,1,2,0:T(8,128)S(1)}, f32[2,16,16,256]{3,1,2,0:T(8,128)}, u32[]{:S(2)}, u32[]{:S(2)}) collective-permute-start(f32[2,16,16,256]{3,1,2,0:T(8,128)S(1)} %add_dynamic-update-slice_fusion), channel_id=1, source_target_pairs={{0,3},{1,0},{2,1},{3,2},{4,7},{5,4},{6,5},{7,6},{8,11},{9,8},{10,9... | collective-permute-start | bytes 1572872 | tf_op jit(solution)/shard_map/ppermute | solution.py:68

commit v20 on v18

--- a/solution.py
+++ b/solution.py
@@ -80,14 +80,26 @@
     backward = [(target, source) for source, target in forward]
     low = lax.ppermute(jnp.stack([science[:, rows - width :], inv_variance[:, rows - width :]]), "sky", forward)
     high = lax.ppermute(jnp.stack([science[:, :width], inv_variance[:, :width]]), "sky", backward)
-    bordered = [
-        jnp.concatenate([low[0] * low[1], science * inv_variance, high[0] * high[1]], axis=1),
-        jnp.concatenate([low[1], inv_variance, high[1]], axis=1),
-    ]
+    bordered = jnp.concatenate(
+        [
+            jnp.concatenate([low[0] * low[1], science * inv_variance, high[0] * high[1]], axis=1),
+            jnp.concatenate([low[1], inv_variance, high[1]], axis=1),
+        ],
+        axis=2,
+    )
 
-    psi = correlate_rows(bordered[0], toeplitz(psf_kernel, cols))
-    phi = correlate_rows(bordered[1], toeplitz(psf_kernel * psf_kernel, cols))
-    images = jnp.stack([psi, phi])
+    kernel = jnp.concatenate([toeplitz(psf_kernel, cols), toeplitz(psf_kernel * psf_kernel, cols)], axis=2)
+    both = lax.conv_general_dilated(
+        bordered,
+        kernel,
+        window_strides=(1,),
+        padding="VALID",
+        dimension_numbers=("NHC", "HIO", "NHC"),
+        feature_group_count=2,
+        precision=lax.Precision.HIGH,
+        preferred_element_type=jnp.float32,
+    )
+    images = jnp.stack([both[..., :cols], both[..., cols:]])
 
     first = lax.axis_index("sky") * rows - reach
     row_ids = first + lax.broadcasted_iota(jnp.int32, (1, 1, rows + 2 * reach, 1), 2)

time: 54.5 us -> 59.8 us (1.097)
  other arithmetic: 4.48 us -> 11.1 us
  local copies, waits for them, and re-layouts: 2.56 us -> 6.11 us
  waiting for transfers between devices: 24.9 us -> 21.6 us
  starting transfers between devices: 9.69 us -> 8.46 us
    select_n x0 -> x2, other arithmetic: none -> 8.14 us  [toeplitz(): out = jnp.where(tap == b, taps[:, b][:, None, None], out)]
    concatenate x0 -> x1, local copies, waits for them, and re-layouts: none -> 2.32 us  [shards(): jnp.concatenate([jnp.concatenate([low[0] * low[1], science * inv_variance...]
    ppermute x1, waiting for transfers between devices: 1.77 us -> 0.01 us  [shards(): lax.ppermute(jnp.stack([science[:, :width], inv_variance[:, :width]]), 's...]
    mul x1, other arithmetic: 1.84 us -> 0.1 us  [shards(): science * inv_variance]
    ppermute x1, starting transfers between devices: 3.64 us -> 1.92 us  [shards(): lax.ppermute(jnp.stack([science[:, :width], inv_variance[:, :width]]), 's...]
    ppermute x1, waiting for transfers between devices: 1.55 us -> 0.01 us  [shards(): lax.ppermute(jnp.stack([science[:, rows - width:], inv_variance[:, rows -...]
    another operation x1, local copies, waits for them, and re-layouts: 0.05 us -> 1.31 us  [shards(): jnp.stack([science[:, rows - width:], inv_variance[:, rows - width:]])]
    ppermute x1, waiting for transfers between devices: 5.9 us -> 6.64 us  [ring_reduce_scatter(): from_left = lax.ppermute(far[:, :half], axis, right)]
  transfers between devices with their start and end apart: 6 -> 6, of which waited for: 5 -> 3; matrix products, arithmetic and copies ran while one was open for 6% -> 19% of each run, Pallas kernels for 0% -> 0%
where the time goes in v20:
time: 59.8 us; the launch traced here: 59.4 us
  waiting for transfers between devices  21.6 us (36%)
  matrix products  11.8 us (20%)
  other arithmetic  11.1 us (19%)
  starting transfers between devices  8.46 us (14%)
  local copies, waits for them, and re-layouts  6.11 us (10%)
    ppermute x1, waiting for transfers between devices, ring_reduce_scatter(): got_left = lax.ppermute(ahead, axis, right)  11.8 us
    conv_general_dilated x1, matrix products, shards(): lax.conv_general_dilated(bordered, kernel, window_strides=(1,), padding='...  10.5 us
    select_n x2, other arithmetic, toeplitz(): out = jnp.where(tap == b, taps[:, b][:, None, None], out)  8.14 us
    ppermute x1, waiting for transfers between devices, ring_reduce_scatter(): from_left = lax.ppermute(far[:, :half], axis, right)  6.64 us
    ppermute x1, waiting for transfers between devices, ring_reduce_scatter(): got_right = lax.ppermute(behind, axis, left)  3.21 us
    ppermute x1, starting transfers between devices, shards(): lax.ppermute(jnp.stack([science[:, rows - width:], inv_variance[:, rows -...  2.41 us
    concatenate x1, local copies, waits for them, and re-layouts, shards(): jnp.concatenate([jnp.concatenate([low[0] * low[1], science * inv_variance...  2.32 us
    ppermute x1, starting transfers between devices, shards(): lax.ppermute(jnp.stack([science[:, :width], inv_variance[:, :width]]), 's...  1.92 us
  transfers between devices with their start and end apart: 6, of which 3 were waited for; matrix products, arithmetic and copies ran while one was open for 19% of the time, Pallas kernels for 0%

profile of v20, /device:TPU:54, one launch (start us, length us, event | category | flops | bytes accessed | tf_op | source)
XLA Modules:
  0.0 59.4 jit_solution(11298361477542272543)
XLA Ops:
  0.0 1.3 %slice_bitcast_fusion.13 = (f32[1,8,21,256]{3,2,1,0:T(8,128)S(1)}, f32[1,8,21,256]{3,2,1,0:T(8,128)S(1)}, f32[1,8,21,256]{3,2,1,0:T(8,128)S(1)}, f32[1,8,21,256]{3,2,1,0:T(8,128)S(1)}) fusion(f32[8,64,256]{2,1,0:T(8,128)} %param.5, f32[8,64,256]{2,1,0:T(8,128)} %param.4), kind=kLoop, calls=%fused_computation.56 | loop fusion | bytes 1376256 | tf_op jit(solution)/shard_map/stack | solution.py:81
  1.4 1.9 %collective-permute-start.1 = (f32[2,8,21,256]{3,2,1,0:T(8,128)S(1)}, f32[2,8,21,256]{3,2,1,0:T(8,128)S(1)}, u32[]{:S(2)}, u32[]{:S(2)}) collective-permute-start(f32[2,8,21,256]{3,2,1,0:T(8,128)S(1)} %pad_maximum_fusion.3), channel_id=1, source_target_pairs={{4,0},{8,4},{12,8},{16,12},{20,16},{24,20},{28,24},{32,28},{36,32}... | collective-permute-start | bytes 1032200 | tf_op jit(solution)/shard_map/ppermute | solution.py:82
  3.3 2.4 %collective-permute-start = (f32[2,8,21,256]{3,2,1,0:T(8,128)S(1)}, f32[2,8,21,256]{3,2,1,0:T(8,128)S(1)}, u32[]{:S(2)}, u32[]{:S(2)}) collective-permute-start(f32[2,8,21,256]{3,2,1,0:T(8,128)S(1)} %pad_maximum_fusion.2), channel_id=1, source_target_pairs={{0,4},{4,8},{8,12},{12,16},{16,20},{20,24},{24,28},{28,32},{32,36}... | collective-permute-start | bytes 1032200 | tf_op jit(solution)/shard_map/ppermute | solution.py:81
  6.1 0.4 slice_reduce_fusion.21
  6.5 0.4 slice_reduce_fusion.10
  6.9 0.1 constant_dynamic-slice_fusion
  7.0 0.1 copy.23
  7.1 4.1 %select_select_fusion.1 = f32[11,256,1,256]{3,1,2,0:T(8,128)} fusion(f32[11]{0:T(128)S(1)} %get-tuple-element.15, f32[11]{0:T(128)S(1)} %get-tuple-element.6, f32[11]{0:T(128)S(1)} %get-tuple-element.7, f32[11]{0:T(128)S(1)} %get-tuple-element.8, f32[11]{0:T(128)S(1)} %get-tuple-element.9, f32[11]{0:T(128)S(1)} %get-tuple-element.10, ...), kind=kLoop, calls=%fused_computation.5 | loop fusion | flops 7929856 | bytes 3604964 | tf_op jit(solution)/shard_map/jit(_where)/select_n | solution.py:30
  11.2 4.0 %select_select_fusion = f32[11,256,1,256]{3,1,2,0:T(8,128)} fusion(f32[11]{0:T(128)S(1)} %get-tuple-element.17, f32[11]{0:T(128)S(1)} %get-tuple-element.18, f32[11]{0:T(128)S(1)} %get-tuple-element.19, f32[11]{0:T(128)S(1)} %get-tuple-element.20, f32[11]{0:T(128)S(1)} %get-tuple-element.21, f32[11]{0:T(128)S(1)} %get-tuple-element.22, ...), kind=kLoop, calls=%fused_computation.4 | loop fusion | flops 7929856 | bytes 3604964 | tf_op jit(solution)/shard_map/jit(_where)/select_n | solution.py:30
  15.2 0.1 mul.32
  15.6 0.2 maximum_maximum_fusion
  15.8 2.3 %reshape.160 = f32[8,106,2,256]{3,2,1,0:T(2,128)} reshape(f32[8,106,512]{2,1,0:T(8,128)S(1)} %maximum_maximum_fusion) | data formatting | bytes 3473408 | tf_op jit(solution)/shard_map/concatenate | solution.py:83
  18.1 10.5 %fusion = f32[8,96,2,256]{3,0,2,1:T(8,128)S(1)} fusion(f32[11,256,1,256]{3,1,2,0:T(8,128)} %select_select_fusion, f32[11,256,1,256]{3,1,2,0:T(8,128)} %select_select_fusion.1, f32[8,106,2,256]{3,2,1,0:T(2,128)} %reshape.160), kind=kOutput, calls=%fused_computation | convolution fusion | flops 6645219328 | bytes 9076736 | tf_op jit(solution)/shard_map/conv_general_dilated | solution.py:92
  28.6 0.1 slice_bitcast_fusion.6
  28.7 0.2 maximum_select_fusion
  29.0 0.1 fusion.8
  29.1 0.1 fusion.7
  29.1 0.1 fusion.6
  29.2 0.1 fusion.5
  29.3 1.3 %convolution_bitcast_fusion = f32[2,64,256,16]{2,3,1,0:T(8,128)S(1)} fusion(f32[2,5,8,64,256]{4,2,1,3,0:T(8,128)S(1)} %fusion.5, pred[5,8,16]{2,1,0:T(8,128)(4,1)S(1)} %constant_dynamic-update-slice_fusion), kind=kOutput, calls=%fused_computation.8 | convolution fusion | flops 125829120 | bytes 7340672 | tf_op jit(solution)/shard_map/otk,cotrw->ckrw/dot_general | solution.py:115
  30.6 0.2 dynamic-slice_bitcast_fusion.2
  30.8 0.6 collective-permute-start.2
  31.4 1.5 %collective-permute-start.4 = (f32[2,8,16,256]{3,1,2,0:T(8,128)S(1)}, f32[2,8,16,256]{3,1,2,0:T(8,128)S(1)}, u32[]{:S(2)}, u32[]{:S(2)}) collective-permute-start(f32[2,8,16,256]{3,1,2,0:T(8,128)S(1)} %get-tuple-element.35), channel_id=1, source_target_pairs={{0,3},{1,0},{2,1},{3,2},{4,7},{5,4},{6,5},{7,6},{8,11},{9,8},{10,9... | collective-permute-start | bytes 786440 | tf_op jit(solution)/shard_map/ppermute | solution.py:61
  32.9 6.6 %collective-permute-done.2 = f32[2,8,16,256]{3,1,2,0:T(8,128)S(1)} collective-permute-done((f32[2,8,16,256]{3,1,2,0:T(8,128)S(1)}, f32[2,8,16,256]{3,1,2,0:T(8,128)S(1)}, u32[]{:S(2)}, u32[]{:S(2)}) %collective-permute-start.2) | collective-permute-done | bytes 262176 | tf_op jit(solution)/shard_map/ppermute | solution.py:60
  39.6 0.8 %pad_maximum_fusion = f32[2,16,16,256]{3,1,2,0:T(8,128)} fusion(f32[2,8,16,256]{3,1,2,0:T(8,128)S(1)} %get-tuple-element.33, f32[2,8,16,256]{3,1,2,0:T(8,128)S(1)} %get-tuple-element.32), kind=kLoop, calls=%fused_computation.22 | loop fusion | flops 131072 | bytes 1048576 | tf_op jit(solution)/shard_map/concatenate | solution.py:63
  40.5 1.7 %collective-permute-start.3 = (f32[2,16,16,256]{3,1,2,0:T(8,128)}, f32[2,16,16,256]{3,1,2,0:T(8,128)S(1)}, u32[]{:S(2)}, u32[]{:S(2)}) collective-permute-start(f32[2,16,16,256]{3,1,2,0:T(8,128)} %pad_maximum_fusion), channel_id=1, source_target_pairs={{0,1},{1,2},{2,3},{3,0},{4,5},{5,6},{6,7},{7,4},{8,9},{9,10},{10,1... | collective-permute-start | bytes 1572872 | tf_op jit(solution)/shard_map/ppermute | solution.py:66
  42.3 0.8 %pad_maximum_fusion.1 = f32[2,16,16,256]{3,1,2,0:T(8,128)} fusion(f32[2,8,16,256]{3,1,2,0:T(8,128)S(1)} %get-tuple-element.37, f32[2,8,16,256]{3,1,2,0:T(8,128)S(1)} %get-tuple-element.36), kind=kLoop, calls=%fused_computation.23 | loop fusion | flops 131072 | bytes 1048576 | tf_op jit(solution)/shard_map/concatenate | solution.py:65
  43.1 0.3 collective-permute-start.5
  43.4 11.8 %collective-permute-done.3 = f32[2,16,16,256]{3,1,2,0:T(8,128)S(1)} collective-permute-done((f32[2,16,16,256]{3,1,2,0:T(8,128)}, f32[2,16,16,256]{3,1,2,0:T(8,128)S(1)}, u32[]{:S(2)}, u32[]{:S(2)}) %collective-permute-start.3) | collective-permute-done | bytes 524320 | tf_op jit(solution)/shard_map/ppermute | solution.py:66
  55.2 3.2 %collective-permute-done.5 = f32[2,16,16,256]{3,1,2,0:T(8,128)S(1)} collective-permute-done((f32[2,16,16,256]{3,1,2,0:T(8,128)}, f32[2,16,16,256]{3,1,2,0:T(8,128)S(1)}, u32[]{:S(2)}, u32[]{:S(2)}) %collective-permute-start.5) | collective-permute-done | bytes 524320 | tf_op jit(solution)/shard_map/ppermute | solution.py:67
  58.4 0.1 fusion.10
  58.6 0.9 %copy.18 = f32[16,16,256]{2,1,0:T(8,128)} copy(f32[16,16,256]{2,0,1:T(8,128)S(1)} %fusion.12) | data formatting | bytes 524288 | tf_op jit(solution)/shard_map/div | solution.py:120
  (35 shorter events, 0.8 us)
Async XLA Ops:
  0.0 6.9 %copy-start = (s32[32,16]{0,1:T(8,128)S(1)}, s32[32,16]{0,1:T(8,128)}, u32[]{:S(2)}) copy-start(s32[32,16]{0,1:T(8,128)} %param.7) | copy-start | bytes 6148
  0.0 6.1 %copy-start.3 = (f32[11,11]{1,0:T(8,128)S(1)}, f32[11,11]{1,0:T(8,128)}, u32[]{:S(2)}) copy-start(f32[11,11]{1,0:T(8,128)} %param.6) | copy-start | bytes 1456
  1.4 14.1 %collective-permute-start.1 = (f32[2,8,21,256]{3,2,1,0:T(8,128)S(1)}, f32[2,8,21,256]{3,2,1,0:T(8,128)S(1)}, u32[]{:S(2)}, u32[]{:S(2)}) collective-permute-start(f32[2,8,21,256]{3,2,1,0:T(8,128)S(1)} %pad_maximum_fusion.3), channel_id=1, source_target_pairs={{4,0},{8,4},{12,8},{16,12},{20,16},{24,20},{28,24},{32,28},{36,32}... | collective-permute-start | bytes 1032200 | tf_op jit(solution)/shard_map/ppermute | solution.py:82
  3.3 12.2 %collective-permute-start = (f32[2,8,21,256]{3,2,1,0:T(8,128)S(1)}, f32[2,8,21,256]{3,2,1,0:T(8,128)S(1)}, u32[]{:S(2)}, u32[]{:S(2)}) collective-permute-start(f32[2,8,21,256]{3,2,1,0:T(8,128)S(1)} %pad_maximum_fusion.2), channel_id=1, source_target_pairs={{0,4},{4,8},{8,12},{12,16},{16,20},{20,24},{24,28},{28,32},{32,36}... | collective-permute-start | bytes 1032200 | tf_op jit(solution)/shard_map/ppermute | solution.py:81
  7.1 8.2 %copy-start.1 = (f32[8,64,256]{2,1,0:T(8,128)S(1)}, f32[8,64,256]{2,1,0:T(8,128)}, u32[]{:S(2)}) copy-start(f32[8,64,256]{2,1,0:T(8,128)} %param.5) | copy-start | bytes 1572868
  7.1 8.2 %copy-start.2 = (f32[8,64,256]{2,1,0:T(8,128)S(1)}, f32[8,64,256]{2,1,0:T(8,128)}, u32[]{:S(2)}) copy-start(f32[8,64,256]{2,1,0:T(8,128)} %param.4) | copy-start | bytes 1572868
  30.8 8.7 %collective-permute-start.2 = (f32[2,8,16,256]{3,1,2,0:T(8,128)S(1)}, f32[2,8,16,256]{3,1,2,0:T(8,128)S(1)}, u32[]{:S(2)}, u32[]{:S(2)}) collective-permute-start(f32[2,8,16,256]{3,1,2,0:T(8,128)S(1)} %get-tuple-element.34), channel_id=1, source_target_pairs={{0,1},{1,2},{2,3},{3,0},{4,5},{5,6},{6,7},{7,4},{8,9},{9,10},{10,1... | collective-permute-start | bytes 786440 | tf_op jit(solution)/shard_map/ppermute | solution.py:60
  31.4 10.8 %collective-permute-start.4 = (f32[2,8,16,256]{3,1,2,0:T(8,128)S(1)}, f32[2,8,16,256]{3,1,2,0:T(8,128)S(1)}, u32[]{:S(2)}, u32[]{:S(2)}) collective-permute-start(f32[2,8,16,256]{3,1,2,0:T(8,128)S(1)} %get-tuple-element.35), channel_id=1, source_target_pairs={{0,3},{1,0},{2,1},{3,2},{4,7},{5,4},{6,5},{7,6},{8,11},{9,8},{10,9... | collective-permute-start | bytes 786440 | tf_op jit(solution)/shard_map/ppermute | solution.py:61
  40.5 14.7 %collective-permute-start.3 = (f32[2,16,16,256]{3,1,2,0:T(8,128)}, f32[2,16,16,256]{3,1,2,0:T(8,128)S(1)}, u32[]{:S(2)}, u32[]{:S(2)}) collective-permute-start(f32[2,16,16,256]{3,1,2,0:T(8,128)} %pad_maximum_fusion), channel_id=1, source_target_pairs={{0,1},{1,2},{2,3},{3,0},{4,5},{5,6},{6,7},{7,4},{8,9},{9,10},{10,1... | collective-permute-start | bytes 1572872 | tf_op jit(solution)/shard_map/ppermute | solution.py:66
  43.1 15.3 %collective-permute-start.5 = (f32[2,16,16,256]{3,1,2,0:T(8,128)}, f32[2,16,16,256]{3,1,2,0:T(8,128)S(1)}, u32[]{:S(2)}, u32[]{:S(2)}) collective-permute-start(f32[2,16,16,256]{3,1,2,0:T(8,128)} %pad_maximum_fusion.1), channel_id=1, source_target_pairs={{0,3},{1,0},{2,1},{3,2},{4,7},{5,4},{6,5},{7,6},{8,11},{9,8},{10,9... | collective-permute-start | bytes 1572872 | tf_op jit(solution)/shard_map/ppermute | solution.py:67
